TPU v7x, 32 devices: a whole 2x2x4 slice. The times are simulated.
32 devices in a mesh: groups: 2 (over x), seq: 16 (over z, y, core).
Axes of the slice: x: 2, y: 2, z: 4, core: 2. Of those that a mesh axis runs over, the one named last changes fastest.
Arguments:
- video_q: bfloat16 [16384, 2048], P(('groups', 'seq')), parts along dimension 0, may hold values from -64 to 64
- video_k: bfloat16 [16384, 2048], P(('groups', 'seq')), parts along dimension 0, may hold values from -6 to 6
- video_v: bfloat16 [16384, 2048], P(('groups', 'seq')), parts along dimension 0, may hold values from -4 to 4
- audio_q: bfloat16 [256, 2048], P(('groups', 'seq')), parts along dimension 0, may hold values from -64 to 64
- audio_k: bfloat16 [256, 2048], P(('groups', 'seq')), parts along dimension 0, may hold values from -6 to 6
- audio_v: bfloat16 [256, 2048], P(('groups', 'seq')), parts along dimension 0, may hold values from -4 to 4
Outputs:
- video_out: bfloat16 [16384, 2048], P(('groups', 'seq')), parts along dimension 0
- audio_out: bfloat16 [256, 2048], P(('groups', 'seq')), parts along dimension 0
There are 2 independent parts, one for each index of `groups`. A program takes and returns all parts, laid end to end along the dimension named above; each array names one. Nothing has to cross between parts.
All inputs are finite; a program needn't handle non-finite values.
Results may differ from a plain program's by a relative error of at most 0.007.
Values may be sent and summed in bfloat16 or wider, within the bound.
No kernel may reach another device: no remote copies, remote signals or barrier semaphores. Data moves between devices by JAX's collectives and lax.ppermute only.
A program may use at most 128 MiB of HBM per device.

v0:
```python
import math

import jax
import jax.numpy as jnp
from jax import lax
from jax.sharding import PartitionSpec as P

lowest_score = -1e30


def spread(scales):
    return jnp.repeat(scales, 64, axis=1)


def partial_block(queries, keys, values):
    head_count = queries.shape[1] // 64
    query_heads = queries.reshape(queries.shape[0], head_count, 64)
    key_heads = keys.reshape(keys.shape[0], head_count, 64)
    value_heads = values.reshape(values.shape[0], head_count, 64)
    scores = (
        jnp.einsum("rhd,shd->hrs", query_heads, key_heads, preferred_element_type=jnp.float32)
        * 0.125
    )
    highest = jnp.max(scores, axis=2)
    weights = jnp.exp(scores - highest[:, :, None])
    totals = jnp.sum(weights, axis=2)
    summed = jnp.einsum(
        "hrs,shd->rhd",
        weights.astype(jnp.bfloat16),
        value_heads,
        preferred_element_type=jnp.float32,
    )
    return (highest.T, totals.T, summed.reshape(queries.shape[0], head_count * 64))


def combine(earlier, later):
    highest = jnp.maximum(earlier[0], later[0])
    earlier_scale = jnp.exp(earlier[0] - highest)
    later_scale = jnp.exp(later[0] - highest)
    totals = earlier[1] * earlier_scale + later[1] * later_scale
    summed = earlier[2] * spread(earlier_scale) + later[2] * spread(later_scale)
    return (highest, totals, summed)


def blocked_partial(queries, keys, values):
    row_count = queries.shape[0]
    model_width = queries.shape[1]
    block_rows = math.gcd(row_count, 128)
    stacked = queries.reshape(row_count // block_rows, block_rows, model_width)
    newest = lax.map(lambda query_rows: partial_block(query_rows, keys, values), stacked)
    return tuple((member.reshape(row_count, member.shape[2]) for member in newest))


def empty_state(row_count, model_width):
    head_count = model_width // 64
    return (
        jnp.full((row_count, head_count), lowest_score, jnp.float32),
        jnp.zeros((row_count, head_count), jnp.float32),
        jnp.zeros((row_count, model_width), jnp.float32),
    )


def local(video_q, video_k, video_v, audio_q, audio_k, audio_v):
    tok_rows = video_q.shape[0]
    model_width = video_q.shape[1]
    pieces = (
        lax.all_gather(audio_k, "seq", axis=0, tiled=True),
        lax.all_gather(audio_v, "seq", axis=0, tiled=True),
    )
    newest = blocked_partial(video_q, pieces[0], pieces[1])
    highest, totals, summed = combine(empty_state(tok_rows, model_width), newest)
    video_out = (summed / spread(totals)).astype(jnp.bfloat16)
    key_heads, value_heads, query_heads = (
        lax.all_to_all(video_k, "seq", split_axis=1, concat_axis=0, tiled=True),
        lax.all_to_all(video_v, "seq", split_axis=1, concat_axis=0, tiled=True),
        lax.all_to_all(audio_q, "seq", split_axis=1, concat_axis=0, tiled=True),
    )
    total_keys = key_heads.shape[0]
    columns = key_heads.shape[1]
    key_block = math.gcd(total_keys, 4096)
    block_count = total_keys // key_block

    def advance(running, pieces):
        return (combine(running, partial_block(query_heads, pieces[0], pieces[1])), None)

    state, ignored = lax.scan(
        advance,
        empty_state(query_heads.shape[0], columns),
        (
            key_heads.reshape(block_count, key_block, columns),
            value_heads.reshape(block_count, key_block, columns),
        ),
    )
    head_out = (state[2] / spread(state[1])).astype(jnp.bfloat16)
    audio_out = lax.all_to_all(head_out, "seq", split_axis=0, concat_axis=1, tiled=True)
    return (video_out, audio_out)


def solution(mesh):
    placed = (
        P(("groups", "seq"), None),
        P(("groups", "seq"), None),
        P(("groups", "seq"), None),
        P(("groups", "seq"), None),
        P(("groups", "seq"), None),
        P(("groups", "seq"), None),
    )
    return jax.shard_map(
        local,
        mesh=mesh,
        in_specs=placed,
        out_specs=(P(("groups", "seq"), None), P(("groups", "seq"), None)),
        check_vma=False,
    )
```

profile of v0, /device:TPU:0, one launch (start us, length us, event | category | flops | bytes accessed | tf_op | source)
XLA Modules:
  0.0 264.3 jit_solution(13597468701080333482)
XLA Ops:
  0.6 7.4 %all-to-all-start.1 = ((bf16[8,16,128]{2,0,1:T(8,128)(2,1)}), bf16[8,16,128]{2,0,1:T(8,128)(2,1)S(1)}, u32[]{:S(2)}, u32[]{:S(2)}) async-start(bf16[8,16,128]{2,0,1:T(8,128)(2,1)} %bitcast.158), calls=%async_computation.1 | async-start | bytes 65536 | tf_op jit(solution)/shard_map/all_to_all | solution.py:76
  8.0 3.9 %copy.57 = bf16[512,2048]{0,1:T(8,128)(2,1)} copy(bf16[512,2048]{1,0:T(8,128)(2,1)} %param.11) | data formatting | bytes 4194304 | tf_op args[1]
  12.0 2.7 %all-to-all-done.1 = bf16[8,16,128]{2,0,1:T(8,128)(2,1)S(1)} async-done(((bf16[8,16,128]{2,0,1:T(8,128)(2,1)}), bf16[8,16,128]{2,0,1:T(8,128)(2,1)S(1)}, u32[]{:S(2)}, u32[]{:S(2)}) %all-to-all-start.1) | async-done | bytes 32800 | tf_op jit(solution)/shard_map/all_to_all | solution.py:76
  14.7 4.6 %all-to-all-start = ((bf16[512,16,128]{0,2,1:T(8,128)(2,1)}), bf16[512,16,128]{0,2,1:T(8,128)(2,1)}, u32[]{:S(2)}, u32[]{:S(2)}) async-start(bf16[512,16,128]{0,2,1:T(8,128)(2,1)} %bitcast.13), calls=%async_computation | async-start | bytes 4194304 | tf_op jit(solution)/shard_map/all_to_all | solution.py:74
  19.3 56.4 %all_gather.6 = bf16[128,2048]{1,0:T(8,128)(2,1)S(1)} all-gather(bf16[8,2048]{1,0:T(8,128)(2,1)S(1)} %copy-done.1), channel_id=1, replica_groups=mesh['groups'=2,'seq'=16] {'seq'}, dimensions={0}, use_global_device_ids=true | all-gather | bytes 557056 | tf_op jit(solution)/shard_map/all_gather | solution.py:67
  76.0 25.5 %all_gather.7 = bf16[128,2048]{1,0:T(8,128)(2,1)} all-gather(bf16[8,2048]{1,0:T(8,128)(2,1)S(1)} %copy-done.2), channel_id=1, replica_groups=mesh['groups'=2,'seq'=16] {'seq'}, dimensions={0}, use_global_device_ids=true | all-gather | bytes 557056 | tf_op jit(solution)/shard_map/all_gather | solution.py:68
  101.5 1.3 copy.53
  102.9 2.6 copy.59
  105.4 4.5 %all-to-all-start.2 = ((bf16[512,16,128]{0,2,1:T(8,128)(2,1)}), bf16[512,16,128]{0,2,1:T(8,128)(2,1)}, u32[]{:S(2)}, u32[]{:S(2)}) async-start(bf16[512,16,128]{0,2,1:T(8,128)(2,1)} %bitcast.19), calls=%async_computation.2 | async-start | bytes 4194304 | tf_op jit(solution)/shard_map/all_to_all | solution.py:75
  109.9 122.1 %while.29 = (s32[]{:T(128)}, f32[4,128,32]{1,0,2:T(4,128)S(1)}, f32[4,128,32]{1,0,2:T(4,128)S(1)}, f32[4,128,2048]{1,0,2:T(4,128)}, bf16[4,128,2048]{2,1,0:T(8,1...) while((s32[]{:T(128)}, f32[4,128,32]{1,0,2:T(4,128)S(1)}, ...), condition=%wide.region_3.4_spmd, body=%wide.region_0.3_spmd.sunk | while | flops 138403840 | bytes 13238389 | solution.py:50
  109.9 1.1 constant_dynamic-slice_fusion.5
  111.3 0.5 multiply_reduce_fusion.2
  112.2 0.5 fusion.56
  112.9 27.5 %dynamic_update_slice.16 = f32[4,128,2048]{1,0,2:T(4,128)} dynamic-update-slice(f32[4,128,2048]{1,0,2:T(4,128)} %get-tuple-element.322, f32[1,128,2048]{1,0,2:T(1,128)S(1)} %bitcast.142, s32[]{:T(128)S(6)} %copy.101, s32[]{:T(128)} %constant.28.clone.1..sunk, s32[]{:T(128)} %constant.28.clone.1..sunk) | dynamic-update-slice | bytes 2097156 | tf_op jit(solution)/shard_map/while/body/jit(dynamic_update_index_in_dim)/dynamic_update_slice | solution.py:50
  140.4 1.1 constant_dynamic-slice_fusion.5
  141.8 0.5 multiply_reduce_fusion.2
  142.3 0.4 fusion.55
  142.7 0.5 fusion.56
  143.4 27.5 %dynamic_update_slice.16 = f32[4,128,2048]{1,0,2:T(4,128)} dynamic-update-slice(f32[4,128,2048]{1,0,2:T(4,128)} %get-tuple-element.322, f32[1,128,2048]{1,0,2:T(1,128)S(1)} %bitcast.142, s32[]{:T(128)S(6)} %copy.101, s32[]{:T(128)} %constant.28.clone.1..sunk, s32[]{:T(128)} %constant.28.clone.1..sunk) | dynamic-update-slice | bytes 2097156 | tf_op jit(solution)/shard_map/while/body/jit(dynamic_update_index_in_dim)/dynamic_update_slice | solution.py:50
  170.9 1.1 constant_dynamic-slice_fusion.5
  172.3 0.5 multiply_reduce_fusion.2
  173.2 0.5 fusion.56
  173.9 27.5 %dynamic_update_slice.16 = f32[4,128,2048]{1,0,2:T(4,128)} dynamic-update-slice(f32[4,128,2048]{1,0,2:T(4,128)} %get-tuple-element.322, f32[1,128,2048]{1,0,2:T(1,128)S(1)} %bitcast.142, s32[]{:T(128)S(6)} %copy.101, s32[]{:T(128)} %constant.28.clone.1..sunk, s32[]{:T(128)} %constant.28.clone.1..sunk) | dynamic-update-slice | bytes 2097156 | tf_op jit(solution)/shard_map/while/body/jit(dynamic_update_index_in_dim)/dynamic_update_slice | solution.py:50
  201.4 1.1 constant_dynamic-slice_fusion.5
  202.8 0.5 multiply_reduce_fusion.2
  203.7 0.5 fusion.56
  204.4 27.5 %dynamic_update_slice.16 = f32[4,128,2048]{1,0,2:T(4,128)} dynamic-update-slice(f32[4,128,2048]{1,0,2:T(4,128)} %get-tuple-element.322, f32[1,128,2048]{1,0,2:T(1,128)S(1)} %bitcast.142, s32[]{:T(128)S(6)} %copy.101, s32[]{:T(128)} %constant.28.clone.1..sunk, s32[]{:T(128)} %constant.28.clone.1..sunk) | dynamic-update-slice | bytes 2097156 | tf_op jit(solution)/shard_map/while/body/jit(dynamic_update_index_in_dim)/dynamic_update_slice | solution.py:50
  232.1 3.9 %copy.58 = bf16[16,512,128]{2,1,0:T(8,128)(2,1)} copy(bf16[16,512,128]{1,2,0:T(8,128)(2,1)} %bitcast.14) | data formatting | bytes 4194304 | tf_op jit(solution)/shard_map/all_to_all | solution.py:74
  236.0 3.9 %copy.60 = bf16[16,512,128]{2,1,0:T(8,128)(2,1)} copy(bf16[16,512,128]{1,2,0:T(8,128)(2,1)} %bitcast.20) | data formatting | bytes 4194304 | tf_op jit(solution)/shard_map/all_to_all | solution.py:75
  239.9 10.5 %while.30 = (s32[]{:T(128)}, f32[128,2]{0,1:T(2,128)S(1)}, f32[128,2]{0,1:T(2,128)S(1)}, f32[128,128]{0,1:T(8,128)S(1)}, bf16[2,4096,128]{2,1,0:T(8,128)(2,1)}, ...) while((s32[]{:T(128)}, f32[128,2]{0,1:T(2,128)S(1)}, ...), condition=%wide.region_7.8_spmd.clone, body=%wide.region_4.7_spmd.clone.sunk | while | flops 274793984 | bytes 23378036 | solution.py:86
  239.9 1.7 constant_dynamic-slice_fusion.6
  241.6 0.5 copy.92
  242.1 0.5 copy.93
  242.7 0.9 fusion.61
  243.6 0.6 fusion.62
  244.2 0.9 fusion.64
  245.2 1.7 constant_dynamic-slice_fusion.6
  246.9 0.5 copy.92
  247.4 0.5 copy.93
  247.9 0.9 fusion.61
  248.9 0.6 fusion.62
  249.5 0.9 fusion.64
  250.5 0.7 copy.64
  251.2 5.9 %all-to-all-start.3 = ((bf16[16,8,128]{2,1,0:T(8,128)(2,1)}), bf16[16,8,128]{2,1,0:T(8,128)(2,1)S(1)}, u32[]{:S(2)}, u32[]{:S(2)}) async-start(bf16[16,8,128]{2,1,0:T(8,128)(2,1)} %bitcast.23), calls=%async_computation.3 | async-start | bytes 65536 | tf_op jit(solution)/shard_map/all_to_all | solution.py:95
  257.1 2.9 %fusion.23 = bf16[512,2048]{0,1:T(8,128)(2,1)S(1)} fusion(f32[256,8,4,128]{3,2,1,0:T(4,128)} %bitcast.150, f32[512,32]{0,1:T(8,128)S(1)} %get-tuple-element.202, f32[512,32]{0,1:T(8,128)S(1)} %get-tuple-element.203, f32[512,32]{0,1:T(8,128)S(1)} %get-tuple-element.201), kind=kLoop, calls=%fused_computation.33 | loop fusion | flops 4194304 | bytes 6488064 | tf_op jit(solution)/shard_map/convert_element_type | solution.py:72
  260.0 2.4 copy.65
  262.4 1.3 all-to-all-done.3
  263.7 0.6 copy.122
  (37 shorter events, 3.6 us)
Async XLA Ops:
  0.6 14.0 %all-to-all-start.1 = ((bf16[8,16,128]{2,0,1:T(8,128)(2,1)}), bf16[8,16,128]{2,0,1:T(8,128)(2,1)S(1)}, u32[]{:S(2)}, u32[]{:S(2)}) async-start(bf16[8,16,128]{2,0,1:T(8,128)(2,1)} %bitcast.158), calls=%async_computation.1 | async-start | bytes 65536 | tf_op jit(solution)/shard_map/all_to_all | solution.py:76
  14.7 4.6 %copy-start.1 = (bf16[8,2048]{1,0:T(8,128)(2,1)S(1)}, bf16[8,2048]{1,0:T(8,128)(2,1)}, u32[]{:S(2)}) copy-start(bf16[8,2048]{1,0:T(8,128)(2,1)} %param.14) | copy-start | bytes 98308
  14.7 61.4 %copy-start.2 = (bf16[8,2048]{1,0:T(8,128)(2,1)S(1)}, bf16[8,2048]{1,0:T(8,128)(2,1)}, u32[]{:S(2)}) copy-start(bf16[8,2048]{1,0:T(8,128)(2,1)} %param.15) | copy-start | bytes 98308
  14.7 90.8 %all-to-all-start = ((bf16[512,16,128]{0,2,1:T(8,128)(2,1)}), bf16[512,16,128]{0,2,1:T(8,128)(2,1)}, u32[]{:S(2)}, u32[]{:S(2)}) async-start(bf16[512,16,128]{0,2,1:T(8,128)(2,1)} %bitcast.13), calls=%async_computation | async-start | bytes 4194304 | tf_op jit(solution)/shard_map/all_to_all | solution.py:74
  19.2 83.6 %copy-start = (bf16[512,2048]{1,0:T(8,128)(2,1)S(1)}, bf16[512,2048]{1,0:T(8,128)(2,1)}, u32[]{:S(2)}) copy-start(bf16[512,2048]{1,0:T(8,128)(2,1)} %param.12) | copy-start | bytes 6291460
  105.4 130.6 %all-to-all-start.2 = ((bf16[512,16,128]{0,2,1:T(8,128)(2,1)}), bf16[512,16,128]{0,2,1:T(8,128)(2,1)}, u32[]{:S(2)}, u32[]{:S(2)}) async-start(bf16[512,16,128]{0,2,1:T(8,128)(2,1)} %bitcast.19), calls=%async_computation.2 | async-start | bytes 4194304 | tf_op jit(solution)/shard_map/all_to_all | solution.py:75
  251.2 12.5 %all-to-all-start.3 = ((bf16[16,8,128]{2,1,0:T(8,128)(2,1)}), bf16[16,8,128]{2,1,0:T(8,128)(2,1)S(1)}, u32[]{:S(2)}, u32[]{:S(2)}) async-start(bf16[16,8,128]{2,1,0:T(8,128)(2,1)} %bitcast.23), calls=%async_computation.3 | async-start | bytes 65536 | tf_op jit(solution)/shard_map/all_to_all | solution.py:95
where the time goes:
time: 268 us; the launch traced here: 264 us
  local copies, waits for them, and re-layouts  142 us (53%)
  blocking collectives  81.9 us (31%)
  starting transfers between devices  22.3 us (8%)
  matrix products  7.69 us (3%)
  other arithmetic  5.8 us (2%)
  waiting for transfers between devices  4.06 us (2%)
    dynamic_update_slice x12, local copies, waits for them, and re-layouts, blocked_partial(): lax.map(lambda query_rows: partial_block(query_rows, keys, values), stacked)  111 us
    all_gather x1, blocking collectives, local(): lax.all_gather(audio_k, 'seq', axis=0, tiled=True)  56.4 us
    all_gather x1, blocking collectives, local(): lax.all_gather(audio_v, 'seq', axis=0, tiled=True)  25.5 us
    unnamed x11, local copies, waits for them, and re-layouts  9.6 us
    all_to_all x1, starting transfers between devices, local(): lax.all_to_all(audio_q, 'seq', split_axis=1, concat_axis=0, tiled=True)  7.4 us
    all_to_all x1, starting transfers between devices, local(): lax.all_to_all(head_out, 'seq', split_axis=0, concat_axis=1, tiled=True)  5.89 us
    dynamic_slice x6, local copies, waits for them, and re-layouts, local(): lax.scan(advance, empty_state(query_heads.shape[0], columns), (key_heads....  5.49 us
    dynamic_slice x8, local copies, waits for them, and re-layouts, blocked_partial(): lax.map(lambda query_rows: partial_block(query_rows, keys, values), stacked)  5.4 us
  transfers between devices with their start and end apart: 4, of which 2 were waited for; matrix products, arithmetic and copies ran while one was open for 53% of the time, Pallas kernels for 0%

commit v1 on v0

v1 whole, which is shorter than its diff:
```python
import jax
import jax.numpy as jnp
from jax import lax
from jax.sharding import PartitionSpec as P

HEAD_DIM = 64


def spread(scales):
    return jnp.repeat(scales, HEAD_DIM, axis=1)


def exchange(value, bit, count):
    pairs = [(source, source ^ bit) for source in range(count)]
    return lax.ppermute(value, "seq", pairs)


def gather_rows(block):
    count = lax.axis_size("seq")
    me = lax.axis_index("seq")
    held = block[None]
    bit = count // 2
    while bit >= 1:
        arrived = exchange(held, bit, count)
        upper = (me & bit) != 0
        low = jnp.where(upper, arrived, held)
        high = jnp.where(upper, held, arrived)
        held = jnp.stack([low, high], axis=1).reshape((-1,) + block.shape)
        bit //= 2
    return held.reshape((count * block.shape[0],) + block.shape[1:])


def merge(first, second, heads):
    width = heads * HEAD_DIM
    top = jnp.maximum(first[:, width + heads :], second[:, width + heads :])
    first_scale = jnp.exp(first[:, width + heads :] - top)
    second_scale = jnp.exp(second[:, width + heads :] - top)
    totals = first[:, width : width + heads] * first_scale + second[:, width : width + heads] * second_scale
    summed = first[:, :width] * spread(first_scale) + second[:, :width] * spread(second_scale)
    return jnp.concatenate([summed, totals, top], axis=1)


def scatter_rows(state, heads):
    count = lax.axis_size("seq")
    me = lax.axis_index("seq")
    rows = state.shape[0] // count
    held = state.reshape((count, rows, state.shape[1]))
    bit = 1
    while bit < count:
        pairs = held.reshape((-1, 2, rows, state.shape[1]))
        upper = (me & bit) != 0
        keep = jnp.where(upper, pairs[:, 1], pairs[:, 0])
        give = jnp.where(upper, pairs[:, 0], pairs[:, 1])
        arrived = exchange(give, bit, count)
        held = merge(
            keep.reshape((-1, state.shape[1])), arrived.reshape((-1, state.shape[1])), heads
        ).reshape((-1, rows, state.shape[1]))
        bit *= 2
    return held.reshape((rows, state.shape[1]))


def attend_block(queries, keys, values):
    heads = queries.shape[1] // HEAD_DIM
    query_heads = queries.reshape(queries.shape[0], heads, HEAD_DIM)
    key_heads = keys.reshape(keys.shape[0], heads, HEAD_DIM)
    value_heads = values.reshape(values.shape[0], heads, HEAD_DIM)
    scores = (
        jnp.einsum("rhd,shd->hrs", query_heads, key_heads, preferred_element_type=jnp.float32)
        * 0.125
    )
    highest = jnp.max(scores, axis=2)
    weights = jnp.exp(scores - highest[:, :, None])
    totals = jnp.sum(weights, axis=2)
    summed = jnp.einsum(
        "hrs,shd->rhd",
        weights.astype(jnp.bfloat16),
        value_heads,
        preferred_element_type=jnp.float32,
    )
    return highest.T, totals.T, summed.reshape(queries.shape[0], heads * HEAD_DIM)


def local(video_q, video_k, video_v, audio_q, audio_k, audio_v):
    width = video_q.shape[1]
    heads = width // HEAD_DIM
    packed = jnp.concatenate([audio_q, audio_k, audio_v], axis=1)
    gathered = gather_rows(packed)
    all_queries = gathered[:, :width]
    all_keys = gathered[:, width : 2 * width]
    all_values = gathered[:, 2 * width :]

    highest, totals, summed = attend_block(all_queries, video_k, video_v)
    state = jnp.concatenate([summed, totals, highest], axis=1)
    mine = scatter_rows(state, heads)
    audio_out = (mine[:, :width] / spread(mine[:, width : width + heads])).astype(jnp.bfloat16)

    ignored, video_totals, video_sums = attend_block(video_q, all_keys, all_values)
    video_out = (video_sums / spread(video_totals)).astype(jnp.bfloat16)
    return video_out, audio_out


def solution(mesh):
    placed = P(("groups", "seq"), None)
    return jax.shard_map(
        local,
        mesh=mesh,
        in_specs=(placed,) * 6,
        out_specs=(placed, placed),
        check_vma=False,
    )
```

time: 268 us -> 94.9 us (0.35); the launches traced: 264 us -> 94.2 us
  local copies, waits for them, and re-layouts: 142 us -> 26.7 us
  blocking collectives: 81.9 us -> 0 us
  waiting for transfers between devices: 4.06 us -> 20.3 us
  matrix products: 7.69 us -> 18.4 us
  starting transfers between devices: 22.3 us -> 13.9 us
  other arithmetic: 5.8 us -> 14.1 us
    dynamic_update_slice x12 -> x0, local copies, waits for them, and re-layouts: 111 us -> none  [blocked_partial(): lax.map(lambda query_rows: partial_block(query_rows, keys, values), stacked)]
    all_gather x2 -> x0, blocking collectives: 81.9 us -> none  [the longest x1 56.4 us: local(): lax.all_gather(audio_k, 'seq', axis=0, tiled=True)]
    all_to_all x4 -> x0, starting transfers between devices: 22.3 us -> none  [the longest x1 7.4 us: local(): lax.all_to_all(audio_q, 'seq', split_axis=1, concat_axis=0, tiled=True)]
    ppermute x0 -> x8, waiting for transfers between devices: none -> 20.3 us  [exchange(): return lax.ppermute(value, 'seq', pairs)]
    ppermute x0 -> x8, starting transfers between devices: none -> 13.9 us  [exchange(): return lax.ppermute(value, 'seq', pairs)]
    dynamic_slice x14 -> x0, local copies, waits for them, and re-layouts: 10.9 us -> none  [the longest x6 5.49 us: local(): lax.scan(advance, empty_state(query_heads.shape[0], columns), (key_heads....]
    dot_general x12 -> x4, matrix products: 7.69 us -> 18.4 us  [the longest x2 9.81 us: attend_block(): jnp.einsum('hrs,shd->rhd', weights.astype(jnp.bfloat16), value_heads, pre...]
    all_to_all x2 -> x0, local copies, waits for them, and re-layouts: 7.82 us -> none  [the longest x1 3.92 us: local(): lax.all_to_all(video_k, 'seq', split_axis=1, concat_axis=0, tiled=True)]
  transfers between devices with their start and end apart: 4 -> 8, of which waited for: 2 -> 4; matrix products, arithmetic and copies ran while one was open for 53% -> 31% of each run, Pallas kernels for 0% -> 0%
where the time goes in v1:
time: 94.9 us; the launch traced here: 94.2 us
  local copies, waits for them, and re-layouts  26.7 us (28%)
  waiting for transfers between devices  20.3 us (21%)
  matrix products  18.4 us (19%)
  other arithmetic  14.1 us (15%)
  starting transfers between devices  13.9 us (15%)
    ppermute x8, waiting for transfers between devices, exchange(): return lax.ppermute(value, 'seq', pairs)  20.3 us
    unnamed x14, local copies, waits for them, and re-layouts  14.7 us
    ppermute x8, starting transfers between devices, exchange(): return lax.ppermute(value, 'seq', pairs)  13.9 us
    dot_general x2, matrix products, attend_block(): jnp.einsum('hrs,shd->rhd', weights.astype(jnp.bfloat16), value_heads, pre...  9.81 us
    dot_general x2, matrix products, attend_block(): jnp.einsum('rhd,shd->hrs', query_heads, key_heads, preferred_element_type...  8.56 us
    reduce_sum x2, other arithmetic, attend_block(): totals = jnp.sum(weights, axis=2)  7.05 us
    reshape x9, local copies, waits for them, and re-layouts, spread(): return jnp.repeat(scales, HEAD_DIM, axis=1)  3.26 us
    another operation x7, other arithmetic, gather_rows(): held = jnp.stack([low, high], axis=1).reshape((-1,) + block.shape)  2.44 us
  transfers between devices with their start and end apart: 8, of which 4 were waited for; matrix products, arithmetic and copies ran while one was open for 31% of the time, Pallas kernels for 0%

profile of v1, /device:TPU:0, one launch (start us, length us, event | category | flops | bytes accessed | tf_op | source)
XLA Modules:
  0.0 94.2 jit_solution(4882380521867733600)
XLA Ops:
  0.6 0.9 %maximum_bitcast_fusion.1 = bf16[1,8,6144]{2,1,0:T(8,128)(2,1)S(1)} fusion(bf16[8,2048]{1,0:T(8,128)(2,1)} %param.11, bf16[8,2048]{1,0:T(8,128)(2,1)} %param.10, bf16[8,2048]{1,0:T(8,128)(2,1)} %param.9), kind=kLoop, calls=%fused_computation.43 | loop fusion | flops 294912 | bytes 196608 | tf_op jit(solution)/shard_map/broadcast_in_dim | solution.py:21
  1.6 4.1 %collective-permute-start = (bf16[1,8,6144]{2,1,0:T(8,128)(2,1)S(1)}, bf16[1,8,6144]{2,1,0:T(8,128)(2,1)S(1)}, u32[]{:S(2)}, u32[]{:S(2)}) collective-permute-start(bf16[1,8,6144]{2,1,0:T(8,128)(2,1)S(1)} %maximum_bitcast_fusion.1), channel_id=1, source_target_pairs={{0,8},{1,9},{2,10},{3,11},{4,12},{5,13},{6,14},{7,15},{8,0},{9,1},... | collective-permute-start | bytes 294920 | tf_op jit(solution)/shard_map/ppermute | solution.py:15
  5.7 4.9 %collective-permute-done = bf16[1,8,6144]{2,1,0:T(8,128)(2,1)S(1)} collective-permute-done((bf16[1,8,6144]{2,1,0:T(8,128)(2,1)S(1)}, bf16[1,8,6144]{2,1,0:T(8,128)(2,1)S(1)}, u32[]{:S(2)}, u32[]{:S(2)}) %collective-permute-start) | collective-permute-done | bytes 98336 | tf_op jit(solution)/shard_map/ppermute | solution.py:15
  10.6 0.8 select_bitcast_fusion.13
  11.4 0.8 collective-permute-start.1
  12.2 5.4 %collective-permute-done.1 = bf16[2,8,6144]{2,1,0:T(8,128)(2,1)S(1)} collective-permute-done((bf16[2,8,6144]{2,1,0:T(8,128)(2,1)S(1)}, bf16[2,8,6144]{2,1,0:T(8,128)(2,1)S(1)}, u32[]{:S(2)}, u32[]{:S(2)}) %collective-permute-start.1) | collective-permute-done | bytes 196640 | tf_op jit(solution)/shard_map/ppermute | solution.py:15
  17.7 1.3 %collective-permute-start.2 = (bf16[4,8,6144]{2,1,0:T(8,128)(2,1)S(1)}, bf16[4,8,6144]{2,1,0:T(8,128)(2,1)S(1)}, u32[]{:S(2)}, u32[]{:S(2)}) collective-permute-start(bf16[4,8,6144]{2,1,0:T(8,128)(2,1)S(1)} %bitcast.105), channel_id=1, source_target_pairs={{0,2},{1,3},{2,0},{3,1},{4,6},{5,7},{6,4},{7,5},{8,10},{9,11},{10,... | collective-permute-start | bytes 1179656 | tf_op jit(solution)/shard_map/ppermute | solution.py:15
  19.0 8.1 %collective-permute-done.2 = bf16[4,8,6144]{2,1,0:T(8,128)(2,1)S(1)} collective-permute-done((bf16[4,8,6144]{2,1,0:T(8,128)(2,1)S(1)}, bf16[4,8,6144]{2,1,0:T(8,128)(2,1)S(1)}, u32[]{:S(2)}, u32[]{:S(2)}) %collective-permute-start.2) | collective-permute-done | bytes 393248 | tf_op jit(solution)/shard_map/ppermute | solution.py:15
  27.4 2.5 %copy.48 = bf16[512,2048]{0,1:T(8,128)(2,1)} copy(bf16[512,2048]{1,0:T(8,128)(2,1)S(1)} %copy-done.2) | data formatting | bytes 4194304 | tf_op args[1]
  29.9 2.9 %copy.49 = bf16[512,2048]{0,1:T(8,128)(2,1)S(1)} copy(bf16[512,2048]{1,0:T(8,128)(2,1)} %param.8) | data formatting | bytes 4194304 | tf_op args[2]
  32.8 1.2 %select_bitcast_fusion.1 = (bf16[8,1,8,6144]{3,2,0,1:T(8,128)(2,1)S(1)}, bf16[8,1,8,6144]{3,2,0,1:T(8,128)(2,1)S(1)}) fusion(bf16[8,8,6144]{2,1,0:T(8,128)(2,1)} %collective-permute-done.3, pred[]{:T(512)S(6)} %ne.16, bf16[4,2,8,6144]{3,2,1,0:T(8,128)(2,1)S(1)} %copy.41), kind=kLoop, calls=%fused_computation.21 | loop fusion | flops 786432 | bytes 3145729 | tf_op jit(solution)/shard_map/stack | solution.py:28
  34.1 0.1 pad_maximum_fusion
  34.2 0.1 copy.42
  34.4 1.1 %fusion.35 = (bf16[128,2048]{1,0:T(8,128)(2,1)S(1)}, bf16[128,2048]{1,0:T(8,128)(2,1)}, bf16[128,2048]{1,0:T(8,128)(2,1)}) fusion(bf16[128,6144]{1,0:T(8,128)(2,1)S(1)} %bitcast.99), kind=kLoop, calls=%fused_computation.80 | loop fusion | bytes 3145728 | tf_op jit(solution)/shard_map/slice | solution.py:88
  35.5 0.3 copy.47
  35.8 3.0 %multiply_reduce_fusion = (f32[32,128]{1,0:T(8,128)S(1)}, f32[32,128,512]{2,1,0:T(8,128)S(1)}) fusion(bf16[128,32,64]{0,2,1:T(8,128)(2,1)S(1)} %bitcast.104, bf16[512,32,64]{0,2,1:T(8,128)(2,1)} %bitcast.98), kind=kOutput, calls=%fused_computation.4 | convolution fusion | flops 272625664 | bytes 11026432 | tf_op jit(solution)/shard_map/rhd,shd->hrs/dot_general | solution.py:68
  38.8 3.2 %copy-done = f32[32,128,512]{2,1,0:T(8,128)} copy-done((f32[32,128,512]{2,1,0:T(8,128)}, f32[32,128,512]{2,1,0:T(8,128)S(1)}, u32[]{:S(2)}) %copy-start) | copy-done | bytes 8388632
  42.0 2.1 %fusion.1 = f32[32,128]{1,0:T(8,128)S(1)} fusion(f32[32,128,512]{2,1,0:T(8,128)S(1)} %get-tuple-element.47, f32[32,128]{1,0:T(8,128)S(1)} %get-tuple-element.46), kind=kLoop, calls=%fused_computation.5 | loop fusion | flops 6287360 | bytes 8421376 | tf_op jit(solution)/shard_map/reduce_sum | solution.py:73
  44.1 4.5 %fusion.16 = f32[128,32,64]{0,2,1:T(8,128)S(1)} fusion(bf16[512,32,64]{0,2,1:T(8,128)(2,1)S(1)} %bitcast.97, f32[32,128,512]{2,1,0:T(8,128)} %copy-done, f32[32,128]{1,0:T(8,128)S(1)} %get-tuple-element.46), kind=kOutput, calls=%fused_computation.18 | convolution fusion | flops 274726912 | bytes 11550720 | tf_op jit(solution)/shard_map/hrs,shd->rhd/dot_general | solution.py:74
  48.7 1.8 %copy.50 = f32[128,32,64]{2,1,0:T(8,128)S(1)} copy(f32[128,32,64]{0,2,1:T(8,128)S(1)} %fusion.16) | data formatting | bytes 2097152 | tf_op jit(solution)/shard_map/hrs,shd->rhd/transpose | solution.py:74
  50.5 0.7 concatenate.23
  51.3 0.3 concatenate.26
  51.5 0.9 select_bitcast_fusion.3
  52.4 0.5 collective-permute-start.4
  52.9 3.0 %copy.45 = bf16[512,2048]{0,1:T(8,128)(2,1)S(1)} copy(bf16[512,2048]{1,0:T(8,128)(2,1)} %param.6) | data formatting | bytes 4194304 | tf_op args[0]
  55.9 2.1 %copy.44 = bf16[128,2048]{0,1:T(8,128)(2,1)} copy(bf16[128,2048]{1,0:T(8,128)(2,1)} %get-tuple-element.26) | data formatting | bytes 1048576 | tf_op jit(solution)/shard_map/slice | solution.py:89
  58.1 0.7 copy-done.4
  58.8 0.3 broadcast_in_dim.37
  59.1 1.2 %reshape.146 = f32[64,2048]{1,0:T(8,128)} reshape(f32[64,32,64]{2,1,0:T(8,128)S(1)} %broadcast_in_dim.37) | data formatting | bytes 1048576 | tf_op jit(solution)/shard_map/reshape | solution.py:10
  60.3 0.3 broadcast_in_dim.38
  60.7 1.2 %reshape.147 = f32[64,2048]{1,0:T(8,128)} reshape(f32[64,32,64]{2,1,0:T(8,128)S(1)} %broadcast_in_dim.38) | data formatting | bytes 1048576 | tf_op jit(solution)/shard_map/reshape | solution.py:10
  61.8 1.6 %fusion.19 = f32[64,2048]{1,0:T(8,128)S(1)} fusion(f32[64,2048]{1,0:T(8,128)} %reshape.147, f32[64,2112]{1,0:T(8,128)} %bitcast.108, f32[64,2048]{1,0:T(8,128)} %reshape.146, f32[64,2112]{1,0:T(8,128)} %copy-done.1), kind=kLoop, calls=%fused_computation.25 | loop fusion | flops 393216 | bytes 2621440 | tf_op jit(solution)/shard_map/add | solution.py:39
  63.6 1.4 %collective-permute-start.5 = (f32[4,8,2112]{2,1,0:T(8,128)S(1)}, f32[4,8,2112]{2,1,0:T(8,128)S(1)}, u32[]{:S(2)}, u32[]{:S(2)}) collective-permute-start(f32[4,8,2112]{2,1,0:T(8,128)S(1)} %get-tuple-element.35), channel_id=1, source_target_pairs={{0,2},{1,3},{2,0},{3,1},{4,6},{5,7},{6,4},{7,5},{8,10},{9,11},{10,... | collective-permute-start | bytes 811016 | tf_op jit(solution)/shard_map/ppermute | solution.py:15
  65.0 5.6 %bitcast_reduce_fusion = (f32[32,512]{1,0:T(8,128)S(1)}, f32[32,128,512]{2,1,0:T(8,128)}) fusion(bf16[128,32,64]{0,2,1:T(8,128)(2,1)} %bitcast.103, bf16[512,32,64]{0,2,1:T(8,128)(2,1)S(1)} %bitcast.96), kind=kOutput, calls=%fused_computation.1 | convolution fusion | flops 272613376 | bytes 11075584 | tf_op jit(solution)/shard_map/rhd,shd->hrs/dot_general | solution.py:68
  70.5 1.9 %collective-permute-done.5 = f32[4,8,2112]{2,1,0:T(8,128)S(1)} collective-permute-done((f32[4,8,2112]{2,1,0:T(8,128)S(1)}, f32[4,8,2112]{2,1,0:T(8,128)S(1)}, u32[]{:S(2)}, u32[]{:S(2)}) %collective-permute-start.5) | collective-permute-done | bytes 270368 | tf_op jit(solution)/shard_map/ppermute | solution.py:15
  72.5 0.2 broadcast_in_dim.39
  72.7 0.2 reshape.149
  72.9 0.2 broadcast_in_dim.40
  73.1 0.2 reshape.150
  73.5 2.3 %collective-permute-start.6 = (f32[2,8,2112]{2,1,0:T(8,128)S(1)}, f32[2,8,2112]{2,1,0:T(8,128)S(1)}, u32[]{:S(2)}, u32[]{:S(2)}) collective-permute-start(f32[2,8,2112]{2,1,0:T(8,128)S(1)} %get-tuple-element.39), channel_id=1, source_target_pairs={{0,4},{1,5},{2,6},{3,7},{4,0},{5,1},{6,2},{7,3},{8,12},{9,13},{10,... | collective-permute-start | bytes 405512 | tf_op jit(solution)/shard_map/ppermute | solution.py:15
  75.8 5.0 %fusion.3 = f32[32,512]{1,0:T(8,128)S(1)} fusion(f32[32,128,512]{2,1,0:T(8,128)} %get-tuple-element.45, f32[32,512]{1,0:T(8,128)S(1)} %get-tuple-element.44), kind=kLoop, calls=%fused_computation.7 | loop fusion | flops 6275072 | bytes 8519680 | tf_op jit(solution)/shard_map/reduce_sum | solution.py:73
  80.8 0.3 copy.43
  81.2 0.1 broadcast_in_dim.41
  81.4 0.1 broadcast_in_dim.42
  81.8 3.4 %collective-permute-start.7 = (f32[1,8,2112]{2,1,0:T(8,128)S(1)}, f32[1,8,2112]{2,1,0:T(8,128)S(1)}, u32[]{:S(2)}, u32[]{:S(2)}) collective-permute-start(f32[1,8,2112]{2,1,0:T(8,128)S(1)} %get-tuple-element.43), channel_id=1, source_target_pairs={{0,8},{1,9},{2,10},{3,11},{4,12},{5,13},{6,14},{7,15},{8,0},{9,1},... | collective-permute-start | bytes 202760 | tf_op jit(solution)/shard_map/ppermute | solution.py:15
  85.3 5.3 %fusion.9 = bf16[512,32,64]{0,2,1:T(8,128)(2,1)S(1)} fusion(f32[512,32]{0,1:T(8,128)S(1)} %bitcast.120, bf16[128,32,64]{0,2,1:T(8,128)(2,1)S(1)} %bitcast.110, f32[32,128,512]{2,1,0:T(8,128)} %get-tuple-element.45, f32[32,512]{1,0:T(8,128)S(1)} %get-tuple-element.44), kind=kOutput, calls=%fused_computation.12 | convolution fusion | flops 276824064 | bytes 11141120 | tf_op jit(solution)/shard_map/hrs,shd->rhd/dot_general | solution.py:74
  90.5 2.4 %copy.53 = bf16[512,2048]{1,0:T(8,128)(2,1)} copy(bf16[512,2048]{0,1:T(8,128)(2,1)S(1)} %bitcast.102) | data formatting | bytes 4194304
  93.6 0.6 fusion.24
  (41 shorter events, 2.1 us)
Async XLA Ops:
  0.6 26.8 %copy-start.2 = (bf16[512,2048]{1,0:T(8,128)(2,1)S(1)}, bf16[512,2048]{1,0:T(8,128)(2,1)}, u32[]{:S(2)}) copy-start(bf16[512,2048]{1,0:T(8,128)(2,1)} %param.7) | copy-start | bytes 6291460
  1.6 9.0 %collective-permute-start = (bf16[1,8,6144]{2,1,0:T(8,128)(2,1)S(1)}, bf16[1,8,6144]{2,1,0:T(8,128)(2,1)S(1)}, u32[]{:S(2)}, u32[]{:S(2)}) collective-permute-start(bf16[1,8,6144]{2,1,0:T(8,128)(2,1)S(1)} %maximum_bitcast_fusion.1), channel_id=1, source_target_pairs={{0,8},{1,9},{2,10},{3,11},{4,12},{5,13},{6,14},{7,15},{8,0},{9,1},... | collective-permute-start | bytes 294920 | tf_op jit(solution)/shard_map/ppermute | solution.py:15
  11.4 6.2 %collective-permute-start.1 = (bf16[2,8,6144]{2,1,0:T(8,128)(2,1)S(1)}, bf16[2,8,6144]{2,1,0:T(8,128)(2,1)S(1)}, u32[]{:S(2)}, u32[]{:S(2)}) collective-permute-start(bf16[2,8,6144]{2,1,0:T(8,128)(2,1)S(1)} %maximum_bitcast_fusion), channel_id=1, source_target_pairs={{0,4},{1,5},{2,6},{3,7},{4,0},{5,1},{6,2},{7,3},{8,12},{9,13},{10,... | collective-permute-start | bytes 589832 | tf_op jit(solution)/shard_map/ppermute | solution.py:15
  17.7 9.4 %collective-permute-start.2 = (bf16[4,8,6144]{2,1,0:T(8,128)(2,1)S(1)}, bf16[4,8,6144]{2,1,0:T(8,128)(2,1)S(1)}, u32[]{:S(2)}, u32[]{:S(2)}) collective-permute-start(bf16[4,8,6144]{2,1,0:T(8,128)(2,1)S(1)} %bitcast.105), channel_id=1, source_target_pairs={{0,2},{1,3},{2,0},{3,1},{4,6},{5,7},{6,4},{7,5},{8,10},{9,11},{10,... | collective-permute-start | bytes 1179656 | tf_op jit(solution)/shard_map/ppermute | solution.py:15
  27.3 5.5 %collective-permute-start.3 = (bf16[8,8,6144]{2,1,0:T(8,128)(2,1)S(1)}, bf16[8,8,6144]{2,1,0:T(8,128)(2,1)}, u32[]{:S(2)}, u32[]{:S(2)}) collective-permute-start(bf16[8,8,6144]{2,1,0:T(8,128)(2,1)S(1)} %bitcast.100), channel_id=1, source_target_pairs={{0,1},{1,0},{2,3},{3,2},{4,5},{5,4},{6,7},{7,6},{8,9},{9,8},{10,11... | collective-permute-start | bytes 2359304 | tf_op jit(solution)/shard_map/ppermute | solution.py:15
  38.8 3.2 %copy-start = (f32[32,128,512]{2,1,0:T(8,128)}, f32[32,128,512]{2,1,0:T(8,128)S(1)}, u32[]{:S(2)}) copy-start(f32[32,128,512]{2,1,0:T(8,128)S(1)} %get-tuple-element.47) | copy-start | bytes 25165828
  52.4 5.7 %copy-start.1 = (f32[64,2112]{1,0:T(8,128)}, f32[64,2112]{1,0:T(8,128)S(1)}, u32[]{:S(2)}) copy-start(f32[64,2112]{1,0:T(8,128)S(1)} %get-tuple-element.30) | copy-start | bytes 1622020
  52.4 5.6 %collective-permute-start.4 = (f32[8,8,2112]{2,1,0:T(8,128)}, f32[8,8,2112]{2,1,0:T(8,128)S(1)}, u32[]{:S(2)}, u32[]{:S(2)}) collective-permute-start(f32[8,8,2112]{2,1,0:T(8,128)} %get-tuple-element.31), channel_id=1, source_target_pairs={{0,1},{1,0},{2,3},{3,2},{4,5},{5,4},{6,7},{7,6},{8,9},{9,8},{10,11... | collective-permute-start | bytes 1622024 | tf_op jit(solution)/shard_map/ppermute | solution.py:15
  58.0 0.8 copy-start.4
  63.6 8.8 %collective-permute-start.5 = (f32[4,8,2112]{2,1,0:T(8,128)S(1)}, f32[4,8,2112]{2,1,0:T(8,128)S(1)}, u32[]{:S(2)}, u32[]{:S(2)}) collective-permute-start(f32[4,8,2112]{2,1,0:T(8,128)S(1)} %get-tuple-element.35), channel_id=1, source_target_pairs={{0,2},{1,3},{2,0},{3,1},{4,6},{5,7},{6,4},{7,5},{8,10},{9,11},{10,... | collective-permute-start | bytes 811016 | tf_op jit(solution)/shard_map/ppermute | solution.py:15
  70.5 10.3 %copy-start.3 = (bf16[128,2048]{1,0:T(8,128)(2,1)S(1)}, bf16[128,2048]{1,0:T(8,128)(2,1)}, u32[]{:S(2)}) copy-start(bf16[128,2048]{1,0:T(8,128)(2,1)} %get-tuple-element.27) | copy-start | bytes 1572868
  73.5 7.6 %collective-permute-start.6 = (f32[2,8,2112]{2,1,0:T(8,128)S(1)}, f32[2,8,2112]{2,1,0:T(8,128)S(1)}, u32[]{:S(2)}, u32[]{:S(2)}) collective-permute-start(f32[2,8,2112]{2,1,0:T(8,128)S(1)} %get-tuple-element.39), channel_id=1, source_target_pairs={{0,4},{1,5},{2,6},{3,7},{4,0},{5,1},{6,2},{7,3},{8,12},{9,13},{10,... | collective-permute-start | bytes 405512 | tf_op jit(solution)/shard_map/ppermute | solution.py:15
  81.8 11.1 %collective-permute-start.7 = (f32[1,8,2112]{2,1,0:T(8,128)S(1)}, f32[1,8,2112]{2,1,0:T(8,128)S(1)}, u32[]{:S(2)}, u32[]{:S(2)}) collective-permute-start(f32[1,8,2112]{2,1,0:T(8,128)S(1)} %get-tuple-element.43), channel_id=1, source_target_pairs={{0,8},{1,9},{2,10},{3,11},{4,12},{5,13},{6,14},{7,15},{8,0},{9,1},... | collective-permute-start | bytes 202760 | tf_op jit(solution)/shard_map/ppermute | solution.py:15

commit v2 on v1

--- a/solution.py
+++ b/solution.py
@@ -1,6 +1,8 @@
 import jax
 import jax.numpy as jnp
 from jax import lax
+from jax.experimental import pallas as pl
+from jax.experimental.pallas import tpu as pltpu
 from jax.sharding import PartitionSpec as P
 
 HEAD_DIM = 64
@@ -59,25 +61,123 @@
     return held.reshape((rows, state.shape[1]))
 
 
-def attend_block(queries, keys, values):
-    heads = queries.shape[1] // HEAD_DIM
-    query_heads = queries.reshape(queries.shape[0], heads, HEAD_DIM)
-    key_heads = keys.reshape(keys.shape[0], heads, HEAD_DIM)
-    value_heads = values.reshape(values.shape[0], heads, HEAD_DIM)
-    scores = (
-        jnp.einsum("rhd,shd->hrs", query_heads, key_heads, preferred_element_type=jnp.float32)
+def head_masks(rows):
+    lane = lax.broadcasted_iota(jnp.int32, (rows, 2 * HEAD_DIM), 1)
+    return lane < HEAD_DIM
+
+
+def pair_scores(queries, keys, first):
+    masked = jnp.where(first, queries, jnp.zeros_like(queries))
+    return (
+        lax.dot_general(
+            masked, keys, (((1,), (1,)), ((), ())), preferred_element_type=jnp.float32
+        )
         * 0.125
     )
-    highest = jnp.max(scores, axis=2)
-    weights = jnp.exp(scores - highest[:, :, None])
-    totals = jnp.sum(weights, axis=2)
-    summed = jnp.einsum(
-        "hrs,shd->rhd",
-        weights.astype(jnp.bfloat16),
-        value_heads,
-        preferred_element_type=jnp.float32,
-    )
-    return highest.T, totals.T, summed.reshape(queries.shape[0], heads * HEAD_DIM)
+
+
+def video_kernel(query_ref, key_ref, value_ref, out_ref):
+    queries = query_ref[...]
+    keys = key_ref[...]
+    values = value_ref[...]
+    first = head_masks(queries.shape[0])
+    results = []
+    for lanes in (first, jnp.logical_not(first)):
+        scores = pair_scores(queries, keys, lanes)
+        highest = jnp.max(scores, axis=1, keepdims=True)
+        weights = jnp.exp(scores - highest)
+        totals = jnp.sum(weights, axis=1, keepdims=True)
+        summed = jnp.dot(
+            weights.astype(jnp.bfloat16), values, preferred_element_type=jnp.float32
+        )
+        results.append(summed / totals)
+    out_ref[...] = jnp.where(first, results[0], results[1]).astype(out_ref.dtype)
+
+
+def video_attention(queries, keys, values):
+    rows, width = queries.shape
+    pairs = width // (2 * HEAD_DIM)
+    key_rows = keys.shape[0]
+    return pl.pallas_call(
+        video_kernel,
+        grid=(pairs,),
+        in_specs=[
+            pl.BlockSpec((rows, 2 * HEAD_DIM), lambda p: (0, p)),
+            pl.BlockSpec((key_rows, 2 * HEAD_DIM), lambda p: (0, p)),
+            pl.BlockSpec((key_rows, 2 * HEAD_DIM), lambda p: (0, p)),
+        ],
+        out_specs=pl.BlockSpec((rows, 2 * HEAD_DIM), lambda p: (0, p)),
+        out_shape=jax.ShapeDtypeStruct((rows, width), jnp.bfloat16),
+        cost_estimate=pl.CostEstimate(
+            flops=8 * rows * key_rows * width,
+            transcendentals=rows * key_rows * width // HEAD_DIM,
+            bytes_accessed=2 * (2 * rows * width + 2 * key_rows * width),
+        ),
+    )(queries, keys, values)
+
+
+def audio_kernel(query_ref, key_ref, value_ref, sum_ref, total_ref, top_ref):
+    pair = pl.program_id(0)
+    queries = query_ref[...]
+    keys = key_ref[...]
+    values = value_ref[...]
+    rows = queries.shape[0]
+    first = head_masks(rows)
+
+    @pl.when(pair == 0)
+    def _():
+        total_ref[...] = jnp.zeros_like(total_ref)
+        top_ref[...] = jnp.zeros_like(top_ref)
+
+    column = lax.broadcasted_iota(jnp.int32, total_ref.shape, 1)
+    results = []
+    totals_now = total_ref[...]
+    tops_now = top_ref[...]
+    for half, lanes in enumerate((first, jnp.logical_not(first))):
+        scores = pair_scores(queries, keys, lanes)
+        highest = jnp.max(scores, axis=1, keepdims=True)
+        weights = jnp.exp(scores - highest)
+        totals = jnp.sum(weights, axis=1, keepdims=True)
+        results.append(
+            jnp.dot(weights.astype(jnp.bfloat16), values, preferred_element_type=jnp.float32)
+        )
+        here = column == 2 * pair + half
+        totals_now = jnp.where(here, totals, totals_now)
+        tops_now = jnp.where(here, highest, tops_now)
+    total_ref[...] = totals_now
+    top_ref[...] = tops_now
+    sum_ref[...] = jnp.where(first, results[0], results[1])
+
+
+def audio_partial(queries, keys, values):
+    rows, width = queries.shape
+    heads = width // HEAD_DIM
+    key_rows = keys.shape[0]
+    return pl.pallas_call(
+        audio_kernel,
+        grid=(heads // 2,),
+        in_specs=[
+            pl.BlockSpec((rows, 2 * HEAD_DIM), lambda p: (0, p)),
+            pl.BlockSpec((key_rows, 2 * HEAD_DIM), lambda p: (0, p)),
+            pl.BlockSpec((key_rows, 2 * HEAD_DIM), lambda p: (0, p)),
+        ],
+        out_specs=[
+            pl.BlockSpec((rows, 2 * HEAD_DIM), lambda p: (0, p)),
+            pl.BlockSpec((rows, heads), lambda p: (0, 0)),
+            pl.BlockSpec((rows, heads), lambda p: (0, 0)),
+        ],
+        out_shape=[
+            jax.ShapeDtypeStruct((rows, width), jnp.float32),
+            jax.ShapeDtypeStruct((rows, heads), jnp.float32),
+            jax.ShapeDtypeStruct((rows, heads), jnp.float32),
+        ],
+        compiler_params=pltpu.CompilerParams(dimension_semantics=("arbitrary",)),
+        cost_estimate=pl.CostEstimate(
+            flops=8 * rows * key_rows * width,
+            transcendentals=rows * key_rows * heads,
+            bytes_accessed=2 * rows * width + 4 * key_rows * width + 4 * rows * width,
+        ),
+    )(queries, keys, values)
 
 
 def local(video_q, video_k, video_v, audio_q, audio_k, audio_v):
@@ -89,13 +189,12 @@
     all_keys = gathered[:, width : 2 * width]
     all_values = gathered[:, 2 * width :]
 
-    highest, totals, summed = attend_block(all_queries, video_k, video_v)
+    summed, totals, highest = audio_partial(all_queries, video_k, video_v)
     state = jnp.concatenate([summed, totals, highest], axis=1)
     mine = scatter_rows(state, heads)
     audio_out = (mine[:, :width] / spread(mine[:, width : width + heads])).astype(jnp.bfloat16)
 
-    ignored, video_totals, video_sums = attend_block(video_q, all_keys, all_values)
-    video_out = (video_sums / spread(video_totals)).astype(jnp.bfloat16)
+    video_out = video_attention(video_q, all_keys, all_values)
     return video_out, audio_out
 
 

time: 94.9 us -> 89 us (0.938)
  Pallas kernels: 0 us -> 30.5 us
  local copies, waits for them, and re-layouts: 26.7 us -> 6.17 us
  matrix products: 18.4 us -> 0 us
  waiting for transfers between devices: 20.3 us -> 33.1 us
  other arithmetic: 14.1 us -> 3.49 us
    pallas_call x0 -> x2, Pallas kernels: none -> 30.5 us  [the longest x1 15.5 us: audio_partial(): pl.pallas_call(audio_kernel, grid=(heads // 2,), in_specs=[pl.BlockSpec((...]
    dot_general x4 -> x0, matrix products: 18.4 us -> none  [the longest x2 9.81 us: attend_block(): jnp.einsum('hrs,shd->rhd', weights.astype(jnp.bfloat16), value_heads, pre...]
    unnamed x14 -> x0, local copies, waits for them, and re-layouts: 14.7 us -> none
    ppermute x8, waiting for transfers between devices: 20.3 us -> 33.1 us  [exchange(): return lax.ppermute(value, 'seq', pairs)]
    reduce_sum x2 -> x0, other arithmetic: 7.05 us -> none  [attend_block(): totals = jnp.sum(weights, axis=2)]
    slice x2 -> x0, local copies, waits for them, and re-layouts: 2.34 us -> none  [the longest x1 2.07 us: local(): all_keys = gathered[:, width:2 * width]]
    transpose x3 -> x0, local copies, waits for them, and re-layouts: 2.02 us -> none  [the longest x1 1.83 us: attend_block(): jnp.einsum('hrs,shd->rhd', weights.astype(jnp.bfloat16), value_heads, pre...]
    reshape x9, local copies, waits for them, and re-layouts: 3.26 us -> 1.62 us  [spread(): return jnp.repeat(scales, HEAD_DIM, axis=1)]
  transfers between devices with their start and end apart: 8 -> 8, of which waited for: 4 -> 7; matrix products, arithmetic and copies ran while one was open for 31% -> 0% of each run, Pallas kernels for 0% -> 17%
where the time goes in v2:
time: 89 us; the launch traced here: 88.1 us
  waiting for transfers between devices  33.1 us (37%)
  Pallas kernels  30.5 us (34%)
  starting transfers between devices  14.1 us (16%)
  local copies, waits for them, and re-layouts  6.17 us (7%)
  other arithmetic  3.49 us (4%)
    ppermute x8, waiting for transfers between devices, exchange(): return lax.ppermute(value, 'seq', pairs)  33.1 us
    pallas_call x1, Pallas kernels, audio_partial(): pl.pallas_call(audio_kernel, grid=(heads // 2,), in_specs=[pl.BlockSpec((...  15.5 us
    pallas_call x1, Pallas kernels, video_attention(): pl.pallas_call(video_kernel, grid=(pairs,), in_specs=[pl.BlockSpec((rows,...  14.9 us
    ppermute x8, starting transfers between devices, exchange(): return lax.ppermute(value, 'seq', pairs)  14.1 us
  transfers between devices with their start and end apart: 8, of which 7 were waited for; matrix products, arithmetic and copies ran while one was open for 0% of the time, Pallas kernels for 17%

profile of v2, /device:TPU:0, one launch (start us, length us, event | category | flops | bytes accessed | tf_op | source)
XLA Modules:
  0.0 88.1 jit_solution(13195588774305833777)
XLA Ops:
  0.6 0.8 maximum_bitcast_fusion.1
  1.4 4.1 %collective-permute-start = (bf16[1,8,6144]{2,1,0:T(8,128)(2,1)S(1)}, bf16[1,8,6144]{2,1,0:T(8,128)(2,1)S(1)}, u32[]{:S(2)}, u32[]{:S(2)}) collective-permute-start(bf16[1,8,6144]{2,1,0:T(8,128)(2,1)S(1)} %maximum_bitcast_fusion.1), channel_id=1, source_target_pairs={{0,8},{1,9},{2,10},{3,11},{4,12},{5,13},{6,14},{7,15},{8,0},{9,1},... | collective-permute-start | bytes 294920 | tf_op jit(solution)/shard_map/ppermute | solution.py:17
  5.5 4.9 %collective-permute-done = bf16[1,8,6144]{2,1,0:T(8,128)(2,1)S(1)} collective-permute-done((bf16[1,8,6144]{2,1,0:T(8,128)(2,1)S(1)}, bf16[1,8,6144]{2,1,0:T(8,128)(2,1)S(1)}, u32[]{:S(2)}, u32[]{:S(2)}) %collective-permute-start) | collective-permute-done | bytes 98336 | tf_op jit(solution)/shard_map/ppermute | solution.py:17
  10.4 0.8 select_bitcast_fusion.13
  11.3 0.8 collective-permute-start.1
  12.1 5.4 %collective-permute-done.1 = bf16[2,8,6144]{2,1,0:T(8,128)(2,1)S(1)} collective-permute-done((bf16[2,8,6144]{2,1,0:T(8,128)(2,1)S(1)}, bf16[2,8,6144]{2,1,0:T(8,128)(2,1)S(1)}, u32[]{:S(2)}, u32[]{:S(2)}) %collective-permute-start.1) | collective-permute-done | bytes 196640 | tf_op jit(solution)/shard_map/ppermute | solution.py:17
  17.5 1.3 %collective-permute-start.2 = (bf16[4,8,6144]{2,1,0:T(8,128)(2,1)S(1)}, bf16[4,8,6144]{2,1,0:T(8,128)(2,1)S(1)}, u32[]{:S(2)}, u32[]{:S(2)}) collective-permute-start(bf16[4,8,6144]{2,1,0:T(8,128)(2,1)S(1)} %bitcast.65), channel_id=1, source_target_pairs={{0,2},{1,3},{2,0},{3,1},{4,6},{5,7},{6,4},{7,5},{8,10},{9,11},{10,... | collective-permute-start | bytes 1179656 | tf_op jit(solution)/shard_map/ppermute | solution.py:17
  18.8 8.1 %collective-permute-done.2 = bf16[4,8,6144]{2,1,0:T(8,128)(2,1)S(1)} collective-permute-done((bf16[4,8,6144]{2,1,0:T(8,128)(2,1)S(1)}, bf16[4,8,6144]{2,1,0:T(8,128)(2,1)S(1)}, u32[]{:S(2)}, u32[]{:S(2)}) %collective-permute-start.2) | collective-permute-done | bytes 393248 | tf_op jit(solution)/shard_map/ppermute | solution.py:17
  27.3 2.3 %collective-permute-done.3 = bf16[8,8,6144]{2,1,0:T(8,128)(2,1)S(1)} collective-permute-done((bf16[8,8,6144]{2,1,0:T(8,128)(2,1)S(1)}, bf16[8,8,6144]{2,1,0:T(8,128)(2,1)S(1)}, u32[]{:S(2)}, u32[]{:S(2)}) %collective-permute-start.3) | collective-permute-done | bytes 786464 | tf_op jit(solution)/shard_map/ppermute | solution.py:17
  29.5 0.2 select_bitcast_fusion.1
  29.7 0.1 pad_maximum_fusion
  29.8 0.1 copy.14
  30.0 1.2 %fusion.14 = (bf16[128,2048]{1,0:T(8,128)(2,1)}, bf16[128,2048]{1,0:T(8,128)(2,1)}, bf16[128,2048]{1,0:T(8,128)(2,1)}) fusion(bf16[128,6144]{1,0:T(8,128)(2,1)S(1)} %bitcast.61), kind=kLoop, calls=%fused_computation.60 | loop fusion | bytes 3145728 | tf_op jit(solution)/shard_map/slice | solution.py:188
  31.2 15.5 %shard_map.78 = (f32[128,2048]{1,0:T(8,128)}, f32[128,32]{1,0:T(8,128)}, f32[128,32]{1,0:T(8,128)}) custom-call(bf16[128,2048]{1,0:T(8,128)(2,1)} %get-tuple-element.23.query_ref, bf16[512,2048]{1,0:T(8,128)(2,1)} %key_ref.1, bf16[512,2048]{1,0:T(8,128)(2,1)} %value_ref.1), custom_call_target="tpu_custom_call" | custom-call | flops 1073741824 | bytes 5767168 | tf_op jit(solution)/shard_map/pallas_call | solution.py:156
  46.7 1.3 %concatenate.16 = f32[128,2112]{1,0:T(8,128)S(1)} concatenate(f32[128,2048]{1,0:T(8,128)} %get-tuple-element.5, f32[128,32]{1,0:T(8,128)} %get-tuple-element.6, f32[128,32]{1,0:T(8,128)} %get-tuple-element.7), dimensions={1} | concatenate | bytes 2162688 | tf_op jit(solution)/shard_map/concatenate | solution.py:193
  48.2 0.2 collective-permute-start.4
  48.3 1.8 %collective-permute-done.4 = f32[8,8,2112]{2,1,0:T(8,128)S(1)} collective-permute-done((f32[8,8,2112]{2,1,0:T(8,128)S(1)}, f32[8,8,2112]{2,1,0:T(8,128)S(1)}, u32[]{:S(2)}, u32[]{:S(2)}) %collective-permute-start.4) | collective-permute-done | bytes 540704 | tf_op jit(solution)/shard_map/ppermute | solution.py:17
  50.2 0.1 fusion.6
  50.3 0.3 broadcast_in_dim.31
  50.6 0.4 reshape.109
  51.0 0.3 broadcast_in_dim.32
  51.3 0.4 reshape.110
  51.7 0.1 fusion
  51.8 0.1 concatenate.17
  51.9 1.4 %collective-permute-start.5 = (f32[4,8,2112]{2,1,0:T(8,128)S(1)}, f32[4,8,2112]{2,1,0:T(8,128)S(1)}, u32[]{:S(2)}, u32[]{:S(2)}) collective-permute-start(f32[4,8,2112]{2,1,0:T(8,128)S(1)} %get-tuple-element.33), channel_id=1, source_target_pairs={{0,2},{1,3},{2,0},{3,1},{4,6},{5,7},{6,4},{7,5},{8,10},{9,11},{10,... | collective-permute-start | bytes 811016 | tf_op jit(solution)/shard_map/ppermute | solution.py:17
  53.3 7.4 %collective-permute-done.5 = f32[4,8,2112]{2,1,0:T(8,128)S(1)} collective-permute-done((f32[4,8,2112]{2,1,0:T(8,128)S(1)}, f32[4,8,2112]{2,1,0:T(8,128)S(1)}, u32[]{:S(2)}, u32[]{:S(2)}) %collective-permute-start.5) | collective-permute-done | bytes 270368 | tf_op jit(solution)/shard_map/ppermute | solution.py:17
  60.7 0.1 fusion.7
  60.8 0.2 broadcast_in_dim.33
  61.0 0.2 reshape.112
  61.1 0.2 broadcast_in_dim.34
  61.3 0.2 reshape.113
  61.7 2.3 %collective-permute-start.6 = (f32[2,8,2112]{2,1,0:T(8,128)S(1)}, f32[2,8,2112]{2,1,0:T(8,128)S(1)}, u32[]{:S(2)}, u32[]{:S(2)}) collective-permute-start(f32[2,8,2112]{2,1,0:T(8,128)S(1)} %get-tuple-element.37), channel_id=1, source_target_pairs={{0,4},{1,5},{2,6},{3,7},{4,0},{5,1},{6,2},{7,3},{8,12},{9,13},{10,... | collective-permute-start | bytes 405512 | tf_op jit(solution)/shard_map/ppermute | solution.py:17
  64.0 3.1 %collective-permute-done.6 = f32[2,8,2112]{2,1,0:T(8,128)S(1)} collective-permute-done((f32[2,8,2112]{2,1,0:T(8,128)S(1)}, f32[2,8,2112]{2,1,0:T(8,128)S(1)}, u32[]{:S(2)}, u32[]{:S(2)}) %collective-permute-start.6) | collective-permute-done | bytes 135200 | tf_op jit(solution)/shard_map/ppermute | solution.py:17
  67.2 0.1 fusion.8
  67.3 0.1 broadcast_in_dim.35
  67.4 0.1 reshape.115
  67.5 0.1 broadcast_in_dim.36
  67.7 0.1 reshape.116
  67.8 0.1 concatenate.19
  67.9 3.9 %collective-permute-start.7 = (f32[1,8,2112]{2,1,0:T(8,128)S(1)}, f32[1,8,2112]{2,1,0:T(8,128)S(1)}, u32[]{:S(2)}, u32[]{:S(2)}) collective-permute-start(f32[1,8,2112]{2,1,0:T(8,128)S(1)} %get-tuple-element.41), channel_id=1, source_target_pairs={{0,8},{1,9},{2,10},{3,11},{4,12},{5,13},{6,14},{7,15},{8,0},{9,1},... | collective-permute-start | bytes 202760 | tf_op jit(solution)/shard_map/ppermute | solution.py:17
  71.8 14.9 %shard_map.77 = bf16[512,2048]{1,0:T(8,128)(2,1)} custom-call(bf16[512,2048]{1,0:T(8,128)(2,1)} %query_ref.1, bf16[128,2048]{1,0:T(8,128)(2,1)} %get-tuple-element.25.key_ref, bf16[128,2048]{1,0:T(8,128)(2,1)} %get-tuple-element.24.value_ref), custom_call_target="tpu_custom_call" | custom-call | flops 1073741824 | bytes 5242880 | tf_op jit(solution)/shard_map/pallas_call | solution.py:101
  86.8 0.1 broadcast_in_dim.39
  86.9 0.1 reshape.120
  87.0 0.1 broadcast_in_dim.37
  87.1 0.1 reshape.118
  87.2 0.1 broadcast_in_dim.38
  87.3 0.1 reshape.119
  87.4 0.6 fusion.5
  (16 shorter events, 0.8 us)
Async XLA Ops:
  1.4 9.0 %collective-permute-start = (bf16[1,8,6144]{2,1,0:T(8,128)(2,1)S(1)}, bf16[1,8,6144]{2,1,0:T(8,128)(2,1)S(1)}, u32[]{:S(2)}, u32[]{:S(2)}) collective-permute-start(bf16[1,8,6144]{2,1,0:T(8,128)(2,1)S(1)} %maximum_bitcast_fusion.1), channel_id=1, source_target_pairs={{0,8},{1,9},{2,10},{3,11},{4,12},{5,13},{6,14},{7,15},{8,0},{9,1},... | collective-permute-start | bytes 294920 | tf_op jit(solution)/shard_map/ppermute | solution.py:17
  11.3 6.2 %collective-permute-start.1 = (bf16[2,8,6144]{2,1,0:T(8,128)(2,1)S(1)}, bf16[2,8,6144]{2,1,0:T(8,128)(2,1)S(1)}, u32[]{:S(2)}, u32[]{:S(2)}) collective-permute-start(bf16[2,8,6144]{2,1,0:T(8,128)(2,1)S(1)} %maximum_bitcast_fusion), channel_id=1, source_target_pairs={{0,4},{1,5},{2,6},{3,7},{4,0},{5,1},{6,2},{7,3},{8,12},{9,13},{10,... | collective-permute-start | bytes 589832 | tf_op jit(solution)/shard_map/ppermute | solution.py:17
  17.5 9.4 %collective-permute-start.2 = (bf16[4,8,6144]{2,1,0:T(8,128)(2,1)S(1)}, bf16[4,8,6144]{2,1,0:T(8,128)(2,1)S(1)}, u32[]{:S(2)}, u32[]{:S(2)}) collective-permute-start(bf16[4,8,6144]{2,1,0:T(8,128)(2,1)S(1)} %bitcast.65), channel_id=1, source_target_pairs={{0,2},{1,3},{2,0},{3,1},{4,6},{5,7},{6,4},{7,5},{8,10},{9,11},{10,... | collective-permute-start | bytes 1179656 | tf_op jit(solution)/shard_map/ppermute | solution.py:17
  27.2 2.4 %collective-permute-start.3 = (bf16[8,8,6144]{2,1,0:T(8,128)(2,1)S(1)}, bf16[8,8,6144]{2,1,0:T(8,128)(2,1)S(1)}, u32[]{:S(2)}, u32[]{:S(2)}) collective-permute-start(bf16[8,8,6144]{2,1,0:T(8,128)(2,1)S(1)} %bitcast.63), channel_id=1, source_target_pairs={{0,1},{1,0},{2,3},{3,2},{4,5},{5,4},{6,7},{7,6},{8,9},{9,8},{10,11... | collective-permute-start | bytes 2359304 | tf_op jit(solution)/shard_map/ppermute | solution.py:17
  48.2 2.0 %collective-permute-start.4 = (f32[8,8,2112]{2,1,0:T(8,128)S(1)}, f32[8,8,2112]{2,1,0:T(8,128)S(1)}, u32[]{:S(2)}, u32[]{:S(2)}) collective-permute-start(f32[8,8,2112]{2,1,0:T(8,128)S(1)} %get-tuple-element.29), channel_id=1, source_target_pairs={{0,1},{1,0},{2,3},{3,2},{4,5},{5,4},{6,7},{7,6},{8,9},{9,8},{10,11... | collective-permute-start | bytes 1622024 | tf_op jit(solution)/shard_map/ppermute | solution.py:17
  51.9 8.8 %collective-permute-start.5 = (f32[4,8,2112]{2,1,0:T(8,128)S(1)}, f32[4,8,2112]{2,1,0:T(8,128)S(1)}, u32[]{:S(2)}, u32[]{:S(2)}) collective-permute-start(f32[4,8,2112]{2,1,0:T(8,128)S(1)} %get-tuple-element.33), channel_id=1, source_target_pairs={{0,2},{1,3},{2,0},{3,1},{4,6},{5,7},{6,4},{7,5},{8,10},{9,11},{10,... | collective-permute-start | bytes 811016 | tf_op jit(solution)/shard_map/ppermute | solution.py:17
  61.7 5.5 %collective-permute-start.6 = (f32[2,8,2112]{2,1,0:T(8,128)S(1)}, f32[2,8,2112]{2,1,0:T(8,128)S(1)}, u32[]{:S(2)}, u32[]{:S(2)}) collective-permute-start(f32[2,8,2112]{2,1,0:T(8,128)S(1)} %get-tuple-element.37), channel_id=1, source_target_pairs={{0,4},{1,5},{2,6},{3,7},{4,0},{5,1},{6,2},{7,3},{8,12},{9,13},{10,... | collective-permute-start | bytes 405512 | tf_op jit(solution)/shard_map/ppermute | solution.py:17
  67.9 18.8 %collective-permute-start.7 = (f32[1,8,2112]{2,1,0:T(8,128)S(1)}, f32[1,8,2112]{2,1,0:T(8,128)S(1)}, u32[]{:S(2)}, u32[]{:S(2)}) collective-permute-start(f32[1,8,2112]{2,1,0:T(8,128)S(1)} %get-tuple-element.41), channel_id=1, source_target_pairs={{0,8},{1,9},{2,10},{3,11},{4,12},{5,13},{6,14},{7,15},{8,0},{9,1},... | collective-permute-start | bytes 202760 | tf_op jit(solution)/shard_map/ppermute | solution.py:17

commit v3 on v2

--- a/solution.py
+++ b/solution.py
@@ -76,44 +76,53 @@
     )
 
 
-def video_kernel(query_ref, key_ref, value_ref, out_ref):
+def video_kernel(query_ref, key_ref, value_ref, earlier_ref, out_ref):
+    del earlier_ref
     queries = query_ref[...]
     keys = key_ref[...]
     values = value_ref[...]
     first = head_masks(queries.shape[0])
-    results = []
+    sums = []
+    counts = []
     for lanes in (first, jnp.logical_not(first)):
         scores = pair_scores(queries, keys, lanes)
         highest = jnp.max(scores, axis=1, keepdims=True)
         weights = jnp.exp(scores - highest)
-        totals = jnp.sum(weights, axis=1, keepdims=True)
-        summed = jnp.dot(
-            weights.astype(jnp.bfloat16), values, preferred_element_type=jnp.float32
+        counts.append(jnp.sum(weights, axis=1, keepdims=True))
+        sums.append(
+            jnp.dot(weights.astype(jnp.bfloat16), values, preferred_element_type=jnp.float32)
         )
-        results.append(summed / totals)
-    out_ref[...] = jnp.where(first, results[0], results[1]).astype(out_ref.dtype)
-
-
-def video_attention(queries, keys, values):
+    summed = jnp.where(first, sums[0], sums[1])
+    totals = jnp.where(first, counts[0], counts[1])
+    out_ref[...] = (summed / totals).astype(out_ref.dtype)
+
+
+def video_attention(queries, keys, values, groups):
     rows, width = queries.shape
-    pairs = width // (2 * HEAD_DIM)
+    pairs = width // (2 * HEAD_DIM) // groups
     key_rows = keys.shape[0]
-    return pl.pallas_call(
-        video_kernel,
-        grid=(pairs,),
-        in_specs=[
-            pl.BlockSpec((rows, 2 * HEAD_DIM), lambda p: (0, p)),
-            pl.BlockSpec((key_rows, 2 * HEAD_DIM), lambda p: (0, p)),
-            pl.BlockSpec((key_rows, 2 * HEAD_DIM), lambda p: (0, p)),
-        ],
-        out_specs=pl.BlockSpec((rows, 2 * HEAD_DIM), lambda p: (0, p)),
-        out_shape=jax.ShapeDtypeStruct((rows, width), jnp.bfloat16),
-        cost_estimate=pl.CostEstimate(
-            flops=8 * rows * key_rows * width,
-            transcendentals=rows * key_rows * width // HEAD_DIM,
-            bytes_accessed=2 * (2 * rows * width + 2 * key_rows * width),
-        ),
-    )(queries, keys, values)
+    out = jnp.zeros((rows, width), jnp.bfloat16)
+    for group in range(groups):
+        first_pair = group * pairs
+        out = pl.pallas_call(
+            video_kernel,
+            grid=(pairs,),
+            in_specs=[
+                pl.BlockSpec((rows, 2 * HEAD_DIM), lambda p, f=first_pair: (0, p + f)),
+                pl.BlockSpec((key_rows, 2 * HEAD_DIM), lambda p, f=first_pair: (0, p + f)),
+                pl.BlockSpec((key_rows, 2 * HEAD_DIM), lambda p, f=first_pair: (0, p + f)),
+                pl.BlockSpec(memory_space=pl.ANY),
+            ],
+            out_specs=pl.BlockSpec((rows, 2 * HEAD_DIM), lambda p, f=first_pair: (0, p + f)),
+            out_shape=jax.ShapeDtypeStruct((rows, width), jnp.bfloat16),
+            input_output_aliases={3: 0},
+            cost_estimate=pl.CostEstimate(
+                flops=8 * rows * key_rows * width // groups,
+                transcendentals=rows * key_rows * width // HEAD_DIM // groups,
+                bytes_accessed=2 * (2 * rows * width + 2 * key_rows * width) // groups,
+            ),
+        )(queries, keys, values, out)
+    return out
 
 
 def audio_kernel(query_ref, key_ref, value_ref, sum_ref, total_ref, top_ref):
@@ -149,17 +158,18 @@
     sum_ref[...] = jnp.where(first, results[0], results[1])
 
 
-def audio_partial(queries, keys, values):
+def audio_partial(queries, keys, values, group, groups):
     rows, width = queries.shape
-    heads = width // HEAD_DIM
+    heads = width // HEAD_DIM // groups
+    first_pair = group * heads // 2
     key_rows = keys.shape[0]
     return pl.pallas_call(
         audio_kernel,
         grid=(heads // 2,),
         in_specs=[
-            pl.BlockSpec((rows, 2 * HEAD_DIM), lambda p: (0, p)),
-            pl.BlockSpec((key_rows, 2 * HEAD_DIM), lambda p: (0, p)),
-            pl.BlockSpec((key_rows, 2 * HEAD_DIM), lambda p: (0, p)),
+            pl.BlockSpec((rows, 2 * HEAD_DIM), lambda p: (0, p + first_pair)),
+            pl.BlockSpec((key_rows, 2 * HEAD_DIM), lambda p: (0, p + first_pair)),
+            pl.BlockSpec((key_rows, 2 * HEAD_DIM), lambda p: (0, p + first_pair)),
         ],
         out_specs=[
             pl.BlockSpec((rows, 2 * HEAD_DIM), lambda p: (0, p)),
@@ -167,15 +177,15 @@
             pl.BlockSpec((rows, heads), lambda p: (0, 0)),
         ],
         out_shape=[
-            jax.ShapeDtypeStruct((rows, width), jnp.float32),
+            jax.ShapeDtypeStruct((rows, heads * HEAD_DIM), jnp.float32),
             jax.ShapeDtypeStruct((rows, heads), jnp.float32),
             jax.ShapeDtypeStruct((rows, heads), jnp.float32),
         ],
         compiler_params=pltpu.CompilerParams(dimension_semantics=("arbitrary",)),
         cost_estimate=pl.CostEstimate(
-            flops=8 * rows * key_rows * width,
+            flops=8 * rows * key_rows * width // groups,
             transcendentals=rows * key_rows * heads,
-            bytes_accessed=2 * rows * width + 4 * key_rows * width + 4 * rows * width,
+            bytes_accessed=(2 * rows * width + 4 * key_rows * width + 4 * rows * width) // groups,
         ),
     )(queries, keys, values)
 
@@ -183,18 +193,24 @@
 def local(video_q, video_k, video_v, audio_q, audio_k, audio_v):
     width = video_q.shape[1]
     heads = width // HEAD_DIM
-    packed = jnp.concatenate([audio_q, audio_k, audio_v], axis=1)
+    groups = 4
+    all_queries = gather_rows(audio_q)
+    all_queries, packed = lax.optimization_barrier(
+        (all_queries, jnp.concatenate([audio_k, audio_v], axis=1))
+    )
     gathered = gather_rows(packed)
-    all_queries = gathered[:, :width]
-    all_keys = gathered[:, width : 2 * width]
-    all_values = gathered[:, 2 * width :]
-
-    summed, totals, highest = audio_partial(all_queries, video_k, video_v)
-    state = jnp.concatenate([summed, totals, highest], axis=1)
+    all_keys = gathered[:, :width]
+    all_values = gathered[:, width:]
+
+    parts = [audio_partial(all_queries, video_k, video_v, g, groups) for g in range(groups)]
+    state = jnp.concatenate(
+        [part[0] for part in parts] + [part[1] for part in parts] + [part[2] for part in parts],
+        axis=1,
+    )
     mine = scatter_rows(state, heads)
     audio_out = (mine[:, :width] / spread(mine[:, width : width + heads])).astype(jnp.bfloat16)
 
-    video_out = video_attention(video_q, all_keys, all_values)
+    video_out = video_attention(video_q, all_keys, all_values, groups)
     return video_out, audio_out
 
 

time: 89 us -> 93.5 us (1.051)
  waiting for transfers between devices: 33.1 us -> 24.8 us
  Pallas kernels: 30.5 us -> 38.5 us
  starting transfers between devices: 14.1 us -> 16.4 us
  local copies, waits for them, and re-layouts: 6.17 us -> 8.33 us
    ppermute x8 -> x12, waiting for transfers between devices: 33.1 us -> 24.8 us  [exchange(): return lax.ppermute(value, 'seq', pairs)]
    pallas_call x1 -> x4, Pallas kernels: 15.5 us -> 19.7 us  [audio_partial(): pl.pallas_call(audio_kernel, grid=(heads // 2,), in_specs=[pl.BlockSpec((...]
    pallas_call x1 -> x4, Pallas kernels: 14.9 us -> 18.8 us  [video_attention(): pl.pallas_call(video_kernel, grid=(pairs,), in_specs=[pl.BlockSpec((rows,...]
    ppermute x8 -> x12, starting transfers between devices: 14.1 us -> 16.4 us  [exchange(): return lax.ppermute(value, 'seq', pairs)]
    broadcast_in_dim x0 -> x1, local copies, waits for them, and re-layouts: none -> 1.57 us  [video_attention(): out = jnp.zeros((rows, width), jnp.bfloat16)]
    another operation x7 -> x14, other arithmetic: 1.35 us -> 2.27 us  [gather_rows(): held = jnp.stack([low, high], axis=1).reshape((-1,) + block.shape)]
  transfers between devices with their start and end apart: 8 -> 12, of which waited for: 7 -> 8; matrix products, arithmetic and copies ran while one was open for 0% -> 8% of each run, Pallas kernels for 17% -> 41%
where the time goes in v3:
time: 93.5 us; the launch traced here: 92.8 us
  Pallas kernels  38.5 us (41%)
  waiting for transfers between devices  24.8 us (27%)
  starting transfers between devices  16.4 us (18%)
  local copies, waits for them, and re-layouts  8.33 us (9%)
  other arithmetic  3.61 us (4%)
  between operations  1.07 us (1%)
    ppermute x12, waiting for transfers between devices, exchange(): return lax.ppermute(value, 'seq', pairs)  24.8 us
    pallas_call x4, Pallas kernels, audio_partial(): pl.pallas_call(audio_kernel, grid=(heads // 2,), in_specs=[pl.BlockSpec((...  19.7 us
    pallas_call x4, Pallas kernels, video_attention(): pl.pallas_call(video_kernel, grid=(pairs,), in_specs=[pl.BlockSpec((rows,...  18.8 us
    ppermute x12, starting transfers between devices, exchange(): return lax.ppermute(value, 'seq', pairs)  16.4 us
    another operation x14, other arithmetic, gather_rows(): held = jnp.stack([low, high], axis=1).reshape((-1,) + block.shape)  2.27 us
  transfers between devices with their start and end apart: 12, of which 8 were waited for; matrix products, arithmetic and copies ran while one was open for 8% of the time, Pallas kernels for 41%

profile of v3, /device:TPU:0, one launch (start us, length us, event | category | flops | bytes accessed | tf_op | source)
XLA Modules:
  0.0 92.8 jit_solution(4248226727319800038)
XLA Ops:
  0.7 4.1 %collective-permute-start = (bf16[1,8,2048]{2,1,0:T(8,128)(2,1)}, bf16[1,8,2048]{2,1,0:T(8,128)(2,1)S(1)}, u32[]{:S(2)}, u32[]{:S(2)}) collective-permute-start(bf16[1,8,2048]{2,1,0:T(8,128)(2,1)} %bitcast.114), channel_id=1, source_target_pairs={{0,8},{1,9},{2,10},{3,11},{4,12},{5,13},{6,14},{7,15},{8,0},{9,1},... | collective-permute-start | bytes 98312 | tf_op jit(solution)/shard_map/ppermute | solution.py:17
  4.8 2.5 %collective-permute-done = bf16[1,8,2048]{2,1,0:T(8,128)(2,1)S(1)} collective-permute-done((bf16[1,8,2048]{2,1,0:T(8,128)(2,1)}, bf16[1,8,2048]{2,1,0:T(8,128)(2,1)S(1)}, u32[]{:S(2)}, u32[]{:S(2)}) %collective-permute-start) | collective-permute-done | bytes 32800 | tf_op jit(solution)/shard_map/ppermute | solution.py:17
  7.2 0.8 select_bitcast_fusion.23
  8.0 1.6 %collective-permute-start.1 = (bf16[2,8,2048]{2,1,0:T(8,128)(2,1)S(1)}, bf16[2,8,2048]{2,1,0:T(8,128)(2,1)S(1)}, u32[]{:S(2)}, u32[]{:S(2)}) collective-permute-start(bf16[2,8,2048]{2,1,0:T(8,128)(2,1)S(1)} %maximum_bitcast_fusion.1), channel_id=1, source_target_pairs={{0,4},{1,5},{2,6},{3,7},{4,0},{5,1},{6,2},{7,3},{8,12},{9,13},{10,... | collective-permute-start | bytes 196616 | tf_op jit(solution)/shard_map/ppermute | solution.py:17
  9.6 2.7 %collective-permute-done.1 = bf16[2,8,2048]{2,1,0:T(8,128)(2,1)S(1)} collective-permute-done((bf16[2,8,2048]{2,1,0:T(8,128)(2,1)S(1)}, bf16[2,8,2048]{2,1,0:T(8,128)(2,1)S(1)}, u32[]{:S(2)}, u32[]{:S(2)}) %collective-permute-start.1) | collective-permute-done | bytes 65568 | tf_op jit(solution)/shard_map/ppermute | solution.py:17
  12.4 1.8 %collective-permute-start.2 = (bf16[4,8,2048]{2,1,0:T(8,128)(2,1)S(1)}, bf16[4,8,2048]{2,1,0:T(8,128)(2,1)S(1)}, u32[]{:S(2)}, u32[]{:S(2)}) collective-permute-start(bf16[4,8,2048]{2,1,0:T(8,128)(2,1)S(1)} %bitcast.106), channel_id=1, source_target_pairs={{0,2},{1,3},{2,0},{3,1},{4,6},{5,7},{6,4},{7,5},{8,10},{9,11},{10,... | collective-permute-start | bytes 393224 | tf_op jit(solution)/shard_map/ppermute | solution.py:17
  14.2 3.2 %collective-permute-done.2 = bf16[4,8,2048]{2,1,0:T(8,128)(2,1)S(1)} collective-permute-done((bf16[4,8,2048]{2,1,0:T(8,128)(2,1)S(1)}, bf16[4,8,2048]{2,1,0:T(8,128)(2,1)S(1)}, u32[]{:S(2)}, u32[]{:S(2)}) %collective-permute-start.2) | collective-permute-done | bytes 131104 | tf_op jit(solution)/shard_map/ppermute | solution.py:17
  17.6 1.5 %collective-permute-done.3 = bf16[8,8,2048]{2,1,0:T(8,128)(2,1)S(1)} collective-permute-done((bf16[8,8,2048]{2,1,0:T(8,128)(2,1)S(1)}, bf16[8,8,2048]{2,1,0:T(8,128)(2,1)S(1)}, u32[]{:S(2)}, u32[]{:S(2)}) %collective-permute-start.3) | collective-permute-done | bytes 262176 | tf_op jit(solution)/shard_map/ppermute | solution.py:17
  19.2 0.8 copy.22
  20.0 2.6 %collective-permute-start.4 = (bf16[1,8,4096]{2,1,0:T(8,128)(2,1)S(1)}, bf16[1,8,4096]{2,1,0:T(8,128)(2,1)S(1)}, u32[]{:S(2)}, u32[]{:S(2)}) collective-permute-start(bf16[1,8,4096]{2,1,0:T(8,128)(2,1)S(1)} %bitcast.109), channel_id=1, source_target_pairs={{0,8},{1,9},{2,10},{3,11},{4,12},{5,13},{6,14},{7,15},{8,0},{9,1},... | collective-permute-start | bytes 196616 | tf_op jit(solution)/shard_map/ppermute | solution.py:17
  22.6 4.9 %shard_map.84 = (f32[128,512]{1,0:T(8,128)}, f32[128,8]{1,0:T(8,128)}, f32[128,8]{1,0:T(8,128)}) custom-call(bf16[128,2048]{1,0:T(8,128)(2,1)} %bitcast.92, bf16[512,2048]{1,0:T(8,128)(2,1)} %key_ref.7, bf16[512,2048]{1,0:T(8,128)(2,1)} %value_ref.7), custom_call_target="tpu_custom_call" | custom-call | flops 268435456 | bytes 1441792 | tf_op jit(solution)/shard_map/pallas_call | solution.py:166
  27.5 4.9 %shard_map.83 = (f32[128,512]{1,0:T(8,128)}, f32[128,8]{1,0:T(8,128)}, f32[128,8]{1,0:T(8,128)}) custom-call(bf16[128,2048]{1,0:T(8,128)(2,1)} %bitcast.93, bf16[512,2048]{1,0:T(8,128)(2,1)} %key_ref.7, bf16[512,2048]{1,0:T(8,128)(2,1)} %value_ref.7), custom_call_target="tpu_custom_call" | custom-call | flops 268435456 | bytes 1441792 | tf_op jit(solution)/shard_map/pallas_call | solution.py:166
  32.4 4.9 %shard_map.82 = (f32[128,512]{1,0:T(8,128)}, f32[128,8]{1,0:T(8,128)}, f32[128,8]{1,0:T(8,128)}) custom-call(bf16[128,2048]{1,0:T(8,128)(2,1)} %bitcast.94, bf16[512,2048]{1,0:T(8,128)(2,1)} %key_ref.7, bf16[512,2048]{1,0:T(8,128)(2,1)} %value_ref.7), custom_call_target="tpu_custom_call" | custom-call | flops 268435456 | bytes 1441792 | tf_op jit(solution)/shard_map/pallas_call | solution.py:166
  37.4 5.0 %shard_map.81 = (f32[128,512]{1,0:T(8,128)}, f32[128,8]{1,0:T(8,128)}, f32[128,8]{1,0:T(8,128)}) custom-call(bf16[128,2048]{1,0:T(8,128)(2,1)} %bitcast.95, bf16[512,2048]{1,0:T(8,128)(2,1)} %key_ref.7, bf16[512,2048]{1,0:T(8,128)(2,1)} %value_ref.7), custom_call_target="tpu_custom_call" | custom-call | flops 268435456 | bytes 1441792 | tf_op jit(solution)/shard_map/pallas_call | solution.py:166
  42.4 1.2 %concatenate.16 = f32[128,2112]{1,0:T(8,128)S(1)} concatenate(f32[128,512]{1,0:T(8,128)} %get-tuple-element.18, f32[128,512]{1,0:T(8,128)S(1)} %copy-done.2, f32[128,512]{1,0:T(8,128)S(1)} %copy-done.1, f32[128,512]{1,0:T(8,128)S(1)} %copy-done, f32[128,8]{1,0:T(8,128)} %get-tuple-element.22, f32[128,8]{1,0:T(8,128)S(1)} %copy-done.7, f32[128,8]{1,0:T(8,128)S(1)} %copy-done.5, ...), dimensions={1} | concatenate | bytes 2162688 | tf_op jit(solution)/shard_map/concatenate | solution.py:206
  43.8 1.9 %collective-permute-start.5 = (bf16[2,8,4096]{2,1,0:T(8,128)(2,1)S(1)}, bf16[2,8,4096]{2,1,0:T(8,128)(2,1)S(1)}, u32[]{:S(2)}, u32[]{:S(2)}) collective-permute-start(bf16[2,8,4096]{2,1,0:T(8,128)(2,1)S(1)} %maximum_bitcast_fusion), channel_id=1, source_target_pairs={{0,4},{1,5},{2,6},{3,7},{4,0},{5,1},{6,2},{7,3},{8,12},{9,13},{10,... | collective-permute-start | bytes 393224 | tf_op jit(solution)/shard_map/ppermute | solution.py:17
  45.8 3.3 %collective-permute-done.5 = bf16[2,8,4096]{2,1,0:T(8,128)(2,1)S(1)} collective-permute-done((bf16[2,8,4096]{2,1,0:T(8,128)(2,1)S(1)}, bf16[2,8,4096]{2,1,0:T(8,128)(2,1)S(1)}, u32[]{:S(2)}, u32[]{:S(2)}) %collective-permute-start.5) | collective-permute-done | bytes 131104 | tf_op jit(solution)/shard_map/ppermute | solution.py:17
  49.2 1.6 %collective-permute-start.6 = (bf16[4,8,4096]{2,1,0:T(8,128)(2,1)S(1)}, bf16[4,8,4096]{2,1,0:T(8,128)(2,1)}, u32[]{:S(2)}, u32[]{:S(2)}) collective-permute-start(bf16[4,8,4096]{2,1,0:T(8,128)(2,1)S(1)} %bitcast.101), channel_id=1, source_target_pairs={{0,2},{1,3},{2,0},{3,1},{4,6},{5,7},{6,4},{7,5},{8,10},{9,11},{10,... | collective-permute-start | bytes 786440 | tf_op jit(solution)/shard_map/ppermute | solution.py:17
  50.9 0.3 broadcast_in_dim.39
  51.2 0.4 reshape.121
  51.6 0.3 broadcast_in_dim.40
  51.9 0.4 reshape.122
  52.3 0.1 fusion
  52.5 0.6 collective-permute-start.9
  53.1 5.5 %collective-permute-done.6 = bf16[4,8,4096]{2,1,0:T(8,128)(2,1)} collective-permute-done((bf16[4,8,4096]{2,1,0:T(8,128)(2,1)S(1)}, bf16[4,8,4096]{2,1,0:T(8,128)(2,1)}, u32[]{:S(2)}, u32[]{:S(2)}) %collective-permute-start.6) | collective-permute-done | bytes 262176 | tf_op jit(solution)/shard_map/ppermute | solution.py:17
  58.6 1.0 %select_bitcast_fusion.7 = (bf16[4,1,8,4096]{3,2,0,1:T(8,128)(2,1)S(1)}, bf16[4,1,8,4096]{3,2,0,1:T(8,128)(2,1)S(1)}) fusion(bf16[4,8,4096]{2,1,0:T(8,128)(2,1)} %collective-permute-done.6, pred[]{:T(512)S(6)} %ne.9, bf16[2,2,8,4096]{3,2,1,0:T(8,128)(2,1)S(1)} %pad_maximum_fusion.4), kind=kLoop, calls=%fused_computation.18 | loop fusion | flops 262144 | bytes 1048577 | tf_op jit(solution)/shard_map/stack | solution.py:30
  59.6 2.9 %collective-permute-done.9 = f32[4,8,2112]{2,1,0:T(8,128)S(1)} collective-permute-done((f32[4,8,2112]{2,1,0:T(8,128)S(1)}, f32[4,8,2112]{2,1,0:T(8,128)S(1)}, u32[]{:S(2)}, u32[]{:S(2)}) %collective-permute-start.9) | collective-permute-done | bytes 270368 | tf_op jit(solution)/shard_map/ppermute | solution.py:17
  62.5 0.2 broadcast_in_dim.41
  62.7 0.2 reshape.124
  62.9 0.2 broadcast_in_dim.42
  63.1 0.2 reshape.125
  63.5 1.7 %collective-permute-start.10 = (f32[2,8,2112]{2,1,0:T(8,128)S(1)}, f32[2,8,2112]{2,1,0:T(8,128)S(1)}, u32[]{:S(2)}, u32[]{:S(2)}) collective-permute-start(f32[2,8,2112]{2,1,0:T(8,128)S(1)} %get-tuple-element.58), channel_id=1, source_target_pairs={{0,4},{1,5},{2,6},{3,7},{4,0},{5,1},{6,2},{7,3},{8,12},{9,13},{10,... | collective-permute-start | bytes 405512 | tf_op jit(solution)/shard_map/ppermute | solution.py:17
  65.4 3.2 %collective-permute-done.10 = f32[2,8,2112]{2,1,0:T(8,128)S(1)} collective-permute-done((f32[2,8,2112]{2,1,0:T(8,128)S(1)}, f32[2,8,2112]{2,1,0:T(8,128)S(1)}, u32[]{:S(2)}, u32[]{:S(2)}) %collective-permute-start.10) | collective-permute-done | bytes 135200 | tf_op jit(solution)/shard_map/ppermute | solution.py:17
  68.7 0.1 broadcast_in_dim.43
  68.8 0.1 reshape.127
  68.9 0.1 broadcast_in_dim.44
  69.1 0.1 reshape.128
  69.3 0.4 collective-permute-start.11
  69.7 0.1 select_bitcast_fusion.3
  69.8 0.1 pad_maximum_fusion
  70.0 1.1 %fusion.14 = (bf16[128,2048]{1,0:T(8,128)(2,1)}, bf16[128,2048]{1,0:T(8,128)(2,1)}) fusion(bf16[128,4096]{1,0:T(8,128)(2,1)S(1)} %bitcast.97), kind=kLoop, calls=%fused_computation.72 | loop fusion | bytes 2097152 | tf_op jit(solution)/shard_map/slice | solution.py:203
  71.1 1.6 %broadcast_in_dim.38.earlier_ref = bf16[512,2048]{1,0:T(8,128)(2,1)} broadcast(bf16[]{:T(256)} %constant.6.clone.1), dimensions={} | broadcast | bytes 2097154 | tf_op jit(solution)/shard_map/broadcast_in_dim | solution.py:104
  72.6 4.7 %shard_map.77.earlier_ref = bf16[512,2048]{1,0:T(8,128)(2,1)} custom-call(bf16[512,2048]{1,0:T(8,128)(2,1)} %query_ref.7, bf16[128,2048]{1,0:T(8,128)(2,1)} %get-tuple-element.48.key_ref, bf16[128,2048]{1,0:T(8,128)(2,1)} %get-tuple-element.47.value_ref, bf16[512,2048]{1,0:T(8,128)(2,1)} %broadcast_in_dim.38.earlier_ref), custom_call_target="tpu_custom_call", output_to_operand_aliasing={{}: (3, {})} | custom-call | flops 268435456 | bytes 1310720 | tf_op jit(solution)/shard_map/pallas_call | solution.py:107
  77.3 4.7 %shard_map.78.earlier_ref = bf16[512,2048]{1,0:T(8,128)(2,1)} custom-call(bf16[512,2048]{1,0:T(8,128)(2,1)} %query_ref.7, bf16[128,2048]{1,0:T(8,128)(2,1)} %get-tuple-element.48.key_ref, bf16[128,2048]{1,0:T(8,128)(2,1)} %get-tuple-element.47.value_ref, bf16[512,2048]{1,0:T(8,128)(2,1)} %shard_map.77.earlier_ref), custom_call_target="tpu_custom_call", output_to_operand_aliasing={{}: (3, {})} | custom-call | flops 268435456 | bytes 1310720 | tf_op jit(solution)/shard_map/pallas_call | solution.py:107
  82.0 4.7 %shard_map.79.earlier_ref = bf16[512,2048]{1,0:T(8,128)(2,1)} custom-call(bf16[512,2048]{1,0:T(8,128)(2,1)} %query_ref.7, bf16[128,2048]{1,0:T(8,128)(2,1)} %get-tuple-element.48.key_ref, bf16[128,2048]{1,0:T(8,128)(2,1)} %get-tuple-element.47.value_ref, bf16[512,2048]{1,0:T(8,128)(2,1)} %shard_map.78.earlier_ref), custom_call_target="tpu_custom_call", output_to_operand_aliasing={{}: (3, {})} | custom-call | flops 268435456 | bytes 1310720 | tf_op jit(solution)/shard_map/pallas_call | solution.py:107
  86.7 4.7 %shard_map.80 = bf16[512,2048]{1,0:T(8,128)(2,1)} custom-call(bf16[512,2048]{1,0:T(8,128)(2,1)} %query_ref.7, bf16[128,2048]{1,0:T(8,128)(2,1)} %get-tuple-element.48.key_ref, bf16[128,2048]{1,0:T(8,128)(2,1)} %get-tuple-element.47.value_ref, bf16[512,2048]{1,0:T(8,128)(2,1)} %shard_map.79.earlier_ref), custom_call_target="tpu_custom_call", output_to_operand_aliasing={{}: (3, {})} | custom-call | flops 268435456 | bytes 1310720 | tf_op jit(solution)/shard_map/pallas_call | solution.py:107
  91.5 0.1 broadcast_in_dim.47
  92.1 0.6 fusion.5
  (63 shorter events, 2.0 us)
Async XLA Ops:
  0.6 16.9 %copy-start.9 = (bf16[8,2048]{1,0:T(8,128)(2,1)S(1)}, bf16[8,2048]{1,0:T(8,128)(2,1)}, u32[]{:S(2)}) copy-start(bf16[8,2048]{1,0:T(8,128)(2,1)} %param.11) | copy-start | bytes 98308
  0.6 16.9 %copy-start.10 = (bf16[8,2048]{1,0:T(8,128)(2,1)S(1)}, bf16[8,2048]{1,0:T(8,128)(2,1)}, u32[]{:S(2)}) copy-start(bf16[8,2048]{1,0:T(8,128)(2,1)} %param.10) | copy-start | bytes 98308
  0.7 6.6 %collective-permute-start = (bf16[1,8,2048]{2,1,0:T(8,128)(2,1)}, bf16[1,8,2048]{2,1,0:T(8,128)(2,1)S(1)}, u32[]{:S(2)}, u32[]{:S(2)}) collective-permute-start(bf16[1,8,2048]{2,1,0:T(8,128)(2,1)} %bitcast.114), channel_id=1, source_target_pairs={{0,8},{1,9},{2,10},{3,11},{4,12},{5,13},{6,14},{7,15},{8,0},{9,1},... | collective-permute-start | bytes 98312 | tf_op jit(solution)/shard_map/ppermute | solution.py:17
  8.0 4.3 %collective-permute-start.1 = (bf16[2,8,2048]{2,1,0:T(8,128)(2,1)S(1)}, bf16[2,8,2048]{2,1,0:T(8,128)(2,1)S(1)}, u32[]{:S(2)}, u32[]{:S(2)}) collective-permute-start(bf16[2,8,2048]{2,1,0:T(8,128)(2,1)S(1)} %maximum_bitcast_fusion.1), channel_id=1, source_target_pairs={{0,4},{1,5},{2,6},{3,7},{4,0},{5,1},{6,2},{7,3},{8,12},{9,13},{10,... | collective-permute-start | bytes 196616 | tf_op jit(solution)/shard_map/ppermute | solution.py:17
  12.4 5.0 %collective-permute-start.2 = (bf16[4,8,2048]{2,1,0:T(8,128)(2,1)S(1)}, bf16[4,8,2048]{2,1,0:T(8,128)(2,1)S(1)}, u32[]{:S(2)}, u32[]{:S(2)}) collective-permute-start(bf16[4,8,2048]{2,1,0:T(8,128)(2,1)S(1)} %bitcast.106), channel_id=1, source_target_pairs={{0,2},{1,3},{2,0},{3,1},{4,6},{5,7},{6,4},{7,5},{8,10},{9,11},{10,... | collective-permute-start | bytes 393224 | tf_op jit(solution)/shard_map/ppermute | solution.py:17
  17.5 1.6 %collective-permute-start.3 = (bf16[8,8,2048]{2,1,0:T(8,128)(2,1)S(1)}, bf16[8,8,2048]{2,1,0:T(8,128)(2,1)S(1)}, u32[]{:S(2)}, u32[]{:S(2)}) collective-permute-start(bf16[8,8,2048]{2,1,0:T(8,128)(2,1)S(1)} %bitcast.102), channel_id=1, source_target_pairs={{0,1},{1,0},{2,3},{3,2},{4,5},{5,4},{6,7},{7,6},{8,9},{9,8},{10,11... | collective-permute-start | bytes 786440 | tf_op jit(solution)/shard_map/ppermute | solution.py:17
  20.0 23.7 %collective-permute-start.4 = (bf16[1,8,4096]{2,1,0:T(8,128)(2,1)S(1)}, bf16[1,8,4096]{2,1,0:T(8,128)(2,1)S(1)}, u32[]{:S(2)}, u32[]{:S(2)}) collective-permute-start(bf16[1,8,4096]{2,1,0:T(8,128)(2,1)S(1)} %bitcast.109), channel_id=1, source_target_pairs={{0,8},{1,9},{2,10},{3,11},{4,12},{5,13},{6,14},{7,15},{8,0},{9,1},... | collective-permute-start | bytes 196616 | tf_op jit(solution)/shard_map/ppermute | solution.py:17
  37.3 5.0 %copy-start = (f32[128,512]{1,0:T(8,128)S(1)}, f32[128,512]{1,0:T(8,128)}, u32[]{:S(2)}) copy-start(f32[128,512]{1,0:T(8,128)} %get-tuple-element.21) | copy-start | bytes 786436
  37.3 5.0 %copy-start.1 = (f32[128,512]{1,0:T(8,128)S(1)}, f32[128,512]{1,0:T(8,128)}, u32[]{:S(2)}) copy-start(f32[128,512]{1,0:T(8,128)} %get-tuple-element.20) | copy-start | bytes 786436
  37.3 5.0 %copy-start.2 = (f32[128,512]{1,0:T(8,128)S(1)}, f32[128,512]{1,0:T(8,128)}, u32[]{:S(2)}) copy-start(f32[128,512]{1,0:T(8,128)} %get-tuple-element.19) | copy-start | bytes 786436
  37.4 5.0 %copy-start.3 = (f32[128,8]{1,0:T(8,128)S(1)}, f32[128,8]{1,0:T(8,128)}, u32[]{:S(2)}) copy-start(f32[128,8]{1,0:T(8,128)} %get-tuple-element.25) | copy-start | bytes 12292
  37.4 5.0 %copy-start.4 = (f32[128,8]{1,0:T(8,128)S(1)}, f32[128,8]{1,0:T(8,128)}, u32[]{:S(2)}) copy-start(f32[128,8]{1,0:T(8,128)} %get-tuple-element.29) | copy-start | bytes 12292
  37.4 5.0 %copy-start.5 = (f32[128,8]{1,0:T(8,128)S(1)}, f32[128,8]{1,0:T(8,128)}, u32[]{:S(2)}) copy-start(f32[128,8]{1,0:T(8,128)} %get-tuple-element.24) | copy-start | bytes 12292
  37.4 5.0 %copy-start.6 = (f32[128,8]{1,0:T(8,128)S(1)}, f32[128,8]{1,0:T(8,128)}, u32[]{:S(2)}) copy-start(f32[128,8]{1,0:T(8,128)} %get-tuple-element.28) | copy-start | bytes 12292
  37.4 5.0 %copy-start.7 = (f32[128,8]{1,0:T(8,128)S(1)}, f32[128,8]{1,0:T(8,128)}, u32[]{:S(2)}) copy-start(f32[128,8]{1,0:T(8,128)} %get-tuple-element.23) | copy-start | bytes 12292
  37.4 5.0 %copy-start.8 = (f32[128,8]{1,0:T(8,128)S(1)}, f32[128,8]{1,0:T(8,128)}, u32[]{:S(2)}) copy-start(f32[128,8]{1,0:T(8,128)} %get-tuple-element.27) | copy-start | bytes 12292
  43.8 5.4 %collective-permute-start.5 = (bf16[2,8,4096]{2,1,0:T(8,128)(2,1)S(1)}, bf16[2,8,4096]{2,1,0:T(8,128)(2,1)S(1)}, u32[]{:S(2)}, u32[]{:S(2)}) collective-permute-start(bf16[2,8,4096]{2,1,0:T(8,128)(2,1)S(1)} %maximum_bitcast_fusion), channel_id=1, source_target_pairs={{0,4},{1,5},{2,6},{3,7},{4,0},{5,1},{6,2},{7,3},{8,12},{9,13},{10,... | collective-permute-start | bytes 393224 | tf_op jit(solution)/shard_map/ppermute | solution.py:17
  45.7 5.1 %collective-permute-start.8 = (f32[8,8,2112]{2,1,0:T(8,128)S(1)}, f32[8,8,2112]{2,1,0:T(8,128)S(1)}, u32[]{:S(2)}, u32[]{:S(2)}) collective-permute-start(f32[8,8,2112]{2,1,0:T(8,128)S(1)} %get-tuple-element.46), channel_id=1, source_target_pairs={{0,1},{1,0},{2,3},{3,2},{4,5},{5,4},{6,7},{7,6},{8,9},{9,8},{10,11... | collective-permute-start | bytes 1622024 | tf_op jit(solution)/shard_map/ppermute | solution.py:17
  49.2 9.4 %collective-permute-start.6 = (bf16[4,8,4096]{2,1,0:T(8,128)(2,1)S(1)}, bf16[4,8,4096]{2,1,0:T(8,128)(2,1)}, u32[]{:S(2)}, u32[]{:S(2)}) collective-permute-start(bf16[4,8,4096]{2,1,0:T(8,128)(2,1)S(1)} %bitcast.101), channel_id=1, source_target_pairs={{0,2},{1,3},{2,0},{3,1},{4,6},{5,7},{6,4},{7,5},{8,10},{9,11},{10,... | collective-permute-start | bytes 786440 | tf_op jit(solution)/shard_map/ppermute | solution.py:17
  52.5 9.9 %collective-permute-start.9 = (f32[4,8,2112]{2,1,0:T(8,128)S(1)}, f32[4,8,2112]{2,1,0:T(8,128)S(1)}, u32[]{:S(2)}, u32[]{:S(2)}) collective-permute-start(f32[4,8,2112]{2,1,0:T(8,128)S(1)} %get-tuple-element.52), channel_id=1, source_target_pairs={{0,2},{1,3},{2,0},{3,1},{4,6},{5,7},{6,4},{7,5},{8,10},{9,11},{10,... | collective-permute-start | bytes 811016 | tf_op jit(solution)/shard_map/ppermute | solution.py:17
  63.5 5.1 %collective-permute-start.10 = (f32[2,8,2112]{2,1,0:T(8,128)S(1)}, f32[2,8,2112]{2,1,0:T(8,128)S(1)}, u32[]{:S(2)}, u32[]{:S(2)}) collective-permute-start(f32[2,8,2112]{2,1,0:T(8,128)S(1)} %get-tuple-element.58), channel_id=1, source_target_pairs={{0,4},{1,5},{2,6},{3,7},{4,0},{5,1},{6,2},{7,3},{8,12},{9,13},{10,... | collective-permute-start | bytes 405512 | tf_op jit(solution)/shard_map/ppermute | solution.py:17
  65.3 4.4 %collective-permute-start.7 = (bf16[8,8,4096]{2,1,0:T(8,128)(2,1)S(1)}, bf16[8,8,4096]{2,1,0:T(8,128)(2,1)S(1)}, u32[]{:S(2)}, u32[]{:S(2)}) collective-permute-start(bf16[8,8,4096]{2,1,0:T(8,128)(2,1)S(1)} %bitcast.99), channel_id=1, source_target_pairs={{0,1},{1,0},{2,3},{3,2},{4,5},{5,4},{6,7},{7,6},{8,9},{9,8},{10,11... | collective-permute-start | bytes 1572872 | tf_op jit(solution)/shard_map/ppermute | solution.py:17
  69.3 22.1 %collective-permute-start.11 = (f32[1,8,2112]{2,1,0:T(8,128)S(1)}, f32[1,8,2112]{2,1,0:T(8,128)S(1)}, u32[]{:S(2)}, u32[]{:S(2)}) collective-permute-start(f32[1,8,2112]{2,1,0:T(8,128)S(1)} %get-tuple-element.64), channel_id=1, source_target_pairs={{0,8},{1,9},{2,10},{3,11},{4,12},{5,13},{6,14},{7,15},{8,0},{9,1},... | collective-permute-start | bytes 202760 | tf_op jit(solution)/shard_map/ppermute | solution.py:17

commit v4 on v3

--- a/solution.py
+++ b/solution.py
@@ -17,19 +17,29 @@
     return lax.ppermute(value, "seq", pairs)
 
 
-def gather_rows(block):
+def gather_rows(block, during=()):
     count = lax.axis_size("seq")
     me = lax.axis_index("seq")
     held = block[None]
+    results = []
     bit = count // 2
+    step = 0
     while bit >= 1:
+        work = during[step] if step < len(during) else None
+        if work is not None:
+            held, ready = lax.optimization_barrier((held, work[1]))
         arrived = exchange(held, bit, count)
+        if work is not None:
+            done = work[0](ready)
+            arrived, done = lax.optimization_barrier((arrived, done))
+            results.append(done)
         upper = (me & bit) != 0
         low = jnp.where(upper, arrived, held)
         high = jnp.where(upper, held, arrived)
         held = jnp.stack([low, high], axis=1).reshape((-1,) + block.shape)
         bit //= 2
-    return held.reshape((count * block.shape[0],) + block.shape[1:])
+        step += 1
+    return held.reshape((count * block.shape[0],) + block.shape[1:]), results
 
 
 def merge(first, second, heads):
@@ -42,23 +52,34 @@
     return jnp.concatenate([summed, totals, top], axis=1)
 
 
-def scatter_rows(state, heads):
+def scatter_rows(state, heads, during=()):
     count = lax.axis_size("seq")
     me = lax.axis_index("seq")
     rows = state.shape[0] // count
     held = state.reshape((count, rows, state.shape[1]))
+    carried = None
     bit = 1
+    step = 0
     while bit < count:
         pairs = held.reshape((-1, 2, rows, state.shape[1]))
         upper = (me & bit) != 0
         keep = jnp.where(upper, pairs[:, 1], pairs[:, 0])
         give = jnp.where(upper, pairs[:, 0], pairs[:, 1])
+        work = during[step] if step < len(during) else None
+        if work is not None:
+            give, carried = lax.optimization_barrier((give, carried))
         arrived = exchange(give, bit, count)
+        if work is not None:
+            carried = work(carried)
+            arrived, carried = lax.optimization_barrier((arrived, carried))
         held = merge(
             keep.reshape((-1, state.shape[1])), arrived.reshape((-1, state.shape[1])), heads
         ).reshape((-1, rows, state.shape[1]))
         bit *= 2
-    return held.reshape((rows, state.shape[1]))
+        step += 1
+    for work in during[step:]:
+        carried = work(carried)
+    return held.reshape((rows, state.shape[1])), carried
 
 
 def head_masks(rows):
@@ -76,8 +97,8 @@
     )
 
 
-def video_kernel(query_ref, key_ref, value_ref, earlier_ref, out_ref):
-    del earlier_ref
+def video_kernel(query_ref, key_ref, value_ref, *refs):
+    out_ref = refs[-1]
     queries = query_ref[...]
     keys = key_ref[...]
     values = value_ref[...]
@@ -97,32 +118,35 @@
     out_ref[...] = (summed / totals).astype(out_ref.dtype)
 
 
-def video_attention(queries, keys, values, groups):
+def video_part(queries, keys, values, earlier, group, groups):
     rows, width = queries.shape
     pairs = width // (2 * HEAD_DIM) // groups
+    first_pair = group * pairs
     key_rows = keys.shape[0]
-    out = jnp.zeros((rows, width), jnp.bfloat16)
-    for group in range(groups):
-        first_pair = group * pairs
-        out = pl.pallas_call(
-            video_kernel,
-            grid=(pairs,),
-            in_specs=[
-                pl.BlockSpec((rows, 2 * HEAD_DIM), lambda p, f=first_pair: (0, p + f)),
-                pl.BlockSpec((key_rows, 2 * HEAD_DIM), lambda p, f=first_pair: (0, p + f)),
-                pl.BlockSpec((key_rows, 2 * HEAD_DIM), lambda p, f=first_pair: (0, p + f)),
-                pl.BlockSpec(memory_space=pl.ANY),
-            ],
-            out_specs=pl.BlockSpec((rows, 2 * HEAD_DIM), lambda p, f=first_pair: (0, p + f)),
-            out_shape=jax.ShapeDtypeStruct((rows, width), jnp.bfloat16),
-            input_output_aliases={3: 0},
-            cost_estimate=pl.CostEstimate(
-                flops=8 * rows * key_rows * width // groups,
-                transcendentals=rows * key_rows * width // HEAD_DIM // groups,
-                bytes_accessed=2 * (2 * rows * width + 2 * key_rows * width) // groups,
-            ),
-        )(queries, keys, values, out)
-    return out
+    specs = [
+        pl.BlockSpec((rows, 2 * HEAD_DIM), lambda p: (0, p + first_pair)),
+        pl.BlockSpec((key_rows, 2 * HEAD_DIM), lambda p: (0, p + first_pair)),
+        pl.BlockSpec((key_rows, 2 * HEAD_DIM), lambda p: (0, p + first_pair)),
+    ]
+    operands = [queries, keys, values]
+    aliases = {}
+    if earlier is not None:
+        specs.append(pl.BlockSpec(memory_space=pl.ANY))
+        operands.append(earlier)
+        aliases = {3: 0}
+    return pl.pallas_call(
+        video_kernel,
+        grid=(pairs,),
+        in_specs=specs,
+        out_specs=pl.BlockSpec((rows, 2 * HEAD_DIM), lambda p: (0, p + first_pair)),
+        out_shape=jax.ShapeDtypeStruct((rows, width), jnp.bfloat16),
+        input_output_aliases=aliases,
+        cost_estimate=pl.CostEstimate(
+            flops=8 * rows * key_rows * width // groups,
+            transcendentals=rows * key_rows * width // HEAD_DIM // groups,
+            bytes_accessed=2 * (2 * rows * width + 2 * key_rows * width) // groups,
+        ),
+    )(*operands)
 
 
 def audio_kernel(query_ref, key_ref, value_ref, sum_ref, total_ref, top_ref):
@@ -194,23 +218,25 @@
     width = video_q.shape[1]
     heads = width // HEAD_DIM
     groups = 4
-    all_queries = gather_rows(audio_q)
-    all_queries, packed = lax.optimization_barrier(
-        (all_queries, jnp.concatenate([audio_k, audio_v], axis=1))
-    )
-    gathered = gather_rows(packed)
+    all_queries, ignored = gather_rows(audio_q)
+    audio_calls = [
+        (lambda q, g=g: audio_partial(q, video_k, video_v, g, groups), all_queries)
+        for g in range(groups)
+    ]
+    gathered, parts = gather_rows(jnp.concatenate([audio_k, audio_v], axis=1), audio_calls)
+    parts = parts + [call[0](all_queries) for call in audio_calls[len(parts) :]]
     all_keys = gathered[:, :width]
     all_values = gathered[:, width:]
-
-    parts = [audio_partial(all_queries, video_k, video_v, g, groups) for g in range(groups)]
     state = jnp.concatenate(
         [part[0] for part in parts] + [part[1] for part in parts] + [part[2] for part in parts],
         axis=1,
     )
-    mine = scatter_rows(state, heads)
+    video_calls = [
+        lambda earlier, g=g: video_part(video_q, all_keys, all_values, earlier, g, groups)
+        for g in range(groups)
+    ]
+    mine, video_out = scatter_rows(state, heads, video_calls)
     audio_out = (mine[:, :width] / spread(mine[:, width : width + heads])).astype(jnp.bfloat16)
-
-    video_out = video_attention(video_q, all_keys, all_values, groups)
     return video_out, audio_out
 
 

time: 93.5 us -> 81.8 us (0.87)
  waiting for transfers between devices: 24.8 us -> 13.8 us
  local copies, waits for them, and re-layouts: 8.33 us -> 6.76 us
  starting transfers between devices: 16.4 us -> 17.6 us
    ppermute x12, waiting for transfers between devices: 24.8 us -> 13.8 us  [exchange(): return lax.ppermute(value, 'seq', pairs)]
    broadcast_in_dim x1 -> x0, local copies, waits for them, and re-layouts: 1.57 us -> none  [video_attention(): out = jnp.zeros((rows, width), jnp.bfloat16)]
    ppermute x12, starting transfers between devices: 16.4 us -> 17.6 us  [exchange(): return lax.ppermute(value, 'seq', pairs)]
    another operation x14, other arithmetic: 2.27 us -> 1.28 us  [gather_rows(): held = jnp.stack([low, high], axis=1).reshape((-1,) + block.shape)]
  transfers between devices with their start and end apart: 12 -> 12, of which waited for: 8 -> 6; matrix products, arithmetic and copies ran while one was open for 8% -> 2% of each run, Pallas kernels for 41% -> 47%
where the time goes in v4:
time: 81.8 us; the launch traced here: 81.1 us
  Pallas kernels  38.5 us (47%)
  starting transfers between devices  17.6 us (22%)
  waiting for transfers between devices  13.8 us (17%)
  local copies, waits for them, and re-layouts  6.76 us (8%)
  other arithmetic  3.43 us (4%)
  between operations  1.07 us (1%)
    pallas_call x4, Pallas kernels, audio_partial(): pl.pallas_call(audio_kernel, grid=(heads // 2,), in_specs=[pl.BlockSpec((...  19.7 us
    pallas_call x4, Pallas kernels, video_part(): pl.pallas_call(video_kernel, grid=(pairs,), in_specs=specs, out_specs=pl....  18.8 us
    ppermute x12, starting transfers between devices, exchange(): return lax.ppermute(value, 'seq', pairs)  17.6 us
    ppermute x12, waiting for transfers between devices, exchange(): return lax.ppermute(value, 'seq', pairs)  13.8 us
  transfers between devices with their start and end apart: 12, of which 6 were waited for; matrix products, arithmetic and copies ran while one was open for 2% of the time, Pallas kernels for 47%

profile of v4, /device:TPU:0, one launch (start us, length us, event | category | flops | bytes accessed | tf_op | source)
XLA Modules:
  0.0 81.1 jit_solution(15397924924330944681)
XLA Ops:
  0.7 4.1 %collective-permute-start = (bf16[1,8,2048]{2,1,0:T(8,128)(2,1)}, bf16[1,8,2048]{2,1,0:T(8,128)(2,1)S(1)}, u32[]{:S(2)}, u32[]{:S(2)}) collective-permute-start(bf16[1,8,2048]{2,1,0:T(8,128)(2,1)} %bitcast.106), channel_id=1, source_target_pairs={{0,8},{1,9},{2,10},{3,11},{4,12},{5,13},{6,14},{7,15},{8,0},{9,1},... | collective-permute-start | bytes 98312 | tf_op jit(solution)/shard_map/ppermute | solution.py:17
  4.8 2.5 %collective-permute-done = bf16[1,8,2048]{2,1,0:T(8,128)(2,1)S(1)} collective-permute-done((bf16[1,8,2048]{2,1,0:T(8,128)(2,1)}, bf16[1,8,2048]{2,1,0:T(8,128)(2,1)S(1)}, u32[]{:S(2)}, u32[]{:S(2)}) %collective-permute-start) | collective-permute-done | bytes 32800 | tf_op jit(solution)/shard_map/ppermute | solution.py:17
  7.2 0.8 select_bitcast_fusion.23
  8.0 1.6 %collective-permute-start.1 = (bf16[2,8,2048]{2,1,0:T(8,128)(2,1)S(1)}, bf16[2,8,2048]{2,1,0:T(8,128)(2,1)S(1)}, u32[]{:S(2)}, u32[]{:S(2)}) collective-permute-start(bf16[2,8,2048]{2,1,0:T(8,128)(2,1)S(1)} %maximum_bitcast_fusion.2), channel_id=1, source_target_pairs={{0,4},{1,5},{2,6},{3,7},{4,0},{5,1},{6,2},{7,3},{8,12},{9,13},{10,... | collective-permute-start | bytes 196616 | tf_op jit(solution)/shard_map/ppermute | solution.py:17
  9.6 2.7 %collective-permute-done.1 = bf16[2,8,2048]{2,1,0:T(8,128)(2,1)S(1)} collective-permute-done((bf16[2,8,2048]{2,1,0:T(8,128)(2,1)S(1)}, bf16[2,8,2048]{2,1,0:T(8,128)(2,1)S(1)}, u32[]{:S(2)}, u32[]{:S(2)}) %collective-permute-start.1) | collective-permute-done | bytes 65568 | tf_op jit(solution)/shard_map/ppermute | solution.py:17
  12.4 1.8 %collective-permute-start.2 = (bf16[4,8,2048]{2,1,0:T(8,128)(2,1)S(1)}, bf16[4,8,2048]{2,1,0:T(8,128)(2,1)S(1)}, u32[]{:S(2)}, u32[]{:S(2)}) collective-permute-start(bf16[4,8,2048]{2,1,0:T(8,128)(2,1)S(1)} %bitcast.99), channel_id=1, source_target_pairs={{0,2},{1,3},{2,0},{3,1},{4,6},{5,7},{6,4},{7,5},{8,10},{9,11},{10,... | collective-permute-start | bytes 393224 | tf_op jit(solution)/shard_map/ppermute | solution.py:17
  14.2 3.2 %collective-permute-done.2 = bf16[4,8,2048]{2,1,0:T(8,128)(2,1)S(1)} collective-permute-done((bf16[4,8,2048]{2,1,0:T(8,128)(2,1)S(1)}, bf16[4,8,2048]{2,1,0:T(8,128)(2,1)S(1)}, u32[]{:S(2)}, u32[]{:S(2)}) %collective-permute-start.2) | collective-permute-done | bytes 131104 | tf_op jit(solution)/shard_map/ppermute | solution.py:17
  17.6 1.5 %collective-permute-done.3 = bf16[8,8,2048]{2,1,0:T(8,128)(2,1)S(1)} collective-permute-done((bf16[8,8,2048]{2,1,0:T(8,128)(2,1)S(1)}, bf16[8,8,2048]{2,1,0:T(8,128)(2,1)S(1)}, u32[]{:S(2)}, u32[]{:S(2)}) %collective-permute-start.3) | collective-permute-done | bytes 262176 | tf_op jit(solution)/shard_map/ppermute | solution.py:17
  19.2 0.8 %copy.21 = bf16[8,2,8,2048]{3,2,1,0:T(8,128)(2,1)} copy(bf16[8,2,8,2048]{3,2,0,1:T(8,128)(2,1)S(1)} %pad_maximum_fusion.1) | data formatting | bytes 1048576 | tf_op jit(solution)/shard_map/stack | solution.py:39
  20.0 2.6 %collective-permute-start.4 = (bf16[1,8,4096]{2,1,0:T(8,128)(2,1)S(1)}, bf16[1,8,4096]{2,1,0:T(8,128)(2,1)S(1)}, u32[]{:S(2)}, u32[]{:S(2)}) collective-permute-start(bf16[1,8,4096]{2,1,0:T(8,128)(2,1)S(1)} %maximum_bitcast_fusion.1), channel_id=1, source_target_pairs={{0,8},{1,9},{2,10},{3,11},{4,12},{5,13},{6,14},{7,15},{8,0},{9,1},... | collective-permute-start | bytes 196616 | tf_op jit(solution)/shard_map/ppermute | solution.py:17
  22.6 4.9 %shard_map.77 = (f32[128,512]{1,0:T(8,128)}, f32[128,8]{1,0:T(8,128)}, f32[128,8]{1,0:T(8,128)}) custom-call(bf16[128,2048]{1,0:T(8,128)(2,1)} %bitcast.83, bf16[512,2048]{1,0:T(8,128)(2,1)} %key_ref.7, bf16[512,2048]{1,0:T(8,128)(2,1)} %value_ref.7), custom_call_target="tpu_custom_call" | custom-call | flops 268435456 | bytes 1441792 | tf_op jit(solution)/shard_map/pallas_call | solution.py:190
  27.5 1.9 %collective-permute-start.5 = (bf16[2,8,4096]{2,1,0:T(8,128)(2,1)S(1)}, bf16[2,8,4096]{2,1,0:T(8,128)(2,1)S(1)}, u32[]{:S(2)}, u32[]{:S(2)}) collective-permute-start(bf16[2,8,4096]{2,1,0:T(8,128)(2,1)S(1)} %maximum_bitcast_fusion), channel_id=1, source_target_pairs={{0,4},{1,5},{2,6},{3,7},{4,0},{5,1},{6,2},{7,3},{8,12},{9,13},{10,... | collective-permute-start | bytes 393224 | tf_op jit(solution)/shard_map/ppermute | solution.py:17
  29.4 4.9 %shard_map.78 = (f32[128,512]{1,0:T(8,128)}, f32[128,8]{1,0:T(8,128)}, f32[128,8]{1,0:T(8,128)}) custom-call(bf16[128,2048]{1,0:T(8,128)(2,1)} %bitcast.84, bf16[512,2048]{1,0:T(8,128)(2,1)} %key_ref.7, bf16[512,2048]{1,0:T(8,128)(2,1)} %value_ref.7), custom_call_target="tpu_custom_call" | custom-call | flops 268435456 | bytes 1441792 | tf_op jit(solution)/shard_map/pallas_call | solution.py:190
  34.4 1.6 %collective-permute-start.6 = (bf16[4,8,4096]{2,1,0:T(8,128)(2,1)S(1)}, bf16[4,8,4096]{2,1,0:T(8,128)(2,1)S(1)}, u32[]{:S(2)}, u32[]{:S(2)}) collective-permute-start(bf16[4,8,4096]{2,1,0:T(8,128)(2,1)S(1)} %bitcast.93), channel_id=1, source_target_pairs={{0,2},{1,3},{2,0},{3,1},{4,6},{5,7},{6,4},{7,5},{8,10},{9,11},{10,... | collective-permute-start | bytes 786440 | tf_op jit(solution)/shard_map/ppermute | solution.py:17
  36.0 4.9 %shard_map.79 = (f32[128,512]{1,0:T(8,128)}, f32[128,8]{1,0:T(8,128)}, f32[128,8]{1,0:T(8,128)}) custom-call(bf16[128,2048]{1,0:T(8,128)(2,1)} %bitcast.85, bf16[512,2048]{1,0:T(8,128)(2,1)} %key_ref.7, bf16[512,2048]{1,0:T(8,128)(2,1)} %value_ref.7), custom_call_target="tpu_custom_call" | custom-call | flops 268435456 | bytes 1441792 | tf_op jit(solution)/shard_map/pallas_call | solution.py:190
  40.8 1.4 %collective-permute-done.6 = bf16[4,8,4096]{2,1,0:T(8,128)(2,1)S(1)} collective-permute-done((bf16[4,8,4096]{2,1,0:T(8,128)(2,1)S(1)}, bf16[4,8,4096]{2,1,0:T(8,128)(2,1)S(1)}, u32[]{:S(2)}, u32[]{:S(2)}) %collective-permute-start.6) | collective-permute-done | bytes 262176 | tf_op jit(solution)/shard_map/ppermute | solution.py:17
  42.5 5.0 %shard_map.80 = (f32[128,512]{1,0:T(8,128)}, f32[128,8]{1,0:T(8,128)}, f32[128,8]{1,0:T(8,128)}) custom-call(bf16[128,2048]{1,0:T(8,128)(2,1)} %bitcast.86, bf16[512,2048]{1,0:T(8,128)(2,1)} %key_ref.7, bf16[512,2048]{1,0:T(8,128)(2,1)} %value_ref.7), custom_call_target="tpu_custom_call" | custom-call | flops 268435456 | bytes 1441792 | tf_op jit(solution)/shard_map/pallas_call | solution.py:190
  47.6 1.2 %concatenate.16 = f32[128,2112]{1,0:T(8,128)S(1)} concatenate(f32[128,512]{1,0:T(8,128)S(1)} %copy-done, f32[128,512]{1,0:T(8,128)S(1)} %copy-done.1, f32[128,512]{1,0:T(8,128)S(1)} %copy-done.2, f32[128,512]{1,0:T(8,128)} %get-tuple-element.78, f32[128,8]{1,0:T(8,128)S(1)} %copy-done.3, f32[128,8]{1,0:T(8,128)S(1)} %copy-done.5, f32[128,8]{1,0:T(8,128)S(1)} %copy-done.7, ...), dimensions={1} | concatenate | bytes 2162688 | tf_op jit(solution)/shard_map/concatenate | solution.py:230
  48.9 0.9 %select_bitcast_fusion.1 = (f32[64,2112]{1,0:T(8,128)S(1)}, f32[8,8,2112]{2,1,0:T(8,128)}) fusion(f32[8,2,8,2112]{3,2,1,0:T(8,128)S(1)} %bitcast.87, pred[]{:T(512)S(6)} %ne.11), kind=kLoop, calls=%fused_computation.2 | loop fusion | flops 270336 | bytes 2162689 | tf_op jit(solution)/shard_map/jit(_where)/select_n | solution.py:66
  49.8 0.4 collective-permute-start.8
  50.3 0.1 pad_maximum_fusion
  50.5 1.1 %fusion.14 = (bf16[128,2048]{1,0:T(8,128)(2,1)}, bf16[128,2048]{1,0:T(8,128)(2,1)}) fusion(bf16[128,4096]{1,0:T(8,128)(2,1)S(1)} %bitcast.88), kind=kLoop, calls=%fused_computation.72 | loop fusion | bytes 2097152 | tf_op jit(solution)/shard_map/slice | solution.py:229
  51.5 4.7 %shard_map.81.refs_0_ = bf16[512,2048]{1,0:T(8,128)(2,1)} custom-call(bf16[512,2048]{1,0:T(8,128)(2,1)} %query_ref.7, bf16[128,2048]{1,0:T(8,128)(2,1)} %get-tuple-element.120.key_ref, bf16[128,2048]{1,0:T(8,128)(2,1)} %get-tuple-element.119.value_ref), custom_call_target="tpu_custom_call" | custom-call | flops 268435456 | bytes 1310720 | tf_op jit(solution)/shard_map/pallas_call | solution.py:137
  56.3 0.3 broadcast_in_dim.35
  56.7 0.4 reshape.121
  57.0 0.3 broadcast_in_dim.36
  57.4 0.4 reshape.122
  57.7 0.1 fusion
  58.0 1.6 %collective-permute-start.9 = (f32[4,8,2112]{2,1,0:T(8,128)S(1)}, f32[4,8,2112]{2,1,0:T(8,128)S(1)}, u32[]{:S(2)}, u32[]{:S(2)}) collective-permute-start(f32[4,8,2112]{2,1,0:T(8,128)S(1)} %get-tuple-element.90), channel_id=1, source_target_pairs={{0,2},{1,3},{2,0},{3,1},{4,6},{5,7},{6,4},{7,5},{8,10},{9,11},{10,... | collective-permute-start | bytes 811016 | tf_op jit(solution)/shard_map/ppermute | solution.py:17
  59.6 4.7 %shard_map.82.refs_0_ = bf16[512,2048]{1,0:T(8,128)(2,1)} custom-call(bf16[512,2048]{1,0:T(8,128)(2,1)} %query_ref.7, bf16[128,2048]{1,0:T(8,128)(2,1)} %get-tuple-element.120.key_ref, bf16[128,2048]{1,0:T(8,128)(2,1)} %get-tuple-element.119.value_ref, bf16[512,2048]{1,0:T(8,128)(2,1)} %shard_map.81.refs_0_), custom_call_target="tpu_custom_call", output_to_operand_aliasing={{}: (3, {})} | custom-call | flops 268435456 | bytes 1310720 | tf_op jit(solution)/shard_map/pallas_call | solution.py:137
  64.3 2.4 %collective-permute-done.9 = f32[4,8,2112]{2,1,0:T(8,128)S(1)} collective-permute-done((f32[4,8,2112]{2,1,0:T(8,128)S(1)}, f32[4,8,2112]{2,1,0:T(8,128)S(1)}, u32[]{:S(2)}, u32[]{:S(2)}) %collective-permute-start.9) | collective-permute-done | bytes 270368 | tf_op jit(solution)/shard_map/ppermute | solution.py:17
  66.8 0.2 broadcast_in_dim.37
  67.0 0.2 reshape.124
  67.2 0.2 broadcast_in_dim.38
  67.4 0.2 reshape.125
  67.8 0.4 collective-permute-start.10
  68.1 4.7 %shard_map.83.refs_0_ = bf16[512,2048]{1,0:T(8,128)(2,1)} custom-call(bf16[512,2048]{1,0:T(8,128)(2,1)} %query_ref.7, bf16[128,2048]{1,0:T(8,128)(2,1)} %get-tuple-element.120.key_ref, bf16[128,2048]{1,0:T(8,128)(2,1)} %get-tuple-element.119.value_ref, bf16[512,2048]{1,0:T(8,128)(2,1)} %shard_map.82.refs_0_), custom_call_target="tpu_custom_call", output_to_operand_aliasing={{}: (3, {})} | custom-call | flops 268435456 | bytes 1310720 | tf_op jit(solution)/shard_map/pallas_call | solution.py:137
  73.0 0.1 broadcast_in_dim.39
  73.1 0.1 reshape.127
  73.2 0.1 broadcast_in_dim.40
  73.3 0.1 reshape.128
  73.6 1.4 %collective-permute-start.11 = (f32[1,8,2112]{2,1,0:T(8,128)S(1)}, f32[1,8,2112]{2,1,0:T(8,128)S(1)}, u32[]{:S(2)}, u32[]{:S(2)}) collective-permute-start(f32[1,8,2112]{2,1,0:T(8,128)S(1)} %get-tuple-element.98), channel_id=1, source_target_pairs={{0,8},{1,9},{2,10},{3,11},{4,12},{5,13},{6,14},{7,15},{8,0},{9,1},... | collective-permute-start | bytes 202760 | tf_op jit(solution)/shard_map/ppermute | solution.py:17
  75.0 4.7 %shard_map.84 = bf16[512,2048]{1,0:T(8,128)(2,1)} custom-call(bf16[512,2048]{1,0:T(8,128)(2,1)} %query_ref.7, bf16[128,2048]{1,0:T(8,128)(2,1)} %get-tuple-element.120.key_ref, bf16[128,2048]{1,0:T(8,128)(2,1)} %get-tuple-element.119.value_ref, bf16[512,2048]{1,0:T(8,128)(2,1)} %shard_map.83.refs_0_), custom_call_target="tpu_custom_call", output_to_operand_aliasing={{}: (3, {})} | custom-call | flops 268435456 | bytes 1310720 | tf_op jit(solution)/shard_map/pallas_call | solution.py:137
  79.8 0.1 broadcast_in_dim.43
  79.9 0.1 reshape.132
  80.1 0.1 reshape.130
  80.3 0.1 reshape.131
  80.4 0.6 fusion.5
  (62 shorter events, 1.7 us)
Async XLA Ops:
  0.6 16.9 %copy-start.9 = (bf16[8,2048]{1,0:T(8,128)(2,1)S(1)}, bf16[8,2048]{1,0:T(8,128)(2,1)}, u32[]{:S(2)}) copy-start(bf16[8,2048]{1,0:T(8,128)(2,1)} %param.11) | copy-start | bytes 98308
  0.6 16.9 %copy-start.10 = (bf16[8,2048]{1,0:T(8,128)(2,1)S(1)}, bf16[8,2048]{1,0:T(8,128)(2,1)}, u32[]{:S(2)}) copy-start(bf16[8,2048]{1,0:T(8,128)(2,1)} %param.10) | copy-start | bytes 98308
  0.7 6.6 %collective-permute-start = (bf16[1,8,2048]{2,1,0:T(8,128)(2,1)}, bf16[1,8,2048]{2,1,0:T(8,128)(2,1)S(1)}, u32[]{:S(2)}, u32[]{:S(2)}) collective-permute-start(bf16[1,8,2048]{2,1,0:T(8,128)(2,1)} %bitcast.106), channel_id=1, source_target_pairs={{0,8},{1,9},{2,10},{3,11},{4,12},{5,13},{6,14},{7,15},{8,0},{9,1},... | collective-permute-start | bytes 98312 | tf_op jit(solution)/shard_map/ppermute | solution.py:17
  8.0 4.3 %collective-permute-start.1 = (bf16[2,8,2048]{2,1,0:T(8,128)(2,1)S(1)}, bf16[2,8,2048]{2,1,0:T(8,128)(2,1)S(1)}, u32[]{:S(2)}, u32[]{:S(2)}) collective-permute-start(bf16[2,8,2048]{2,1,0:T(8,128)(2,1)S(1)} %maximum_bitcast_fusion.2), channel_id=1, source_target_pairs={{0,4},{1,5},{2,6},{3,7},{4,0},{5,1},{6,2},{7,3},{8,12},{9,13},{10,... | collective-permute-start | bytes 196616 | tf_op jit(solution)/shard_map/ppermute | solution.py:17
  12.4 5.0 %collective-permute-start.2 = (bf16[4,8,2048]{2,1,0:T(8,128)(2,1)S(1)}, bf16[4,8,2048]{2,1,0:T(8,128)(2,1)S(1)}, u32[]{:S(2)}, u32[]{:S(2)}) collective-permute-start(bf16[4,8,2048]{2,1,0:T(8,128)(2,1)S(1)} %bitcast.99), channel_id=1, source_target_pairs={{0,2},{1,3},{2,0},{3,1},{4,6},{5,7},{6,4},{7,5},{8,10},{9,11},{10,... | collective-permute-start | bytes 393224 | tf_op jit(solution)/shard_map/ppermute | solution.py:17
  17.5 1.6 %collective-permute-start.3 = (bf16[8,8,2048]{2,1,0:T(8,128)(2,1)S(1)}, bf16[8,8,2048]{2,1,0:T(8,128)(2,1)S(1)}, u32[]{:S(2)}, u32[]{:S(2)}) collective-permute-start(bf16[8,8,2048]{2,1,0:T(8,128)(2,1)S(1)} %bitcast.95), channel_id=1, source_target_pairs={{0,1},{1,0},{2,3},{3,2},{4,5},{5,4},{6,7},{7,6},{8,9},{9,8},{10,11... | collective-permute-start | bytes 786440 | tf_op jit(solution)/shard_map/ppermute | solution.py:17
  20.0 7.5 %collective-permute-start.4 = (bf16[1,8,4096]{2,1,0:T(8,128)(2,1)S(1)}, bf16[1,8,4096]{2,1,0:T(8,128)(2,1)S(1)}, u32[]{:S(2)}, u32[]{:S(2)}) collective-permute-start(bf16[1,8,4096]{2,1,0:T(8,128)(2,1)S(1)} %maximum_bitcast_fusion.1), channel_id=1, source_target_pairs={{0,8},{1,9},{2,10},{3,11},{4,12},{5,13},{6,14},{7,15},{8,0},{9,1},... | collective-permute-start | bytes 196616 | tf_op jit(solution)/shard_map/ppermute | solution.py:17
  27.5 6.8 %collective-permute-start.5 = (bf16[2,8,4096]{2,1,0:T(8,128)(2,1)S(1)}, bf16[2,8,4096]{2,1,0:T(8,128)(2,1)S(1)}, u32[]{:S(2)}, u32[]{:S(2)}) collective-permute-start(bf16[2,8,4096]{2,1,0:T(8,128)(2,1)S(1)} %maximum_bitcast_fusion), channel_id=1, source_target_pairs={{0,4},{1,5},{2,6},{3,7},{4,0},{5,1},{6,2},{7,3},{8,12},{9,13},{10,... | collective-permute-start | bytes 393224 | tf_op jit(solution)/shard_map/ppermute | solution.py:17
  34.4 7.8 %collective-permute-start.6 = (bf16[4,8,4096]{2,1,0:T(8,128)(2,1)S(1)}, bf16[4,8,4096]{2,1,0:T(8,128)(2,1)S(1)}, u32[]{:S(2)}, u32[]{:S(2)}) collective-permute-start(bf16[4,8,4096]{2,1,0:T(8,128)(2,1)S(1)} %bitcast.93), channel_id=1, source_target_pairs={{0,2},{1,3},{2,0},{3,1},{4,6},{5,7},{6,4},{7,5},{8,10},{9,11},{10,... | collective-permute-start | bytes 786440 | tf_op jit(solution)/shard_map/ppermute | solution.py:17
  42.3 5.2 %copy-start = (f32[128,512]{1,0:T(8,128)S(1)}, f32[128,512]{1,0:T(8,128)}, u32[]{:S(2)}) copy-start(f32[128,512]{1,0:T(8,128)} %get-tuple-element.57) | copy-start | bytes 786436
  42.4 5.2 %copy-start.1 = (f32[128,512]{1,0:T(8,128)S(1)}, f32[128,512]{1,0:T(8,128)}, u32[]{:S(2)}) copy-start(f32[128,512]{1,0:T(8,128)} %get-tuple-element.64) | copy-start | bytes 786436
  42.4 5.2 %copy-start.2 = (f32[128,512]{1,0:T(8,128)S(1)}, f32[128,512]{1,0:T(8,128)}, u32[]{:S(2)}) copy-start(f32[128,512]{1,0:T(8,128)} %get-tuple-element.71) | copy-start | bytes 786436
  42.4 5.2 %copy-start.3 = (f32[128,8]{1,0:T(8,128)S(1)}, f32[128,8]{1,0:T(8,128)}, u32[]{:S(2)}) copy-start(f32[128,8]{1,0:T(8,128)} %get-tuple-element.79) | copy-start | bytes 12292
  42.4 5.2 %copy-start.4 = (f32[128,8]{1,0:T(8,128)S(1)}, f32[128,8]{1,0:T(8,128)}, u32[]{:S(2)}) copy-start(f32[128,8]{1,0:T(8,128)} %get-tuple-element.83) | copy-start | bytes 12292
  42.4 5.2 %copy-start.5 = (f32[128,8]{1,0:T(8,128)S(1)}, f32[128,8]{1,0:T(8,128)}, u32[]{:S(2)}) copy-start(f32[128,8]{1,0:T(8,128)} %get-tuple-element.80) | copy-start | bytes 12292
  42.4 5.2 %copy-start.6 = (f32[128,8]{1,0:T(8,128)S(1)}, f32[128,8]{1,0:T(8,128)}, u32[]{:S(2)}) copy-start(f32[128,8]{1,0:T(8,128)} %get-tuple-element.84) | copy-start | bytes 12292
  42.4 5.2 %copy-start.7 = (f32[128,8]{1,0:T(8,128)S(1)}, f32[128,8]{1,0:T(8,128)}, u32[]{:S(2)}) copy-start(f32[128,8]{1,0:T(8,128)} %get-tuple-element.81) | copy-start | bytes 12292
  42.4 5.2 %copy-start.8 = (f32[128,8]{1,0:T(8,128)S(1)}, f32[128,8]{1,0:T(8,128)}, u32[]{:S(2)}) copy-start(f32[128,8]{1,0:T(8,128)} %get-tuple-element.85) | copy-start | bytes 12292
  42.4 5.1 %collective-permute-start.7 = (bf16[8,8,4096]{2,1,0:T(8,128)(2,1)S(1)}, bf16[8,8,4096]{2,1,0:T(8,128)(2,1)S(1)}, u32[]{:S(2)}, u32[]{:S(2)}) collective-permute-start(bf16[8,8,4096]{2,1,0:T(8,128)(2,1)S(1)} %bitcast.90), channel_id=1, source_target_pairs={{0,1},{1,0},{2,3},{3,2},{4,5},{5,4},{6,7},{7,6},{8,9},{9,8},{10,11... | collective-permute-start | bytes 1572872 | tf_op jit(solution)/shard_map/ppermute | solution.py:17
  49.8 6.4 %collective-permute-start.8 = (f32[8,8,2112]{2,1,0:T(8,128)}, f32[8,8,2112]{2,1,0:T(8,128)S(1)}, u32[]{:S(2)}, u32[]{:S(2)}) collective-permute-start(f32[8,8,2112]{2,1,0:T(8,128)} %get-tuple-element.118), channel_id=1, source_target_pairs={{0,1},{1,0},{2,3},{3,2},{4,5},{5,4},{6,7},{7,6},{8,9},{9,8},{10,11... | collective-permute-start | bytes 1622024 | tf_op jit(solution)/shard_map/ppermute | solution.py:17
  58.0 8.8 %collective-permute-start.9 = (f32[4,8,2112]{2,1,0:T(8,128)S(1)}, f32[4,8,2112]{2,1,0:T(8,128)S(1)}, u32[]{:S(2)}, u32[]{:S(2)}) collective-permute-start(f32[4,8,2112]{2,1,0:T(8,128)S(1)} %get-tuple-element.90), channel_id=1, source_target_pairs={{0,2},{1,3},{2,0},{3,1},{4,6},{5,7},{6,4},{7,5},{8,10},{9,11},{10,... | collective-permute-start | bytes 811016 | tf_op jit(solution)/shard_map/ppermute | solution.py:17
  67.8 5.1 %collective-permute-start.10 = (f32[2,8,2112]{2,1,0:T(8,128)S(1)}, f32[2,8,2112]{2,1,0:T(8,128)S(1)}, u32[]{:S(2)}, u32[]{:S(2)}) collective-permute-start(f32[2,8,2112]{2,1,0:T(8,128)S(1)} %get-tuple-element.94), channel_id=1, source_target_pairs={{0,4},{1,5},{2,6},{3,7},{4,0},{5,1},{6,2},{7,3},{8,12},{9,13},{10,... | collective-permute-start | bytes 405512 | tf_op jit(solution)/shard_map/ppermute | solution.py:17
  73.6 6.1 %collective-permute-start.11 = (f32[1,8,2112]{2,1,0:T(8,128)S(1)}, f32[1,8,2112]{2,1,0:T(8,128)S(1)}, u32[]{:S(2)}, u32[]{:S(2)}) collective-permute-start(f32[1,8,2112]{2,1,0:T(8,128)S(1)} %get-tuple-element.98), channel_id=1, source_target_pairs={{0,8},{1,9},{2,10},{3,11},{4,12},{5,13},{6,14},{7,15},{8,0},{9,1},... | collective-permute-start | bytes 202760 | tf_op jit(solution)/shard_map/ppermute | solution.py:17

commit v5 on v4

--- a/solution.py
+++ b/solution.py
@@ -40,6 +40,38 @@
         bit //= 2
         step += 1
     return held.reshape((count * block.shape[0],) + block.shape[1:]), results
+
+
+def gather_levels(block):
+    count = lax.axis_size("seq")
+    me = lax.axis_index("seq")
+    held = block[None]
+    levels = []
+    bit = count // 2
+    if bit >= 2:
+        levels.append((bit, bit // 2))
+        bit //= 4
+    while bit >= 1:
+        levels.append((bit,))
+        bit //= 2
+    for level in levels:
+        mask = sum(level)
+        offsets = [0]
+        for b in level:
+            offsets = offsets + [o + b for o in offsets]
+        pieces = {0: held}
+        for offset in offsets[1:]:
+            pairs = [(source, source ^ offset) for source in range(count)]
+            pieces[offset] = lax.ppermute(held, "seq", pairs)
+        mine = me & mask
+        ordered = []
+        for target in sorted(offsets):
+            choice = pieces[0]
+            for offset in offsets[1:]:
+                choice = jnp.where((mine ^ offset) == target, pieces[offset], choice)
+            ordered.append(choice)
+        held = jnp.stack(ordered, axis=1).reshape((-1,) + block.shape)
+    return held.reshape((count * block.shape[0],) + block.shape[1:])
 
 
 def merge(first, second, heads):
@@ -87,33 +119,40 @@
     return lane < HEAD_DIM
 
 
-def pair_scores(queries, keys, first):
-    masked = jnp.where(first, queries, jnp.zeros_like(queries))
-    return (
+def split_pair(block):
+    first = head_masks(block.shape[0])
+    zeros = jnp.zeros_like(block)
+    return jnp.concatenate([jnp.where(first, block, zeros), jnp.where(first, zeros, block)], axis=0)
+
+
+def pair_attention(queries, keys, values):
+    key_rows = keys.shape[0]
+    scores = (
         lax.dot_general(
-            masked, keys, (((1,), (1,)), ((), ())), preferred_element_type=jnp.float32
+            queries, split_pair(keys), (((1,), (1,)), ((), ())), preferred_element_type=jnp.float32
         )
         * 0.125
     )
+    weights = []
+    tops = []
+    counts = []
+    for half in range(2):
+        part = scores[:, half * key_rows : (half + 1) * key_rows]
+        highest = jnp.max(part, axis=1, keepdims=True)
+        exps = jnp.exp(part - highest)
+        tops.append(highest)
+        counts.append(jnp.sum(exps, axis=1, keepdims=True))
+        weights.append(exps.astype(jnp.bfloat16))
+    summed = jnp.dot(
+        jnp.concatenate(weights, axis=1), split_pair(values), preferred_element_type=jnp.float32
+    )
+    return summed, tops, counts
 
 
 def video_kernel(query_ref, key_ref, value_ref, *refs):
     out_ref = refs[-1]
-    queries = query_ref[...]
-    keys = key_ref[...]
-    values = value_ref[...]
-    first = head_masks(queries.shape[0])
-    sums = []
-    counts = []
-    for lanes in (first, jnp.logical_not(first)):
-        scores = pair_scores(queries, keys, lanes)
-        highest = jnp.max(scores, axis=1, keepdims=True)
-        weights = jnp.exp(scores - highest)
-        counts.append(jnp.sum(weights, axis=1, keepdims=True))
-        sums.append(
-            jnp.dot(weights.astype(jnp.bfloat16), values, preferred_element_type=jnp.float32)
-        )
-    summed = jnp.where(first, sums[0], sums[1])
+    summed, tops, counts = pair_attention(query_ref[...], key_ref[...], value_ref[...])
+    first = head_masks(summed.shape[0])
     totals = jnp.where(first, counts[0], counts[1])
     out_ref[...] = (summed / totals).astype(out_ref.dtype)
 
@@ -151,35 +190,23 @@
 
 def audio_kernel(query_ref, key_ref, value_ref, sum_ref, total_ref, top_ref):
     pair = pl.program_id(0)
-    queries = query_ref[...]
-    keys = key_ref[...]
-    values = value_ref[...]
-    rows = queries.shape[0]
-    first = head_masks(rows)
 
     @pl.when(pair == 0)
     def _():
         total_ref[...] = jnp.zeros_like(total_ref)
         top_ref[...] = jnp.zeros_like(top_ref)
 
+    summed, tops, counts = pair_attention(query_ref[...], key_ref[...], value_ref[...])
     column = lax.broadcasted_iota(jnp.int32, total_ref.shape, 1)
-    results = []
     totals_now = total_ref[...]
     tops_now = top_ref[...]
-    for half, lanes in enumerate((first, jnp.logical_not(first))):
-        scores = pair_scores(queries, keys, lanes)
-        highest = jnp.max(scores, axis=1, keepdims=True)
-        weights = jnp.exp(scores - highest)
-        totals = jnp.sum(weights, axis=1, keepdims=True)
-        results.append(
-            jnp.dot(weights.astype(jnp.bfloat16), values, preferred_element_type=jnp.float32)
-        )
+    for half in range(2):
         here = column == 2 * pair + half
-        totals_now = jnp.where(here, totals, totals_now)
-        tops_now = jnp.where(here, highest, tops_now)
+        totals_now = jnp.where(here, counts[half], totals_now)
+        tops_now = jnp.where(here, tops[half], tops_now)
     total_ref[...] = totals_now
     top_ref[...] = tops_now
-    sum_ref[...] = jnp.where(first, results[0], results[1])
+    sum_ref[...] = summed
 
 
 def audio_partial(queries, keys, values, group, groups):
@@ -218,7 +245,7 @@
     width = video_q.shape[1]
     heads = width // HEAD_DIM
     groups = 4
-    all_queries, ignored = gather_rows(audio_q)
+    all_queries = gather_levels(audio_q)
     audio_calls = [
         (lambda q, g=g: audio_partial(q, video_k, video_v, g, groups), all_queries)
         for g in range(groups)

time: 81.8 us -> 77.9 us (0.952)
  Pallas kernels: 38.5 us -> 33.9 us
  starting transfers between devices: 17.6 us -> 15.4 us
  waiting for transfers between devices: 13.8 us -> 15.9 us
    ppermute x0 -> x5, waiting for transfers between devices: none -> 10.1 us  [gather_levels(): pieces[offset] = lax.ppermute(held, 'seq', pairs)]
    ppermute x12 -> x8, starting transfers between devices: 17.6 us -> 8.03 us  [exchange(): return lax.ppermute(value, 'seq', pairs)]
    ppermute x12 -> x8, waiting for transfers between devices: 13.8 us -> 5.75 us  [exchange(): return lax.ppermute(value, 'seq', pairs)]
    ppermute x0 -> x5, starting transfers between devices: none -> 7.34 us  [gather_levels(): pieces[offset] = lax.ppermute(held, 'seq', pairs)]
    pallas_call x4, Pallas kernels: 19.7 us -> 17.1 us  [audio_partial(): pl.pallas_call(audio_kernel, grid=(heads // 2,), in_specs=[pl.BlockSpec((...]
    pallas_call x4, Pallas kernels: 18.8 us -> 16.9 us  [video_part(): pl.pallas_call(video_kernel, grid=(pairs,), in_specs=specs, out_specs=pl....]
    another operation x14 -> x7, other arithmetic: 1.28 us -> 0.32 us  [gather_rows(): held = jnp.stack([low, high], axis=1).reshape((-1,) + block.shape)]
    another operation x0 -> x5, other arithmetic: none -> 0.94 us  [gather_levels(): held = jnp.stack(ordered, axis=1).reshape((-1,) + block.shape)]
  transfers between devices with their start and end apart: 12 -> 13, of which waited for: 6 -> 9; matrix products, arithmetic and copies ran while one was open for 2% -> 3% of each run, Pallas kernels for 47% -> 44%
where the time goes in v5:
time: 77.9 us; the launch traced here: 77.1 us
  Pallas kernels  33.9 us (44%)
  waiting for transfers between devices  15.9 us (20%)
  starting transfers between devices  15.4 us (20%)
  local copies, waits for them, and re-layouts  6.73 us (9%)
  other arithmetic  4.2 us (5%)
  between operations  1.03 us (1%)
    pallas_call x4, Pallas kernels, audio_partial(): pl.pallas_call(audio_kernel, grid=(heads // 2,), in_specs=[pl.BlockSpec((...  17.1 us
    pallas_call x4, Pallas kernels, video_part(): pl.pallas_call(video_kernel, grid=(pairs,), in_specs=specs, out_specs=pl....  16.9 us
    ppermute x5, waiting for transfers between devices, gather_levels(): pieces[offset] = lax.ppermute(held, 'seq', pairs)  10.1 us
    ppermute x8, starting transfers between devices, exchange(): return lax.ppermute(value, 'seq', pairs)  8.03 us
    ppermute x5, starting transfers between devices, gather_levels(): pieces[offset] = lax.ppermute(held, 'seq', pairs)  7.34 us
    ppermute x8, waiting for transfers between devices, exchange(): return lax.ppermute(value, 'seq', pairs)  5.75 us
    reshape x9, local copies, waits for them, and re-layouts, spread(): return jnp.repeat(scales, HEAD_DIM, axis=1)  1.62 us
    broadcast_in_dim x9, local copies, waits for them, and re-layouts, spread(): return jnp.repeat(scales, HEAD_DIM, axis=1)  1.57 us
  transfers between devices with their start and end apart: 13, of which 9 were waited for; matrix products, arithmetic and copies ran while one was open for 3% of the time, Pallas kernels for 44%

profile of v5, /device:TPU:0, one launch (start us, length us, event | category | flops | bytes accessed | tf_op | source)
XLA Modules:
  0.0 77.1 jit_solution(14052085136069647566)
XLA Ops:
  0.6 4.1 %collective-permute-start.2 = (bf16[1,8,2048]{2,1,0:T(8,128)(2,1)}, bf16[1,8,2048]{2,1,0:T(8,128)(2,1)S(1)}, u32[]{:S(2)}, u32[]{:S(2)}) collective-permute-start(bf16[1,8,2048]{2,1,0:T(8,128)(2,1)} %bitcast.104), channel_id=1, source_target_pairs={{0,8},{1,9},{2,10},{3,11},{4,12},{5,13},{6,14},{7,15},{8,0},{9,1},... | collective-permute-start | bytes 98312 | tf_op jit(solution)/shard_map/ppermute | solution.py:65
  4.7 1.6 %collective-permute-start.1 = (bf16[1,8,2048]{2,1,0:T(8,128)(2,1)}, bf16[1,8,2048]{2,1,0:T(8,128)(2,1)S(1)}, u32[]{:S(2)}, u32[]{:S(2)}) collective-permute-start(bf16[1,8,2048]{2,1,0:T(8,128)(2,1)} %bitcast.105), channel_id=1, source_target_pairs={{0,4},{1,5},{2,6},{3,7},{4,0},{5,1},{6,2},{7,3},{8,12},{9,13},{10,... | collective-permute-start | bytes 98312 | tf_op jit(solution)/shard_map/ppermute | solution.py:65
  6.3 1.0 %collective-permute-done.2 = bf16[1,8,2048]{2,1,0:T(8,128)(2,1)S(1)} collective-permute-done((bf16[1,8,2048]{2,1,0:T(8,128)(2,1)}, bf16[1,8,2048]{2,1,0:T(8,128)(2,1)S(1)}, u32[]{:S(2)}, u32[]{:S(2)}) %collective-permute-start.2) | collective-permute-done | bytes 32800 | tf_op jit(solution)/shard_map/ppermute | solution.py:65
  7.3 1.6 %collective-permute-done.1 = bf16[1,8,2048]{2,1,0:T(8,128)(2,1)S(1)} collective-permute-done((bf16[1,8,2048]{2,1,0:T(8,128)(2,1)}, bf16[1,8,2048]{2,1,0:T(8,128)(2,1)S(1)}, u32[]{:S(2)}, u32[]{:S(2)}) %collective-permute-start.1) | collective-permute-done | bytes 32800 | tf_op jit(solution)/shard_map/ppermute | solution.py:65
  8.9 3.4 %collective-permute-done = bf16[1,8,2048]{2,1,0:T(8,128)(2,1)S(1)} collective-permute-done((bf16[1,8,2048]{2,1,0:T(8,128)(2,1)}, bf16[1,8,2048]{2,1,0:T(8,128)(2,1)S(1)}, u32[]{:S(2)}, u32[]{:S(2)}) %collective-permute-start) | collective-permute-done | bytes 32800 | tf_op jit(solution)/shard_map/ppermute | solution.py:65
  12.2 0.8 %select_bitcast_fusion.23 = (bf16[1,1,8,2048]{3,2,1,0:T(8,128)(2,1)S(1)}, bf16[1,1,8,2048]{3,2,1,0:T(8,128)(2,1)S(1)}, bf16[1,1,8,2048]{3,2,1,0:T(8,128)(2,1)S(1)}, bf16[1,1,8,2048]{3,2,1,0:T(8,128)(2,1)S(1)}) fusion(bf16[1,8,2048]{2,1,0:T(8,128)(2,1)S(1)} %collective-permute-done, bf16[1,8,2048]{2,1,0:T(8,128)(2,1)S(1)} %collective-permute-done.1, ...), kind=kLoop, calls=%fused_computation.50 | loop fusion | flops 196608 | bytes 262156 | tf_op jit(solution)/shard_map/stack | solution.py:73
  13.0 1.6 %collective-permute-start.3 = (bf16[4,8,2048]{2,1,0:T(8,128)(2,1)S(1)}, bf16[4,8,2048]{2,1,0:T(8,128)(2,1)S(1)}, u32[]{:S(2)}, u32[]{:S(2)}) collective-permute-start(bf16[4,8,2048]{2,1,0:T(8,128)(2,1)S(1)} %maximum_bitcast_fusion), channel_id=1, source_target_pairs={{0,2},{1,3},{2,0},{3,1},{4,6},{5,7},{6,4},{7,5},{8,10},{9,11},{10,... | collective-permute-start | bytes 393224 | tf_op jit(solution)/shard_map/ppermute | solution.py:65
  14.6 3.4 %collective-permute-done.3 = bf16[4,8,2048]{2,1,0:T(8,128)(2,1)S(1)} collective-permute-done((bf16[4,8,2048]{2,1,0:T(8,128)(2,1)S(1)}, bf16[4,8,2048]{2,1,0:T(8,128)(2,1)S(1)}, u32[]{:S(2)}, u32[]{:S(2)}) %collective-permute-start.3) | collective-permute-done | bytes 131104 | tf_op jit(solution)/shard_map/ppermute | solution.py:65
  18.2 0.8 %maximum_bitcast_fusion.2 = bf16[1,8,4096]{2,1,0:T(8,128)(2,1)S(1)} fusion(bf16[8,2048]{1,0:T(8,128)(2,1)} %param.11, bf16[8,2048]{1,0:T(8,128)(2,1)} %param.10), kind=kLoop, calls=%fused_computation.38 | loop fusion | flops 131072 | bytes 131072 | tf_op jit(solution)/shard_map/broadcast_in_dim | solution.py:23
  19.0 0.7 collective-permute-done.4
  19.9 0.8 %copy.19 = bf16[8,2,8,2048]{3,2,1,0:T(8,128)(2,1)} copy(bf16[8,2,8,2048]{3,2,0,1:T(8,128)(2,1)S(1)} %pad_maximum_fusion.1) | data formatting | bytes 1048576 | tf_op jit(solution)/shard_map/stack | solution.py:73
  20.7 4.2 %shard_map.77 = (f32[128,512]{1,0:T(8,128)}, f32[128,8]{1,0:T(8,128)}, f32[128,8]{1,0:T(8,128)}) custom-call(bf16[128,2048]{1,0:T(8,128)(2,1)} %bitcast.82, bf16[512,2048]{1,0:T(8,128)(2,1)} %key_ref.7, bf16[512,2048]{1,0:T(8,128)(2,1)} %value_ref.7), custom_call_target="tpu_custom_call" | custom-call | flops 268435456 | bytes 1441792 | tf_op jit(solution)/shard_map/pallas_call | solution.py:217
  24.9 0.9 %collective-permute-done.5 = bf16[1,8,4096]{2,1,0:T(8,128)(2,1)S(1)} collective-permute-done((bf16[1,8,4096]{2,1,0:T(8,128)(2,1)S(1)}, bf16[1,8,4096]{2,1,0:T(8,128)(2,1)S(1)}, u32[]{:S(2)}, u32[]{:S(2)}) %collective-permute-start.5) | collective-permute-done | bytes 65568 | tf_op jit(solution)/shard_map/ppermute | solution.py:17
  26.0 4.3 %shard_map.78 = (f32[128,512]{1,0:T(8,128)}, f32[128,8]{1,0:T(8,128)}, f32[128,8]{1,0:T(8,128)}) custom-call(bf16[128,2048]{1,0:T(8,128)(2,1)} %bitcast.83, bf16[512,2048]{1,0:T(8,128)(2,1)} %key_ref.7, bf16[512,2048]{1,0:T(8,128)(2,1)} %value_ref.7), custom_call_target="tpu_custom_call" | custom-call | flops 268435456 | bytes 1441792 | tf_op jit(solution)/shard_map/pallas_call | solution.py:217
  30.2 0.7 collective-permute-done.6
  31.0 1.6 %collective-permute-start.7 = (bf16[4,8,4096]{2,1,0:T(8,128)(2,1)S(1)}, bf16[4,8,4096]{2,1,0:T(8,128)(2,1)S(1)}, u32[]{:S(2)}, u32[]{:S(2)}) collective-permute-start(bf16[4,8,4096]{2,1,0:T(8,128)(2,1)S(1)} %bitcast.93), channel_id=1, source_target_pairs={{0,2},{1,3},{2,0},{3,1},{4,6},{5,7},{6,4},{7,5},{8,10},{9,11},{10,... | collective-permute-start | bytes 786440 | tf_op jit(solution)/shard_map/ppermute | solution.py:17
  32.6 4.2 %shard_map.79 = (f32[128,512]{1,0:T(8,128)}, f32[128,8]{1,0:T(8,128)}, f32[128,8]{1,0:T(8,128)}) custom-call(bf16[128,2048]{1,0:T(8,128)(2,1)} %bitcast.84, bf16[512,2048]{1,0:T(8,128)(2,1)} %key_ref.7, bf16[512,2048]{1,0:T(8,128)(2,1)} %value_ref.7), custom_call_target="tpu_custom_call" | custom-call | flops 268435456 | bytes 1441792 | tf_op jit(solution)/shard_map/pallas_call | solution.py:217
  36.8 1.3 %collective-permute-done.7 = bf16[4,8,4096]{2,1,0:T(8,128)(2,1)S(1)} collective-permute-done((bf16[4,8,4096]{2,1,0:T(8,128)(2,1)S(1)}, bf16[4,8,4096]{2,1,0:T(8,128)(2,1)S(1)}, u32[]{:S(2)}, u32[]{:S(2)}) %collective-permute-start.7) | collective-permute-done | bytes 262176 | tf_op jit(solution)/shard_map/ppermute | solution.py:17
  38.4 4.4 %shard_map.80 = (f32[128,512]{1,0:T(8,128)}, f32[128,8]{1,0:T(8,128)}, f32[128,8]{1,0:T(8,128)}) custom-call(bf16[128,2048]{1,0:T(8,128)(2,1)} %bitcast.85, bf16[512,2048]{1,0:T(8,128)(2,1)} %key_ref.7, bf16[512,2048]{1,0:T(8,128)(2,1)} %value_ref.7), custom_call_target="tpu_custom_call" | custom-call | flops 268435456 | bytes 1441792 | tf_op jit(solution)/shard_map/pallas_call | solution.py:217
  42.8 1.2 %concatenate.16 = f32[128,2112]{1,0:T(8,128)S(1)} concatenate(f32[128,512]{1,0:T(8,128)S(1)} %copy-done, f32[128,512]{1,0:T(8,128)S(1)} %copy-done.1, f32[128,512]{1,0:T(8,128)S(1)} %copy-done.2, f32[128,512]{1,0:T(8,128)} %get-tuple-element.78, f32[128,8]{1,0:T(8,128)S(1)} %copy-done.3, f32[128,8]{1,0:T(8,128)S(1)} %copy-done.5, f32[128,8]{1,0:T(8,128)S(1)} %copy-done.7, ...), dimensions={1} | concatenate | bytes 2162688 | tf_op jit(solution)/shard_map/concatenate | solution.py:257
  44.1 0.9 %select_bitcast_fusion.1 = (f32[64,2112]{1,0:T(8,128)S(1)}, f32[8,8,2112]{2,1,0:T(8,128)}) fusion(f32[8,2,8,2112]{3,2,1,0:T(8,128)S(1)} %bitcast.86, pred[]{:T(512)S(6)} %ne.19), kind=kLoop, calls=%fused_computation.2 | loop fusion | flops 270336 | bytes 2162689 | tf_op jit(solution)/shard_map/jit(_where)/select_n | solution.py:98
  45.0 0.5 collective-permute-start.9
  45.6 0.1 pad_maximum_fusion
  45.8 1.1 %fusion.14 = (bf16[128,2048]{1,0:T(8,128)(2,1)}, bf16[128,2048]{1,0:T(8,128)(2,1)}) fusion(bf16[128,4096]{1,0:T(8,128)(2,1)S(1)} %bitcast.87), kind=kLoop, calls=%fused_computation.71 | loop fusion | bytes 2097152 | tf_op jit(solution)/shard_map/slice | solution.py:256
  46.8 4.2 %shard_map.81.refs_0_ = bf16[512,2048]{1,0:T(8,128)(2,1)} custom-call(bf16[512,2048]{1,0:T(8,128)(2,1)} %query_ref.7, bf16[128,2048]{1,0:T(8,128)(2,1)} %get-tuple-element.120.key_ref, bf16[128,2048]{1,0:T(8,128)(2,1)} %get-tuple-element.119.value_ref), custom_call_target="tpu_custom_call" | custom-call | flops 268435456 | bytes 1310720 | tf_op jit(solution)/shard_map/pallas_call | solution.py:176
  51.2 0.3 broadcast_in_dim.35
  51.5 0.4 reshape.117
  51.9 0.3 broadcast_in_dim.36
  52.2 0.4 reshape.118
  52.6 0.1 fusion
  52.8 1.6 %collective-permute-start.10 = (f32[4,8,2112]{2,1,0:T(8,128)S(1)}, f32[4,8,2112]{2,1,0:T(8,128)S(1)}, u32[]{:S(2)}, u32[]{:S(2)}) collective-permute-start(f32[4,8,2112]{2,1,0:T(8,128)S(1)} %get-tuple-element.90), channel_id=1, source_target_pairs={{0,2},{1,3},{2,0},{3,1},{4,6},{5,7},{6,4},{7,5},{8,10},{9,11},{10,... | collective-permute-start | bytes 811016 | tf_op jit(solution)/shard_map/ppermute | solution.py:17
  54.4 4.2 %shard_map.82.refs_0_ = bf16[512,2048]{1,0:T(8,128)(2,1)} custom-call(bf16[512,2048]{1,0:T(8,128)(2,1)} %query_ref.7, bf16[128,2048]{1,0:T(8,128)(2,1)} %get-tuple-element.120.key_ref, bf16[128,2048]{1,0:T(8,128)(2,1)} %get-tuple-element.119.value_ref, bf16[512,2048]{1,0:T(8,128)(2,1)} %shard_map.81.refs_0_), custom_call_target="tpu_custom_call", output_to_operand_aliasing={{}: (3, {})} | custom-call | flops 268435456 | bytes 1310720 | tf_op jit(solution)/shard_map/pallas_call | solution.py:176
  58.6 2.9 %collective-permute-done.10 = f32[4,8,2112]{2,1,0:T(8,128)S(1)} collective-permute-done((f32[4,8,2112]{2,1,0:T(8,128)S(1)}, f32[4,8,2112]{2,1,0:T(8,128)S(1)}, u32[]{:S(2)}, u32[]{:S(2)}) %collective-permute-start.10) | collective-permute-done | bytes 270368 | tf_op jit(solution)/shard_map/ppermute | solution.py:17
  61.6 0.2 broadcast_in_dim.37
  61.8 0.2 reshape.120
  61.9 0.2 broadcast_in_dim.38
  62.1 0.2 reshape.121
  62.5 1.5 %collective-permute-start.11 = (f32[2,8,2112]{2,1,0:T(8,128)S(1)}, f32[2,8,2112]{2,1,0:T(8,128)S(1)}, u32[]{:S(2)}, u32[]{:S(2)}) collective-permute-start(f32[2,8,2112]{2,1,0:T(8,128)S(1)} %get-tuple-element.94), channel_id=1, source_target_pairs={{0,4},{1,5},{2,6},{3,7},{4,0},{5,1},{6,2},{7,3},{8,12},{9,13},{10,... | collective-permute-start | bytes 405512 | tf_op jit(solution)/shard_map/ppermute | solution.py:17
  64.0 4.2 %shard_map.83.refs_0_ = bf16[512,2048]{1,0:T(8,128)(2,1)} custom-call(bf16[512,2048]{1,0:T(8,128)(2,1)} %query_ref.7, bf16[128,2048]{1,0:T(8,128)(2,1)} %get-tuple-element.120.key_ref, bf16[128,2048]{1,0:T(8,128)(2,1)} %get-tuple-element.119.value_ref, bf16[512,2048]{1,0:T(8,128)(2,1)} %shard_map.82.refs_0_), custom_call_target="tpu_custom_call", output_to_operand_aliasing={{}: (3, {})} | custom-call | flops 268435456 | bytes 1310720 | tf_op jit(solution)/shard_map/pallas_call | solution.py:176
  68.3 0.1 broadcast_in_dim.39
  68.4 0.1 reshape.123
  68.5 0.1 broadcast_in_dim.40
  68.6 0.1 reshape.124
  68.9 2.7 %collective-permute-start.12 = (f32[1,8,2112]{2,1,0:T(8,128)S(1)}, f32[1,8,2112]{2,1,0:T(8,128)S(1)}, u32[]{:S(2)}, u32[]{:S(2)}) collective-permute-start(f32[1,8,2112]{2,1,0:T(8,128)S(1)} %get-tuple-element.98), channel_id=1, source_target_pairs={{0,8},{1,9},{2,10},{3,11},{4,12},{5,13},{6,14},{7,15},{8,0},{9,1},... | collective-permute-start | bytes 202760 | tf_op jit(solution)/shard_map/ppermute | solution.py:17
  71.6 4.2 %shard_map.84 = bf16[512,2048]{1,0:T(8,128)(2,1)} custom-call(bf16[512,2048]{1,0:T(8,128)(2,1)} %query_ref.7, bf16[128,2048]{1,0:T(8,128)(2,1)} %get-tuple-element.120.key_ref, bf16[128,2048]{1,0:T(8,128)(2,1)} %get-tuple-element.119.value_ref, bf16[512,2048]{1,0:T(8,128)(2,1)} %shard_map.83.refs_0_), custom_call_target="tpu_custom_call", output_to_operand_aliasing={{}: (3, {})} | custom-call | flops 268435456 | bytes 1310720 | tf_op jit(solution)/shard_map/pallas_call | solution.py:176
  75.9 0.1 broadcast_in_dim.43
  76.0 0.1 reshape.128
  76.5 0.6 fusion.5
  (57 shorter events, 1.9 us)
Async XLA Ops:
  0.6 6.7 %collective-permute-start.2 = (bf16[1,8,2048]{2,1,0:T(8,128)(2,1)}, bf16[1,8,2048]{2,1,0:T(8,128)(2,1)S(1)}, u32[]{:S(2)}, u32[]{:S(2)}) collective-permute-start(bf16[1,8,2048]{2,1,0:T(8,128)(2,1)} %bitcast.104), channel_id=1, source_target_pairs={{0,8},{1,9},{2,10},{3,11},{4,12},{5,13},{6,14},{7,15},{8,0},{9,1},... | collective-permute-start | bytes 98312 | tf_op jit(solution)/shard_map/ppermute | solution.py:65
  4.7 4.1 %collective-permute-start.1 = (bf16[1,8,2048]{2,1,0:T(8,128)(2,1)}, bf16[1,8,2048]{2,1,0:T(8,128)(2,1)S(1)}, u32[]{:S(2)}, u32[]{:S(2)}) collective-permute-start(bf16[1,8,2048]{2,1,0:T(8,128)(2,1)} %bitcast.105), channel_id=1, source_target_pairs={{0,4},{1,5},{2,6},{3,7},{4,0},{5,1},{6,2},{7,3},{8,12},{9,13},{10,... | collective-permute-start | bytes 98312 | tf_op jit(solution)/shard_map/ppermute | solution.py:65
  6.3 5.9 %collective-permute-start = (bf16[1,8,2048]{2,1,0:T(8,128)(2,1)}, bf16[1,8,2048]{2,1,0:T(8,128)(2,1)S(1)}, u32[]{:S(2)}, u32[]{:S(2)}) collective-permute-start(bf16[1,8,2048]{2,1,0:T(8,128)(2,1)} %bitcast.106), channel_id=1, source_target_pairs={{0,12},{1,13},{2,14},{3,15},{4,8},{5,9},{6,10},{7,11},{8,4},{9,5},... | collective-permute-start | bytes 98312 | tf_op jit(solution)/shard_map/ppermute | solution.py:65
  13.0 5.0 %collective-permute-start.3 = (bf16[4,8,2048]{2,1,0:T(8,128)(2,1)S(1)}, bf16[4,8,2048]{2,1,0:T(8,128)(2,1)S(1)}, u32[]{:S(2)}, u32[]{:S(2)}) collective-permute-start(bf16[4,8,2048]{2,1,0:T(8,128)(2,1)S(1)} %maximum_bitcast_fusion), channel_id=1, source_target_pairs={{0,2},{1,3},{2,0},{3,1},{4,6},{5,7},{6,4},{7,5},{8,10},{9,11},{10,... | collective-permute-start | bytes 393224 | tf_op jit(solution)/shard_map/ppermute | solution.py:65
  18.1 1.6 %collective-permute-start.4 = (bf16[8,8,2048]{2,1,0:T(8,128)(2,1)S(1)}, bf16[8,8,2048]{2,1,0:T(8,128)(2,1)S(1)}, u32[]{:S(2)}, u32[]{:S(2)}) collective-permute-start(bf16[8,8,2048]{2,1,0:T(8,128)(2,1)S(1)} %bitcast.92), channel_id=1, source_target_pairs={{0,1},{1,0},{2,3},{3,2},{4,5},{5,4},{6,7},{7,6},{8,9},{9,8},{10,11... | collective-permute-start | bytes 786440 | tf_op jit(solution)/shard_map/ppermute | solution.py:65
  20.7 5.2 %collective-permute-start.5 = (bf16[1,8,4096]{2,1,0:T(8,128)(2,1)S(1)}, bf16[1,8,4096]{2,1,0:T(8,128)(2,1)S(1)}, u32[]{:S(2)}, u32[]{:S(2)}) collective-permute-start(bf16[1,8,4096]{2,1,0:T(8,128)(2,1)S(1)} %maximum_bitcast_fusion.2), channel_id=1, source_target_pairs={{0,8},{1,9},{2,10},{3,11},{4,12},{5,13},{6,14},{7,15},{8,0},{9,1},... | collective-permute-start | bytes 196616 | tf_op jit(solution)/shard_map/ppermute | solution.py:17
  25.9 5.0 %collective-permute-start.6 = (bf16[2,8,4096]{2,1,0:T(8,128)(2,1)S(1)}, bf16[2,8,4096]{2,1,0:T(8,128)(2,1)S(1)}, u32[]{:S(2)}, u32[]{:S(2)}) collective-permute-start(bf16[2,8,4096]{2,1,0:T(8,128)(2,1)S(1)} %maximum_bitcast_fusion.1), channel_id=1, source_target_pairs={{0,4},{1,5},{2,6},{3,7},{4,0},{5,1},{6,2},{7,3},{8,12},{9,13},{10,... | collective-permute-start | bytes 393224 | tf_op jit(solution)/shard_map/ppermute | solution.py:17
  31.0 7.1 %collective-permute-start.7 = (bf16[4,8,4096]{2,1,0:T(8,128)(2,1)S(1)}, bf16[4,8,4096]{2,1,0:T(8,128)(2,1)S(1)}, u32[]{:S(2)}, u32[]{:S(2)}) collective-permute-start(bf16[4,8,4096]{2,1,0:T(8,128)(2,1)S(1)} %bitcast.93), channel_id=1, source_target_pairs={{0,2},{1,3},{2,0},{3,1},{4,6},{5,7},{6,4},{7,5},{8,10},{9,11},{10,... | collective-permute-start | bytes 786440 | tf_op jit(solution)/shard_map/ppermute | solution.py:17
  38.2 4.5 %collective-permute-start.8 = (bf16[8,8,4096]{2,1,0:T(8,128)(2,1)S(1)}, bf16[8,8,4096]{2,1,0:T(8,128)(2,1)S(1)}, u32[]{:S(2)}, u32[]{:S(2)}) collective-permute-start(bf16[8,8,4096]{2,1,0:T(8,128)(2,1)S(1)} %bitcast.89), channel_id=1, source_target_pairs={{0,1},{1,0},{2,3},{3,2},{4,5},{5,4},{6,7},{7,6},{8,9},{9,8},{10,11... | collective-permute-start | bytes 1572872 | tf_op jit(solution)/shard_map/ppermute | solution.py:17
  38.3 4.4 %copy-start = (f32[128,512]{1,0:T(8,128)S(1)}, f32[128,512]{1,0:T(8,128)}, u32[]{:S(2)}) copy-start(f32[128,512]{1,0:T(8,128)} %get-tuple-element.57) | copy-start | bytes 786436
  38.3 4.4 %copy-start.1 = (f32[128,512]{1,0:T(8,128)S(1)}, f32[128,512]{1,0:T(8,128)}, u32[]{:S(2)}) copy-start(f32[128,512]{1,0:T(8,128)} %get-tuple-element.64) | copy-start | bytes 786436
  38.3 4.4 %copy-start.2 = (f32[128,512]{1,0:T(8,128)S(1)}, f32[128,512]{1,0:T(8,128)}, u32[]{:S(2)}) copy-start(f32[128,512]{1,0:T(8,128)} %get-tuple-element.71) | copy-start | bytes 786436
  38.3 4.4 %copy-start.3 = (f32[128,8]{1,0:T(8,128)S(1)}, f32[128,8]{1,0:T(8,128)}, u32[]{:S(2)}) copy-start(f32[128,8]{1,0:T(8,128)} %get-tuple-element.79) | copy-start | bytes 12292
  38.4 4.4 %copy-start.4 = (f32[128,8]{1,0:T(8,128)S(1)}, f32[128,8]{1,0:T(8,128)}, u32[]{:S(2)}) copy-start(f32[128,8]{1,0:T(8,128)} %get-tuple-element.83) | copy-start | bytes 12292
  38.4 4.4 %copy-start.5 = (f32[128,8]{1,0:T(8,128)S(1)}, f32[128,8]{1,0:T(8,128)}, u32[]{:S(2)}) copy-start(f32[128,8]{1,0:T(8,128)} %get-tuple-element.80) | copy-start | bytes 12292
  38.4 4.4 %copy-start.6 = (f32[128,8]{1,0:T(8,128)S(1)}, f32[128,8]{1,0:T(8,128)}, u32[]{:S(2)}) copy-start(f32[128,8]{1,0:T(8,128)} %get-tuple-element.84) | copy-start | bytes 12292
  38.4 4.4 %copy-start.7 = (f32[128,8]{1,0:T(8,128)S(1)}, f32[128,8]{1,0:T(8,128)}, u32[]{:S(2)}) copy-start(f32[128,8]{1,0:T(8,128)} %get-tuple-element.81) | copy-start | bytes 12292
  38.4 4.4 %copy-start.8 = (f32[128,8]{1,0:T(8,128)S(1)}, f32[128,8]{1,0:T(8,128)}, u32[]{:S(2)}) copy-start(f32[128,8]{1,0:T(8,128)} %get-tuple-element.85) | copy-start | bytes 12292
  45.0 6.0 %collective-permute-start.9 = (f32[8,8,2112]{2,1,0:T(8,128)}, f32[8,8,2112]{2,1,0:T(8,128)S(1)}, u32[]{:S(2)}, u32[]{:S(2)}) collective-permute-start(f32[8,8,2112]{2,1,0:T(8,128)} %get-tuple-element.118), channel_id=1, source_target_pairs={{0,1},{1,0},{2,3},{3,2},{4,5},{5,4},{6,7},{7,6},{8,9},{9,8},{10,11... | collective-permute-start | bytes 1622024 | tf_op jit(solution)/shard_map/ppermute | solution.py:17
  52.8 8.7 %collective-permute-start.10 = (f32[4,8,2112]{2,1,0:T(8,128)S(1)}, f32[4,8,2112]{2,1,0:T(8,128)S(1)}, u32[]{:S(2)}, u32[]{:S(2)}) collective-permute-start(f32[4,8,2112]{2,1,0:T(8,128)S(1)} %get-tuple-element.90), channel_id=1, source_target_pairs={{0,2},{1,3},{2,0},{3,1},{4,6},{5,7},{6,4},{7,5},{8,10},{9,11},{10,... | collective-permute-start | bytes 811016 | tf_op jit(solution)/shard_map/ppermute | solution.py:17
  62.5 5.7 %collective-permute-start.11 = (f32[2,8,2112]{2,1,0:T(8,128)S(1)}, f32[2,8,2112]{2,1,0:T(8,128)S(1)}, u32[]{:S(2)}, u32[]{:S(2)}) collective-permute-start(f32[2,8,2112]{2,1,0:T(8,128)S(1)} %get-tuple-element.94), channel_id=1, source_target_pairs={{0,4},{1,5},{2,6},{3,7},{4,0},{5,1},{6,2},{7,3},{8,12},{9,13},{10,... | collective-permute-start | bytes 405512 | tf_op jit(solution)/shard_map/ppermute | solution.py:17
  68.9 6.9 %collective-permute-start.12 = (f32[1,8,2112]{2,1,0:T(8,128)S(1)}, f32[1,8,2112]{2,1,0:T(8,128)S(1)}, u32[]{:S(2)}, u32[]{:S(2)}) collective-permute-start(f32[1,8,2112]{2,1,0:T(8,128)S(1)} %get-tuple-element.98), channel_id=1, source_target_pairs={{0,8},{1,9},{2,10},{3,11},{4,12},{5,13},{6,14},{7,15},{8,0},{9,1},... | collective-permute-start | bytes 202760 | tf_op jit(solution)/shard_map/ppermute | solution.py:17

commit v6 on v5

--- a/solution.py
+++ b/solution.py
@@ -17,61 +17,29 @@
     return lax.ppermute(value, "seq", pairs)
 
 
-def gather_rows(block, during=()):
+def gather_rows(block, during=(), carried=None):
     count = lax.axis_size("seq")
     me = lax.axis_index("seq")
     held = block[None]
-    results = []
     bit = count // 2
     step = 0
     while bit >= 1:
         work = during[step] if step < len(during) else None
         if work is not None:
-            held, ready = lax.optimization_barrier((held, work[1]))
+            held, carried = lax.optimization_barrier((held, carried))
         arrived = exchange(held, bit, count)
         if work is not None:
-            done = work[0](ready)
-            arrived, done = lax.optimization_barrier((arrived, done))
-            results.append(done)
+            carried = work(carried)
+            arrived, carried = lax.optimization_barrier((arrived, carried))
         upper = (me & bit) != 0
         low = jnp.where(upper, arrived, held)
         high = jnp.where(upper, held, arrived)
         held = jnp.stack([low, high], axis=1).reshape((-1,) + block.shape)
         bit //= 2
         step += 1
-    return held.reshape((count * block.shape[0],) + block.shape[1:]), results
-
-
-def gather_levels(block):
-    count = lax.axis_size("seq")
-    me = lax.axis_index("seq")
-    held = block[None]
-    levels = []
-    bit = count // 2
-    if bit >= 2:
-        levels.append((bit, bit // 2))
-        bit //= 4
-    while bit >= 1:
-        levels.append((bit,))
-        bit //= 2
-    for level in levels:
-        mask = sum(level)
-        offsets = [0]
-        for b in level:
-            offsets = offsets + [o + b for o in offsets]
-        pieces = {0: held}
-        for offset in offsets[1:]:
-            pairs = [(source, source ^ offset) for source in range(count)]
-            pieces[offset] = lax.ppermute(held, "seq", pairs)
-        mine = me & mask
-        ordered = []
-        for target in sorted(offsets):
-            choice = pieces[0]
-            for offset in offsets[1:]:
-                choice = jnp.where((mine ^ offset) == target, pieces[offset], choice)
-            ordered.append(choice)
-        held = jnp.stack(ordered, axis=1).reshape((-1,) + block.shape)
-    return held.reshape((count * block.shape[0],) + block.shape[1:])
+    for work in during[step:]:
+        carried = work(carried)
+    return held.reshape((count * block.shape[0],) + block.shape[1:]), carried
 
 
 def merge(first, second, heads):
@@ -157,17 +125,18 @@
     out_ref[...] = (summed / totals).astype(out_ref.dtype)
 
 
-def video_part(queries, keys, values, earlier, group, groups):
+def video_part(queries, packed, earlier, group, groups):
     rows, width = queries.shape
     pairs = width // (2 * HEAD_DIM) // groups
     first_pair = group * pairs
-    key_rows = keys.shape[0]
+    value_pair = first_pair + width // (2 * HEAD_DIM)
+    key_rows = packed.shape[0]
     specs = [
         pl.BlockSpec((rows, 2 * HEAD_DIM), lambda p: (0, p + first_pair)),
         pl.BlockSpec((key_rows, 2 * HEAD_DIM), lambda p: (0, p + first_pair)),
-        pl.BlockSpec((key_rows, 2 * HEAD_DIM), lambda p: (0, p + first_pair)),
+        pl.BlockSpec((key_rows, 2 * HEAD_DIM), lambda p: (0, p + value_pair)),
     ]
-    operands = [queries, keys, values]
+    operands = [queries, packed, packed]
     aliases = {}
     if earlier is not None:
         specs.append(pl.BlockSpec(memory_space=pl.ANY))
@@ -188,7 +157,8 @@
     )(*operands)
 
 
-def audio_kernel(query_ref, key_ref, value_ref, sum_ref, total_ref, top_ref):
+def audio_kernel(query_ref, key_ref, value_ref, *refs):
+    sum_ref, total_ref, top_ref = refs[-3:]
     pair = pl.program_id(0)
 
     @pl.when(pair == 0)
@@ -209,57 +179,67 @@
     sum_ref[...] = summed
 
 
-def audio_partial(queries, keys, values, group, groups):
+def audio_part(queries, keys, values, earlier, group, groups):
     rows, width = queries.shape
     heads = width // HEAD_DIM // groups
     first_pair = group * heads // 2
     key_rows = keys.shape[0]
+    state_width = width + 2 * width // HEAD_DIM
+    specs = [
+        pl.BlockSpec((rows, 2 * HEAD_DIM), lambda p: (0, p + first_pair)),
+        pl.BlockSpec((key_rows, 2 * HEAD_DIM), lambda p: (0, p + first_pair)),
+        pl.BlockSpec((key_rows, 2 * HEAD_DIM), lambda p: (0, p + first_pair)),
+    ]
+    operands = [queries, keys, values]
+    aliases = {}
+    if earlier is not None:
+        specs.append(pl.BlockSpec(memory_space=pl.ANY))
+        operands.append(earlier)
+        aliases = {3: 0}
     return pl.pallas_call(
         audio_kernel,
         grid=(heads // 2,),
-        in_specs=[
+        in_specs=specs,
+        out_specs=[
             pl.BlockSpec((rows, 2 * HEAD_DIM), lambda p: (0, p + first_pair)),
-            pl.BlockSpec((key_rows, 2 * HEAD_DIM), lambda p: (0, p + first_pair)),
-            pl.BlockSpec((key_rows, 2 * HEAD_DIM), lambda p: (0, p + first_pair)),
-        ],
-        out_specs=[
-            pl.BlockSpec((rows, 2 * HEAD_DIM), lambda p: (0, p)),
             pl.BlockSpec((rows, heads), lambda p: (0, 0)),
             pl.BlockSpec((rows, heads), lambda p: (0, 0)),
         ],
         out_shape=[
-            jax.ShapeDtypeStruct((rows, heads * HEAD_DIM), jnp.float32),
+            jax.ShapeDtypeStruct((rows, state_width), jnp.float32),
             jax.ShapeDtypeStruct((rows, heads), jnp.float32),
             jax.ShapeDtypeStruct((rows, heads), jnp.float32),
         ],
+        input_output_aliases=aliases,
         compiler_params=pltpu.CompilerParams(dimension_semantics=("arbitrary",)),
         cost_estimate=pl.CostEstimate(
             flops=8 * rows * key_rows * width // groups,
             transcendentals=rows * key_rows * heads,
             bytes_accessed=(2 * rows * width + 4 * key_rows * width + 4 * rows * width) // groups,
         ),
-    )(queries, keys, values)
+    )(*operands)
 
 
 def local(video_q, video_k, video_v, audio_q, audio_k, audio_v):
     width = video_q.shape[1]
     heads = width // HEAD_DIM
     groups = 4
-    all_queries = gather_levels(audio_q)
-    audio_calls = [
-        (lambda q, g=g: audio_partial(q, video_k, video_v, g, groups), all_queries)
-        for g in range(groups)
-    ]
-    gathered, parts = gather_rows(jnp.concatenate([audio_k, audio_v], axis=1), audio_calls)
-    parts = parts + [call[0](all_queries) for call in audio_calls[len(parts) :]]
-    all_keys = gathered[:, :width]
-    all_values = gathered[:, width:]
-    state = jnp.concatenate(
-        [part[0] for part in parts] + [part[1] for part in parts] + [part[2] for part in parts],
-        axis=1,
+    all_queries, ignored = gather_rows(audio_q)
+
+    def audio_step(carried, g):
+        queries, state, totals, tops = carried
+        state, total, top = audio_part(queries, video_k, video_v, state, g, groups)
+        return queries, state, totals + (total,), tops + (top,)
+
+    audio_calls = [lambda c, g=g: audio_step(c, g) for g in range(groups)]
+    packed, (ignored, state, totals, tops) = gather_rows(
+        jnp.concatenate([audio_k, audio_v], axis=1), audio_calls, (all_queries, None, (), ())
+    )
+    state = lax.dynamic_update_slice(
+        state, jnp.concatenate(totals + tops, axis=1), (0, width)
     )
     video_calls = [
-        lambda earlier, g=g: video_part(video_q, all_keys, all_values, earlier, g, groups)
+        lambda earlier, g=g: video_part(video_q, packed, earlier, g, groups)
         for g in range(groups)
     ]
     mine, video_out = scatter_rows(state, heads, video_calls)

time: 77.9 us -> 80.2 us (1.030)
  starting transfers between devices: 15.4 us -> 18.3 us
    ppermute x8 -> x12, starting transfers between devices: 8.03 us -> 18.3 us  [exchange(): return lax.ppermute(value, 'seq', pairs)]
    ppermute x5 -> x0, waiting for transfers between devices: 10.1 us -> none  [gather_levels(): pieces[offset] = lax.ppermute(held, 'seq', pairs)]
    ppermute x8 -> x12, waiting for transfers between devices: 5.75 us -> 15.2 us  [exchange(): return lax.ppermute(value, 'seq', pairs)]
    ppermute x5 -> x0, starting transfers between devices: 7.34 us -> none  [gather_levels(): pieces[offset] = lax.ppermute(held, 'seq', pairs)]
    another operation x2 -> x4, local copies, waits for them, and re-layouts: 0.13 us -> 1.93 us  [gather_rows(): held = jnp.stack([low, high], axis=1).reshape((-1,) + block.shape)]
    slice x1 -> x0, local copies, waits for them, and re-layouts: 1.07 us -> none  [local(): all_values = gathered[:, width:]]
    another operation x7 -> x14, other arithmetic: 0.32 us -> 1.28 us  [gather_rows(): held = jnp.stack([low, high], axis=1).reshape((-1,) + block.shape)]
    another operation x5 -> x0, other arithmetic: 0.94 us -> none  [gather_levels(): held = jnp.stack(ordered, axis=1).reshape((-1,) + block.shape)]
  transfers between devices with their start and end apart: 13 -> 12, of which waited for: 9 -> 7; matrix products, arithmetic and copies ran while one was open for 3% -> 2% of each run, Pallas kernels for 44% -> 43%
where the time goes in v6:
time: 80.2 us; the launch traced here: 79.4 us
  Pallas kernels  33.9 us (42%)
  starting transfers between devices  18.3 us (23%)
  waiting for transfers between devices  15.2 us (19%)
  local copies, waits for them, and re-layouts  7.11 us (9%)
  other arithmetic  3.85 us (5%)
  between operations  1.02 us (1%)
    ppermute x12, starting transfers between devices, exchange(): return lax.ppermute(value, 'seq', pairs)  18.3 us
    pallas_call x4, Pallas kernels, audio_part(): pl.pallas_call(audio_kernel, grid=(heads // 2,), in_specs=specs, out_spec...  17 us
    pallas_call x4, Pallas kernels, video_part(): pl.pallas_call(video_kernel, grid=(pairs,), in_specs=specs, out_specs=pl....  16.9 us
    ppermute x12, waiting for transfers between devices, exchange(): return lax.ppermute(value, 'seq', pairs)  15.2 us
    another operation x4, local copies, waits for them, and re-layouts, gather_rows(): held = jnp.stack([low, high], axis=1).reshape((-1,) + block.shape)  1.93 us
    reshape x9, local copies, waits for them, and re-layouts, spread(): return jnp.repeat(scales, HEAD_DIM, axis=1)  1.62 us
  transfers between devices with their start and end apart: 12, of which 7 were waited for; matrix products, arithmetic and copies ran while one was open for 2% of the time, Pallas kernels for 43%

profile of v6, /device:TPU:0, one launch (start us, length us, event | category | flops | bytes accessed | tf_op | source)
XLA Modules:
  0.0 79.4 jit_solution(14103642445669951520)
XLA Ops:
  0.6 4.1 %collective-permute-start = (bf16[1,8,2048]{2,1,0:T(8,128)(2,1)}, bf16[1,8,2048]{2,1,0:T(8,128)(2,1)S(1)}, u32[]{:S(2)}, u32[]{:S(2)}) collective-permute-start(bf16[1,8,2048]{2,1,0:T(8,128)(2,1)} %bitcast.113), channel_id=1, source_target_pairs={{0,8},{1,9},{2,10},{3,11},{4,12},{5,13},{6,14},{7,15},{8,0},{9,1},... | collective-permute-start | bytes 98312 | tf_op jit(solution)/shard_map/ppermute | solution.py:17
  4.7 2.5 %collective-permute-done = bf16[1,8,2048]{2,1,0:T(8,128)(2,1)S(1)} collective-permute-done((bf16[1,8,2048]{2,1,0:T(8,128)(2,1)}, bf16[1,8,2048]{2,1,0:T(8,128)(2,1)S(1)}, u32[]{:S(2)}, u32[]{:S(2)}) %collective-permute-start) | collective-permute-done | bytes 32800 | tf_op jit(solution)/shard_map/ppermute | solution.py:17
  7.2 0.8 select_bitcast_fusion.23
  8.0 1.6 %collective-permute-start.1 = (bf16[2,8,2048]{2,1,0:T(8,128)(2,1)S(1)}, bf16[2,8,2048]{2,1,0:T(8,128)(2,1)S(1)}, u32[]{:S(2)}, u32[]{:S(2)}) collective-permute-start(bf16[2,8,2048]{2,1,0:T(8,128)(2,1)S(1)} %maximum_bitcast_fusion.2), channel_id=1, source_target_pairs={{0,4},{1,5},{2,6},{3,7},{4,0},{5,1},{6,2},{7,3},{8,12},{9,13},{10,... | collective-permute-start | bytes 196616 | tf_op jit(solution)/shard_map/ppermute | solution.py:17
  9.6 2.7 %collective-permute-done.1 = bf16[2,8,2048]{2,1,0:T(8,128)(2,1)S(1)} collective-permute-done((bf16[2,8,2048]{2,1,0:T(8,128)(2,1)S(1)}, bf16[2,8,2048]{2,1,0:T(8,128)(2,1)S(1)}, u32[]{:S(2)}, u32[]{:S(2)}) %collective-permute-start.1) | collective-permute-done | bytes 65568 | tf_op jit(solution)/shard_map/ppermute | solution.py:17
  12.4 1.8 %collective-permute-start.2 = (bf16[4,8,2048]{2,1,0:T(8,128)(2,1)S(1)}, bf16[4,8,2048]{2,1,0:T(8,128)(2,1)S(1)}, u32[]{:S(2)}, u32[]{:S(2)}) collective-permute-start(bf16[4,8,2048]{2,1,0:T(8,128)(2,1)S(1)} %bitcast.106), channel_id=1, source_target_pairs={{0,2},{1,3},{2,0},{3,1},{4,6},{5,7},{6,4},{7,5},{8,10},{9,11},{10,... | collective-permute-start | bytes 393224 | tf_op jit(solution)/shard_map/ppermute | solution.py:17
  14.2 3.2 %collective-permute-done.2 = bf16[4,8,2048]{2,1,0:T(8,128)(2,1)S(1)} collective-permute-done((bf16[4,8,2048]{2,1,0:T(8,128)(2,1)S(1)}, bf16[4,8,2048]{2,1,0:T(8,128)(2,1)S(1)}, u32[]{:S(2)}, u32[]{:S(2)}) %collective-permute-start.2) | collective-permute-done | bytes 131104 | tf_op jit(solution)/shard_map/ppermute | solution.py:17
  17.6 1.5 %collective-permute-done.3 = bf16[8,8,2048]{2,1,0:T(8,128)(2,1)S(1)} collective-permute-done((bf16[8,8,2048]{2,1,0:T(8,128)(2,1)S(1)}, bf16[8,8,2048]{2,1,0:T(8,128)(2,1)S(1)}, u32[]{:S(2)}, u32[]{:S(2)}) %collective-permute-start.3) | collective-permute-done | bytes 262176 | tf_op jit(solution)/shard_map/ppermute | solution.py:17
  19.2 0.8 %copy.24 = bf16[8,2,8,2048]{3,2,1,0:T(8,128)(2,1)} copy(bf16[8,2,8,2048]{3,2,0,1:T(8,128)(2,1)S(1)} %pad_maximum_fusion.1) | data formatting | bytes 1048576 | tf_op jit(solution)/shard_map/stack | solution.py:37
  20.0 2.6 %collective-permute-start.4 = (bf16[1,8,4096]{2,1,0:T(8,128)(2,1)S(1)}, bf16[1,8,4096]{2,1,0:T(8,128)(2,1)S(1)}, u32[]{:S(2)}, u32[]{:S(2)}) collective-permute-start(bf16[1,8,4096]{2,1,0:T(8,128)(2,1)S(1)} %maximum_bitcast_fusion.1), channel_id=1, source_target_pairs={{0,8},{1,9},{2,10},{3,11},{4,12},{5,13},{6,14},{7,15},{8,0},{9,1},... | collective-permute-start | bytes 196616 | tf_op jit(solution)/shard_map/ppermute | solution.py:17
  22.6 4.2 %shard_map.77 = (f32[128,2112]{1,0:T(8,128)}, f32[128,8]{1,0:T(8,128)}, f32[128,8]{1,0:T(8,128)}) custom-call(bf16[128,2048]{1,0:T(8,128)(2,1)} %bitcast.92, bf16[512,2048]{1,0:T(8,128)(2,1)} %key_ref.7, bf16[512,2048]{1,0:T(8,128)(2,1)} %value_ref.7), custom_call_target="tpu_custom_call" | custom-call | flops 268435456 | bytes 1441792 | tf_op jit(solution)/shard_map/pallas_call | solution.py:199
  26.9 1.9 %collective-permute-start.5 = (bf16[2,8,4096]{2,1,0:T(8,128)(2,1)S(1)}, bf16[2,8,4096]{2,1,0:T(8,128)(2,1)S(1)}, u32[]{:S(2)}, u32[]{:S(2)}) collective-permute-start(bf16[2,8,4096]{2,1,0:T(8,128)(2,1)S(1)} %maximum_bitcast_fusion), channel_id=1, source_target_pairs={{0,4},{1,5},{2,6},{3,7},{4,0},{5,1},{6,2},{7,3},{8,12},{9,13},{10,... | collective-permute-start | bytes 393224 | tf_op jit(solution)/shard_map/ppermute | solution.py:17
  28.8 4.2 %shard_map.78 = (f32[128,2112]{1,0:T(8,128)}, f32[128,8]{1,0:T(8,128)}, f32[128,8]{1,0:T(8,128)}) custom-call(bf16[128,2048]{1,0:T(8,128)(2,1)} %bitcast.93, bf16[512,2048]{1,0:T(8,128)(2,1)} %key_ref.7, bf16[512,2048]{1,0:T(8,128)(2,1)} %value_ref.7, f32[128,2112]{1,0:T(8,128)} %get-tuple-element.94.refs_0_), custom_call_target="tpu_custom_call", output_to_operand_aliasing={{0}: (3, {})} | custom-call | flops 268435456 | bytes 1441792 | tf_op jit(solution)/shard_map/pallas_call | solution.py:199
  33.1 1.6 %collective-permute-start.6 = (bf16[4,8,4096]{2,1,0:T(8,128)(2,1)S(1)}, bf16[4,8,4096]{2,1,0:T(8,128)(2,1)S(1)}, u32[]{:S(2)}, u32[]{:S(2)}) collective-permute-start(bf16[4,8,4096]{2,1,0:T(8,128)(2,1)S(1)} %bitcast.100), channel_id=1, source_target_pairs={{0,2},{1,3},{2,0},{3,1},{4,6},{5,7},{6,4},{7,5},{8,10},{9,11},{10,... | collective-permute-start | bytes 786440 | tf_op jit(solution)/shard_map/ppermute | solution.py:17
  34.7 4.3 %shard_map.79 = (f32[128,2112]{1,0:T(8,128)}, f32[128,8]{1,0:T(8,128)}, f32[128,8]{1,0:T(8,128)}) custom-call(bf16[128,2048]{1,0:T(8,128)(2,1)} %bitcast.94, bf16[512,2048]{1,0:T(8,128)(2,1)} %key_ref.7, bf16[512,2048]{1,0:T(8,128)(2,1)} %value_ref.7, f32[128,2112]{1,0:T(8,128)} %get-tuple-element.109.refs_0_), custom_call_target="tpu_custom_call", output_to_operand_aliasing={{0}: (3, {})} | custom-call | flops 268435456 | bytes 1441792 | tf_op jit(solution)/shard_map/pallas_call | solution.py:199
  38.9 2.0 %collective-permute-done.6 = bf16[4,8,4096]{2,1,0:T(8,128)(2,1)S(1)} collective-permute-done((bf16[4,8,4096]{2,1,0:T(8,128)(2,1)S(1)}, bf16[4,8,4096]{2,1,0:T(8,128)(2,1)S(1)}, u32[]{:S(2)}, u32[]{:S(2)}) %collective-permute-start.6) | collective-permute-done | bytes 262176 | tf_op jit(solution)/shard_map/ppermute | solution.py:17
  41.2 4.3 %shard_map.80 = (f32[128,2112]{1,0:T(8,128)}, f32[128,8]{1,0:T(8,128)}, f32[128,8]{1,0:T(8,128)}) custom-call(bf16[128,2048]{1,0:T(8,128)(2,1)} %bitcast.95, bf16[512,2048]{1,0:T(8,128)(2,1)} %key_ref.7, bf16[512,2048]{1,0:T(8,128)(2,1)} %value_ref.7, f32[128,2112]{1,0:T(8,128)} %get-tuple-element.128.refs_0_), custom_call_target="tpu_custom_call", output_to_operand_aliasing={{0}: (3, {})} | custom-call | flops 268435456 | bytes 1441792 | tf_op jit(solution)/shard_map/pallas_call | solution.py:199
  45.6 1.1 %concatenate.16 = f32[128,64]{1,0:T(8,128)S(1)} concatenate(f32[128,8]{1,0:T(8,128)S(1)} %copy-done, f32[128,8]{1,0:T(8,128)S(1)} %copy-done.2, f32[128,8]{1,0:T(8,128)S(1)} %copy-done.4, f32[128,8]{1,0:T(8,128)} %get-tuple-element.142, f32[128,8]{1,0:T(8,128)S(1)} %copy-done.1, f32[128,8]{1,0:T(8,128)S(1)} %copy-done.3, f32[128,8]{1,0:T(8,128)S(1)} %copy-done.5, ...), dimensions={1} | concatenate | bytes 65536 | tf_op jit(solution)/shard_map/concatenate | solution.py:239
  46.6 0.6 constant_dynamic-update-slice_fusion
  47.3 1.3 %select_bitcast_fusion.1 = (f32[64,2112]{1,0:T(8,128)S(1)}, f32[8,8,2112]{2,1,0:T(8,128)S(1)}) fusion(f32[8,2,8,2112]{3,2,1,0:T(8,128)} %bitcast.91, pred[]{:T(512)S(6)} %ne.11), kind=kLoop, calls=%fused_computation.2 | loop fusion | flops 270336 | bytes 2162689 | tf_op jit(solution)/shard_map/jit(_where)/select_n | solution.py:66
  48.6 0.5 collective-permute-start.8
  49.2 0.1 pad_maximum_fusion
  49.3 1.1 %copy.27 = bf16[8,2,8,4096]{3,2,1,0:T(8,128)(2,1)} copy(bf16[8,2,8,4096]{3,2,0,1:T(8,128)(2,1)S(1)} %pad_maximum_fusion) | data formatting | bytes 2097152 | tf_op jit(solution)/shard_map/stack | solution.py:37
  50.3 4.2 %shard_map.81.refs_0_ = bf16[512,2048]{1,0:T(8,128)(2,1)} custom-call(bf16[512,2048]{1,0:T(8,128)(2,1)} %query_ref.7, bf16[128,4096]{1,0:T(8,128)(2,1)} %bitcast.83, bf16[128,4096]{1,0:T(8,128)(2,1)} %bitcast.84), custom_call_target="tpu_custom_call" | custom-call | flops 268435456 | bytes 1310720 | tf_op jit(solution)/shard_map/pallas_call | solution.py:145
  54.6 0.3 broadcast_in_dim.35
  55.0 0.4 reshape.121
  55.3 0.3 broadcast_in_dim.36
  55.7 0.4 reshape.122
  56.0 0.1 fusion
  56.3 1.6 %collective-permute-start.9 = (f32[4,8,2112]{2,1,0:T(8,128)S(1)}, f32[4,8,2112]{2,1,0:T(8,128)S(1)}, u32[]{:S(2)}, u32[]{:S(2)}) collective-permute-start(f32[4,8,2112]{2,1,0:T(8,128)S(1)} %get-tuple-element.150), channel_id=1, source_target_pairs={{0,2},{1,3},{2,0},{3,1},{4,6},{5,7},{6,4},{7,5},{8,10},{9,11},{10,... | collective-permute-start | bytes 811016 | tf_op jit(solution)/shard_map/ppermute | solution.py:17
  57.9 4.2 %shard_map.82.refs_0_ = bf16[512,2048]{1,0:T(8,128)(2,1)} custom-call(bf16[512,2048]{1,0:T(8,128)(2,1)} %query_ref.7, bf16[128,4096]{1,0:T(8,128)(2,1)} %bitcast.85, bf16[128,4096]{1,0:T(8,128)(2,1)} %bitcast.86, bf16[512,2048]{1,0:T(8,128)(2,1)} %shard_map.81.refs_0_), custom_call_target="tpu_custom_call", output_to_operand_aliasing={{}: (3, {})} | custom-call | flops 268435456 | bytes 1310720 | tf_op jit(solution)/shard_map/pallas_call | solution.py:145
  62.1 2.9 %collective-permute-done.9 = f32[4,8,2112]{2,1,0:T(8,128)S(1)} collective-permute-done((f32[4,8,2112]{2,1,0:T(8,128)S(1)}, f32[4,8,2112]{2,1,0:T(8,128)S(1)}, u32[]{:S(2)}, u32[]{:S(2)}) %collective-permute-start.9) | collective-permute-done | bytes 270368 | tf_op jit(solution)/shard_map/ppermute | solution.py:17
  65.0 0.2 broadcast_in_dim.37
  65.2 0.2 reshape.124
  65.4 0.2 broadcast_in_dim.38
  65.6 0.2 reshape.125
  66.0 0.5 collective-permute-start.10
  66.5 4.2 %shard_map.83.refs_0_ = bf16[512,2048]{1,0:T(8,128)(2,1)} custom-call(bf16[512,2048]{1,0:T(8,128)(2,1)} %query_ref.7, bf16[128,4096]{1,0:T(8,128)(2,1)} %bitcast.87, bf16[128,4096]{1,0:T(8,128)(2,1)} %bitcast.88, bf16[512,2048]{1,0:T(8,128)(2,1)} %shard_map.82.refs_0_), custom_call_target="tpu_custom_call", output_to_operand_aliasing={{}: (3, {})} | custom-call | flops 268435456 | bytes 1310720 | tf_op jit(solution)/shard_map/pallas_call | solution.py:145
  70.7 0.4 collective-permute-done.10
  71.2 0.1 broadcast_in_dim.39
  71.3 0.1 reshape.127
  71.4 0.1 broadcast_in_dim.40
  71.6 0.1 reshape.128
  71.8 2.1 %collective-permute-start.11 = (f32[1,8,2112]{2,1,0:T(8,128)S(1)}, f32[1,8,2112]{2,1,0:T(8,128)S(1)}, u32[]{:S(2)}, u32[]{:S(2)}) collective-permute-start(f32[1,8,2112]{2,1,0:T(8,128)S(1)} %get-tuple-element.158), channel_id=1, source_target_pairs={{0,8},{1,9},{2,10},{3,11},{4,12},{5,13},{6,14},{7,15},{8,0},{9,1},... | collective-permute-start | bytes 202760 | tf_op jit(solution)/shard_map/ppermute | solution.py:17
  73.9 4.2 %shard_map.84 = bf16[512,2048]{1,0:T(8,128)(2,1)} custom-call(bf16[512,2048]{1,0:T(8,128)(2,1)} %query_ref.7, bf16[128,4096]{1,0:T(8,128)(2,1)} %bitcast.89, bf16[128,4096]{1,0:T(8,128)(2,1)} %bitcast.90, bf16[512,2048]{1,0:T(8,128)(2,1)} %shard_map.83.refs_0_), custom_call_target="tpu_custom_call", output_to_operand_aliasing={{}: (3, {})} | custom-call | flops 268435456 | bytes 1310720 | tf_op jit(solution)/shard_map/pallas_call | solution.py:145
  78.2 0.1 broadcast_in_dim.43
  78.3 0.1 reshape.132
  78.8 0.6 fusion.5
  (56 shorter events, 1.8 us)
Async XLA Ops:
  0.6 6.6 %collective-permute-start = (bf16[1,8,2048]{2,1,0:T(8,128)(2,1)}, bf16[1,8,2048]{2,1,0:T(8,128)(2,1)S(1)}, u32[]{:S(2)}, u32[]{:S(2)}) collective-permute-start(bf16[1,8,2048]{2,1,0:T(8,128)(2,1)} %bitcast.113), channel_id=1, source_target_pairs={{0,8},{1,9},{2,10},{3,11},{4,12},{5,13},{6,14},{7,15},{8,0},{9,1},... | collective-permute-start | bytes 98312 | tf_op jit(solution)/shard_map/ppermute | solution.py:17
  8.0 9.6 %copy-start.6 = (bf16[8,2048]{1,0:T(8,128)(2,1)S(1)}, bf16[8,2048]{1,0:T(8,128)(2,1)}, u32[]{:S(2)}) copy-start(bf16[8,2048]{1,0:T(8,128)(2,1)} %param.11) | copy-start | bytes 98308
  8.0 9.6 %copy-start.7 = (bf16[8,2048]{1,0:T(8,128)(2,1)S(1)}, bf16[8,2048]{1,0:T(8,128)(2,1)}, u32[]{:S(2)}) copy-start(bf16[8,2048]{1,0:T(8,128)(2,1)} %param.10) | copy-start | bytes 98308
  8.0 4.3 %collective-permute-start.1 = (bf16[2,8,2048]{2,1,0:T(8,128)(2,1)S(1)}, bf16[2,8,2048]{2,1,0:T(8,128)(2,1)S(1)}, u32[]{:S(2)}, u32[]{:S(2)}) collective-permute-start(bf16[2,8,2048]{2,1,0:T(8,128)(2,1)S(1)} %maximum_bitcast_fusion.2), channel_id=1, source_target_pairs={{0,4},{1,5},{2,6},{3,7},{4,0},{5,1},{6,2},{7,3},{8,12},{9,13},{10,... | collective-permute-start | bytes 196616 | tf_op jit(solution)/shard_map/ppermute | solution.py:17
  12.4 5.0 %collective-permute-start.2 = (bf16[4,8,2048]{2,1,0:T(8,128)(2,1)S(1)}, bf16[4,8,2048]{2,1,0:T(8,128)(2,1)S(1)}, u32[]{:S(2)}, u32[]{:S(2)}) collective-permute-start(bf16[4,8,2048]{2,1,0:T(8,128)(2,1)S(1)} %bitcast.106), channel_id=1, source_target_pairs={{0,2},{1,3},{2,0},{3,1},{4,6},{5,7},{6,4},{7,5},{8,10},{9,11},{10,... | collective-permute-start | bytes 393224 | tf_op jit(solution)/shard_map/ppermute | solution.py:17
  17.5 1.6 %collective-permute-start.3 = (bf16[8,8,2048]{2,1,0:T(8,128)(2,1)S(1)}, bf16[8,8,2048]{2,1,0:T(8,128)(2,1)S(1)}, u32[]{:S(2)}, u32[]{:S(2)}) collective-permute-start(bf16[8,8,2048]{2,1,0:T(8,128)(2,1)S(1)} %bitcast.102), channel_id=1, source_target_pairs={{0,1},{1,0},{2,3},{3,2},{4,5},{5,4},{6,7},{7,6},{8,9},{9,8},{10,11... | collective-permute-start | bytes 786440 | tf_op jit(solution)/shard_map/ppermute | solution.py:17
  20.0 6.8 %collective-permute-start.4 = (bf16[1,8,4096]{2,1,0:T(8,128)(2,1)S(1)}, bf16[1,8,4096]{2,1,0:T(8,128)(2,1)S(1)}, u32[]{:S(2)}, u32[]{:S(2)}) collective-permute-start(bf16[1,8,4096]{2,1,0:T(8,128)(2,1)S(1)} %maximum_bitcast_fusion.1), channel_id=1, source_target_pairs={{0,8},{1,9},{2,10},{3,11},{4,12},{5,13},{6,14},{7,15},{8,0},{9,1},... | collective-permute-start | bytes 196616 | tf_op jit(solution)/shard_map/ppermute | solution.py:17
  26.9 6.1 %collective-permute-start.5 = (bf16[2,8,4096]{2,1,0:T(8,128)(2,1)S(1)}, bf16[2,8,4096]{2,1,0:T(8,128)(2,1)S(1)}, u32[]{:S(2)}, u32[]{:S(2)}) collective-permute-start(bf16[2,8,4096]{2,1,0:T(8,128)(2,1)S(1)} %maximum_bitcast_fusion), channel_id=1, source_target_pairs={{0,4},{1,5},{2,6},{3,7},{4,0},{5,1},{6,2},{7,3},{8,12},{9,13},{10,... | collective-permute-start | bytes 393224 | tf_op jit(solution)/shard_map/ppermute | solution.py:17
  33.1 7.9 %collective-permute-start.6 = (bf16[4,8,4096]{2,1,0:T(8,128)(2,1)S(1)}, bf16[4,8,4096]{2,1,0:T(8,128)(2,1)S(1)}, u32[]{:S(2)}, u32[]{:S(2)}) collective-permute-start(bf16[4,8,4096]{2,1,0:T(8,128)(2,1)S(1)} %bitcast.100), channel_id=1, source_target_pairs={{0,2},{1,3},{2,0},{3,1},{4,6},{5,7},{6,4},{7,5},{8,10},{9,11},{10,... | collective-permute-start | bytes 786440 | tf_op jit(solution)/shard_map/ppermute | solution.py:17
  41.1 4.4 %copy-start = (f32[128,8]{1,0:T(8,128)S(1)}, f32[128,8]{1,0:T(8,128)}, u32[]{:S(2)}) copy-start(f32[128,8]{1,0:T(8,128)} %get-tuple-element.139) | copy-start | bytes 12292
  41.1 4.4 %copy-start.1 = (f32[128,8]{1,0:T(8,128)S(1)}, f32[128,8]{1,0:T(8,128)}, u32[]{:S(2)}) copy-start(f32[128,8]{1,0:T(8,128)} %get-tuple-element.143) | copy-start | bytes 12292
  41.1 4.4 %copy-start.2 = (f32[128,8]{1,0:T(8,128)S(1)}, f32[128,8]{1,0:T(8,128)}, u32[]{:S(2)}) copy-start(f32[128,8]{1,0:T(8,128)} %get-tuple-element.140) | copy-start | bytes 12292
  41.1 4.4 %copy-start.3 = (f32[128,8]{1,0:T(8,128)S(1)}, f32[128,8]{1,0:T(8,128)}, u32[]{:S(2)}) copy-start(f32[128,8]{1,0:T(8,128)} %get-tuple-element.144) | copy-start | bytes 12292
  41.1 4.4 %copy-start.4 = (f32[128,8]{1,0:T(8,128)S(1)}, f32[128,8]{1,0:T(8,128)}, u32[]{:S(2)}) copy-start(f32[128,8]{1,0:T(8,128)} %get-tuple-element.141) | copy-start | bytes 12292
  41.1 4.4 %copy-start.5 = (f32[128,8]{1,0:T(8,128)S(1)}, f32[128,8]{1,0:T(8,128)}, u32[]{:S(2)}) copy-start(f32[128,8]{1,0:T(8,128)} %get-tuple-element.145) | copy-start | bytes 12292
  41.1 4.4 %collective-permute-start.7 = (bf16[8,8,4096]{2,1,0:T(8,128)(2,1)S(1)}, bf16[8,8,4096]{2,1,0:T(8,128)(2,1)S(1)}, u32[]{:S(2)}, u32[]{:S(2)}) collective-permute-start(bf16[8,8,4096]{2,1,0:T(8,128)(2,1)S(1)} %bitcast.97), channel_id=1, source_target_pairs={{0,1},{1,0},{2,3},{3,2},{4,5},{5,4},{6,7},{7,6},{8,9},{9,8},{10,11... | collective-permute-start | bytes 1572872 | tf_op jit(solution)/shard_map/ppermute | solution.py:17
  48.6 6.0 %collective-permute-start.8 = (f32[8,8,2112]{2,1,0:T(8,128)S(1)}, f32[8,8,2112]{2,1,0:T(8,128)S(1)}, u32[]{:S(2)}, u32[]{:S(2)}) collective-permute-start(f32[8,8,2112]{2,1,0:T(8,128)S(1)} %get-tuple-element.178), channel_id=1, source_target_pairs={{0,1},{1,0},{2,3},{3,2},{4,5},{5,4},{6,7},{7,6},{8,9},{9,8},{10,11... | collective-permute-start | bytes 1622024 | tf_op jit(solution)/shard_map/ppermute | solution.py:17
  56.3 8.7 %collective-permute-start.9 = (f32[4,8,2112]{2,1,0:T(8,128)S(1)}, f32[4,8,2112]{2,1,0:T(8,128)S(1)}, u32[]{:S(2)}, u32[]{:S(2)}) collective-permute-start(f32[4,8,2112]{2,1,0:T(8,128)S(1)} %get-tuple-element.150), channel_id=1, source_target_pairs={{0,2},{1,3},{2,0},{3,1},{4,6},{5,7},{6,4},{7,5},{8,10},{9,11},{10,... | collective-permute-start | bytes 811016 | tf_op jit(solution)/shard_map/ppermute | solution.py:17
  66.0 5.1 %collective-permute-start.10 = (f32[2,8,2112]{2,1,0:T(8,128)S(1)}, f32[2,8,2112]{2,1,0:T(8,128)S(1)}, u32[]{:S(2)}, u32[]{:S(2)}) collective-permute-start(f32[2,8,2112]{2,1,0:T(8,128)S(1)} %get-tuple-element.154), channel_id=1, source_target_pairs={{0,4},{1,5},{2,6},{3,7},{4,0},{5,1},{6,2},{7,3},{8,12},{9,13},{10,... | collective-permute-start | bytes 405512 | tf_op jit(solution)/shard_map/ppermute | solution.py:17
  71.8 6.3 %collective-permute-start.11 = (f32[1,8,2112]{2,1,0:T(8,128)S(1)}, f32[1,8,2112]{2,1,0:T(8,128)S(1)}, u32[]{:S(2)}, u32[]{:S(2)}) collective-permute-start(f32[1,8,2112]{2,1,0:T(8,128)S(1)} %get-tuple-element.158), channel_id=1, source_target_pairs={{0,8},{1,9},{2,10},{3,11},{4,12},{5,13},{6,14},{7,15},{8,0},{9,1},... | collective-permute-start | bytes 202760 | tf_op jit(solution)/shard_map/ppermute | solution.py:17

commit v7 on v5

--- a/solution.py
+++ b/solution.py
@@ -151,10 +151,30 @@
 
 def video_kernel(query_ref, key_ref, value_ref, *refs):
     out_ref = refs[-1]
-    summed, tops, counts = pair_attention(query_ref[...], key_ref[...], value_ref[...])
-    first = head_masks(summed.shape[0])
-    totals = jnp.where(first, counts[0], counts[1])
-    out_ref[...] = (summed / totals).astype(out_ref.dtype)
+    queries = query_ref[...]
+    key_rows = key_ref.shape[0]
+    scores = (
+        lax.dot_general(
+            split_pair(key_ref[...]), queries, (((1,), (1,)), ((), ())),
+            preferred_element_type=jnp.float32,
+        )
+        * 0.125
+    )
+    weights = []
+    counts = []
+    for half in range(2):
+        part = scores[half * key_rows : (half + 1) * key_rows]
+        highest = jnp.max(part, axis=0, keepdims=True)
+        exps = jnp.exp(part - highest)
+        counts.append(jnp.sum(exps, axis=0, keepdims=True))
+        weights.append(exps.astype(jnp.bfloat16))
+    summed = lax.dot_general(
+        split_pair(value_ref[...]), jnp.concatenate(weights, axis=0), (((0,), (0,)), ((), ())),
+        preferred_element_type=jnp.float32,
+    )
+    lane = lax.broadcasted_iota(jnp.int32, summed.shape, 0)
+    totals = jnp.where(lane < HEAD_DIM, counts[0], counts[1])
+    out_ref[...] = (summed / totals).T.astype(out_ref.dtype)
 
 
 def video_part(queries, keys, values, earlier, group, groups):

time: 77.9 us -> 78.2 us (level)
  no operation moved by 1% of the time
where the time goes in v7:
time: 78.2 us; the launch traced here: 77.4 us
  Pallas kernels  34.3 us (44%)
  waiting for transfers between devices  15.8 us (20%)
  starting transfers between devices  15.4 us (20%)
  local copies, waits for them, and re-layouts  6.73 us (9%)
  other arithmetic  4.2 us (5%)
  between operations  1.03 us (1%)
    pallas_call x4, Pallas kernels, video_part(): pl.pallas_call(video_kernel, grid=(pairs,), in_specs=specs, out_specs=pl....  17.2 us
    pallas_call x4, Pallas kernels, audio_partial(): pl.pallas_call(audio_kernel, grid=(heads // 2,), in_specs=[pl.BlockSpec((...  17.1 us
    ppermute x5, waiting for transfers between devices, gather_levels(): pieces[offset] = lax.ppermute(held, 'seq', pairs)  10.1 us
    ppermute x8, starting transfers between devices, exchange(): return lax.ppermute(value, 'seq', pairs)  8.03 us
    ppermute x5, starting transfers between devices, gather_levels(): pieces[offset] = lax.ppermute(held, 'seq', pairs)  7.34 us
    ppermute x8, waiting for transfers between devices, exchange(): return lax.ppermute(value, 'seq', pairs)  5.67 us
    reshape x9, local copies, waits for them, and re-layouts, spread(): return jnp.repeat(scales, HEAD_DIM, axis=1)  1.62 us
    broadcast_in_dim x9, local copies, waits for them, and re-layouts, spread(): return jnp.repeat(scales, HEAD_DIM, axis=1)  1.57 us
  transfers between devices with their start and end apart: 13, of which 9 were waited for; matrix products, arithmetic and copies ran while one was open for 3% of the time, Pallas kernels for 44%

profile of v7, /device:TPU:0, one launch (start us, length us, event | category | flops | bytes accessed | tf_op | source)
XLA Modules:
  0.0 77.4 jit_solution(8019876544389093457)
XLA Ops:
  0.6 4.1 %collective-permute-start.2 = (bf16[1,8,2048]{2,1,0:T(8,128)(2,1)}, bf16[1,8,2048]{2,1,0:T(8,128)(2,1)S(1)}, u32[]{:S(2)}, u32[]{:S(2)}) collective-permute-start(bf16[1,8,2048]{2,1,0:T(8,128)(2,1)} %bitcast.104), channel_id=1, source_target_pairs={{0,8},{1,9},{2,10},{3,11},{4,12},{5,13},{6,14},{7,15},{8,0},{9,1},... | collective-permute-start | bytes 98312 | tf_op jit(solution)/shard_map/ppermute | solution.py:65
  4.7 1.6 %collective-permute-start.1 = (bf16[1,8,2048]{2,1,0:T(8,128)(2,1)}, bf16[1,8,2048]{2,1,0:T(8,128)(2,1)S(1)}, u32[]{:S(2)}, u32[]{:S(2)}) collective-permute-start(bf16[1,8,2048]{2,1,0:T(8,128)(2,1)} %bitcast.105), channel_id=1, source_target_pairs={{0,4},{1,5},{2,6},{3,7},{4,0},{5,1},{6,2},{7,3},{8,12},{9,13},{10,... | collective-permute-start | bytes 98312 | tf_op jit(solution)/shard_map/ppermute | solution.py:65
  6.3 1.0 %collective-permute-done.2 = bf16[1,8,2048]{2,1,0:T(8,128)(2,1)S(1)} collective-permute-done((bf16[1,8,2048]{2,1,0:T(8,128)(2,1)}, bf16[1,8,2048]{2,1,0:T(8,128)(2,1)S(1)}, u32[]{:S(2)}, u32[]{:S(2)}) %collective-permute-start.2) | collective-permute-done | bytes 32800 | tf_op jit(solution)/shard_map/ppermute | solution.py:65
  7.3 1.6 %collective-permute-done.1 = bf16[1,8,2048]{2,1,0:T(8,128)(2,1)S(1)} collective-permute-done((bf16[1,8,2048]{2,1,0:T(8,128)(2,1)}, bf16[1,8,2048]{2,1,0:T(8,128)(2,1)S(1)}, u32[]{:S(2)}, u32[]{:S(2)}) %collective-permute-start.1) | collective-permute-done | bytes 32800 | tf_op jit(solution)/shard_map/ppermute | solution.py:65
  8.9 3.4 %collective-permute-done = bf16[1,8,2048]{2,1,0:T(8,128)(2,1)S(1)} collective-permute-done((bf16[1,8,2048]{2,1,0:T(8,128)(2,1)}, bf16[1,8,2048]{2,1,0:T(8,128)(2,1)S(1)}, u32[]{:S(2)}, u32[]{:S(2)}) %collective-permute-start) | collective-permute-done | bytes 32800 | tf_op jit(solution)/shard_map/ppermute | solution.py:65
  12.2 0.8 %select_bitcast_fusion.23 = (bf16[1,1,8,2048]{3,2,1,0:T(8,128)(2,1)S(1)}, bf16[1,1,8,2048]{3,2,1,0:T(8,128)(2,1)S(1)}, bf16[1,1,8,2048]{3,2,1,0:T(8,128)(2,1)S(1)}, bf16[1,1,8,2048]{3,2,1,0:T(8,128)(2,1)S(1)}) fusion(bf16[1,8,2048]{2,1,0:T(8,128)(2,1)S(1)} %collective-permute-done, bf16[1,8,2048]{2,1,0:T(8,128)(2,1)S(1)} %collective-permute-done.1, ...), kind=kLoop, calls=%fused_computation.50 | loop fusion | flops 196608 | bytes 262156 | tf_op jit(solution)/shard_map/stack | solution.py:73
  13.0 1.6 %collective-permute-start.3 = (bf16[4,8,2048]{2,1,0:T(8,128)(2,1)S(1)}, bf16[4,8,2048]{2,1,0:T(8,128)(2,1)S(1)}, u32[]{:S(2)}, u32[]{:S(2)}) collective-permute-start(bf16[4,8,2048]{2,1,0:T(8,128)(2,1)S(1)} %maximum_bitcast_fusion), channel_id=1, source_target_pairs={{0,2},{1,3},{2,0},{3,1},{4,6},{5,7},{6,4},{7,5},{8,10},{9,11},{10,... | collective-permute-start | bytes 393224 | tf_op jit(solution)/shard_map/ppermute | solution.py:65
  14.6 3.4 %collective-permute-done.3 = bf16[4,8,2048]{2,1,0:T(8,128)(2,1)S(1)} collective-permute-done((bf16[4,8,2048]{2,1,0:T(8,128)(2,1)S(1)}, bf16[4,8,2048]{2,1,0:T(8,128)(2,1)S(1)}, u32[]{:S(2)}, u32[]{:S(2)}) %collective-permute-start.3) | collective-permute-done | bytes 131104 | tf_op jit(solution)/shard_map/ppermute | solution.py:65
  18.2 0.8 %maximum_bitcast_fusion.2 = bf16[1,8,4096]{2,1,0:T(8,128)(2,1)S(1)} fusion(bf16[8,2048]{1,0:T(8,128)(2,1)} %param.11, bf16[8,2048]{1,0:T(8,128)(2,1)} %param.10), kind=kLoop, calls=%fused_computation.38 | loop fusion | flops 131072 | bytes 131072 | tf_op jit(solution)/shard_map/broadcast_in_dim | solution.py:23
  19.0 0.7 collective-permute-done.4
  19.9 0.8 %copy.19 = bf16[8,2,8,2048]{3,2,1,0:T(8,128)(2,1)} copy(bf16[8,2,8,2048]{3,2,0,1:T(8,128)(2,1)S(1)} %pad_maximum_fusion.1) | data formatting | bytes 1048576 | tf_op jit(solution)/shard_map/stack | solution.py:73
  20.7 4.2 %shard_map.77 = (f32[128,512]{1,0:T(8,128)}, f32[128,8]{1,0:T(8,128)}, f32[128,8]{1,0:T(8,128)}) custom-call(bf16[128,2048]{1,0:T(8,128)(2,1)} %bitcast.82, bf16[512,2048]{1,0:T(8,128)(2,1)} %key_ref.7, bf16[512,2048]{1,0:T(8,128)(2,1)} %value_ref.7), custom_call_target="tpu_custom_call" | custom-call | flops 268435456 | bytes 1441792 | tf_op jit(solution)/shard_map/pallas_call | solution.py:237
  24.9 0.9 %collective-permute-done.5 = bf16[1,8,4096]{2,1,0:T(8,128)(2,1)S(1)} collective-permute-done((bf16[1,8,4096]{2,1,0:T(8,128)(2,1)S(1)}, bf16[1,8,4096]{2,1,0:T(8,128)(2,1)S(1)}, u32[]{:S(2)}, u32[]{:S(2)}) %collective-permute-start.5) | collective-permute-done | bytes 65568 | tf_op jit(solution)/shard_map/ppermute | solution.py:17
  26.0 4.3 %shard_map.78 = (f32[128,512]{1,0:T(8,128)}, f32[128,8]{1,0:T(8,128)}, f32[128,8]{1,0:T(8,128)}) custom-call(bf16[128,2048]{1,0:T(8,128)(2,1)} %bitcast.83, bf16[512,2048]{1,0:T(8,128)(2,1)} %key_ref.7, bf16[512,2048]{1,0:T(8,128)(2,1)} %value_ref.7), custom_call_target="tpu_custom_call" | custom-call | flops 268435456 | bytes 1441792 | tf_op jit(solution)/shard_map/pallas_call | solution.py:237
  30.2 0.7 collective-permute-done.6
  31.0 1.6 %collective-permute-start.7 = (bf16[4,8,4096]{2,1,0:T(8,128)(2,1)S(1)}, bf16[4,8,4096]{2,1,0:T(8,128)(2,1)S(1)}, u32[]{:S(2)}, u32[]{:S(2)}) collective-permute-start(bf16[4,8,4096]{2,1,0:T(8,128)(2,1)S(1)} %bitcast.93), channel_id=1, source_target_pairs={{0,2},{1,3},{2,0},{3,1},{4,6},{5,7},{6,4},{7,5},{8,10},{9,11},{10,... | collective-permute-start | bytes 786440 | tf_op jit(solution)/shard_map/ppermute | solution.py:17
  32.6 4.2 %shard_map.79 = (f32[128,512]{1,0:T(8,128)}, f32[128,8]{1,0:T(8,128)}, f32[128,8]{1,0:T(8,128)}) custom-call(bf16[128,2048]{1,0:T(8,128)(2,1)} %bitcast.84, bf16[512,2048]{1,0:T(8,128)(2,1)} %key_ref.7, bf16[512,2048]{1,0:T(8,128)(2,1)} %value_ref.7), custom_call_target="tpu_custom_call" | custom-call | flops 268435456 | bytes 1441792 | tf_op jit(solution)/shard_map/pallas_call | solution.py:237
  36.8 1.3 %collective-permute-done.7 = bf16[4,8,4096]{2,1,0:T(8,128)(2,1)S(1)} collective-permute-done((bf16[4,8,4096]{2,1,0:T(8,128)(2,1)S(1)}, bf16[4,8,4096]{2,1,0:T(8,128)(2,1)S(1)}, u32[]{:S(2)}, u32[]{:S(2)}) %collective-permute-start.7) | collective-permute-done | bytes 262176 | tf_op jit(solution)/shard_map/ppermute | solution.py:17
  38.4 4.4 %shard_map.80 = (f32[128,512]{1,0:T(8,128)}, f32[128,8]{1,0:T(8,128)}, f32[128,8]{1,0:T(8,128)}) custom-call(bf16[128,2048]{1,0:T(8,128)(2,1)} %bitcast.85, bf16[512,2048]{1,0:T(8,128)(2,1)} %key_ref.7, bf16[512,2048]{1,0:T(8,128)(2,1)} %value_ref.7), custom_call_target="tpu_custom_call" | custom-call | flops 268435456 | bytes 1441792 | tf_op jit(solution)/shard_map/pallas_call | solution.py:237
  42.8 1.2 %concatenate.16 = f32[128,2112]{1,0:T(8,128)S(1)} concatenate(f32[128,512]{1,0:T(8,128)S(1)} %copy-done, f32[128,512]{1,0:T(8,128)S(1)} %copy-done.1, f32[128,512]{1,0:T(8,128)S(1)} %copy-done.2, f32[128,512]{1,0:T(8,128)} %get-tuple-element.78, f32[128,8]{1,0:T(8,128)S(1)} %copy-done.3, f32[128,8]{1,0:T(8,128)S(1)} %copy-done.5, f32[128,8]{1,0:T(8,128)S(1)} %copy-done.7, ...), dimensions={1} | concatenate | bytes 2162688 | tf_op jit(solution)/shard_map/concatenate | solution.py:277
  44.1 0.9 %select_bitcast_fusion.1 = (f32[64,2112]{1,0:T(8,128)S(1)}, f32[8,8,2112]{2,1,0:T(8,128)}) fusion(f32[8,2,8,2112]{3,2,1,0:T(8,128)S(1)} %bitcast.86, pred[]{:T(512)S(6)} %ne.19), kind=kLoop, calls=%fused_computation.2 | loop fusion | flops 270336 | bytes 2162689 | tf_op jit(solution)/shard_map/jit(_where)/select_n | solution.py:98
  45.0 0.5 collective-permute-start.9
  45.6 0.1 pad_maximum_fusion
  45.8 1.1 %fusion.14 = (bf16[128,2048]{1,0:T(8,128)(2,1)}, bf16[128,2048]{1,0:T(8,128)(2,1)}) fusion(bf16[128,4096]{1,0:T(8,128)(2,1)S(1)} %bitcast.87), kind=kLoop, calls=%fused_computation.71 | loop fusion | bytes 2097152 | tf_op jit(solution)/shard_map/slice | solution.py:276
  46.8 4.3 %shard_map.81.refs_0_ = bf16[512,2048]{1,0:T(8,128)(2,1)} custom-call(bf16[512,2048]{1,0:T(8,128)(2,1)} %query_ref.7, bf16[128,2048]{1,0:T(8,128)(2,1)} %get-tuple-element.120.key_ref, bf16[128,2048]{1,0:T(8,128)(2,1)} %get-tuple-element.119.value_ref), custom_call_target="tpu_custom_call" | custom-call | flops 268435456 | bytes 1310720 | tf_op jit(solution)/shard_map/pallas_call | solution.py:196
  51.2 0.3 broadcast_in_dim.35
  51.6 0.4 reshape.117
  51.9 0.3 broadcast_in_dim.36
  52.3 0.4 reshape.118
  52.6 0.1 fusion
  52.9 1.6 %collective-permute-start.10 = (f32[4,8,2112]{2,1,0:T(8,128)S(1)}, f32[4,8,2112]{2,1,0:T(8,128)S(1)}, u32[]{:S(2)}, u32[]{:S(2)}) collective-permute-start(f32[4,8,2112]{2,1,0:T(8,128)S(1)} %get-tuple-element.90), channel_id=1, source_target_pairs={{0,2},{1,3},{2,0},{3,1},{4,6},{5,7},{6,4},{7,5},{8,10},{9,11},{10,... | collective-permute-start | bytes 811016 | tf_op jit(solution)/shard_map/ppermute | solution.py:17
  54.5 4.3 %shard_map.82.refs_0_ = bf16[512,2048]{1,0:T(8,128)(2,1)} custom-call(bf16[512,2048]{1,0:T(8,128)(2,1)} %query_ref.7, bf16[128,2048]{1,0:T(8,128)(2,1)} %get-tuple-element.120.key_ref, bf16[128,2048]{1,0:T(8,128)(2,1)} %get-tuple-element.119.value_ref, bf16[512,2048]{1,0:T(8,128)(2,1)} %shard_map.81.refs_0_), custom_call_target="tpu_custom_call", output_to_operand_aliasing={{}: (3, {})} | custom-call | flops 268435456 | bytes 1310720 | tf_op jit(solution)/shard_map/pallas_call | solution.py:196
  58.8 2.8 %collective-permute-done.10 = f32[4,8,2112]{2,1,0:T(8,128)S(1)} collective-permute-done((f32[4,8,2112]{2,1,0:T(8,128)S(1)}, f32[4,8,2112]{2,1,0:T(8,128)S(1)}, u32[]{:S(2)}, u32[]{:S(2)}) %collective-permute-start.10) | collective-permute-done | bytes 270368 | tf_op jit(solution)/shard_map/ppermute | solution.py:17
  61.6 0.2 broadcast_in_dim.37
  61.8 0.2 reshape.120
  62.0 0.2 broadcast_in_dim.38
  62.2 0.2 reshape.121
  62.6 1.5 %collective-permute-start.11 = (f32[2,8,2112]{2,1,0:T(8,128)S(1)}, f32[2,8,2112]{2,1,0:T(8,128)S(1)}, u32[]{:S(2)}, u32[]{:S(2)}) collective-permute-start(f32[2,8,2112]{2,1,0:T(8,128)S(1)} %get-tuple-element.94), channel_id=1, source_target_pairs={{0,4},{1,5},{2,6},{3,7},{4,0},{5,1},{6,2},{7,3},{8,12},{9,13},{10,... | collective-permute-start | bytes 405512 | tf_op jit(solution)/shard_map/ppermute | solution.py:17
  64.0 4.3 %shard_map.83.refs_0_ = bf16[512,2048]{1,0:T(8,128)(2,1)} custom-call(bf16[512,2048]{1,0:T(8,128)(2,1)} %query_ref.7, bf16[128,2048]{1,0:T(8,128)(2,1)} %get-tuple-element.120.key_ref, bf16[128,2048]{1,0:T(8,128)(2,1)} %get-tuple-element.119.value_ref, bf16[512,2048]{1,0:T(8,128)(2,1)} %shard_map.82.refs_0_), custom_call_target="tpu_custom_call", output_to_operand_aliasing={{}: (3, {})} | custom-call | flops 268435456 | bytes 1310720 | tf_op jit(solution)/shard_map/pallas_call | solution.py:196
  68.4 0.1 broadcast_in_dim.39
  68.6 0.1 reshape.123
  68.7 0.1 broadcast_in_dim.40
  68.8 0.1 reshape.124
  69.1 2.7 %collective-permute-start.12 = (f32[1,8,2112]{2,1,0:T(8,128)S(1)}, f32[1,8,2112]{2,1,0:T(8,128)S(1)}, u32[]{:S(2)}, u32[]{:S(2)}) collective-permute-start(f32[1,8,2112]{2,1,0:T(8,128)S(1)} %get-tuple-element.98), channel_id=1, source_target_pairs={{0,8},{1,9},{2,10},{3,11},{4,12},{5,13},{6,14},{7,15},{8,0},{9,1},... | collective-permute-start | bytes 202760 | tf_op jit(solution)/shard_map/ppermute | solution.py:17
  71.8 4.3 %shard_map.84 = bf16[512,2048]{1,0:T(8,128)(2,1)} custom-call(bf16[512,2048]{1,0:T(8,128)(2,1)} %query_ref.7, bf16[128,2048]{1,0:T(8,128)(2,1)} %get-tuple-element.120.key_ref, bf16[128,2048]{1,0:T(8,128)(2,1)} %get-tuple-element.119.value_ref, bf16[512,2048]{1,0:T(8,128)(2,1)} %shard_map.83.refs_0_), custom_call_target="tpu_custom_call", output_to_operand_aliasing={{}: (3, {})} | custom-call | flops 268435456 | bytes 1310720 | tf_op jit(solution)/shard_map/pallas_call | solution.py:196
  76.2 0.1 broadcast_in_dim.43
  76.3 0.1 reshape.128
  76.8 0.6 fusion.5
  (57 shorter events, 1.9 us)
Async XLA Ops:
  0.6 6.7 %collective-permute-start.2 = (bf16[1,8,2048]{2,1,0:T(8,128)(2,1)}, bf16[1,8,2048]{2,1,0:T(8,128)(2,1)S(1)}, u32[]{:S(2)}, u32[]{:S(2)}) collective-permute-start(bf16[1,8,2048]{2,1,0:T(8,128)(2,1)} %bitcast.104), channel_id=1, source_target_pairs={{0,8},{1,9},{2,10},{3,11},{4,12},{5,13},{6,14},{7,15},{8,0},{9,1},... | collective-permute-start | bytes 98312 | tf_op jit(solution)/shard_map/ppermute | solution.py:65
  4.7 4.1 %collective-permute-start.1 = (bf16[1,8,2048]{2,1,0:T(8,128)(2,1)}, bf16[1,8,2048]{2,1,0:T(8,128)(2,1)S(1)}, u32[]{:S(2)}, u32[]{:S(2)}) collective-permute-start(bf16[1,8,2048]{2,1,0:T(8,128)(2,1)} %bitcast.105), channel_id=1, source_target_pairs={{0,4},{1,5},{2,6},{3,7},{4,0},{5,1},{6,2},{7,3},{8,12},{9,13},{10,... | collective-permute-start | bytes 98312 | tf_op jit(solution)/shard_map/ppermute | solution.py:65
  6.3 5.9 %collective-permute-start = (bf16[1,8,2048]{2,1,0:T(8,128)(2,1)}, bf16[1,8,2048]{2,1,0:T(8,128)(2,1)S(1)}, u32[]{:S(2)}, u32[]{:S(2)}) collective-permute-start(bf16[1,8,2048]{2,1,0:T(8,128)(2,1)} %bitcast.106), channel_id=1, source_target_pairs={{0,12},{1,13},{2,14},{3,15},{4,8},{5,9},{6,10},{7,11},{8,4},{9,5},... | collective-permute-start | bytes 98312 | tf_op jit(solution)/shard_map/ppermute | solution.py:65
  13.0 5.0 %collective-permute-start.3 = (bf16[4,8,2048]{2,1,0:T(8,128)(2,1)S(1)}, bf16[4,8,2048]{2,1,0:T(8,128)(2,1)S(1)}, u32[]{:S(2)}, u32[]{:S(2)}) collective-permute-start(bf16[4,8,2048]{2,1,0:T(8,128)(2,1)S(1)} %maximum_bitcast_fusion), channel_id=1, source_target_pairs={{0,2},{1,3},{2,0},{3,1},{4,6},{5,7},{6,4},{7,5},{8,10},{9,11},{10,... | collective-permute-start | bytes 393224 | tf_op jit(solution)/shard_map/ppermute | solution.py:65
  18.1 1.6 %collective-permute-start.4 = (bf16[8,8,2048]{2,1,0:T(8,128)(2,1)S(1)}, bf16[8,8,2048]{2,1,0:T(8,128)(2,1)S(1)}, u32[]{:S(2)}, u32[]{:S(2)}) collective-permute-start(bf16[8,8,2048]{2,1,0:T(8,128)(2,1)S(1)} %bitcast.92), channel_id=1, source_target_pairs={{0,1},{1,0},{2,3},{3,2},{4,5},{5,4},{6,7},{7,6},{8,9},{9,8},{10,11... | collective-permute-start | bytes 786440 | tf_op jit(solution)/shard_map/ppermute | solution.py:65
  20.7 5.2 %collective-permute-start.5 = (bf16[1,8,4096]{2,1,0:T(8,128)(2,1)S(1)}, bf16[1,8,4096]{2,1,0:T(8,128)(2,1)S(1)}, u32[]{:S(2)}, u32[]{:S(2)}) collective-permute-start(bf16[1,8,4096]{2,1,0:T(8,128)(2,1)S(1)} %maximum_bitcast_fusion.2), channel_id=1, source_target_pairs={{0,8},{1,9},{2,10},{3,11},{4,12},{5,13},{6,14},{7,15},{8,0},{9,1},... | collective-permute-start | bytes 196616 | tf_op jit(solution)/shard_map/ppermute | solution.py:17
  25.9 5.0 %collective-permute-start.6 = (bf16[2,8,4096]{2,1,0:T(8,128)(2,1)S(1)}, bf16[2,8,4096]{2,1,0:T(8,128)(2,1)S(1)}, u32[]{:S(2)}, u32[]{:S(2)}) collective-permute-start(bf16[2,8,4096]{2,1,0:T(8,128)(2,1)S(1)} %maximum_bitcast_fusion.1), channel_id=1, source_target_pairs={{0,4},{1,5},{2,6},{3,7},{4,0},{5,1},{6,2},{7,3},{8,12},{9,13},{10,... | collective-permute-start | bytes 393224 | tf_op jit(solution)/shard_map/ppermute | solution.py:17
  31.0 7.1 %collective-permute-start.7 = (bf16[4,8,4096]{2,1,0:T(8,128)(2,1)S(1)}, bf16[4,8,4096]{2,1,0:T(8,128)(2,1)S(1)}, u32[]{:S(2)}, u32[]{:S(2)}) collective-permute-start(bf16[4,8,4096]{2,1,0:T(8,128)(2,1)S(1)} %bitcast.93), channel_id=1, source_target_pairs={{0,2},{1,3},{2,0},{3,1},{4,6},{5,7},{6,4},{7,5},{8,10},{9,11},{10,... | collective-permute-start | bytes 786440 | tf_op jit(solution)/shard_map/ppermute | solution.py:17
  38.2 4.5 %collective-permute-start.8 = (bf16[8,8,4096]{2,1,0:T(8,128)(2,1)S(1)}, bf16[8,8,4096]{2,1,0:T(8,128)(2,1)S(1)}, u32[]{:S(2)}, u32[]{:S(2)}) collective-permute-start(bf16[8,8,4096]{2,1,0:T(8,128)(2,1)S(1)} %bitcast.89), channel_id=1, source_target_pairs={{0,1},{1,0},{2,3},{3,2},{4,5},{5,4},{6,7},{7,6},{8,9},{9,8},{10,11... | collective-permute-start | bytes 1572872 | tf_op jit(solution)/shard_map/ppermute | solution.py:17
  38.3 4.4 %copy-start = (f32[128,512]{1,0:T(8,128)S(1)}, f32[128,512]{1,0:T(8,128)}, u32[]{:S(2)}) copy-start(f32[128,512]{1,0:T(8,128)} %get-tuple-element.57) | copy-start | bytes 786436
  38.3 4.4 %copy-start.1 = (f32[128,512]{1,0:T(8,128)S(1)}, f32[128,512]{1,0:T(8,128)}, u32[]{:S(2)}) copy-start(f32[128,512]{1,0:T(8,128)} %get-tuple-element.64) | copy-start | bytes 786436
  38.3 4.4 %copy-start.2 = (f32[128,512]{1,0:T(8,128)S(1)}, f32[128,512]{1,0:T(8,128)}, u32[]{:S(2)}) copy-start(f32[128,512]{1,0:T(8,128)} %get-tuple-element.71) | copy-start | bytes 786436
  38.3 4.4 %copy-start.3 = (f32[128,8]{1,0:T(8,128)S(1)}, f32[128,8]{1,0:T(8,128)}, u32[]{:S(2)}) copy-start(f32[128,8]{1,0:T(8,128)} %get-tuple-element.79) | copy-start | bytes 12292
  38.4 4.4 %copy-start.4 = (f32[128,8]{1,0:T(8,128)S(1)}, f32[128,8]{1,0:T(8,128)}, u32[]{:S(2)}) copy-start(f32[128,8]{1,0:T(8,128)} %get-tuple-element.83) | copy-start | bytes 12292
  38.4 4.4 %copy-start.5 = (f32[128,8]{1,0:T(8,128)S(1)}, f32[128,8]{1,0:T(8,128)}, u32[]{:S(2)}) copy-start(f32[128,8]{1,0:T(8,128)} %get-tuple-element.80) | copy-start | bytes 12292
  38.4 4.4 %copy-start.6 = (f32[128,8]{1,0:T(8,128)S(1)}, f32[128,8]{1,0:T(8,128)}, u32[]{:S(2)}) copy-start(f32[128,8]{1,0:T(8,128)} %get-tuple-element.84) | copy-start | bytes 12292
  38.4 4.4 %copy-start.7 = (f32[128,8]{1,0:T(8,128)S(1)}, f32[128,8]{1,0:T(8,128)}, u32[]{:S(2)}) copy-start(f32[128,8]{1,0:T(8,128)} %get-tuple-element.81) | copy-start | bytes 12292
  38.4 4.4 %copy-start.8 = (f32[128,8]{1,0:T(8,128)S(1)}, f32[128,8]{1,0:T(8,128)}, u32[]{:S(2)}) copy-start(f32[128,8]{1,0:T(8,128)} %get-tuple-element.85) | copy-start | bytes 12292
  45.0 6.1 %collective-permute-start.9 = (f32[8,8,2112]{2,1,0:T(8,128)}, f32[8,8,2112]{2,1,0:T(8,128)S(1)}, u32[]{:S(2)}, u32[]{:S(2)}) collective-permute-start(f32[8,8,2112]{2,1,0:T(8,128)} %get-tuple-element.118), channel_id=1, source_target_pairs={{0,1},{1,0},{2,3},{3,2},{4,5},{5,4},{6,7},{7,6},{8,9},{9,8},{10,11... | collective-permute-start | bytes 1622024 | tf_op jit(solution)/shard_map/ppermute | solution.py:17
  52.9 8.7 %collective-permute-start.10 = (f32[4,8,2112]{2,1,0:T(8,128)S(1)}, f32[4,8,2112]{2,1,0:T(8,128)S(1)}, u32[]{:S(2)}, u32[]{:S(2)}) collective-permute-start(f32[4,8,2112]{2,1,0:T(8,128)S(1)} %get-tuple-element.90), channel_id=1, source_target_pairs={{0,2},{1,3},{2,0},{3,1},{4,6},{5,7},{6,4},{7,5},{8,10},{9,11},{10,... | collective-permute-start | bytes 811016 | tf_op jit(solution)/shard_map/ppermute | solution.py:17
  62.6 5.8 %collective-permute-start.11 = (f32[2,8,2112]{2,1,0:T(8,128)S(1)}, f32[2,8,2112]{2,1,0:T(8,128)S(1)}, u32[]{:S(2)}, u32[]{:S(2)}) collective-permute-start(f32[2,8,2112]{2,1,0:T(8,128)S(1)} %get-tuple-element.94), channel_id=1, source_target_pairs={{0,4},{1,5},{2,6},{3,7},{4,0},{5,1},{6,2},{7,3},{8,12},{9,13},{10,... | collective-permute-start | bytes 405512 | tf_op jit(solution)/shard_map/ppermute | solution.py:17
  69.1 7.0 %collective-permute-start.12 = (f32[1,8,2112]{2,1,0:T(8,128)S(1)}, f32[1,8,2112]{2,1,0:T(8,128)S(1)}, u32[]{:S(2)}, u32[]{:S(2)}) collective-permute-start(f32[1,8,2112]{2,1,0:T(8,128)S(1)} %get-tuple-element.98), channel_id=1, source_target_pairs={{0,8},{1,9},{2,10},{3,11},{4,12},{5,13},{6,14},{7,15},{8,0},{9,1},... | collective-permute-start | bytes 202760 | tf_op jit(solution)/shard_map/ppermute | solution.py:17

commit v8 on v5

--- a/solution.py
+++ b/solution.py
@@ -149,23 +149,49 @@
     return summed, tops, counts
 
 
+PER_STEP = 2
+
+
 def video_kernel(query_ref, key_ref, value_ref, *refs):
     out_ref = refs[-1]
-    summed, tops, counts = pair_attention(query_ref[...], key_ref[...], value_ref[...])
-    first = head_masks(summed.shape[0])
-    totals = jnp.where(first, counts[0], counts[1])
-    out_ref[...] = (summed / totals).astype(out_ref.dtype)
+    key_rows = key_ref.shape[0]
+    for sub in range(PER_STEP):
+        lanes = slice(sub * 2 * HEAD_DIM, (sub + 1) * 2 * HEAD_DIM)
+        queries = query_ref[:, lanes]
+        scores = (
+            lax.dot_general(
+                split_pair(key_ref[:, lanes]), queries, (((1,), (1,)), ((), ())),
+                preferred_element_type=jnp.float32,
+            )
+            * 0.125
+        )
+        weights = []
+        counts = []
+        for half in range(2):
+            part = scores[half * key_rows : (half + 1) * key_rows]
+            highest = jnp.max(part, axis=0, keepdims=True)
+            exps = jnp.exp(part - highest)
+            counts.append(jnp.sum(exps, axis=0, keepdims=True))
+            weights.append(exps.astype(jnp.bfloat16))
+        summed = lax.dot_general(
+            split_pair(value_ref[:, lanes]), jnp.concatenate(weights, axis=0),
+            (((0,), (0,)), ((), ())), preferred_element_type=jnp.float32,
+        )
+        lane = lax.broadcasted_iota(jnp.int32, summed.shape, 0)
+        totals = jnp.where(lane < HEAD_DIM, counts[0], counts[1])
+        out_ref[:, lanes] = (summed / totals).T.astype(out_ref.dtype)
 
 
 def video_part(queries, keys, values, earlier, group, groups):
     rows, width = queries.shape
     pairs = width // (2 * HEAD_DIM) // groups
-    first_pair = group * pairs
+    first_pair = group * pairs // PER_STEP
     key_rows = keys.shape[0]
+    lanes = 2 * HEAD_DIM * PER_STEP
     specs = [
-        pl.BlockSpec((rows, 2 * HEAD_DIM), lambda p: (0, p + first_pair)),
-        pl.BlockSpec((key_rows, 2 * HEAD_DIM), lambda p: (0, p + first_pair)),
-        pl.BlockSpec((key_rows, 2 * HEAD_DIM), lambda p: (0, p + first_pair)),
+        pl.BlockSpec((rows, lanes), lambda p: (0, p + first_pair)),
+        pl.BlockSpec((key_rows, lanes), lambda p: (0, p + first_pair)),
+        pl.BlockSpec((key_rows, lanes), lambda p: (0, p + first_pair)),
     ]
     operands = [queries, keys, values]
     aliases = {}
@@ -175,9 +201,9 @@
         aliases = {3: 0}
     return pl.pallas_call(
         video_kernel,
-        grid=(pairs,),
+        grid=(pairs // PER_STEP,),
         in_specs=specs,
-        out_specs=pl.BlockSpec((rows, 2 * HEAD_DIM), lambda p: (0, p + first_pair)),
+        out_specs=pl.BlockSpec((rows, lanes), lambda p: (0, p + first_pair)),
         out_shape=jax.ShapeDtypeStruct((rows, width), jnp.bfloat16),
         input_output_aliases=aliases,
         cost_estimate=pl.CostEstimate(
@@ -189,41 +215,46 @@
 
 
 def audio_kernel(query_ref, key_ref, value_ref, sum_ref, total_ref, top_ref):
-    pair = pl.program_id(0)
-
-    @pl.when(pair == 0)
+    step = pl.program_id(0)
+
+    @pl.when(step == 0)
     def _():
         total_ref[...] = jnp.zeros_like(total_ref)
         top_ref[...] = jnp.zeros_like(top_ref)
 
-    summed, tops, counts = pair_attention(query_ref[...], key_ref[...], value_ref[...])
     column = lax.broadcasted_iota(jnp.int32, total_ref.shape, 1)
     totals_now = total_ref[...]
     tops_now = top_ref[...]
-    for half in range(2):
-        here = column == 2 * pair + half
-        totals_now = jnp.where(here, counts[half], totals_now)
-        tops_now = jnp.where(here, tops[half], tops_now)
+    for sub in range(PER_STEP):
+        lanes = slice(sub * 2 * HEAD_DIM, (sub + 1) * 2 * HEAD_DIM)
+        summed, tops, counts = pair_attention(
+            query_ref[:, lanes], key_ref[:, lanes], value_ref[:, lanes]
+        )
+        for half in range(2):
+            here = column == 2 * (step * PER_STEP + sub) + half
+            totals_now = jnp.where(here, counts[half], totals_now)
+            tops_now = jnp.where(here, tops[half], tops_now)
+        sum_ref[:, lanes] = summed
     total_ref[...] = totals_now
     top_ref[...] = tops_now
-    sum_ref[...] = summed
 
 
 def audio_partial(queries, keys, values, group, groups):
     rows, width = queries.shape
     heads = width // HEAD_DIM // groups
-    first_pair = group * heads // 2
+    first_pair = group * heads // 2 // PER_STEP
+    lanes = 2 * HEAD_DIM * PER_STEP
     key_rows = keys.shape[0]
     return pl.pallas_call(
         audio_kernel,
-        grid=(heads // 2,),
+        grid=(heads // 2 // PER_STEP,),
         in_specs=[
-            pl.BlockSpec((rows, 2 * HEAD_DIM), lambda p: (0, p + first_pair)),
-            pl.BlockSpec((key_rows, 2 * HEAD_DIM), lambda p: (0, p + first_pair)),
-            pl.BlockSpec((key_rows, 2 * HEAD_DIM), lambda p: (0, p + first_pair)),
+            pl.BlockSpec((rows, lanes), lambda p: (0, p + first_pair)),
+            pl.BlockSpec((key_rows, lanes), lambda p: (0, p + first_pair)),
+            pl.BlockSpec((key_rows, lanes), lambda p: (0, p + first_pair)),
         ],
         out_specs=[
-            pl.BlockSpec((rows, 2 * HEAD_DIM), lambda p: (0, p)),
+            pl.BlockSpec((rows, lanes), lambda p: (0, p)),
             pl.BlockSpec((rows, heads), lambda p: (0, 0)),
             pl.BlockSpec((rows, heads), lambda p: (0, 0)),
         ],

time: 77.9 us -> 73.9 us (0.949)
  Pallas kernels: 33.9 us -> 27.7 us
  waiting for transfers between devices: 15.9 us -> 19.3 us
  starting transfers between devices: 15.4 us -> 14.5 us
    pallas_call x8, Pallas kernels: 33.9 us -> 27.7 us  [the longest x4 14.1 us: video_part(): pl.pallas_call(video_kernel, grid=(pairs // PER_STEP,), in_specs=specs, o...]
    ppermute x8, waiting for transfers between devices: 5.75 us -> 9.2 us  [exchange(): return lax.ppermute(value, 'seq', pairs)]
    ppermute x8, starting transfers between devices: 8.03 us -> 7.17 us  [exchange(): return lax.ppermute(value, 'seq', pairs)]
  transfers between devices with their start and end apart: 13 -> 13, of which waited for: 9 -> 11; matrix products, arithmetic and copies ran while one was open for 3% -> 3% of each run, Pallas kernels for 44% -> 38%
where the time goes in v8:
time: 73.9 us; the launch traced here: 73.4 us
  Pallas kernels  27.7 us (37%)
  waiting for transfers between devices  19.3 us (26%)
  starting transfers between devices  14.5 us (20%)
  local copies, waits for them, and re-layouts  6.73 us (9%)
  other arithmetic  4.2 us (6%)
  between operations  1.03 us (1%)
    pallas_call x4, Pallas kernels, video_part(): pl.pallas_call(video_kernel, grid=(pairs // PER_STEP,), in_specs=specs, o...  14.1 us
    pallas_call x4, Pallas kernels, audio_partial(): pl.pallas_call(audio_kernel, grid=(heads // 2 // PER_STEP,), in_specs=[pl...  13.5 us
    ppermute x5, waiting for transfers between devices, gather_levels(): pieces[offset] = lax.ppermute(held, 'seq', pairs)  10.1 us
    ppermute x8, waiting for transfers between devices, exchange(): return lax.ppermute(value, 'seq', pairs)  9.2 us
    ppermute x5, starting transfers between devices, gather_levels(): pieces[offset] = lax.ppermute(held, 'seq', pairs)  7.34 us
    ppermute x8, starting transfers between devices, exchange(): return lax.ppermute(value, 'seq', pairs)  7.17 us
    reshape x9, local copies, waits for them, and re-layouts, spread(): return jnp.repeat(scales, HEAD_DIM, axis=1)  1.62 us
    broadcast_in_dim x9, local copies, waits for them, and re-layouts, spread(): return jnp.repeat(scales, HEAD_DIM, axis=1)  1.57 us
  transfers between devices with their start and end apart: 13, of which 11 were waited for; matrix products, arithmetic and copies ran while one was open for 3% of the time, Pallas kernels for 38%

profile of v8, /device:TPU:0, one launch (start us, length us, event | category | flops | bytes accessed | tf_op | source)
XLA Modules:
  0.0 73.4 jit_solution(9336392658432690195)
XLA Ops:
  0.6 4.1 %collective-permute-start.2 = (bf16[1,8,2048]{2,1,0:T(8,128)(2,1)}, bf16[1,8,2048]{2,1,0:T(8,128)(2,1)S(1)}, u32[]{:S(2)}, u32[]{:S(2)}) collective-permute-start(bf16[1,8,2048]{2,1,0:T(8,128)(2,1)} %bitcast.104), channel_id=1, source_target_pairs={{0,8},{1,9},{2,10},{3,11},{4,12},{5,13},{6,14},{7,15},{8,0},{9,1},... | collective-permute-start | bytes 98312 | tf_op jit(solution)/shard_map/ppermute | solution.py:65
  4.7 1.6 %collective-permute-start.1 = (bf16[1,8,2048]{2,1,0:T(8,128)(2,1)}, bf16[1,8,2048]{2,1,0:T(8,128)(2,1)S(1)}, u32[]{:S(2)}, u32[]{:S(2)}) collective-permute-start(bf16[1,8,2048]{2,1,0:T(8,128)(2,1)} %bitcast.105), channel_id=1, source_target_pairs={{0,4},{1,5},{2,6},{3,7},{4,0},{5,1},{6,2},{7,3},{8,12},{9,13},{10,... | collective-permute-start | bytes 98312 | tf_op jit(solution)/shard_map/ppermute | solution.py:65
  6.3 1.0 %collective-permute-done.2 = bf16[1,8,2048]{2,1,0:T(8,128)(2,1)S(1)} collective-permute-done((bf16[1,8,2048]{2,1,0:T(8,128)(2,1)}, bf16[1,8,2048]{2,1,0:T(8,128)(2,1)S(1)}, u32[]{:S(2)}, u32[]{:S(2)}) %collective-permute-start.2) | collective-permute-done | bytes 32800 | tf_op jit(solution)/shard_map/ppermute | solution.py:65
  7.3 1.6 %collective-permute-done.1 = bf16[1,8,2048]{2,1,0:T(8,128)(2,1)S(1)} collective-permute-done((bf16[1,8,2048]{2,1,0:T(8,128)(2,1)}, bf16[1,8,2048]{2,1,0:T(8,128)(2,1)S(1)}, u32[]{:S(2)}, u32[]{:S(2)}) %collective-permute-start.1) | collective-permute-done | bytes 32800 | tf_op jit(solution)/shard_map/ppermute | solution.py:65
  8.9 3.4 %collective-permute-done = bf16[1,8,2048]{2,1,0:T(8,128)(2,1)S(1)} collective-permute-done((bf16[1,8,2048]{2,1,0:T(8,128)(2,1)}, bf16[1,8,2048]{2,1,0:T(8,128)(2,1)S(1)}, u32[]{:S(2)}, u32[]{:S(2)}) %collective-permute-start) | collective-permute-done | bytes 32800 | tf_op jit(solution)/shard_map/ppermute | solution.py:65
  12.2 0.8 %select_bitcast_fusion.23 = (bf16[1,1,8,2048]{3,2,1,0:T(8,128)(2,1)S(1)}, bf16[1,1,8,2048]{3,2,1,0:T(8,128)(2,1)S(1)}, bf16[1,1,8,2048]{3,2,1,0:T(8,128)(2,1)S(1)}, bf16[1,1,8,2048]{3,2,1,0:T(8,128)(2,1)S(1)}) fusion(bf16[1,8,2048]{2,1,0:T(8,128)(2,1)S(1)} %collective-permute-done, bf16[1,8,2048]{2,1,0:T(8,128)(2,1)S(1)} %collective-permute-done.1, ...), kind=kLoop, calls=%fused_computation.50 | loop fusion | flops 196608 | bytes 262156 | tf_op jit(solution)/shard_map/stack | solution.py:73
  13.0 1.6 %collective-permute-start.3 = (bf16[4,8,2048]{2,1,0:T(8,128)(2,1)S(1)}, bf16[4,8,2048]{2,1,0:T(8,128)(2,1)S(1)}, u32[]{:S(2)}, u32[]{:S(2)}) collective-permute-start(bf16[4,8,2048]{2,1,0:T(8,128)(2,1)S(1)} %maximum_bitcast_fusion), channel_id=1, source_target_pairs={{0,2},{1,3},{2,0},{3,1},{4,6},{5,7},{6,4},{7,5},{8,10},{9,11},{10,... | collective-permute-start | bytes 393224 | tf_op jit(solution)/shard_map/ppermute | solution.py:65
  14.6 3.4 %collective-permute-done.3 = bf16[4,8,2048]{2,1,0:T(8,128)(2,1)S(1)} collective-permute-done((bf16[4,8,2048]{2,1,0:T(8,128)(2,1)S(1)}, bf16[4,8,2048]{2,1,0:T(8,128)(2,1)S(1)}, u32[]{:S(2)}, u32[]{:S(2)}) %collective-permute-start.3) | collective-permute-done | bytes 131104 | tf_op jit(solution)/shard_map/ppermute | solution.py:65
  18.2 0.8 %maximum_bitcast_fusion.2 = bf16[1,8,4096]{2,1,0:T(8,128)(2,1)S(1)} fusion(bf16[8,2048]{1,0:T(8,128)(2,1)} %param.11, bf16[8,2048]{1,0:T(8,128)(2,1)} %param.10), kind=kLoop, calls=%fused_computation.38 | loop fusion | flops 131072 | bytes 131072 | tf_op jit(solution)/shard_map/broadcast_in_dim | solution.py:23
  19.0 0.7 %collective-permute-done.4 = bf16[8,8,2048]{2,1,0:T(8,128)(2,1)S(1)} collective-permute-done((bf16[8,8,2048]{2,1,0:T(8,128)(2,1)S(1)}, bf16[8,8,2048]{2,1,0:T(8,128)(2,1)S(1)}, u32[]{:S(2)}, u32[]{:S(2)}) %collective-permute-start.4) | collective-permute-done | bytes 262176 | tf_op jit(solution)/shard_map/ppermute | solution.py:65
  19.9 0.8 %copy.19 = bf16[8,2,8,2048]{3,2,1,0:T(8,128)(2,1)} copy(bf16[8,2,8,2048]{3,2,0,1:T(8,128)(2,1)S(1)} %pad_maximum_fusion.1) | data formatting | bytes 1048576 | tf_op jit(solution)/shard_map/stack | solution.py:73
  20.7 3.3 %shard_map.77 = (f32[128,512]{1,0:T(8,128)}, f32[128,8]{1,0:T(8,128)}, f32[128,8]{1,0:T(8,128)}) custom-call(bf16[128,2048]{1,0:T(8,128)(2,1)} %bitcast.82, bf16[512,2048]{1,0:T(8,128)(2,1)} %key_ref.7, bf16[512,2048]{1,0:T(8,128)(2,1)} %value_ref.7), custom_call_target="tpu_custom_call" | custom-call | flops 268435456 | bytes 1441792 | tf_op jit(solution)/shard_map/pallas_call | solution.py:248
  24.0 1.8 %collective-permute-done.5 = bf16[1,8,4096]{2,1,0:T(8,128)(2,1)S(1)} collective-permute-done((bf16[1,8,4096]{2,1,0:T(8,128)(2,1)S(1)}, bf16[1,8,4096]{2,1,0:T(8,128)(2,1)S(1)}, u32[]{:S(2)}, u32[]{:S(2)}) %collective-permute-start.5) | collective-permute-done | bytes 65568 | tf_op jit(solution)/shard_map/ppermute | solution.py:17
  26.0 3.4 %shard_map.78 = (f32[128,512]{1,0:T(8,128)}, f32[128,8]{1,0:T(8,128)}, f32[128,8]{1,0:T(8,128)}) custom-call(bf16[128,2048]{1,0:T(8,128)(2,1)} %bitcast.83, bf16[512,2048]{1,0:T(8,128)(2,1)} %key_ref.7, bf16[512,2048]{1,0:T(8,128)(2,1)} %value_ref.7), custom_call_target="tpu_custom_call" | custom-call | flops 268435456 | bytes 1441792 | tf_op jit(solution)/shard_map/pallas_call | solution.py:248
  29.4 1.6 %collective-permute-done.6 = bf16[2,8,4096]{2,1,0:T(8,128)(2,1)S(1)} collective-permute-done((bf16[2,8,4096]{2,1,0:T(8,128)(2,1)S(1)}, bf16[2,8,4096]{2,1,0:T(8,128)(2,1)S(1)}, u32[]{:S(2)}, u32[]{:S(2)}) %collective-permute-start.6) | collective-permute-done | bytes 131104 | tf_op jit(solution)/shard_map/ppermute | solution.py:17
  31.0 1.6 %collective-permute-start.7 = (bf16[4,8,4096]{2,1,0:T(8,128)(2,1)S(1)}, bf16[4,8,4096]{2,1,0:T(8,128)(2,1)S(1)}, u32[]{:S(2)}, u32[]{:S(2)}) collective-permute-start(bf16[4,8,4096]{2,1,0:T(8,128)(2,1)S(1)} %bitcast.93), channel_id=1, source_target_pairs={{0,2},{1,3},{2,0},{3,1},{4,6},{5,7},{6,4},{7,5},{8,10},{9,11},{10,... | collective-permute-start | bytes 786440 | tf_op jit(solution)/shard_map/ppermute | solution.py:17
  32.6 3.4 %shard_map.79 = (f32[128,512]{1,0:T(8,128)}, f32[128,8]{1,0:T(8,128)}, f32[128,8]{1,0:T(8,128)}) custom-call(bf16[128,2048]{1,0:T(8,128)(2,1)} %bitcast.84, bf16[512,2048]{1,0:T(8,128)(2,1)} %key_ref.7, bf16[512,2048]{1,0:T(8,128)(2,1)} %value_ref.7), custom_call_target="tpu_custom_call" | custom-call | flops 268435456 | bytes 1441792 | tf_op jit(solution)/shard_map/pallas_call | solution.py:248
  35.9 1.5 %collective-permute-done.7 = bf16[4,8,4096]{2,1,0:T(8,128)(2,1)S(1)} collective-permute-done((bf16[4,8,4096]{2,1,0:T(8,128)(2,1)S(1)}, bf16[4,8,4096]{2,1,0:T(8,128)(2,1)S(1)}, u32[]{:S(2)}, u32[]{:S(2)}) %collective-permute-start.7) | collective-permute-done | bytes 262176 | tf_op jit(solution)/shard_map/ppermute | solution.py:17
  37.7 3.5 %shard_map.80 = (f32[128,512]{1,0:T(8,128)}, f32[128,8]{1,0:T(8,128)}, f32[128,8]{1,0:T(8,128)}) custom-call(bf16[128,2048]{1,0:T(8,128)(2,1)} %bitcast.85, bf16[512,2048]{1,0:T(8,128)(2,1)} %key_ref.7, bf16[512,2048]{1,0:T(8,128)(2,1)} %value_ref.7), custom_call_target="tpu_custom_call" | custom-call | flops 268435456 | bytes 1441792 | tf_op jit(solution)/shard_map/pallas_call | solution.py:248
  41.3 1.2 %concatenate.16 = f32[128,2112]{1,0:T(8,128)S(1)} concatenate(f32[128,512]{1,0:T(8,128)S(1)} %copy-done, f32[128,512]{1,0:T(8,128)S(1)} %copy-done.1, f32[128,512]{1,0:T(8,128)S(1)} %copy-done.2, f32[128,512]{1,0:T(8,128)} %get-tuple-element.78, f32[128,8]{1,0:T(8,128)S(1)} %copy-done.3, f32[128,8]{1,0:T(8,128)S(1)} %copy-done.5, f32[128,8]{1,0:T(8,128)S(1)} %copy-done.7, ...), dimensions={1} | concatenate | bytes 2162688 | tf_op jit(solution)/shard_map/concatenate | solution.py:288
  42.5 0.9 %select_bitcast_fusion.1 = (f32[64,2112]{1,0:T(8,128)S(1)}, f32[8,8,2112]{2,1,0:T(8,128)}) fusion(f32[8,2,8,2112]{3,2,1,0:T(8,128)S(1)} %bitcast.86, pred[]{:T(512)S(6)} %ne.19), kind=kLoop, calls=%fused_computation.2 | loop fusion | flops 270336 | bytes 2162689 | tf_op jit(solution)/shard_map/jit(_where)/select_n | solution.py:98
  43.5 0.5 collective-permute-start.9
  44.2 1.1 %fusion.14 = (bf16[128,2048]{1,0:T(8,128)(2,1)}, bf16[128,2048]{1,0:T(8,128)(2,1)}) fusion(bf16[128,4096]{1,0:T(8,128)(2,1)S(1)} %bitcast.87), kind=kLoop, calls=%fused_computation.71 | loop fusion | bytes 2097152 | tf_op jit(solution)/shard_map/slice | solution.py:287
  45.3 3.5 %shard_map.81.refs_0_ = bf16[512,2048]{1,0:T(8,128)(2,1)} custom-call(bf16[512,2048]{1,0:T(8,128)(2,1)} %query_ref.7, bf16[128,2048]{1,0:T(8,128)(2,1)} %get-tuple-element.120.key_ref, bf16[128,2048]{1,0:T(8,128)(2,1)} %get-tuple-element.119.value_ref), custom_call_target="tpu_custom_call" | custom-call | flops 268435456 | bytes 1310720 | tf_op jit(solution)/shard_map/pallas_call | solution.py:202
  48.9 0.3 broadcast_in_dim.35
  49.3 0.4 reshape.117
  49.6 0.3 broadcast_in_dim.36
  50.0 0.4 reshape.118
  50.3 0.1 fusion
  50.6 1.6 %collective-permute-start.10 = (f32[4,8,2112]{2,1,0:T(8,128)S(1)}, f32[4,8,2112]{2,1,0:T(8,128)S(1)}, u32[]{:S(2)}, u32[]{:S(2)}) collective-permute-start(f32[4,8,2112]{2,1,0:T(8,128)S(1)} %get-tuple-element.90), channel_id=1, source_target_pairs={{0,2},{1,3},{2,0},{3,1},{4,6},{5,7},{6,4},{7,5},{8,10},{9,11},{10,... | collective-permute-start | bytes 811016 | tf_op jit(solution)/shard_map/ppermute | solution.py:17
  52.1 3.5 %shard_map.82.refs_0_ = bf16[512,2048]{1,0:T(8,128)(2,1)} custom-call(bf16[512,2048]{1,0:T(8,128)(2,1)} %query_ref.7, bf16[128,2048]{1,0:T(8,128)(2,1)} %get-tuple-element.120.key_ref, bf16[128,2048]{1,0:T(8,128)(2,1)} %get-tuple-element.119.value_ref, bf16[512,2048]{1,0:T(8,128)(2,1)} %shard_map.81.refs_0_), custom_call_target="tpu_custom_call", output_to_operand_aliasing={{}: (3, {})} | custom-call | flops 268435456 | bytes 1310720 | tf_op jit(solution)/shard_map/pallas_call | solution.py:202
  55.7 3.6 %collective-permute-done.10 = f32[4,8,2112]{2,1,0:T(8,128)S(1)} collective-permute-done((f32[4,8,2112]{2,1,0:T(8,128)S(1)}, f32[4,8,2112]{2,1,0:T(8,128)S(1)}, u32[]{:S(2)}, u32[]{:S(2)}) %collective-permute-start.10) | collective-permute-done | bytes 270368 | tf_op jit(solution)/shard_map/ppermute | solution.py:17
  59.3 0.2 broadcast_in_dim.37
  59.5 0.2 reshape.120
  59.7 0.2 broadcast_in_dim.38
  59.9 0.2 reshape.121
  60.3 1.0 %collective-permute-start.11 = (f32[2,8,2112]{2,1,0:T(8,128)S(1)}, f32[2,8,2112]{2,1,0:T(8,128)S(1)}, u32[]{:S(2)}, u32[]{:S(2)}) collective-permute-start(f32[2,8,2112]{2,1,0:T(8,128)S(1)} %get-tuple-element.94), channel_id=1, source_target_pairs={{0,4},{1,5},{2,6},{3,7},{4,0},{5,1},{6,2},{7,3},{8,12},{9,13},{10,... | collective-permute-start | bytes 405512 | tf_op jit(solution)/shard_map/ppermute | solution.py:17
  61.3 3.5 %shard_map.83.refs_0_ = bf16[512,2048]{1,0:T(8,128)(2,1)} custom-call(bf16[512,2048]{1,0:T(8,128)(2,1)} %query_ref.7, bf16[128,2048]{1,0:T(8,128)(2,1)} %get-tuple-element.120.key_ref, bf16[128,2048]{1,0:T(8,128)(2,1)} %get-tuple-element.119.value_ref, bf16[512,2048]{1,0:T(8,128)(2,1)} %shard_map.82.refs_0_), custom_call_target="tpu_custom_call", output_to_operand_aliasing={{}: (3, {})} | custom-call | flops 268435456 | bytes 1310720 | tf_op jit(solution)/shard_map/pallas_call | solution.py:202
  64.8 0.6 collective-permute-done.11
  65.5 0.1 broadcast_in_dim.39
  65.6 0.1 reshape.123
  65.7 0.1 broadcast_in_dim.40
  65.8 0.1 reshape.124
  66.1 2.3 %collective-permute-start.12 = (f32[1,8,2112]{2,1,0:T(8,128)S(1)}, f32[1,8,2112]{2,1,0:T(8,128)S(1)}, u32[]{:S(2)}, u32[]{:S(2)}) collective-permute-start(f32[1,8,2112]{2,1,0:T(8,128)S(1)} %get-tuple-element.98), channel_id=1, source_target_pairs={{0,8},{1,9},{2,10},{3,11},{4,12},{5,13},{6,14},{7,15},{8,0},{9,1},... | collective-permute-start | bytes 202760 | tf_op jit(solution)/shard_map/ppermute | solution.py:17
  68.4 3.5 %shard_map.84 = bf16[512,2048]{1,0:T(8,128)(2,1)} custom-call(bf16[512,2048]{1,0:T(8,128)(2,1)} %query_ref.7, bf16[128,2048]{1,0:T(8,128)(2,1)} %get-tuple-element.120.key_ref, bf16[128,2048]{1,0:T(8,128)(2,1)} %get-tuple-element.119.value_ref, bf16[512,2048]{1,0:T(8,128)(2,1)} %shard_map.83.refs_0_), custom_call_target="tpu_custom_call", output_to_operand_aliasing={{}: (3, {})} | custom-call | flops 268435456 | bytes 1310720 | tf_op jit(solution)/shard_map/pallas_call | solution.py:202
  71.9 0.2 collective-permute-done.12
  72.2 0.1 broadcast_in_dim.43
  72.8 0.6 fusion.5
  (57 shorter events, 2.1 us)
Async XLA Ops:
  0.6 6.7 %collective-permute-start.2 = (bf16[1,8,2048]{2,1,0:T(8,128)(2,1)}, bf16[1,8,2048]{2,1,0:T(8,128)(2,1)S(1)}, u32[]{:S(2)}, u32[]{:S(2)}) collective-permute-start(bf16[1,8,2048]{2,1,0:T(8,128)(2,1)} %bitcast.104), channel_id=1, source_target_pairs={{0,8},{1,9},{2,10},{3,11},{4,12},{5,13},{6,14},{7,15},{8,0},{9,1},... | collective-permute-start | bytes 98312 | tf_op jit(solution)/shard_map/ppermute | solution.py:65
  4.7 4.1 %collective-permute-start.1 = (bf16[1,8,2048]{2,1,0:T(8,128)(2,1)}, bf16[1,8,2048]{2,1,0:T(8,128)(2,1)S(1)}, u32[]{:S(2)}, u32[]{:S(2)}) collective-permute-start(bf16[1,8,2048]{2,1,0:T(8,128)(2,1)} %bitcast.105), channel_id=1, source_target_pairs={{0,4},{1,5},{2,6},{3,7},{4,0},{5,1},{6,2},{7,3},{8,12},{9,13},{10,... | collective-permute-start | bytes 98312 | tf_op jit(solution)/shard_map/ppermute | solution.py:65
  6.3 5.9 %collective-permute-start = (bf16[1,8,2048]{2,1,0:T(8,128)(2,1)}, bf16[1,8,2048]{2,1,0:T(8,128)(2,1)S(1)}, u32[]{:S(2)}, u32[]{:S(2)}) collective-permute-start(bf16[1,8,2048]{2,1,0:T(8,128)(2,1)} %bitcast.106), channel_id=1, source_target_pairs={{0,12},{1,13},{2,14},{3,15},{4,8},{5,9},{6,10},{7,11},{8,4},{9,5},... | collective-permute-start | bytes 98312 | tf_op jit(solution)/shard_map/ppermute | solution.py:65
  13.0 5.0 %collective-permute-start.3 = (bf16[4,8,2048]{2,1,0:T(8,128)(2,1)S(1)}, bf16[4,8,2048]{2,1,0:T(8,128)(2,1)S(1)}, u32[]{:S(2)}, u32[]{:S(2)}) collective-permute-start(bf16[4,8,2048]{2,1,0:T(8,128)(2,1)S(1)} %maximum_bitcast_fusion), channel_id=1, source_target_pairs={{0,2},{1,3},{2,0},{3,1},{4,6},{5,7},{6,4},{7,5},{8,10},{9,11},{10,... | collective-permute-start | bytes 393224 | tf_op jit(solution)/shard_map/ppermute | solution.py:65
  18.1 1.6 %collective-permute-start.4 = (bf16[8,8,2048]{2,1,0:T(8,128)(2,1)S(1)}, bf16[8,8,2048]{2,1,0:T(8,128)(2,1)S(1)}, u32[]{:S(2)}, u32[]{:S(2)}) collective-permute-start(bf16[8,8,2048]{2,1,0:T(8,128)(2,1)S(1)} %bitcast.92), channel_id=1, source_target_pairs={{0,1},{1,0},{2,3},{3,2},{4,5},{5,4},{6,7},{7,6},{8,9},{9,8},{10,11... | collective-permute-start | bytes 786440 | tf_op jit(solution)/shard_map/ppermute | solution.py:65
  20.7 5.2 %collective-permute-start.5 = (bf16[1,8,4096]{2,1,0:T(8,128)(2,1)S(1)}, bf16[1,8,4096]{2,1,0:T(8,128)(2,1)S(1)}, u32[]{:S(2)}, u32[]{:S(2)}) collective-permute-start(bf16[1,8,4096]{2,1,0:T(8,128)(2,1)S(1)} %maximum_bitcast_fusion.2), channel_id=1, source_target_pairs={{0,8},{1,9},{2,10},{3,11},{4,12},{5,13},{6,14},{7,15},{8,0},{9,1},... | collective-permute-start | bytes 196616 | tf_op jit(solution)/shard_map/ppermute | solution.py:17
  25.9 5.0 %collective-permute-start.6 = (bf16[2,8,4096]{2,1,0:T(8,128)(2,1)S(1)}, bf16[2,8,4096]{2,1,0:T(8,128)(2,1)S(1)}, u32[]{:S(2)}, u32[]{:S(2)}) collective-permute-start(bf16[2,8,4096]{2,1,0:T(8,128)(2,1)S(1)} %maximum_bitcast_fusion.1), channel_id=1, source_target_pairs={{0,4},{1,5},{2,6},{3,7},{4,0},{5,1},{6,2},{7,3},{8,12},{9,13},{10,... | collective-permute-start | bytes 393224 | tf_op jit(solution)/shard_map/ppermute | solution.py:17
  31.0 6.4 %collective-permute-start.7 = (bf16[4,8,4096]{2,1,0:T(8,128)(2,1)S(1)}, bf16[4,8,4096]{2,1,0:T(8,128)(2,1)S(1)}, u32[]{:S(2)}, u32[]{:S(2)}) collective-permute-start(bf16[4,8,4096]{2,1,0:T(8,128)(2,1)S(1)} %bitcast.93), channel_id=1, source_target_pairs={{0,2},{1,3},{2,0},{3,1},{4,6},{5,7},{6,4},{7,5},{8,10},{9,11},{10,... | collective-permute-start | bytes 786440 | tf_op jit(solution)/shard_map/ppermute | solution.py:17
  37.6 3.6 %collective-permute-start.8 = (bf16[8,8,4096]{2,1,0:T(8,128)(2,1)S(1)}, bf16[8,8,4096]{2,1,0:T(8,128)(2,1)S(1)}, u32[]{:S(2)}, u32[]{:S(2)}) collective-permute-start(bf16[8,8,4096]{2,1,0:T(8,128)(2,1)S(1)} %bitcast.89), channel_id=1, source_target_pairs={{0,1},{1,0},{2,3},{3,2},{4,5},{5,4},{6,7},{7,6},{8,9},{9,8},{10,11... | collective-permute-start | bytes 1572872 | tf_op jit(solution)/shard_map/ppermute | solution.py:17
  37.7 3.6 %copy-start = (f32[128,512]{1,0:T(8,128)S(1)}, f32[128,512]{1,0:T(8,128)}, u32[]{:S(2)}) copy-start(f32[128,512]{1,0:T(8,128)} %get-tuple-element.57) | copy-start | bytes 786436
  37.7 3.6 %copy-start.1 = (f32[128,512]{1,0:T(8,128)S(1)}, f32[128,512]{1,0:T(8,128)}, u32[]{:S(2)}) copy-start(f32[128,512]{1,0:T(8,128)} %get-tuple-element.64) | copy-start | bytes 786436
  37.7 3.6 %copy-start.2 = (f32[128,512]{1,0:T(8,128)S(1)}, f32[128,512]{1,0:T(8,128)}, u32[]{:S(2)}) copy-start(f32[128,512]{1,0:T(8,128)} %get-tuple-element.71) | copy-start | bytes 786436
  37.7 3.6 %copy-start.3 = (f32[128,8]{1,0:T(8,128)S(1)}, f32[128,8]{1,0:T(8,128)}, u32[]{:S(2)}) copy-start(f32[128,8]{1,0:T(8,128)} %get-tuple-element.79) | copy-start | bytes 12292
  37.7 3.6 %copy-start.4 = (f32[128,8]{1,0:T(8,128)S(1)}, f32[128,8]{1,0:T(8,128)}, u32[]{:S(2)}) copy-start(f32[128,8]{1,0:T(8,128)} %get-tuple-element.83) | copy-start | bytes 12292
  37.7 3.6 %copy-start.5 = (f32[128,8]{1,0:T(8,128)S(1)}, f32[128,8]{1,0:T(8,128)}, u32[]{:S(2)}) copy-start(f32[128,8]{1,0:T(8,128)} %get-tuple-element.80) | copy-start | bytes 12292
  37.7 3.6 %copy-start.6 = (f32[128,8]{1,0:T(8,128)S(1)}, f32[128,8]{1,0:T(8,128)}, u32[]{:S(2)}) copy-start(f32[128,8]{1,0:T(8,128)} %get-tuple-element.84) | copy-start | bytes 12292
  37.7 3.6 %copy-start.7 = (f32[128,8]{1,0:T(8,128)S(1)}, f32[128,8]{1,0:T(8,128)}, u32[]{:S(2)}) copy-start(f32[128,8]{1,0:T(8,128)} %get-tuple-element.81) | copy-start | bytes 12292
  37.7 3.6 %copy-start.8 = (f32[128,8]{1,0:T(8,128)S(1)}, f32[128,8]{1,0:T(8,128)}, u32[]{:S(2)}) copy-start(f32[128,8]{1,0:T(8,128)} %get-tuple-element.85) | copy-start | bytes 12292
  43.5 5.3 %collective-permute-start.9 = (f32[8,8,2112]{2,1,0:T(8,128)}, f32[8,8,2112]{2,1,0:T(8,128)S(1)}, u32[]{:S(2)}, u32[]{:S(2)}) collective-permute-start(f32[8,8,2112]{2,1,0:T(8,128)} %get-tuple-element.118), channel_id=1, source_target_pairs={{0,1},{1,0},{2,3},{3,2},{4,5},{5,4},{6,7},{7,6},{8,9},{9,8},{10,11... | collective-permute-start | bytes 1622024 | tf_op jit(solution)/shard_map/ppermute | solution.py:17
  50.6 8.7 %collective-permute-start.10 = (f32[4,8,2112]{2,1,0:T(8,128)S(1)}, f32[4,8,2112]{2,1,0:T(8,128)S(1)}, u32[]{:S(2)}, u32[]{:S(2)}) collective-permute-start(f32[4,8,2112]{2,1,0:T(8,128)S(1)} %get-tuple-element.90), channel_id=1, source_target_pairs={{0,2},{1,3},{2,0},{3,1},{4,6},{5,7},{6,4},{7,5},{8,10},{9,11},{10,... | collective-permute-start | bytes 811016 | tf_op jit(solution)/shard_map/ppermute | solution.py:17
  60.3 5.1 %collective-permute-start.11 = (f32[2,8,2112]{2,1,0:T(8,128)S(1)}, f32[2,8,2112]{2,1,0:T(8,128)S(1)}, u32[]{:S(2)}, u32[]{:S(2)}) collective-permute-start(f32[2,8,2112]{2,1,0:T(8,128)S(1)} %get-tuple-element.94), channel_id=1, source_target_pairs={{0,4},{1,5},{2,6},{3,7},{4,0},{5,1},{6,2},{7,3},{8,12},{9,13},{10,... | collective-permute-start | bytes 405512 | tf_op jit(solution)/shard_map/ppermute | solution.py:17
  66.1 6.0 %collective-permute-start.12 = (f32[1,8,2112]{2,1,0:T(8,128)S(1)}, f32[1,8,2112]{2,1,0:T(8,128)S(1)}, u32[]{:S(2)}, u32[]{:S(2)}) collective-permute-start(f32[1,8,2112]{2,1,0:T(8,128)S(1)} %get-tuple-element.98), channel_id=1, source_target_pairs={{0,8},{1,9},{2,10},{3,11},{4,12},{5,13},{6,14},{7,15},{8,0},{9,1},... | collective-permute-start | bytes 202760 | tf_op jit(solution)/shard_map/ppermute | solution.py:17

commit v9 on v8

--- a/solution.py
+++ b/solution.py
@@ -15,63 +15,6 @@
 def exchange(value, bit, count):
     pairs = [(source, source ^ bit) for source in range(count)]
     return lax.ppermute(value, "seq", pairs)
-
-
-def gather_rows(block, during=()):
-    count = lax.axis_size("seq")
-    me = lax.axis_index("seq")
-    held = block[None]
-    results = []
-    bit = count // 2
-    step = 0
-    while bit >= 1:
-        work = during[step] if step < len(during) else None
-        if work is not None:
-            held, ready = lax.optimization_barrier((held, work[1]))
-        arrived = exchange(held, bit, count)
-        if work is not None:
-            done = work[0](ready)
-            arrived, done = lax.optimization_barrier((arrived, done))
-            results.append(done)
-        upper = (me & bit) != 0
-        low = jnp.where(upper, arrived, held)
-        high = jnp.where(upper, held, arrived)
-        held = jnp.stack([low, high], axis=1).reshape((-1,) + block.shape)
-        bit //= 2
-        step += 1
-    return held.reshape((count * block.shape[0],) + block.shape[1:]), results
-
-
-def gather_levels(block):
-    count = lax.axis_size("seq")
-    me = lax.axis_index("seq")
-    held = block[None]
-    levels = []
-    bit = count // 2
-    if bit >= 2:
-        levels.append((bit, bit // 2))
-        bit //= 4
-    while bit >= 1:
-        levels.append((bit,))
-        bit //= 2
-    for level in levels:
-        mask = sum(level)
-        offsets = [0]
-        for b in level:
-            offsets = offsets + [o + b for o in offsets]
-        pieces = {0: held}
-        for offset in offsets[1:]:
-            pairs = [(source, source ^ offset) for source in range(count)]
-            pieces[offset] = lax.ppermute(held, "seq", pairs)
-        mine = me & mask
-        ordered = []
-        for target in sorted(offsets):
-            choice = pieces[0]
-            for offset in offsets[1:]:
-                choice = jnp.where((mine ^ offset) == target, pieces[offset], choice)
-            ordered.append(choice)
-        held = jnp.stack(ordered, axis=1).reshape((-1,) + block.shape)
-    return held.reshape((count * block.shape[0],) + block.shape[1:])
 
 
 def merge(first, second, heads):
@@ -182,18 +125,19 @@
         out_ref[:, lanes] = (summed / totals).T.astype(out_ref.dtype)
 
 
-def video_part(queries, keys, values, earlier, group, groups):
+def video_part(queries, gathered, earlier, group, groups):
     rows, width = queries.shape
     pairs = width // (2 * HEAD_DIM) // groups
     first_pair = group * pairs // PER_STEP
-    key_rows = keys.shape[0]
+    key_rows = gathered.shape[0]
+    blocks = width // (2 * HEAD_DIM * PER_STEP)
     lanes = 2 * HEAD_DIM * PER_STEP
     specs = [
         pl.BlockSpec((rows, lanes), lambda p: (0, p + first_pair)),
-        pl.BlockSpec((key_rows, lanes), lambda p: (0, p + first_pair)),
-        pl.BlockSpec((key_rows, lanes), lambda p: (0, p + first_pair)),
+        pl.BlockSpec((key_rows, lanes), lambda p: (0, p + first_pair + blocks)),
+        pl.BlockSpec((key_rows, lanes), lambda p: (0, p + first_pair + 2 * blocks)),
     ]
-    operands = [queries, keys, values]
+    operands = [queries, gathered, gathered]
     aliases = {}
     if earlier is not None:
         specs.append(pl.BlockSpec(memory_space=pl.ANY))
@@ -239,19 +183,19 @@
     top_ref[...] = tops_now
 
 
-def audio_partial(queries, keys, values, group, groups):
-    rows, width = queries.shape
-    heads = width // HEAD_DIM // groups
-    first_pair = group * heads // 2 // PER_STEP
+def audio_rows(packed, keys, values):
+    rows = packed.shape[0]
+    width = keys.shape[1]
+    heads = width // HEAD_DIM
+    key_rows = keys.shape[0]
     lanes = 2 * HEAD_DIM * PER_STEP
-    key_rows = keys.shape[0]
-    return pl.pallas_call(
+    summed, totals, tops = pl.pallas_call(
         audio_kernel,
         grid=(heads // 2 // PER_STEP,),
         in_specs=[
-            pl.BlockSpec((rows, lanes), lambda p: (0, p + first_pair)),
-            pl.BlockSpec((key_rows, lanes), lambda p: (0, p + first_pair)),
-            pl.BlockSpec((key_rows, lanes), lambda p: (0, p + first_pair)),
+            pl.BlockSpec((rows, lanes), lambda p: (0, p)),
+            pl.BlockSpec((key_rows, lanes), lambda p: (0, p)),
+            pl.BlockSpec((key_rows, lanes), lambda p: (0, p)),
         ],
         out_specs=[
             pl.BlockSpec((rows, lanes), lambda p: (0, p)),
@@ -259,38 +203,63 @@
             pl.BlockSpec((rows, heads), lambda p: (0, 0)),
         ],
         out_shape=[
-            jax.ShapeDtypeStruct((rows, heads * HEAD_DIM), jnp.float32),
+            jax.ShapeDtypeStruct((rows, width), jnp.float32),
             jax.ShapeDtypeStruct((rows, heads), jnp.float32),
             jax.ShapeDtypeStruct((rows, heads), jnp.float32),
         ],
         compiler_params=pltpu.CompilerParams(dimension_semantics=("arbitrary",)),
         cost_estimate=pl.CostEstimate(
-            flops=8 * rows * key_rows * width // groups,
+            flops=8 * rows * key_rows * width,
             transcendentals=rows * key_rows * heads,
-            bytes_accessed=(2 * rows * width + 4 * key_rows * width + 4 * rows * width) // groups,
+            bytes_accessed=2 * rows * width + 4 * key_rows * width + 4 * rows * width,
         ),
-    )(queries, keys, values)
+    )(packed, keys, values)
+    return jnp.concatenate([summed, totals, tops], axis=1)
+
+
+def fold(mine, other, bit):
+    upper = (lax.axis_index("seq") & bit) != 0
+    low = jnp.where(upper, other, mine)
+    high = jnp.where(upper, mine, other)
+    return jnp.stack([low, high], axis=1).reshape((-1,) + mine.shape[1:])
+
+
+def gather_with_audio(packed, keys, values):
+    count = lax.axis_size("seq")
+    rows = packed.shape[0]
+    held = packed[None]
+    pending = held
+    state = None
+    before = None
+    bit = count // 2
+    while bit >= 1:
+        held, pending = lax.optimization_barrier((held, pending))
+        arrived = exchange(held, bit, count)
+        computed = audio_rows(pending.reshape((-1, packed.shape[1])), keys, values)
+        arrived, computed = lax.optimization_barrier((arrived, computed))
+        computed = computed.reshape((-1, rows, computed.shape[1]))
+        state = computed if state is None else fold(state, computed, before)
+        held = fold(held, arrived, bit)
+        pending = arrived
+        before = bit
+        bit //= 2
+    computed = audio_rows(pending.reshape((-1, packed.shape[1])), keys, values)
+    state = fold(state, computed.reshape((-1, rows, computed.shape[1])), before)
+    return (
+        held.reshape((count * rows, packed.shape[1])),
+        state.reshape((count * rows, state.shape[2])),
+    )
 
 
 def local(video_q, video_k, video_v, audio_q, audio_k, audio_v):
     width = video_q.shape[1]
     heads = width // HEAD_DIM
     groups = 4
-    all_queries = gather_levels(audio_q)
-    audio_calls = [
-        (lambda q, g=g: audio_partial(q, video_k, video_v, g, groups), all_queries)
-        for g in range(groups)
-    ]
-    gathered, parts = gather_rows(jnp.concatenate([audio_k, audio_v], axis=1), audio_calls)
-    parts = parts + [call[0](all_queries) for call in audio_calls[len(parts) :]]
-    all_keys = gathered[:, :width]
-    all_values = gathered[:, width:]
-    state = jnp.concatenate(
-        [part[0] for part in parts] + [part[1] for part in parts] + [part[2] for part in parts],
-        axis=1,
+    gathered, state = gather_with_audio(
+        jnp.concatenate([audio_q, audio_k, audio_v], axis=1), video_k, video_v
     )
     video_calls = [
-        lambda earlier, g=g: video_part(video_q, all_keys, all_values, earlier, g, groups)
+        lambda earlier, g=g: video_part(video_q, gathered, earlier, g, groups)
         for g in range(groups)
     ]
     mine, video_out = scatter_rows(state, heads, video_calls)

time: 73.9 us -> 98.8 us (1.34)
  Pallas kernels: 27.7 us -> 56.2 us
  waiting for transfers between devices: 19.3 us -> 13.9 us
  local copies, waits for them, and re-layouts: 6.73 us -> 10.7 us
  starting transfers between devices: 14.5 us -> 10.8 us
    pallas_call x4 -> x5, Pallas kernels: 13.5 us -> 42.1 us  [audio_rows(): pl.pallas_call(audio_kernel, grid=(heads // 2 // PER_STEP,), in_specs=[pl...]
    ppermute x5 -> x0, waiting for transfers between devices: 10.1 us -> none  [gather_levels(): pieces[offset] = lax.ppermute(held, 'seq', pairs)]
    ppermute x5 -> x0, starting transfers between devices: 7.34 us -> none  [gather_levels(): pieces[offset] = lax.ppermute(held, 'seq', pairs)]
    ppermute x8, waiting for transfers between devices: 9.2 us -> 13.9 us  [exchange(): return lax.ppermute(value, 'seq', pairs)]
    ppermute x8, starting transfers between devices: 7.17 us -> 10.8 us  [exchange(): return lax.ppermute(value, 'seq', pairs)]
    concatenate x1 -> x5, local copies, waits for them, and re-layouts: 1.24 us -> 4 us  [audio_rows(): return jnp.concatenate([summed, totals, tops], axis=1)]
    unnamed x18 -> x16, local copies, waits for them, and re-layouts: 0.04 us -> 1.86 us
    another operation x12 -> x10, other arithmetic: 1.27 us -> 2.61 us  [fold(): return jnp.stack([low, high], axis=1).reshape((-1,) + mine.shape[1:])]
  transfers between devices with their start and end apart: 13 -> 8, of which waited for: 11 -> 4; matrix products, arithmetic and copies ran while one was open for 3% -> 4% of each run, Pallas kernels for 38% -> 40%
where the time goes in v9:
time: 98.8 us; the launch traced here: 97.5 us
  Pallas kernels  56.2 us (57%)
  waiting for transfers between devices  13.9 us (14%)
  starting transfers between devices  10.8 us (11%)
  local copies, waits for them, and re-layouts  10.7 us (11%)
  other arithmetic  4.86 us (5%)
    pallas_call x5, Pallas kernels, audio_rows(): pl.pallas_call(audio_kernel, grid=(heads // 2 // PER_STEP,), in_specs=[pl...  42.1 us
    pallas_call x4, Pallas kernels, video_part(): pl.pallas_call(video_kernel, grid=(pairs // PER_STEP,), in_specs=specs, o...  14.2 us
    ppermute x8, waiting for transfers between devices, exchange(): return lax.ppermute(value, 'seq', pairs)  13.9 us
    ppermute x8, starting transfers between devices, exchange(): return lax.ppermute(value, 'seq', pairs)  10.8 us
    concatenate x5, local copies, waits for them, and re-layouts, audio_rows(): return jnp.concatenate([summed, totals, tops], axis=1)  4 us
    another operation x10, other arithmetic, fold(): return jnp.stack([low, high], axis=1).reshape((-1,) + mine.shape[1:])  2.61 us
  transfers between devices with their start and end apart: 8, of which 4 were waited for; matrix products, arithmetic and copies ran while one was open for 4% of the time, Pallas kernels for 40%

profile of v9, /device:TPU:0, one launch (start us, length us, event | category | flops | bytes accessed | tf_op | source)
XLA Modules:
  0.0 97.5 jit_solution(7334096017867656121)
XLA Ops:
  0.6 0.8 maximum_bitcast_fusion.2
  1.4 4.1 %collective-permute-start = (bf16[1,8,6144]{2,1,0:T(8,128)(2,1)S(1)}, bf16[1,8,6144]{2,1,0:T(8,128)(2,1)S(1)}, u32[]{:S(2)}, u32[]{:S(2)}) collective-permute-start(bf16[1,8,6144]{2,1,0:T(8,128)(2,1)S(1)} %maximum_bitcast_fusion.2), channel_id=1, source_target_pairs={{0,8},{1,9},{2,10},{3,11},{4,12},{5,13},{6,14},{7,15},{8,0},{9,1},... | collective-permute-start | bytes 294920 | tf_op jit(solution)/shard_map/ppermute | solution.py:17
  5.5 8.2 %shard_map.77 = (f32[8,2048]{1,0:T(8,128)}, f32[8,32]{1,0:T(8,128)}, f32[8,32]{1,0:T(8,128)}) custom-call(bf16[8,6144]{1,0:T(8,128)(2,1)} %bitcast.122, bf16[512,2048]{1,0:T(8,128)(2,1)} %key_ref.9, bf16[512,2048]{1,0:T(8,128)(2,1)} %value_ref.9), custom_call_target="tpu_custom_call" | custom-call | flops 67108864 | bytes 4292608 | tf_op jit(solution)/shard_map/pallas_call | solution.py:192
  13.8 0.9 concatenate.28
  14.7 0.9 select_bitcast_fusion.11
  15.7 1.6 %collective-permute-start.1 = (bf16[2,8,6144]{2,1,0:T(8,128)(2,1)S(1)}, bf16[2,8,6144]{2,1,0:T(8,128)(2,1)S(1)}, u32[]{:S(2)}, u32[]{:S(2)}) collective-permute-start(bf16[2,8,6144]{2,1,0:T(8,128)(2,1)S(1)} %maximum_bitcast_fusion), channel_id=1, source_target_pairs={{0,4},{1,5},{2,6},{3,7},{4,0},{5,1},{6,2},{7,3},{8,12},{9,13},{10,... | collective-permute-start | bytes 589832 | tf_op jit(solution)/shard_map/ppermute | solution.py:17
  17.3 8.2 %shard_map.78 = (f32[8,2048]{1,0:T(8,128)}, f32[8,32]{1,0:T(8,128)}, f32[8,32]{1,0:T(8,128)}) custom-call(bf16[8,6144]{1,0:T(8,128)(2,1)} %bitcast.127, bf16[512,2048]{1,0:T(8,128)(2,1)} %key_ref.9, bf16[512,2048]{1,0:T(8,128)(2,1)} %value_ref.9), custom_call_target="tpu_custom_call" | custom-call | flops 67108864 | bytes 4292608 | tf_op jit(solution)/shard_map/pallas_call | solution.py:192
  25.5 0.9 concatenate.29
  26.6 0.6 copy-done.3
  27.2 8.3 %shard_map.79 = (f32[16,2048]{1,0:T(8,128)}, f32[16,32]{1,0:T(8,128)}, f32[16,32]{1,0:T(8,128)}) custom-call(bf16[16,6144]{1,0:T(8,128)(2,1)} %bitcast.123, bf16[512,2048]{1,0:T(8,128)(2,1)} %key_ref.9, bf16[512,2048]{1,0:T(8,128)(2,1)} %value_ref.9), custom_call_target="tpu_custom_call" | custom-call | flops 134217728 | bytes 4390912 | tf_op jit(solution)/shard_map/pallas_call | solution.py:192
  35.5 1.5 %collective-permute-start.2 = (bf16[4,8,6144]{2,1,0:T(8,128)(2,1)S(1)}, bf16[4,8,6144]{2,1,0:T(8,128)(2,1)S(1)}, u32[]{:S(2)}, u32[]{:S(2)}) collective-permute-start(bf16[4,8,6144]{2,1,0:T(8,128)(2,1)S(1)} %bitcast.119), channel_id=1, source_target_pairs={{0,2},{1,3},{2,0},{3,1},{4,6},{5,7},{6,4},{7,5},{8,10},{9,11},{10,... | collective-permute-start | bytes 1179656 | tf_op jit(solution)/shard_map/ppermute | solution.py:17
  37.0 1.0 %concatenate.30 = f32[16,2112]{1,0:T(8,128)S(1)} concatenate(f32[16,2048]{1,0:T(8,128)} %get-tuple-element.61, f32[16,32]{1,0:T(8,128)} %get-tuple-element.62, f32[16,32]{1,0:T(8,128)} %get-tuple-element.63), dimensions={1} | concatenate | bytes 270336 | tf_op jit(solution)/shard_map/concatenate | solution.py:217
  38.0 7.8 %collective-permute-done.2 = bf16[4,8,6144]{2,1,0:T(8,128)(2,1)S(1)} collective-permute-done((bf16[4,8,6144]{2,1,0:T(8,128)(2,1)S(1)}, bf16[4,8,6144]{2,1,0:T(8,128)(2,1)S(1)}, u32[]{:S(2)}, u32[]{:S(2)}) %collective-permute-start.2) | collective-permute-done | bytes 393248 | tf_op jit(solution)/shard_map/ppermute | solution.py:17
  46.0 0.5 copy-done.1
  46.6 8.5 %shard_map.80 = (f32[32,2048]{1,0:T(8,128)}, f32[32,32]{1,0:T(8,128)}, f32[32,32]{1,0:T(8,128)}) custom-call(bf16[32,6144]{1,0:T(8,128)(2,1)} %bitcast.118, bf16[512,2048]{1,0:T(8,128)(2,1)} %key_ref.9, bf16[512,2048]{1,0:T(8,128)(2,1)} %value_ref.9), custom_call_target="tpu_custom_call" | custom-call | flops 268435456 | bytes 4587520 | tf_op jit(solution)/shard_map/pallas_call | solution.py:192
  55.1 1.0 %concatenate.31 = f32[32,2112]{1,0:T(8,128)S(1)} concatenate(f32[32,2048]{1,0:T(8,128)} %get-tuple-element.67, f32[32,32]{1,0:T(8,128)} %get-tuple-element.68, f32[32,32]{1,0:T(8,128)} %get-tuple-element.69), dimensions={1} | concatenate | bytes 540672 | tf_op jit(solution)/shard_map/concatenate | solution.py:217
  56.3 0.7 copy-done
  57.0 8.8 %shard_map.81 = (f32[64,2048]{1,0:T(8,128)}, f32[64,32]{1,0:T(8,128)}, f32[64,32]{1,0:T(8,128)}) custom-call(bf16[64,6144]{1,0:T(8,128)(2,1)} %bitcast.114, bf16[512,2048]{1,0:T(8,128)(2,1)} %key_ref.9, bf16[512,2048]{1,0:T(8,128)(2,1)} %value_ref.9), custom_call_target="tpu_custom_call" | custom-call | flops 536870912 | bytes 4980736 | tf_op jit(solution)/shard_map/pallas_call | solution.py:192
  65.9 1.2 %select_bitcast_fusion.1 = (bf16[8,1,8,6144]{3,2,0,1:T(8,128)(2,1)S(1)}, bf16[8,1,8,6144]{3,2,0,1:T(8,128)(2,1)S(1)}) fusion(bf16[8,8,6144]{2,1,0:T(8,128)(2,1)} %copy-done, bf16[8,8,6144]{2,1,0:T(8,128)(2,1)S(1)} %bitcast.116, pred[]{:T(512)S(6)} %ne.11), kind=kLoop, calls=%fused_computation.3 | loop fusion | flops 786432 | bytes 3145729 | tf_op jit(solution)/shard_map/stack | solution.py:224
  67.1 0.1 pad_maximum_fusion
  67.3 1.3 %copy.28 = bf16[8,2,8,6144]{3,2,1,0:T(8,128)(2,1)} copy(bf16[8,2,8,6144]{3,2,0,1:T(8,128)(2,1)S(1)} %pad_maximum_fusion) | data formatting | bytes 3145728 | tf_op jit(solution)/shard_map/stack | solution.py:224
  68.7 0.6 collective-permute-start.4
  69.3 3.5 %shard_map.82.refs_0_ = bf16[512,2048]{1,0:T(8,128)(2,1)} custom-call(bf16[512,2048]{1,0:T(8,128)(2,1)} %query_ref.7, bf16[128,6144]{1,0:T(8,128)(2,1)} %bitcast.106, bf16[128,6144]{1,0:T(8,128)(2,1)} %bitcast.107), custom_call_target="tpu_custom_call" | custom-call | flops 268435456 | bytes 1310720 | tf_op jit(solution)/shard_map/pallas_call | solution.py:146
  73.0 0.3 broadcast_in_dim.31
  73.4 0.4 reshape.225
  73.7 0.3 broadcast_in_dim.32
  74.1 0.4 reshape.226
  74.4 0.1 fusion.2
  74.7 1.6 %collective-permute-start.5 = (f32[4,8,2112]{2,1,0:T(8,128)S(1)}, f32[4,8,2112]{2,1,0:T(8,128)S(1)}, u32[]{:S(2)}, u32[]{:S(2)}) collective-permute-start(f32[4,8,2112]{2,1,0:T(8,128)S(1)} %get-tuple-element.80), channel_id=1, source_target_pairs={{0,2},{1,3},{2,0},{3,1},{4,6},{5,7},{6,4},{7,5},{8,10},{9,11},{10,... | collective-permute-start | bytes 811016 | tf_op jit(solution)/shard_map/ppermute | solution.py:17
  76.2 3.5 %shard_map.83.refs_0_ = bf16[512,2048]{1,0:T(8,128)(2,1)} custom-call(bf16[512,2048]{1,0:T(8,128)(2,1)} %query_ref.7, bf16[128,6144]{1,0:T(8,128)(2,1)} %bitcast.108, bf16[128,6144]{1,0:T(8,128)(2,1)} %bitcast.109, bf16[512,2048]{1,0:T(8,128)(2,1)} %shard_map.82.refs_0_), custom_call_target="tpu_custom_call", output_to_operand_aliasing={{}: (3, {})} | custom-call | flops 268435456 | bytes 1310720 | tf_op jit(solution)/shard_map/pallas_call | solution.py:146
  79.8 3.5 %collective-permute-done.5 = f32[4,8,2112]{2,1,0:T(8,128)S(1)} collective-permute-done((f32[4,8,2112]{2,1,0:T(8,128)S(1)}, f32[4,8,2112]{2,1,0:T(8,128)S(1)}, u32[]{:S(2)}, u32[]{:S(2)}) %collective-permute-start.5) | collective-permute-done | bytes 270368 | tf_op jit(solution)/shard_map/ppermute | solution.py:17
  83.4 0.2 broadcast_in_dim.33
  83.6 0.2 reshape.228
  83.8 0.2 broadcast_in_dim.34
  84.0 0.2 reshape.229
  84.4 0.5 collective-permute-start.6
  84.9 3.5 %shard_map.84.refs_0_ = bf16[512,2048]{1,0:T(8,128)(2,1)} custom-call(bf16[512,2048]{1,0:T(8,128)(2,1)} %query_ref.7, bf16[128,6144]{1,0:T(8,128)(2,1)} %bitcast.110, bf16[128,6144]{1,0:T(8,128)(2,1)} %bitcast.111, bf16[512,2048]{1,0:T(8,128)(2,1)} %shard_map.83.refs_0_), custom_call_target="tpu_custom_call", output_to_operand_aliasing={{}: (3, {})} | custom-call | flops 268435456 | bytes 1310720 | tf_op jit(solution)/shard_map/pallas_call | solution.py:146
  88.4 1.1 %collective-permute-done.6 = f32[2,8,2112]{2,1,0:T(8,128)S(1)} collective-permute-done((f32[2,8,2112]{2,1,0:T(8,128)S(1)}, f32[2,8,2112]{2,1,0:T(8,128)S(1)}, u32[]{:S(2)}, u32[]{:S(2)}) %collective-permute-start.6) | collective-permute-done | bytes 135200 | tf_op jit(solution)/shard_map/ppermute | solution.py:17
  89.6 0.1 broadcast_in_dim.35
  89.7 0.1 reshape.231
  89.8 0.1 broadcast_in_dim.36
  89.9 0.1 reshape.232
  90.2 0.9 collective-permute-start.7
  91.1 3.5 %shard_map.85 = bf16[512,2048]{1,0:T(8,128)(2,1)} custom-call(bf16[512,2048]{1,0:T(8,128)(2,1)} %query_ref.7, bf16[128,6144]{1,0:T(8,128)(2,1)} %bitcast.112, bf16[128,6144]{1,0:T(8,128)(2,1)} %bitcast.113, bf16[512,2048]{1,0:T(8,128)(2,1)} %shard_map.84.refs_0_), custom_call_target="tpu_custom_call", output_to_operand_aliasing={{}: (3, {})} | custom-call | flops 268435456 | bytes 1310720 | tf_op jit(solution)/shard_map/pallas_call | solution.py:146
  94.7 1.5 %collective-permute-done.7 = f32[1,8,2112]{2,1,0:T(8,128)S(1)} collective-permute-done((f32[1,8,2112]{2,1,0:T(8,128)S(1)}, f32[1,8,2112]{2,1,0:T(8,128)S(1)}, u32[]{:S(2)}, u32[]{:S(2)}) %collective-permute-start.7) | collective-permute-done | bytes 67616 | tf_op jit(solution)/shard_map/ppermute | solution.py:17
  96.2 0.1 broadcast_in_dim.39
  96.3 0.1 reshape.236
  96.8 0.6 fusion.7
  (51 shorter events, 1.9 us)
Async XLA Ops:
  1.4 4.1 %copy-start.2 = (bf16[1,8,6144]{2,1,0:T(8,128)(2,1)}, bf16[1,8,6144]{2,1,0:T(8,128)(2,1)S(1)}, u32[]{:S(2)}) copy-start(bf16[1,8,6144]{2,1,0:T(8,128)(2,1)S(1)} %maximum_bitcast_fusion.2) | copy-start | bytes 294916
  1.4 13.3 %collective-permute-start = (bf16[1,8,6144]{2,1,0:T(8,128)(2,1)S(1)}, bf16[1,8,6144]{2,1,0:T(8,128)(2,1)S(1)}, u32[]{:S(2)}, u32[]{:S(2)}) collective-permute-start(bf16[1,8,6144]{2,1,0:T(8,128)(2,1)S(1)} %maximum_bitcast_fusion.2), channel_id=1, source_target_pairs={{0,8},{1,9},{2,10},{3,11},{4,12},{5,13},{6,14},{7,15},{8,0},{9,1},... | collective-permute-start | bytes 294920 | tf_op jit(solution)/shard_map/ppermute | solution.py:17
  14.7 2.6 %copy-start.5 = (bf16[1,8,6144]{2,1,0:T(8,128)(2,1)}, bf16[1,8,6144]{2,1,0:T(8,128)(2,1)S(1)}, u32[]{:S(2)}) copy-start(bf16[1,8,6144]{2,1,0:T(8,128)(2,1)S(1)} %collective-permute-done) | copy-start | bytes 294916
  15.7 10.8 %collective-permute-start.1 = (bf16[2,8,6144]{2,1,0:T(8,128)(2,1)S(1)}, bf16[2,8,6144]{2,1,0:T(8,128)(2,1)S(1)}, u32[]{:S(2)}, u32[]{:S(2)}) collective-permute-start(bf16[2,8,6144]{2,1,0:T(8,128)(2,1)S(1)} %maximum_bitcast_fusion), channel_id=1, source_target_pairs={{0,4},{1,5},{2,6},{3,7},{4,0},{5,1},{6,2},{7,3},{8,12},{9,13},{10,... | collective-permute-start | bytes 589832 | tf_op jit(solution)/shard_map/ppermute | solution.py:17
  26.5 0.7 copy-start.3
  35.5 10.3 %collective-permute-start.2 = (bf16[4,8,6144]{2,1,0:T(8,128)(2,1)S(1)}, bf16[4,8,6144]{2,1,0:T(8,128)(2,1)S(1)}, u32[]{:S(2)}, u32[]{:S(2)}) collective-permute-start(bf16[4,8,6144]{2,1,0:T(8,128)(2,1)S(1)} %bitcast.119), channel_id=1, source_target_pairs={{0,2},{1,3},{2,0},{3,1},{4,6},{5,7},{6,4},{7,5},{8,10},{9,11},{10,... | collective-permute-start | bytes 1179656 | tf_op jit(solution)/shard_map/ppermute | solution.py:17
  45.7 0.7 copy-start.1
  46.5 9.7 %collective-permute-start.3 = (bf16[8,8,6144]{2,1,0:T(8,128)(2,1)S(1)}, bf16[8,8,6144]{2,1,0:T(8,128)(2,1)S(1)}, u32[]{:S(2)}, u32[]{:S(2)}) collective-permute-start(bf16[8,8,6144]{2,1,0:T(8,128)(2,1)S(1)} %bitcast.115), channel_id=1, source_target_pairs={{0,1},{1,0},{2,3},{3,2},{4,5},{5,4},{6,7},{7,6},{8,9},{9,8},{10,11... | collective-permute-start | bytes 2359304 | tf_op jit(solution)/shard_map/ppermute | solution.py:17
  56.2 0.9 copy-start
  67.3 1.3 %copy-start.4 = (f32[64,2048]{1,0:T(8,128)S(1)}, f32[64,2048]{1,0:T(8,128)}, u32[]{:S(2)}) copy-start(f32[64,2048]{1,0:T(8,128)} %get-tuple-element.75) | copy-start | bytes 1572868
  67.3 1.3 %copy-start.6 = (f32[64,32]{1,0:T(8,128)S(1)}, f32[64,32]{1,0:T(8,128)}, u32[]{:S(2)}) copy-start(f32[64,32]{1,0:T(8,128)} %get-tuple-element.76) | copy-start | bytes 24580
  67.3 1.3 %copy-start.7 = (f32[64,32]{1,0:T(8,128)S(1)}, f32[64,32]{1,0:T(8,128)}, u32[]{:S(2)}) copy-start(f32[64,32]{1,0:T(8,128)} %get-tuple-element.77) | copy-start | bytes 24580
  68.7 4.2 %collective-permute-start.4 = (f32[8,8,2112]{2,1,0:T(8,128)S(1)}, f32[8,8,2112]{2,1,0:T(8,128)S(1)}, u32[]{:S(2)}, u32[]{:S(2)}) collective-permute-start(f32[8,8,2112]{2,1,0:T(8,128)S(1)} %fusion), channel_id=1, source_target_pairs={{0,1},{1,0},{2,3},{3,2},{4,5},{5,4},{6,7},{7,6},{8,9},{9,8},{10,11... | collective-permute-start | bytes 1622024 | tf_op jit(solution)/shard_map/ppermute | solution.py:17
  74.7 8.7 %collective-permute-start.5 = (f32[4,8,2112]{2,1,0:T(8,128)S(1)}, f32[4,8,2112]{2,1,0:T(8,128)S(1)}, u32[]{:S(2)}, u32[]{:S(2)}) collective-permute-start(f32[4,8,2112]{2,1,0:T(8,128)S(1)} %get-tuple-element.80), channel_id=1, source_target_pairs={{0,2},{1,3},{2,0},{3,1},{4,6},{5,7},{6,4},{7,5},{8,10},{9,11},{10,... | collective-permute-start | bytes 811016 | tf_op jit(solution)/shard_map/ppermute | solution.py:17
  84.4 5.1 %collective-permute-start.6 = (f32[2,8,2112]{2,1,0:T(8,128)S(1)}, f32[2,8,2112]{2,1,0:T(8,128)S(1)}, u32[]{:S(2)}, u32[]{:S(2)}) collective-permute-start(f32[2,8,2112]{2,1,0:T(8,128)S(1)} %get-tuple-element.84), channel_id=1, source_target_pairs={{0,4},{1,5},{2,6},{3,7},{4,0},{5,1},{6,2},{7,3},{8,12},{9,13},{10,... | collective-permute-start | bytes 405512 | tf_op jit(solution)/shard_map/ppermute | solution.py:17
  90.2 6.0 %collective-permute-start.7 = (f32[1,8,2112]{2,1,0:T(8,128)S(1)}, f32[1,8,2112]{2,1,0:T(8,128)S(1)}, u32[]{:S(2)}, u32[]{:S(2)}) collective-permute-start(f32[1,8,2112]{2,1,0:T(8,128)S(1)} %get-tuple-element.88), channel_id=1, source_target_pairs={{0,8},{1,9},{2,10},{3,11},{4,12},{5,13},{6,14},{7,15},{8,0},{9,1},... | collective-permute-start | bytes 202760 | tf_op jit(solution)/shard_map/ppermute | solution.py:17

commit v10 on v8

--- a/solution.py
+++ b/solution.py
@@ -84,6 +84,35 @@
     return jnp.concatenate([summed, totals, top], axis=1)
 
 
+def pieces(value, count):
+    terms = []
+    rest = value
+    for ignored in range(count):
+        rounded = lax.reduce_precision(rest, exponent_bits=8, mantissa_bits=7)
+        terms.append(rounded.astype(jnp.bfloat16))
+        rest = rest - rounded
+    return terms
+
+
+def encode(state, heads):
+    width = heads * HEAD_DIM
+    summed = state[..., :width].astype(jnp.bfloat16)
+    totals = pieces(state[..., width : width + heads], 2)
+    tops = pieces(state[..., width + heads :], 3)
+    return jnp.concatenate([summed] + totals + tops, axis=-1)
+
+
+def decode(sent, heads):
+    width = heads * HEAD_DIM
+    summed = sent[..., :width].astype(jnp.float32)
+    parts = [
+        sent[..., width + i * heads : width + (i + 1) * heads].astype(jnp.float32) for i in range(5)
+    ]
+    totals = parts[0] + parts[1]
+    tops = (parts[2] + parts[3]) + parts[4]
+    return jnp.concatenate([summed, totals, tops], axis=-1)
+
+
 def scatter_rows(state, heads, during=()):
     count = lax.axis_size("seq")
     me = lax.axis_index("seq")
@@ -100,7 +129,7 @@
         work = during[step] if step < len(during) else None
         if work is not None:
             give, carried = lax.optimization_barrier((give, carried))
-        arrived = exchange(give, bit, count)
+        arrived = decode(exchange(encode(give, heads), bit, count), heads)
         if work is not None:
             carried = work(carried)
             arrived, carried = lax.optimization_barrier((arrived, carried))

time: 73.9 us -> 70.7 us (0.957)
  waiting for transfers between devices: 19.3 us -> 15.8 us
  local copies, waits for them, and re-layouts: 6.73 us -> 7.49 us
    ppermute x8, waiting for transfers between devices: 9.2 us -> 5.65 us  [exchange(): return lax.ppermute(value, 'seq', pairs)]
    select_n x4, other arithmetic: 0.94 us -> 0.15 us  [scatter_rows(): keep = jnp.where(upper, pairs[:, 1], pairs[:, 0])]
  transfers between devices with their start and end apart: 13 -> 13, of which waited for: 11 -> 9; matrix products, arithmetic and copies ran while one was open for 3% -> 3% of each run, Pallas kernels for 38% -> 39%
where the time goes in v10:
time: 70.7 us; the launch traced here: 70.3 us
  Pallas kernels  27.6 us (39%)
  waiting for transfers between devices  15.8 us (22%)
  starting transfers between devices  14.2 us (20%)
  local copies, waits for them, and re-layouts  7.49 us (11%)
  other arithmetic  4.12 us (6%)
  between operations  1.11 us (2%)
    pallas_call x4, Pallas kernels, video_part(): pl.pallas_call(video_kernel, grid=(pairs // PER_STEP,), in_specs=specs, o...  14.1 us
    pallas_call x4, Pallas kernels, audio_partial(): pl.pallas_call(audio_kernel, grid=(heads // 2 // PER_STEP,), in_specs=[pl...  13.5 us
    ppermute x5, waiting for transfers between devices, gather_levels(): pieces[offset] = lax.ppermute(held, 'seq', pairs)  10.1 us
    ppermute x5, starting transfers between devices, gather_levels(): pieces[offset] = lax.ppermute(held, 'seq', pairs)  7.34 us
    ppermute x8, starting transfers between devices, exchange(): return lax.ppermute(value, 'seq', pairs)  6.89 us
    ppermute x8, waiting for transfers between devices, exchange(): return lax.ppermute(value, 'seq', pairs)  5.65 us
    reshape x9, local copies, waits for them, and re-layouts, spread(): return jnp.repeat(scales, HEAD_DIM, axis=1)  1.62 us
    broadcast_in_dim x9, local copies, waits for them, and re-layouts, spread(): return jnp.repeat(scales, HEAD_DIM, axis=1)  1.57 us
  transfers between devices with their start and end apart: 13, of which 9 were waited for; matrix products, arithmetic and copies ran while one was open for 3% of the time, Pallas kernels for 39%

profile of v10, /device:TPU:0, one launch (start us, length us, event | category | flops | bytes accessed | tf_op | source)
XLA Modules:
  0.0 70.3 jit_solution(11408912274091991916)
XLA Ops:
  0.6 4.1 %collective-permute-start.2 = (bf16[1,8,2048]{2,1,0:T(8,128)(2,1)}, bf16[1,8,2048]{2,1,0:T(8,128)(2,1)S(1)}, u32[]{:S(2)}, u32[]{:S(2)}) collective-permute-start(bf16[1,8,2048]{2,1,0:T(8,128)(2,1)} %bitcast.104), channel_id=1, source_target_pairs={{0,8},{1,9},{2,10},{3,11},{4,12},{5,13},{6,14},{7,15},{8,0},{9,1},... | collective-permute-start | bytes 98312 | tf_op jit(solution)/shard_map/ppermute | solution.py:65
  4.7 1.6 %collective-permute-start.1 = (bf16[1,8,2048]{2,1,0:T(8,128)(2,1)}, bf16[1,8,2048]{2,1,0:T(8,128)(2,1)S(1)}, u32[]{:S(2)}, u32[]{:S(2)}) collective-permute-start(bf16[1,8,2048]{2,1,0:T(8,128)(2,1)} %bitcast.105), channel_id=1, source_target_pairs={{0,4},{1,5},{2,6},{3,7},{4,0},{5,1},{6,2},{7,3},{8,12},{9,13},{10,... | collective-permute-start | bytes 98312 | tf_op jit(solution)/shard_map/ppermute | solution.py:65
  6.3 1.0 %collective-permute-done.2 = bf16[1,8,2048]{2,1,0:T(8,128)(2,1)S(1)} collective-permute-done((bf16[1,8,2048]{2,1,0:T(8,128)(2,1)}, bf16[1,8,2048]{2,1,0:T(8,128)(2,1)S(1)}, u32[]{:S(2)}, u32[]{:S(2)}) %collective-permute-start.2) | collective-permute-done | bytes 32800 | tf_op jit(solution)/shard_map/ppermute | solution.py:65
  7.3 1.6 %collective-permute-done.1 = bf16[1,8,2048]{2,1,0:T(8,128)(2,1)S(1)} collective-permute-done((bf16[1,8,2048]{2,1,0:T(8,128)(2,1)}, bf16[1,8,2048]{2,1,0:T(8,128)(2,1)S(1)}, u32[]{:S(2)}, u32[]{:S(2)}) %collective-permute-start.1) | collective-permute-done | bytes 32800 | tf_op jit(solution)/shard_map/ppermute | solution.py:65
  8.9 3.4 %collective-permute-done = bf16[1,8,2048]{2,1,0:T(8,128)(2,1)S(1)} collective-permute-done((bf16[1,8,2048]{2,1,0:T(8,128)(2,1)}, bf16[1,8,2048]{2,1,0:T(8,128)(2,1)S(1)}, u32[]{:S(2)}, u32[]{:S(2)}) %collective-permute-start) | collective-permute-done | bytes 32800 | tf_op jit(solution)/shard_map/ppermute | solution.py:65
  12.2 0.8 %select_bitcast_fusion.23 = (bf16[1,1,8,2048]{3,2,1,0:T(8,128)(2,1)S(1)}, bf16[1,1,8,2048]{3,2,1,0:T(8,128)(2,1)S(1)}, bf16[1,1,8,2048]{3,2,1,0:T(8,128)(2,1)S(1)}, bf16[1,1,8,2048]{3,2,1,0:T(8,128)(2,1)S(1)}) fusion(bf16[1,8,2048]{2,1,0:T(8,128)(2,1)S(1)} %collective-permute-done, bf16[1,8,2048]{2,1,0:T(8,128)(2,1)S(1)} %collective-permute-done.1, ...), kind=kLoop, calls=%fused_computation.70 | loop fusion | flops 196608 | bytes 262156 | tf_op jit(solution)/shard_map/stack | solution.py:73
  13.0 1.6 %collective-permute-start.3 = (bf16[4,8,2048]{2,1,0:T(8,128)(2,1)S(1)}, bf16[4,8,2048]{2,1,0:T(8,128)(2,1)S(1)}, u32[]{:S(2)}, u32[]{:S(2)}) collective-permute-start(bf16[4,8,2048]{2,1,0:T(8,128)(2,1)S(1)} %maximum_bitcast_fusion), channel_id=1, source_target_pairs={{0,2},{1,3},{2,0},{3,1},{4,6},{5,7},{6,4},{7,5},{8,10},{9,11},{10,... | collective-permute-start | bytes 393224 | tf_op jit(solution)/shard_map/ppermute | solution.py:65
  14.6 3.4 %collective-permute-done.3 = bf16[4,8,2048]{2,1,0:T(8,128)(2,1)S(1)} collective-permute-done((bf16[4,8,2048]{2,1,0:T(8,128)(2,1)S(1)}, bf16[4,8,2048]{2,1,0:T(8,128)(2,1)S(1)}, u32[]{:S(2)}, u32[]{:S(2)}) %collective-permute-start.3) | collective-permute-done | bytes 131104 | tf_op jit(solution)/shard_map/ppermute | solution.py:65
  18.2 0.8 %maximum_bitcast_fusion.2 = bf16[1,8,4096]{2,1,0:T(8,128)(2,1)S(1)} fusion(bf16[8,2048]{1,0:T(8,128)(2,1)} %param.11, bf16[8,2048]{1,0:T(8,128)(2,1)} %param.10), kind=kLoop, calls=%fused_computation.45 | loop fusion | flops 131072 | bytes 131072 | tf_op jit(solution)/shard_map/broadcast_in_dim | solution.py:23
  19.0 0.7 %collective-permute-done.4 = bf16[8,8,2048]{2,1,0:T(8,128)(2,1)S(1)} collective-permute-done((bf16[8,8,2048]{2,1,0:T(8,128)(2,1)S(1)}, bf16[8,8,2048]{2,1,0:T(8,128)(2,1)S(1)}, u32[]{:S(2)}, u32[]{:S(2)}) %collective-permute-start.4) | collective-permute-done | bytes 262176 | tf_op jit(solution)/shard_map/ppermute | solution.py:65
  19.9 0.8 %copy.19 = bf16[8,2,8,2048]{3,2,1,0:T(8,128)(2,1)} copy(bf16[8,2,8,2048]{3,2,0,1:T(8,128)(2,1)S(1)} %pad_maximum_fusion.1) | data formatting | bytes 1048576 | tf_op jit(solution)/shard_map/stack | solution.py:73
  20.7 3.3 %shard_map.77 = (f32[128,512]{1,0:T(8,128)}, f32[128,8]{1,0:T(8,128)}, f32[128,8]{1,0:T(8,128)}) custom-call(bf16[128,2048]{1,0:T(8,128)(2,1)} %bitcast.82, bf16[512,2048]{1,0:T(8,128)(2,1)} %key_ref.7, bf16[512,2048]{1,0:T(8,128)(2,1)} %value_ref.7), custom_call_target="tpu_custom_call" | custom-call | flops 268435456 | bytes 1441792 | tf_op jit(solution)/shard_map/pallas_call | solution.py:277
  24.0 1.8 %collective-permute-done.5 = bf16[1,8,4096]{2,1,0:T(8,128)(2,1)S(1)} collective-permute-done((bf16[1,8,4096]{2,1,0:T(8,128)(2,1)S(1)}, bf16[1,8,4096]{2,1,0:T(8,128)(2,1)S(1)}, u32[]{:S(2)}, u32[]{:S(2)}) %collective-permute-start.5) | collective-permute-done | bytes 65568 | tf_op jit(solution)/shard_map/ppermute | solution.py:17
  26.0 3.4 %shard_map.78 = (f32[128,512]{1,0:T(8,128)}, f32[128,8]{1,0:T(8,128)}, f32[128,8]{1,0:T(8,128)}) custom-call(bf16[128,2048]{1,0:T(8,128)(2,1)} %bitcast.83, bf16[512,2048]{1,0:T(8,128)(2,1)} %key_ref.7, bf16[512,2048]{1,0:T(8,128)(2,1)} %value_ref.7), custom_call_target="tpu_custom_call" | custom-call | flops 268435456 | bytes 1441792 | tf_op jit(solution)/shard_map/pallas_call | solution.py:277
  29.4 1.6 %collective-permute-done.6 = bf16[2,8,4096]{2,1,0:T(8,128)(2,1)S(1)} collective-permute-done((bf16[2,8,4096]{2,1,0:T(8,128)(2,1)S(1)}, bf16[2,8,4096]{2,1,0:T(8,128)(2,1)S(1)}, u32[]{:S(2)}, u32[]{:S(2)}) %collective-permute-start.6) | collective-permute-done | bytes 131104 | tf_op jit(solution)/shard_map/ppermute | solution.py:17
  31.0 1.6 %collective-permute-start.7 = (bf16[4,8,4096]{2,1,0:T(8,128)(2,1)S(1)}, bf16[4,8,4096]{2,1,0:T(8,128)(2,1)S(1)}, u32[]{:S(2)}, u32[]{:S(2)}) collective-permute-start(bf16[4,8,4096]{2,1,0:T(8,128)(2,1)S(1)} %bitcast.97), channel_id=1, source_target_pairs={{0,2},{1,3},{2,0},{3,1},{4,6},{5,7},{6,4},{7,5},{8,10},{9,11},{10,... | collective-permute-start | bytes 786440 | tf_op jit(solution)/shard_map/ppermute | solution.py:17
  32.6 3.3 %shard_map.79 = (f32[128,512]{1,0:T(8,128)}, f32[128,8]{1,0:T(8,128)}, f32[128,8]{1,0:T(8,128)}) custom-call(bf16[128,2048]{1,0:T(8,128)(2,1)} %bitcast.84, bf16[512,2048]{1,0:T(8,128)(2,1)} %key_ref.7, bf16[512,2048]{1,0:T(8,128)(2,1)} %value_ref.7), custom_call_target="tpu_custom_call" | custom-call | flops 268435456 | bytes 1441792 | tf_op jit(solution)/shard_map/pallas_call | solution.py:277
  35.9 1.5 %collective-permute-done.7 = bf16[4,8,4096]{2,1,0:T(8,128)(2,1)S(1)} collective-permute-done((bf16[4,8,4096]{2,1,0:T(8,128)(2,1)S(1)}, bf16[4,8,4096]{2,1,0:T(8,128)(2,1)S(1)}, u32[]{:S(2)}, u32[]{:S(2)}) %collective-permute-start.7) | collective-permute-done | bytes 262176 | tf_op jit(solution)/shard_map/ppermute | solution.py:17
  37.7 3.5 %shard_map.80 = (f32[128,512]{1,0:T(8,128)}, f32[128,8]{1,0:T(8,128)}, f32[128,8]{1,0:T(8,128)}) custom-call(bf16[128,2048]{1,0:T(8,128)(2,1)} %bitcast.85, bf16[512,2048]{1,0:T(8,128)(2,1)} %key_ref.7, bf16[512,2048]{1,0:T(8,128)(2,1)} %value_ref.7), custom_call_target="tpu_custom_call" | custom-call | flops 268435456 | bytes 1441792 | tf_op jit(solution)/shard_map/pallas_call | solution.py:277
  41.3 1.2 %concatenate.40 = f32[128,2112]{1,0:T(8,128)S(1)} concatenate(f32[128,512]{1,0:T(8,128)S(1)} %copy-done, f32[128,512]{1,0:T(8,128)S(1)} %copy-done.1, f32[128,512]{1,0:T(8,128)S(1)} %copy-done.2, f32[128,512]{1,0:T(8,128)} %get-tuple-element.78, f32[128,8]{1,0:T(8,128)S(1)} %copy-done.3, f32[128,8]{1,0:T(8,128)S(1)} %copy-done.5, f32[128,8]{1,0:T(8,128)S(1)} %copy-done.7, ...), dimensions={1} | concatenate | bytes 2162688 | tf_op jit(solution)/shard_map/concatenate | solution.py:317
  42.8 0.1 pad_maximum_fusion
  43.0 0.1 concatenate.41
  43.1 0.5 collective-permute-start.9
  43.7 1.1 %fusion.30 = (bf16[128,2048]{1,0:T(8,128)(2,1)}, bf16[128,2048]{1,0:T(8,128)(2,1)}) fusion(bf16[128,4096]{1,0:T(8,128)(2,1)S(1)} %bitcast.87), kind=kLoop, calls=%fused_computation.127 | loop fusion | bytes 2097152 | tf_op jit(solution)/shard_map/slice | solution.py:316
  44.7 3.5 %shard_map.81.refs_0_ = bf16[512,2048]{1,0:T(8,128)(2,1)} custom-call(bf16[512,2048]{1,0:T(8,128)(2,1)} %query_ref.7, bf16[128,2048]{1,0:T(8,128)(2,1)} %get-tuple-element.120.key_ref, bf16[128,2048]{1,0:T(8,128)(2,1)} %get-tuple-element.119.value_ref), custom_call_target="tpu_custom_call" | custom-call | flops 268435456 | bytes 1310720 | tf_op jit(solution)/shard_map/pallas_call | solution.py:231
  48.6 0.3 broadcast_in_dim.35
  48.9 0.4 reshape.117
  49.3 0.3 broadcast_in_dim.36
  49.6 0.4 reshape.118
  50.0 0.1 fusion
  50.4 1.6 %collective-permute-start.10 = (bf16[4,8,2208]{2,1,0:T(8,128)(2,1)S(1)}, bf16[4,8,2208]{2,1,0:T(8,128)(2,1)S(1)}, u32[]{:S(2)}, u32[]{:S(2)}) collective-permute-start(bf16[4,8,2208]{2,1,0:T(8,128)(2,1)S(1)} %concatenate.44), channel_id=1, source_target_pairs={{0,2},{1,3},{2,0},{3,1},{4,6},{5,7},{6,4},{7,5},{8,10},{9,11},{10,... | collective-permute-start | bytes 423944 | tf_op jit(solution)/shard_map/ppermute | solution.py:17
  52.0 3.5 %shard_map.82.refs_0_ = bf16[512,2048]{1,0:T(8,128)(2,1)} custom-call(bf16[512,2048]{1,0:T(8,128)(2,1)} %query_ref.7, bf16[128,2048]{1,0:T(8,128)(2,1)} %get-tuple-element.120.key_ref, bf16[128,2048]{1,0:T(8,128)(2,1)} %get-tuple-element.119.value_ref, bf16[512,2048]{1,0:T(8,128)(2,1)} %shard_map.81.refs_0_), custom_call_target="tpu_custom_call", output_to_operand_aliasing={{}: (3, {})} | custom-call | flops 268435456 | bytes 1310720 | tf_op jit(solution)/shard_map/pallas_call | solution.py:231
  55.5 0.7 %collective-permute-done.10 = bf16[4,8,2208]{2,1,0:T(8,128)(2,1)S(1)} collective-permute-done((bf16[4,8,2208]{2,1,0:T(8,128)(2,1)S(1)}, bf16[4,8,2208]{2,1,0:T(8,128)(2,1)S(1)}, u32[]{:S(2)}, u32[]{:S(2)}) %collective-permute-start.10) | collective-permute-done | bytes 141344 | tf_op jit(solution)/shard_map/ppermute | solution.py:17
  56.5 0.2 broadcast_in_dim.37
  56.7 0.2 reshape.120
  56.9 0.2 broadcast_in_dim.38
  57.1 0.2 reshape.121
  57.6 1.0 %collective-permute-start.11 = (bf16[2,8,2208]{2,1,0:T(8,128)(2,1)S(1)}, bf16[2,8,2208]{2,1,0:T(8,128)(2,1)S(1)}, u32[]{:S(2)}, u32[]{:S(2)}) collective-permute-start(bf16[2,8,2208]{2,1,0:T(8,128)(2,1)S(1)} %concatenate.47), channel_id=1, source_target_pairs={{0,4},{1,5},{2,6},{3,7},{4,0},{5,1},{6,2},{7,3},{8,12},{9,13},{10,... | collective-permute-start | bytes 211976 | tf_op jit(solution)/shard_map/ppermute | solution.py:17
  58.6 3.5 %shard_map.83.refs_0_ = bf16[512,2048]{1,0:T(8,128)(2,1)} custom-call(bf16[512,2048]{1,0:T(8,128)(2,1)} %query_ref.7, bf16[128,2048]{1,0:T(8,128)(2,1)} %get-tuple-element.120.key_ref, bf16[128,2048]{1,0:T(8,128)(2,1)} %get-tuple-element.119.value_ref, bf16[512,2048]{1,0:T(8,128)(2,1)} %shard_map.82.refs_0_), custom_call_target="tpu_custom_call", output_to_operand_aliasing={{}: (3, {})} | custom-call | flops 268435456 | bytes 1310720 | tf_op jit(solution)/shard_map/pallas_call | solution.py:231
  62.4 0.1 broadcast_in_dim.39
  62.5 0.1 reshape.123
  62.7 0.1 broadcast_in_dim.40
  62.8 0.1 reshape.124
  63.2 2.1 %collective-permute-start.12 = (bf16[1,8,2208]{2,1,0:T(8,128)(2,1)S(1)}, bf16[1,8,2208]{2,1,0:T(8,128)(2,1)S(1)}, u32[]{:S(2)}, u32[]{:S(2)}) collective-permute-start(bf16[1,8,2208]{2,1,0:T(8,128)(2,1)S(1)} %concatenate.50), channel_id=1, source_target_pairs={{0,8},{1,9},{2,10},{3,11},{4,12},{5,13},{6,14},{7,15},{8,0},{9,1},... | collective-permute-start | bytes 105992 | tf_op jit(solution)/shard_map/ppermute | solution.py:17
  65.3 3.5 %shard_map.84 = bf16[512,2048]{1,0:T(8,128)(2,1)} custom-call(bf16[512,2048]{1,0:T(8,128)(2,1)} %query_ref.7, bf16[128,2048]{1,0:T(8,128)(2,1)} %get-tuple-element.120.key_ref, bf16[128,2048]{1,0:T(8,128)(2,1)} %get-tuple-element.119.value_ref, bf16[512,2048]{1,0:T(8,128)(2,1)} %shard_map.83.refs_0_), custom_call_target="tpu_custom_call", output_to_operand_aliasing={{}: (3, {})} | custom-call | flops 268435456 | bytes 1310720 | tf_op jit(solution)/shard_map/pallas_call | solution.py:231
  69.1 0.1 broadcast_in_dim.43
  69.2 0.1 reshape.128
  69.7 0.6 fusion.5
  (81 shorter events, 3.4 us)
Async XLA Ops:
  0.6 6.7 %collective-permute-start.2 = (bf16[1,8,2048]{2,1,0:T(8,128)(2,1)}, bf16[1,8,2048]{2,1,0:T(8,128)(2,1)S(1)}, u32[]{:S(2)}, u32[]{:S(2)}) collective-permute-start(bf16[1,8,2048]{2,1,0:T(8,128)(2,1)} %bitcast.104), channel_id=1, source_target_pairs={{0,8},{1,9},{2,10},{3,11},{4,12},{5,13},{6,14},{7,15},{8,0},{9,1},... | collective-permute-start | bytes 98312 | tf_op jit(solution)/shard_map/ppermute | solution.py:65
  4.7 4.1 %collective-permute-start.1 = (bf16[1,8,2048]{2,1,0:T(8,128)(2,1)}, bf16[1,8,2048]{2,1,0:T(8,128)(2,1)S(1)}, u32[]{:S(2)}, u32[]{:S(2)}) collective-permute-start(bf16[1,8,2048]{2,1,0:T(8,128)(2,1)} %bitcast.105), channel_id=1, source_target_pairs={{0,4},{1,5},{2,6},{3,7},{4,0},{5,1},{6,2},{7,3},{8,12},{9,13},{10,... | collective-permute-start | bytes 98312 | tf_op jit(solution)/shard_map/ppermute | solution.py:65
  6.3 5.9 %collective-permute-start = (bf16[1,8,2048]{2,1,0:T(8,128)(2,1)}, bf16[1,8,2048]{2,1,0:T(8,128)(2,1)S(1)}, u32[]{:S(2)}, u32[]{:S(2)}) collective-permute-start(bf16[1,8,2048]{2,1,0:T(8,128)(2,1)} %bitcast.106), channel_id=1, source_target_pairs={{0,12},{1,13},{2,14},{3,15},{4,8},{5,9},{6,10},{7,11},{8,4},{9,5},... | collective-permute-start | bytes 98312 | tf_op jit(solution)/shard_map/ppermute | solution.py:65
  13.0 5.0 %collective-permute-start.3 = (bf16[4,8,2048]{2,1,0:T(8,128)(2,1)S(1)}, bf16[4,8,2048]{2,1,0:T(8,128)(2,1)S(1)}, u32[]{:S(2)}, u32[]{:S(2)}) collective-permute-start(bf16[4,8,2048]{2,1,0:T(8,128)(2,1)S(1)} %maximum_bitcast_fusion), channel_id=1, source_target_pairs={{0,2},{1,3},{2,0},{3,1},{4,6},{5,7},{6,4},{7,5},{8,10},{9,11},{10,... | collective-permute-start | bytes 393224 | tf_op jit(solution)/shard_map/ppermute | solution.py:65
  18.1 1.6 %collective-permute-start.4 = (bf16[8,8,2048]{2,1,0:T(8,128)(2,1)S(1)}, bf16[8,8,2048]{2,1,0:T(8,128)(2,1)S(1)}, u32[]{:S(2)}, u32[]{:S(2)}) collective-permute-start(bf16[8,8,2048]{2,1,0:T(8,128)(2,1)S(1)} %bitcast.96), channel_id=1, source_target_pairs={{0,1},{1,0},{2,3},{3,2},{4,5},{5,4},{6,7},{7,6},{8,9},{9,8},{10,11... | collective-permute-start | bytes 786440 | tf_op jit(solution)/shard_map/ppermute | solution.py:65
  20.7 5.2 %collective-permute-start.5 = (bf16[1,8,4096]{2,1,0:T(8,128)(2,1)S(1)}, bf16[1,8,4096]{2,1,0:T(8,128)(2,1)S(1)}, u32[]{:S(2)}, u32[]{:S(2)}) collective-permute-start(bf16[1,8,4096]{2,1,0:T(8,128)(2,1)S(1)} %maximum_bitcast_fusion.2), channel_id=1, source_target_pairs={{0,8},{1,9},{2,10},{3,11},{4,12},{5,13},{6,14},{7,15},{8,0},{9,1},... | collective-permute-start | bytes 196616 | tf_op jit(solution)/shard_map/ppermute | solution.py:17
  25.9 5.0 %collective-permute-start.6 = (bf16[2,8,4096]{2,1,0:T(8,128)(2,1)S(1)}, bf16[2,8,4096]{2,1,0:T(8,128)(2,1)S(1)}, u32[]{:S(2)}, u32[]{:S(2)}) collective-permute-start(bf16[2,8,4096]{2,1,0:T(8,128)(2,1)S(1)} %maximum_bitcast_fusion.1), channel_id=1, source_target_pairs={{0,4},{1,5},{2,6},{3,7},{4,0},{5,1},{6,2},{7,3},{8,12},{9,13},{10,... | collective-permute-start | bytes 393224 | tf_op jit(solution)/shard_map/ppermute | solution.py:17
  31.0 6.4 %collective-permute-start.7 = (bf16[4,8,4096]{2,1,0:T(8,128)(2,1)S(1)}, bf16[4,8,4096]{2,1,0:T(8,128)(2,1)S(1)}, u32[]{:S(2)}, u32[]{:S(2)}) collective-permute-start(bf16[4,8,4096]{2,1,0:T(8,128)(2,1)S(1)} %bitcast.97), channel_id=1, source_target_pairs={{0,2},{1,3},{2,0},{3,1},{4,6},{5,7},{6,4},{7,5},{8,10},{9,11},{10,... | collective-permute-start | bytes 786440 | tf_op jit(solution)/shard_map/ppermute | solution.py:17
  37.6 3.6 %collective-permute-start.8 = (bf16[8,8,4096]{2,1,0:T(8,128)(2,1)S(1)}, bf16[8,8,4096]{2,1,0:T(8,128)(2,1)S(1)}, u32[]{:S(2)}, u32[]{:S(2)}) collective-permute-start(bf16[8,8,4096]{2,1,0:T(8,128)(2,1)S(1)} %bitcast.91), channel_id=1, source_target_pairs={{0,1},{1,0},{2,3},{3,2},{4,5},{5,4},{6,7},{7,6},{8,9},{9,8},{10,11... | collective-permute-start | bytes 1572872 | tf_op jit(solution)/shard_map/ppermute | solution.py:17
  37.7 3.6 %copy-start = (f32[128,512]{1,0:T(8,128)S(1)}, f32[128,512]{1,0:T(8,128)}, u32[]{:S(2)}) copy-start(f32[128,512]{1,0:T(8,128)} %get-tuple-element.57) | copy-start | bytes 786436
  37.7 3.5 %copy-start.1 = (f32[128,512]{1,0:T(8,128)S(1)}, f32[128,512]{1,0:T(8,128)}, u32[]{:S(2)}) copy-start(f32[128,512]{1,0:T(8,128)} %get-tuple-element.64) | copy-start | bytes 786436
  37.7 3.5 %copy-start.2 = (f32[128,512]{1,0:T(8,128)S(1)}, f32[128,512]{1,0:T(8,128)}, u32[]{:S(2)}) copy-start(f32[128,512]{1,0:T(8,128)} %get-tuple-element.71) | copy-start | bytes 786436
  37.7 3.5 %copy-start.3 = (f32[128,8]{1,0:T(8,128)S(1)}, f32[128,8]{1,0:T(8,128)}, u32[]{:S(2)}) copy-start(f32[128,8]{1,0:T(8,128)} %get-tuple-element.79) | copy-start | bytes 12292
  37.7 3.5 %copy-start.4 = (f32[128,8]{1,0:T(8,128)S(1)}, f32[128,8]{1,0:T(8,128)}, u32[]{:S(2)}) copy-start(f32[128,8]{1,0:T(8,128)} %get-tuple-element.83) | copy-start | bytes 12292
  37.7 3.5 %copy-start.5 = (f32[128,8]{1,0:T(8,128)S(1)}, f32[128,8]{1,0:T(8,128)}, u32[]{:S(2)}) copy-start(f32[128,8]{1,0:T(8,128)} %get-tuple-element.80) | copy-start | bytes 12292
  37.7 3.5 %copy-start.6 = (f32[128,8]{1,0:T(8,128)S(1)}, f32[128,8]{1,0:T(8,128)}, u32[]{:S(2)}) copy-start(f32[128,8]{1,0:T(8,128)} %get-tuple-element.84) | copy-start | bytes 12292
  37.7 3.5 %copy-start.7 = (f32[128,8]{1,0:T(8,128)S(1)}, f32[128,8]{1,0:T(8,128)}, u32[]{:S(2)}) copy-start(f32[128,8]{1,0:T(8,128)} %get-tuple-element.81) | copy-start | bytes 12292
  37.7 3.5 %copy-start.8 = (f32[128,8]{1,0:T(8,128)S(1)}, f32[128,8]{1,0:T(8,128)}, u32[]{:S(2)}) copy-start(f32[128,8]{1,0:T(8,128)} %get-tuple-element.85) | copy-start | bytes 12292
  43.1 5.1 %collective-permute-start.9 = (bf16[8,8,2208]{2,1,0:T(8,128)(2,1)S(1)}, bf16[8,8,2208]{2,1,0:T(8,128)(2,1)S(1)}, u32[]{:S(2)}, u32[]{:S(2)}) collective-permute-start(bf16[8,8,2208]{2,1,0:T(8,128)(2,1)S(1)} %concatenate.41), channel_id=1, source_target_pairs={{0,1},{1,0},{2,3},{3,2},{4,5},{5,4},{6,7},{7,6},{8,9},{9,8},{10,11... | collective-permute-start | bytes 847880 | tf_op jit(solution)/shard_map/ppermute | solution.py:17
  50.4 5.8 %collective-permute-start.10 = (bf16[4,8,2208]{2,1,0:T(8,128)(2,1)S(1)}, bf16[4,8,2208]{2,1,0:T(8,128)(2,1)S(1)}, u32[]{:S(2)}, u32[]{:S(2)}) collective-permute-start(bf16[4,8,2208]{2,1,0:T(8,128)(2,1)S(1)} %concatenate.44), channel_id=1, source_target_pairs={{0,2},{1,3},{2,0},{3,1},{4,6},{5,7},{6,4},{7,5},{8,10},{9,11},{10,... | collective-permute-start | bytes 423944 | tf_op jit(solution)/shard_map/ppermute | solution.py:17
  57.6 4.5 %collective-permute-start.11 = (bf16[2,8,2208]{2,1,0:T(8,128)(2,1)S(1)}, bf16[2,8,2208]{2,1,0:T(8,128)(2,1)S(1)}, u32[]{:S(2)}, u32[]{:S(2)}) collective-permute-start(bf16[2,8,2208]{2,1,0:T(8,128)(2,1)S(1)} %concatenate.47), channel_id=1, source_target_pairs={{0,4},{1,5},{2,6},{3,7},{4,0},{5,1},{6,2},{7,3},{8,12},{9,13},{10,... | collective-permute-start | bytes 211976 | tf_op jit(solution)/shard_map/ppermute | solution.py:17
  63.2 5.6 %collective-permute-start.12 = (bf16[1,8,2208]{2,1,0:T(8,128)(2,1)S(1)}, bf16[1,8,2208]{2,1,0:T(8,128)(2,1)S(1)}, u32[]{:S(2)}, u32[]{:S(2)}) collective-permute-start(bf16[1,8,2208]{2,1,0:T(8,128)(2,1)S(1)} %concatenate.50), channel_id=1, source_target_pairs={{0,8},{1,9},{2,10},{3,11},{4,12},{5,13},{6,14},{7,15},{8,0},{9,1},... | collective-permute-start | bytes 105992 | tf_op jit(solution)/shard_map/ppermute | solution.py:17

commit v11 on v10

--- a/solution.py
+++ b/solution.py
@@ -305,13 +305,19 @@
     width = video_q.shape[1]
     heads = width // HEAD_DIM
     groups = 4
+    steps = (lax.axis_size("seq") - 1).bit_length()
     all_queries = gather_levels(audio_q)
     audio_calls = [
-        (lambda q, g=g: audio_partial(q, video_k, video_v, g, groups), all_queries)
-        for g in range(groups)
+        (
+            lambda q, gs=gs: tuple(audio_partial(q, video_k, video_v, g, groups) for g in gs),
+            all_queries,
+        )
+        for gs in ((0, 1), (2, 3))
     ]
-    gathered, parts = gather_rows(jnp.concatenate([audio_k, audio_v], axis=1), audio_calls)
-    parts = parts + [call[0](all_queries) for call in audio_calls[len(parts) :]]
+    gathered, results = gather_rows(
+        jnp.concatenate([audio_k, audio_v], axis=1), [None] * (steps - 2) + audio_calls
+    )
+    parts = [part for result in results for part in result]
     all_keys = gathered[:, :width]
     all_values = gathered[:, width:]
     state = jnp.concatenate(

time: 70.7 us -> 65.4 us (0.925)
  waiting for transfers between devices: 15.8 us -> 9.66 us
  other arithmetic: 4.12 us -> 4.91 us
    ppermute x5, waiting for transfers between devices: 10.1 us -> 5.74 us  [gather_levels(): pieces[offset] = lax.ppermute(held, 'seq', pairs)]
    ppermute x8, waiting for transfers between devices: 5.65 us -> 3.92 us  [exchange(): return lax.ppermute(value, 'seq', pairs)]
    another operation x7, other arithmetic: 0.33 us -> 1.11 us  [gather_rows(): held = jnp.stack([low, high], axis=1).reshape((-1,) + block.shape)]
  transfers between devices with their start and end apart: 13 -> 13, of which waited for: 9 -> 6; matrix products, arithmetic and copies ran while one was open for 3% -> 5% of each run, Pallas kernels for 39% -> 43%
where the time goes in v11:
time: 65.4 us; the launch traced here: 64.9 us
  Pallas kernels  27.6 us (42%)
  starting transfers between devices  14.2 us (22%)
  waiting for transfers between devices  9.66 us (15%)
  local copies, waits for them, and re-layouts  7.47 us (11%)
  other arithmetic  4.91 us (8%)
  between operations  1.09 us (2%)
    pallas_call x4, Pallas kernels, video_part(): pl.pallas_call(video_kernel, grid=(pairs // PER_STEP,), in_specs=specs, o...  14.1 us
    pallas_call x4, Pallas kernels, audio_partial(): pl.pallas_call(audio_kernel, grid=(heads // 2 // PER_STEP,), in_specs=[pl...  13.5 us
    ppermute x5, starting transfers between devices, gather_levels(): pieces[offset] = lax.ppermute(held, 'seq', pairs)  7.34 us
    ppermute x8, starting transfers between devices, exchange(): return lax.ppermute(value, 'seq', pairs)  6.83 us
    ppermute x5, waiting for transfers between devices, gather_levels(): pieces[offset] = lax.ppermute(held, 'seq', pairs)  5.74 us
    ppermute x8, waiting for transfers between devices, exchange(): return lax.ppermute(value, 'seq', pairs)  3.92 us
    reshape x9, local copies, waits for them, and re-layouts, spread(): return jnp.repeat(scales, HEAD_DIM, axis=1)  1.62 us
    broadcast_in_dim x9, local copies, waits for them, and re-layouts, spread(): return jnp.repeat(scales, HEAD_DIM, axis=1)  1.57 us
  transfers between devices with their start and end apart: 13, of which 6 were waited for; matrix products, arithmetic and copies ran while one was open for 5% of the time, Pallas kernels for 43%

profile of v11, /device:TPU:0, one launch (start us, length us, event | category | flops | bytes accessed | tf_op | source)
XLA Modules:
  0.0 64.9 jit_solution(14313244097081787032)
XLA Ops:
  0.6 4.1 %collective-permute-start.4 = (bf16[1,8,2048]{2,1,0:T(8,128)(2,1)}, bf16[1,8,2048]{2,1,0:T(8,128)(2,1)S(1)}, u32[]{:S(2)}, u32[]{:S(2)}) collective-permute-start(bf16[1,8,2048]{2,1,0:T(8,128)(2,1)} %bitcast.112), channel_id=1, source_target_pairs={{0,8},{1,9},{2,10},{3,11},{4,12},{5,13},{6,14},{7,15},{8,0},{9,1},... | collective-permute-start | bytes 98312 | tf_op jit(solution)/shard_map/ppermute | solution.py:65
  4.7 1.6 %collective-permute-start.3 = (bf16[1,8,2048]{2,1,0:T(8,128)(2,1)}, bf16[1,8,2048]{2,1,0:T(8,128)(2,1)S(1)}, u32[]{:S(2)}, u32[]{:S(2)}) collective-permute-start(bf16[1,8,2048]{2,1,0:T(8,128)(2,1)} %bitcast.113), channel_id=1, source_target_pairs={{0,4},{1,5},{2,6},{3,7},{4,0},{5,1},{6,2},{7,3},{8,12},{9,13},{10,... | collective-permute-start | bytes 98312 | tf_op jit(solution)/shard_map/ppermute | solution.py:65
  6.3 0.8 %maximum_bitcast_fusion.2 = bf16[1,8,4096]{2,1,0:T(8,128)(2,1)S(1)} fusion(bf16[8,2048]{1,0:T(8,128)(2,1)} %param.11, bf16[8,2048]{1,0:T(8,128)(2,1)} %param.10), kind=kLoop, calls=%fused_computation.45 | loop fusion | flops 131072 | bytes 131072 | tf_op jit(solution)/shard_map/broadcast_in_dim | solution.py:23
  7.1 1.9 %collective-permute-start = (bf16[1,8,4096]{2,1,0:T(8,128)(2,1)S(1)}, bf16[1,8,4096]{2,1,0:T(8,128)(2,1)S(1)}, u32[]{:S(2)}, u32[]{:S(2)}) collective-permute-start(bf16[1,8,4096]{2,1,0:T(8,128)(2,1)S(1)} %maximum_bitcast_fusion.2), channel_id=1, source_target_pairs={{0,8},{1,9},{2,10},{3,11},{4,12},{5,13},{6,14},{7,15},{8,0},{9,1},... | collective-permute-start | bytes 196616 | tf_op jit(solution)/shard_map/ppermute | solution.py:17
  9.0 3.2 %collective-permute-done.2 = bf16[1,8,2048]{2,1,0:T(8,128)(2,1)S(1)} collective-permute-done((bf16[1,8,2048]{2,1,0:T(8,128)(2,1)}, bf16[1,8,2048]{2,1,0:T(8,128)(2,1)S(1)}, u32[]{:S(2)}, u32[]{:S(2)}) %collective-permute-start.2) | collective-permute-done | bytes 32800 | tf_op jit(solution)/shard_map/ppermute | solution.py:65
  12.2 0.8 %select_bitcast_fusion.23 = (bf16[1,1,8,2048]{3,2,1,0:T(8,128)(2,1)S(1)}, bf16[1,1,8,2048]{3,2,1,0:T(8,128)(2,1)S(1)}, bf16[1,1,8,2048]{3,2,1,0:T(8,128)(2,1)S(1)}, bf16[1,1,8,2048]{3,2,1,0:T(8,128)(2,1)S(1)}) fusion(bf16[1,8,2048]{2,1,0:T(8,128)(2,1)S(1)} %collective-permute-done.2, bf16[1,8,2048]{2,1,0:T(8,128)(2,1)S(1)} %collective-permute-done.3, ...), kind=kLoop, calls=%fused_computation.70 | loop fusion | flops 196608 | bytes 262156 | tf_op jit(solution)/shard_map/stack | solution.py:73
  13.0 1.6 %collective-permute-start.5 = (bf16[4,8,2048]{2,1,0:T(8,128)(2,1)S(1)}, bf16[4,8,2048]{2,1,0:T(8,128)(2,1)S(1)}, u32[]{:S(2)}, u32[]{:S(2)}) collective-permute-start(bf16[4,8,2048]{2,1,0:T(8,128)(2,1)S(1)} %maximum_bitcast_fusion.1), channel_id=1, source_target_pairs={{0,2},{1,3},{2,0},{3,1},{4,6},{5,7},{6,4},{7,5},{8,10},{9,11},{10,... | collective-permute-start | bytes 393224 | tf_op jit(solution)/shard_map/ppermute | solution.py:65
  14.6 0.8 %select_bitcast_fusion.19 = (bf16[1,1,8,4096]{3,2,1,0:T(8,128)(2,1)S(1)}, bf16[1,1,8,4096]{3,2,1,0:T(8,128)(2,1)S(1)}) fusion(bf16[1,8,4096]{2,1,0:T(8,128)(2,1)S(1)} %collective-permute-done, pred[]{:T(512)S(6)} %ne.16, bf16[8,2048]{1,0:T(8,128)(2,1)} %param.11, bf16[8,2048]{1,0:T(8,128)(2,1)} %param.10), kind=kLoop, calls=%fused_computation.47 | loop fusion | flops 196608 | bytes 262145 | tf_op jit(solution)/shard_map/stack | solution.py:39
  15.5 0.1 collective-permute-start.1
  15.6 2.5 %collective-permute-done.5 = bf16[4,8,2048]{2,1,0:T(8,128)(2,1)S(1)} collective-permute-done((bf16[4,8,2048]{2,1,0:T(8,128)(2,1)S(1)}, bf16[4,8,2048]{2,1,0:T(8,128)(2,1)S(1)}, u32[]{:S(2)}, u32[]{:S(2)}) %collective-permute-start.5) | collective-permute-done | bytes 131104 | tf_op jit(solution)/shard_map/ppermute | solution.py:65
  18.2 2.3 %collective-permute-done.1 = bf16[2,8,4096]{2,1,0:T(8,128)(2,1)S(1)} collective-permute-done((bf16[2,8,4096]{2,1,0:T(8,128)(2,1)S(1)}, bf16[2,8,4096]{2,1,0:T(8,128)(2,1)S(1)}, u32[]{:S(2)}, u32[]{:S(2)}) %collective-permute-start.1) | collective-permute-done | bytes 131104 | tf_op jit(solution)/shard_map/ppermute | solution.py:17
  20.7 0.8 %copy.20 = bf16[8,2,8,2048]{3,2,1,0:T(8,128)(2,1)} copy(bf16[8,2,8,2048]{3,2,0,1:T(8,128)(2,1)S(1)} %pad_maximum_fusion.1) | data formatting | bytes 1048576 | tf_op jit(solution)/shard_map/stack | solution.py:73
  21.5 0.7 %collective-permute-start.7 = (bf16[4,8,4096]{2,1,0:T(8,128)(2,1)S(1)}, bf16[4,8,4096]{2,1,0:T(8,128)(2,1)S(1)}, u32[]{:S(2)}, u32[]{:S(2)}) collective-permute-start(bf16[4,8,4096]{2,1,0:T(8,128)(2,1)S(1)} %bitcast.105), channel_id=1, source_target_pairs={{0,2},{1,3},{2,0},{3,1},{4,6},{5,7},{6,4},{7,5},{8,10},{9,11},{10,... | collective-permute-start | bytes 786440 | tf_op jit(solution)/shard_map/ppermute | solution.py:17
  22.2 3.3 %shard_map.78 = (f32[128,512]{1,0:T(8,128)}, f32[128,8]{1,0:T(8,128)}, f32[128,8]{1,0:T(8,128)}) custom-call(bf16[128,2048]{1,0:T(8,128)(2,1)} %bitcast.90, bf16[512,2048]{1,0:T(8,128)(2,1)} %key_ref.7, bf16[512,2048]{1,0:T(8,128)(2,1)} %value_ref.7), custom_call_target="tpu_custom_call" | custom-call | flops 268435456 | bytes 1441792 | tf_op jit(solution)/shard_map/pallas_call | solution.py:277
  25.6 3.4 %shard_map.77 = (f32[128,512]{1,0:T(8,128)}, f32[128,8]{1,0:T(8,128)}, f32[128,8]{1,0:T(8,128)}) custom-call(bf16[128,2048]{1,0:T(8,128)(2,1)} %bitcast.91, bf16[512,2048]{1,0:T(8,128)(2,1)} %key_ref.7, bf16[512,2048]{1,0:T(8,128)(2,1)} %value_ref.7), custom_call_target="tpu_custom_call" | custom-call | flops 268435456 | bytes 1441792 | tf_op jit(solution)/shard_map/pallas_call | solution.py:277
  28.9 0.1 collective-permute-done.7
  29.3 3.4 %shard_map.80 = (f32[128,512]{1,0:T(8,128)}, f32[128,8]{1,0:T(8,128)}, f32[128,8]{1,0:T(8,128)}) custom-call(bf16[128,2048]{1,0:T(8,128)(2,1)} %bitcast.92, bf16[512,2048]{1,0:T(8,128)(2,1)} %key_ref.7, bf16[512,2048]{1,0:T(8,128)(2,1)} %value_ref.7), custom_call_target="tpu_custom_call" | custom-call | flops 268435456 | bytes 1441792 | tf_op jit(solution)/shard_map/pallas_call | solution.py:277
  32.7 3.5 %shard_map.79 = (f32[128,512]{1,0:T(8,128)}, f32[128,8]{1,0:T(8,128)}, f32[128,8]{1,0:T(8,128)}) custom-call(bf16[128,2048]{1,0:T(8,128)(2,1)} %bitcast.93, bf16[512,2048]{1,0:T(8,128)(2,1)} %key_ref.7, bf16[512,2048]{1,0:T(8,128)(2,1)} %value_ref.7), custom_call_target="tpu_custom_call" | custom-call | flops 268435456 | bytes 1441792 | tf_op jit(solution)/shard_map/pallas_call | solution.py:277
  36.3 1.2 %concatenate.40 = f32[128,2112]{1,0:T(8,128)S(1)} concatenate(f32[128,512]{1,0:T(8,128)S(1)} %copy-done.1, f32[128,512]{1,0:T(8,128)S(1)} %copy-done, f32[128,512]{1,0:T(8,128)} %get-tuple-element.65, f32[128,512]{1,0:T(8,128)S(1)} %copy-done.2, f32[128,8]{1,0:T(8,128)S(1)} %copy-done.5, f32[128,8]{1,0:T(8,128)S(1)} %copy-done.3, f32[128,8]{1,0:T(8,128)} %get-tuple-element.69, ...), dimensions={1} | concatenate | bytes 2162688 | tf_op jit(solution)/shard_map/concatenate | solution.py:323
  37.8 0.1 pad_maximum_fusion
  38.0 0.1 concatenate.41
  38.1 0.5 collective-permute-start.9
  38.6 1.1 %fusion.30 = (bf16[128,2048]{1,0:T(8,128)(2,1)}, bf16[128,2048]{1,0:T(8,128)(2,1)}) fusion(bf16[128,4096]{1,0:T(8,128)(2,1)S(1)} %bitcast.95), kind=kLoop, calls=%fused_computation.127 | loop fusion | bytes 2097152 | tf_op jit(solution)/shard_map/slice | solution.py:322
  39.7 3.5 %shard_map.81.refs_0_ = bf16[512,2048]{1,0:T(8,128)(2,1)} custom-call(bf16[512,2048]{1,0:T(8,128)(2,1)} %query_ref.7, bf16[128,2048]{1,0:T(8,128)(2,1)} %get-tuple-element.108.key_ref, bf16[128,2048]{1,0:T(8,128)(2,1)} %get-tuple-element.107.value_ref), custom_call_target="tpu_custom_call" | custom-call | flops 268435456 | bytes 1310720 | tf_op jit(solution)/shard_map/pallas_call | solution.py:231
  43.5 0.3 broadcast_in_dim.35
  43.9 0.4 reshape.117
  44.2 0.3 broadcast_in_dim.36
  44.6 0.4 reshape.118
  44.9 0.1 fusion
  45.4 1.6 %collective-permute-start.10 = (bf16[4,8,2208]{2,1,0:T(8,128)(2,1)S(1)}, bf16[4,8,2208]{2,1,0:T(8,128)(2,1)S(1)}, u32[]{:S(2)}, u32[]{:S(2)}) collective-permute-start(bf16[4,8,2208]{2,1,0:T(8,128)(2,1)S(1)} %concatenate.44), channel_id=1, source_target_pairs={{0,2},{1,3},{2,0},{3,1},{4,6},{5,7},{6,4},{7,5},{8,10},{9,11},{10,... | collective-permute-start | bytes 423944 | tf_op jit(solution)/shard_map/ppermute | solution.py:17
  46.9 3.5 %shard_map.82.refs_0_ = bf16[512,2048]{1,0:T(8,128)(2,1)} custom-call(bf16[512,2048]{1,0:T(8,128)(2,1)} %query_ref.7, bf16[128,2048]{1,0:T(8,128)(2,1)} %get-tuple-element.108.key_ref, bf16[128,2048]{1,0:T(8,128)(2,1)} %get-tuple-element.107.value_ref, bf16[512,2048]{1,0:T(8,128)(2,1)} %shard_map.81.refs_0_), custom_call_target="tpu_custom_call", output_to_operand_aliasing={{}: (3, {})} | custom-call | flops 268435456 | bytes 1310720 | tf_op jit(solution)/shard_map/pallas_call | solution.py:231
  50.5 0.7 %collective-permute-done.10 = bf16[4,8,2208]{2,1,0:T(8,128)(2,1)S(1)} collective-permute-done((bf16[4,8,2208]{2,1,0:T(8,128)(2,1)S(1)}, bf16[4,8,2208]{2,1,0:T(8,128)(2,1)S(1)}, u32[]{:S(2)}, u32[]{:S(2)}) %collective-permute-start.10) | collective-permute-done | bytes 141344 | tf_op jit(solution)/shard_map/ppermute | solution.py:17
  51.5 0.2 broadcast_in_dim.37
  51.7 0.2 reshape.120
  51.9 0.2 broadcast_in_dim.38
  52.1 0.2 reshape.121
  52.6 3.5 %shard_map.83.refs_0_ = bf16[512,2048]{1,0:T(8,128)(2,1)} custom-call(bf16[512,2048]{1,0:T(8,128)(2,1)} %query_ref.7, bf16[128,2048]{1,0:T(8,128)(2,1)} %get-tuple-element.108.key_ref, bf16[128,2048]{1,0:T(8,128)(2,1)} %get-tuple-element.107.value_ref, bf16[512,2048]{1,0:T(8,128)(2,1)} %shard_map.82.refs_0_), custom_call_target="tpu_custom_call", output_to_operand_aliasing={{}: (3, {})} | custom-call | flops 268435456 | bytes 1310720 | tf_op jit(solution)/shard_map/pallas_call | solution.py:231
  56.2 0.8 %collective-permute-done.11 = bf16[2,8,2208]{2,1,0:T(8,128)(2,1)S(1)} collective-permute-done((bf16[2,8,2208]{2,1,0:T(8,128)(2,1)S(1)}, bf16[2,8,2208]{2,1,0:T(8,128)(2,1)S(1)}, u32[]{:S(2)}, u32[]{:S(2)}) %collective-permute-start.11) | collective-permute-done | bytes 70688 | tf_op jit(solution)/shard_map/ppermute | solution.py:17
  57.2 0.1 broadcast_in_dim.39
  57.3 0.1 reshape.123
  57.5 0.1 broadcast_in_dim.40
  57.6 0.1 reshape.124
  58.0 1.9 %collective-permute-start.12 = (bf16[1,8,2208]{2,1,0:T(8,128)(2,1)S(1)}, bf16[1,8,2208]{2,1,0:T(8,128)(2,1)S(1)}, u32[]{:S(2)}, u32[]{:S(2)}) collective-permute-start(bf16[1,8,2208]{2,1,0:T(8,128)(2,1)S(1)} %concatenate.50), channel_id=1, source_target_pairs={{0,8},{1,9},{2,10},{3,11},{4,12},{5,13},{6,14},{7,15},{8,0},{9,1},... | collective-permute-start | bytes 105992 | tf_op jit(solution)/shard_map/ppermute | solution.py:17
  59.9 3.5 %shard_map.84 = bf16[512,2048]{1,0:T(8,128)(2,1)} custom-call(bf16[512,2048]{1,0:T(8,128)(2,1)} %query_ref.7, bf16[128,2048]{1,0:T(8,128)(2,1)} %get-tuple-element.108.key_ref, bf16[128,2048]{1,0:T(8,128)(2,1)} %get-tuple-element.107.value_ref, bf16[512,2048]{1,0:T(8,128)(2,1)} %shard_map.83.refs_0_), custom_call_target="tpu_custom_call", output_to_operand_aliasing={{}: (3, {})} | custom-call | flops 268435456 | bytes 1310720 | tf_op jit(solution)/shard_map/pallas_call | solution.py:231
  63.7 0.1 broadcast_in_dim.43
  63.8 0.1 reshape.128
  64.0 0.1 reshape.126
  64.3 0.6 fusion.5
  (81 shorter events, 3.3 us)
Async XLA Ops:
  0.6 8.4 %collective-permute-start.4 = (bf16[1,8,2048]{2,1,0:T(8,128)(2,1)}, bf16[1,8,2048]{2,1,0:T(8,128)(2,1)S(1)}, u32[]{:S(2)}, u32[]{:S(2)}) collective-permute-start(bf16[1,8,2048]{2,1,0:T(8,128)(2,1)} %bitcast.112), channel_id=1, source_target_pairs={{0,8},{1,9},{2,10},{3,11},{4,12},{5,13},{6,14},{7,15},{8,0},{9,1},... | collective-permute-start | bytes 98312 | tf_op jit(solution)/shard_map/ppermute | solution.py:65
  4.7 4.3 %collective-permute-start.3 = (bf16[1,8,2048]{2,1,0:T(8,128)(2,1)}, bf16[1,8,2048]{2,1,0:T(8,128)(2,1)S(1)}, u32[]{:S(2)}, u32[]{:S(2)}) collective-permute-start(bf16[1,8,2048]{2,1,0:T(8,128)(2,1)} %bitcast.113), channel_id=1, source_target_pairs={{0,4},{1,5},{2,6},{3,7},{4,0},{5,1},{6,2},{7,3},{8,12},{9,13},{10,... | collective-permute-start | bytes 98312 | tf_op jit(solution)/shard_map/ppermute | solution.py:65
  6.3 5.9 %collective-permute-start.2 = (bf16[1,8,2048]{2,1,0:T(8,128)(2,1)}, bf16[1,8,2048]{2,1,0:T(8,128)(2,1)S(1)}, u32[]{:S(2)}, u32[]{:S(2)}) collective-permute-start(bf16[1,8,2048]{2,1,0:T(8,128)(2,1)} %bitcast.114), channel_id=1, source_target_pairs={{0,12},{1,13},{2,14},{3,15},{4,8},{5,9},{6,10},{7,11},{8,4},{9,5},... | collective-permute-start | bytes 98312 | tf_op jit(solution)/shard_map/ppermute | solution.py:65
  7.1 7.5 %collective-permute-start = (bf16[1,8,4096]{2,1,0:T(8,128)(2,1)S(1)}, bf16[1,8,4096]{2,1,0:T(8,128)(2,1)S(1)}, u32[]{:S(2)}, u32[]{:S(2)}) collective-permute-start(bf16[1,8,4096]{2,1,0:T(8,128)(2,1)S(1)} %maximum_bitcast_fusion.2), channel_id=1, source_target_pairs={{0,8},{1,9},{2,10},{3,11},{4,12},{5,13},{6,14},{7,15},{8,0},{9,1},... | collective-permute-start | bytes 196616 | tf_op jit(solution)/shard_map/ppermute | solution.py:17
  13.0 5.0 %collective-permute-start.5 = (bf16[4,8,2048]{2,1,0:T(8,128)(2,1)S(1)}, bf16[4,8,2048]{2,1,0:T(8,128)(2,1)S(1)}, u32[]{:S(2)}, u32[]{:S(2)}) collective-permute-start(bf16[4,8,2048]{2,1,0:T(8,128)(2,1)S(1)} %maximum_bitcast_fusion.1), channel_id=1, source_target_pairs={{0,2},{1,3},{2,0},{3,1},{4,6},{5,7},{6,4},{7,5},{8,10},{9,11},{10,... | collective-permute-start | bytes 393224 | tf_op jit(solution)/shard_map/ppermute | solution.py:65
  15.5 5.0 %collective-permute-start.1 = (bf16[2,8,4096]{2,1,0:T(8,128)(2,1)S(1)}, bf16[2,8,4096]{2,1,0:T(8,128)(2,1)S(1)}, u32[]{:S(2)}, u32[]{:S(2)}) collective-permute-start(bf16[2,8,4096]{2,1,0:T(8,128)(2,1)S(1)} %maximum_bitcast_fusion), channel_id=1, source_target_pairs={{0,4},{1,5},{2,6},{3,7},{4,0},{5,1},{6,2},{7,3},{8,12},{9,13},{10,... | collective-permute-start | bytes 393224 | tf_op jit(solution)/shard_map/ppermute | solution.py:17
  18.1 2.4 %collective-permute-start.6 = (bf16[8,8,2048]{2,1,0:T(8,128)(2,1)S(1)}, bf16[8,8,2048]{2,1,0:T(8,128)(2,1)S(1)}, u32[]{:S(2)}, u32[]{:S(2)}) collective-permute-start(bf16[8,8,2048]{2,1,0:T(8,128)(2,1)S(1)} %bitcast.104), channel_id=1, source_target_pairs={{0,1},{1,0},{2,3},{3,2},{4,5},{5,4},{6,7},{7,6},{8,9},{9,8},{10,11... | collective-permute-start | bytes 786440 | tf_op jit(solution)/shard_map/ppermute | solution.py:65
  21.5 7.5 %collective-permute-start.7 = (bf16[4,8,4096]{2,1,0:T(8,128)(2,1)S(1)}, bf16[4,8,4096]{2,1,0:T(8,128)(2,1)S(1)}, u32[]{:S(2)}, u32[]{:S(2)}) collective-permute-start(bf16[4,8,4096]{2,1,0:T(8,128)(2,1)S(1)} %bitcast.105), channel_id=1, source_target_pairs={{0,2},{1,3},{2,0},{3,1},{4,6},{5,7},{6,4},{7,5},{8,10},{9,11},{10,... | collective-permute-start | bytes 786440 | tf_op jit(solution)/shard_map/ppermute | solution.py:17
  29.2 7.0 %collective-permute-start.8 = (bf16[8,8,4096]{2,1,0:T(8,128)(2,1)S(1)}, bf16[8,8,4096]{2,1,0:T(8,128)(2,1)S(1)}, u32[]{:S(2)}, u32[]{:S(2)}) collective-permute-start(bf16[8,8,4096]{2,1,0:T(8,128)(2,1)S(1)} %bitcast.99), channel_id=1, source_target_pairs={{0,1},{1,0},{2,3},{3,2},{4,5},{5,4},{6,7},{7,6},{8,9},{9,8},{10,11... | collective-permute-start | bytes 1572872 | tf_op jit(solution)/shard_map/ppermute | solution.py:17
  32.6 3.5 %copy-start = (f32[128,512]{1,0:T(8,128)S(1)}, f32[128,512]{1,0:T(8,128)}, u32[]{:S(2)}) copy-start(f32[128,512]{1,0:T(8,128)} %get-tuple-element.55) | copy-start | bytes 786436
  32.6 3.5 %copy-start.1 = (f32[128,512]{1,0:T(8,128)S(1)}, f32[128,512]{1,0:T(8,128)}, u32[]{:S(2)}) copy-start(f32[128,512]{1,0:T(8,128)} %get-tuple-element.54) | copy-start | bytes 786436
  32.6 3.5 %copy-start.2 = (f32[128,512]{1,0:T(8,128)S(1)}, f32[128,512]{1,0:T(8,128)}, u32[]{:S(2)}) copy-start(f32[128,512]{1,0:T(8,128)} %get-tuple-element.66) | copy-start | bytes 786436
  32.6 3.6 %copy-start.3 = (f32[128,8]{1,0:T(8,128)S(1)}, f32[128,8]{1,0:T(8,128)}, u32[]{:S(2)}) copy-start(f32[128,8]{1,0:T(8,128)} %get-tuple-element.68) | copy-start | bytes 12292
  32.7 3.6 %copy-start.4 = (f32[128,8]{1,0:T(8,128)S(1)}, f32[128,8]{1,0:T(8,128)}, u32[]{:S(2)}) copy-start(f32[128,8]{1,0:T(8,128)} %get-tuple-element.72) | copy-start | bytes 12292
  32.7 3.6 %copy-start.5 = (f32[128,8]{1,0:T(8,128)S(1)}, f32[128,8]{1,0:T(8,128)}, u32[]{:S(2)}) copy-start(f32[128,8]{1,0:T(8,128)} %get-tuple-element.67) | copy-start | bytes 12292
  32.7 3.6 %copy-start.6 = (f32[128,8]{1,0:T(8,128)S(1)}, f32[128,8]{1,0:T(8,128)}, u32[]{:S(2)}) copy-start(f32[128,8]{1,0:T(8,128)} %get-tuple-element.71) | copy-start | bytes 12292
  32.7 3.6 %copy-start.7 = (f32[128,8]{1,0:T(8,128)S(1)}, f32[128,8]{1,0:T(8,128)}, u32[]{:S(2)}) copy-start(f32[128,8]{1,0:T(8,128)} %get-tuple-element.70) | copy-start | bytes 12292
  32.7 3.6 %copy-start.8 = (f32[128,8]{1,0:T(8,128)S(1)}, f32[128,8]{1,0:T(8,128)}, u32[]{:S(2)}) copy-start(f32[128,8]{1,0:T(8,128)} %get-tuple-element.74) | copy-start | bytes 12292
  38.1 5.1 %collective-permute-start.9 = (bf16[8,8,2208]{2,1,0:T(8,128)(2,1)S(1)}, bf16[8,8,2208]{2,1,0:T(8,128)(2,1)S(1)}, u32[]{:S(2)}, u32[]{:S(2)}) collective-permute-start(bf16[8,8,2208]{2,1,0:T(8,128)(2,1)S(1)} %concatenate.41), channel_id=1, source_target_pairs={{0,1},{1,0},{2,3},{3,2},{4,5},{5,4},{6,7},{7,6},{8,9},{9,8},{10,11... | collective-permute-start | bytes 847880 | tf_op jit(solution)/shard_map/ppermute | solution.py:17
  45.4 5.8 %collective-permute-start.10 = (bf16[4,8,2208]{2,1,0:T(8,128)(2,1)S(1)}, bf16[4,8,2208]{2,1,0:T(8,128)(2,1)S(1)}, u32[]{:S(2)}, u32[]{:S(2)}) collective-permute-start(bf16[4,8,2208]{2,1,0:T(8,128)(2,1)S(1)} %concatenate.44), channel_id=1, source_target_pairs={{0,2},{1,3},{2,0},{3,1},{4,6},{5,7},{6,4},{7,5},{8,10},{9,11},{10,... | collective-permute-start | bytes 423944 | tf_op jit(solution)/shard_map/ppermute | solution.py:17
  52.6 4.4 %collective-permute-start.11 = (bf16[2,8,2208]{2,1,0:T(8,128)(2,1)S(1)}, bf16[2,8,2208]{2,1,0:T(8,128)(2,1)S(1)}, u32[]{:S(2)}, u32[]{:S(2)}) collective-permute-start(bf16[2,8,2208]{2,1,0:T(8,128)(2,1)S(1)} %concatenate.47), channel_id=1, source_target_pairs={{0,4},{1,5},{2,6},{3,7},{4,0},{5,1},{6,2},{7,3},{8,12},{9,13},{10,... | collective-permute-start | bytes 211976 | tf_op jit(solution)/shard_map/ppermute | solution.py:17
  58.0 5.4 %collective-permute-start.12 = (bf16[1,8,2208]{2,1,0:T(8,128)(2,1)S(1)}, bf16[1,8,2208]{2,1,0:T(8,128)(2,1)S(1)}, u32[]{:S(2)}, u32[]{:S(2)}) collective-permute-start(bf16[1,8,2208]{2,1,0:T(8,128)(2,1)S(1)} %concatenate.50), channel_id=1, source_target_pairs={{0,8},{1,9},{2,10},{3,11},{4,12},{5,13},{6,14},{7,15},{8,0},{9,1},... | collective-permute-start | bytes 105992 | tf_op jit(solution)/shard_map/ppermute | solution.py:17

commit v12 on v11

--- a/solution.py
+++ b/solution.py
@@ -9,7 +9,13 @@
 
 
 def spread(scales):
-    return jnp.repeat(scales, HEAD_DIM, axis=1)
+    heads = scales.shape[1]
+    shape = (heads, heads * HEAD_DIM)
+    columns = lax.broadcasted_iota(jnp.int32, shape, 1) // HEAD_DIM
+    expand = (columns == lax.broadcasted_iota(jnp.int32, shape, 0)).astype(jnp.float32)
+    return jnp.dot(
+        scales, expand, precision=lax.Precision.HIGHEST, preferred_element_type=jnp.float32
+    )
 
 
 def exchange(value, bit, count):

time: 65.4 us -> 64.8 us (level)
  matrix products: 0 us -> 3.45 us
  local copies, waits for them, and re-layouts: 7.47 us -> 4.28 us
  other arithmetic: 4.91 us -> 4.01 us
    dot_general x0 -> x9, matrix products: none -> 3.45 us  [spread(): jnp.dot(scales, expand, precision=lax.Precision.HIGHEST, preferred_elemen...]
    reshape x9 -> x0, local copies, waits for them, and re-layouts: 1.62 us -> none  [spread(): return jnp.repeat(scales, HEAD_DIM, axis=1)]
    broadcast_in_dim x9 -> x0, local copies, waits for them, and re-layouts: 1.57 us -> none  [spread(): return jnp.repeat(scales, HEAD_DIM, axis=1)]
  transfers between devices with their start and end apart: 13 -> 13, of which waited for: 6 -> 6; matrix products, arithmetic and copies ran while one was open for 5% -> 6% of each run, Pallas kernels for 43% -> 43%
where the time goes in v12:
time: 64.8 us; the launch traced here: 64.3 us
  Pallas kernels  27.6 us (43%)
  starting transfers between devices  14.2 us (22%)
  waiting for transfers between devices  9.66 us (15%)
  local copies, waits for them, and re-layouts  4.28 us (7%)
  other arithmetic  4.01 us (6%)
  matrix products  3.45 us (5%)
  between operations  1.07 us (2%)
    pallas_call x4, Pallas kernels, video_part(): pl.pallas_call(video_kernel, grid=(pairs // PER_STEP,), in_specs=specs, o...  14.1 us
    pallas_call x4, Pallas kernels, audio_partial(): pl.pallas_call(audio_kernel, grid=(heads // 2 // PER_STEP,), in_specs=[pl...  13.5 us
    ppermute x5, starting transfers between devices, gather_levels(): pieces[offset] = lax.ppermute(held, 'seq', pairs)  7.34 us
    ppermute x8, starting transfers between devices, exchange(): return lax.ppermute(value, 'seq', pairs)  6.84 us
    ppermute x5, waiting for transfers between devices, gather_levels(): pieces[offset] = lax.ppermute(held, 'seq', pairs)  5.74 us
    ppermute x8, waiting for transfers between devices, exchange(): return lax.ppermute(value, 'seq', pairs)  3.92 us
    dot_general x9, matrix products, spread(): jnp.dot(scales, expand, precision=lax.Precision.HIGHEST, preferred_elemen...  3.45 us
  transfers between devices with their start and end apart: 13, of which 6 were waited for; matrix products, arithmetic and copies ran while one was open for 6% of the time, Pallas kernels for 43%

profile of v12, /device:TPU:0, one launch (start us, length us, event | category | flops | bytes accessed | tf_op | source)
XLA Modules:
  0.0 64.3 jit_solution(17142142665845882801)
XLA Ops:
  0.6 4.1 %collective-permute-start.4 = (bf16[1,8,2048]{2,1,0:T(8,128)(2,1)}, bf16[1,8,2048]{2,1,0:T(8,128)(2,1)S(1)}, u32[]{:S(2)}, u32[]{:S(2)}) collective-permute-start(bf16[1,8,2048]{2,1,0:T(8,128)(2,1)} %bitcast.113), channel_id=1, source_target_pairs={{0,8},{1,9},{2,10},{3,11},{4,12},{5,13},{6,14},{7,15},{8,0},{9,1},... | collective-permute-start | bytes 98312 | tf_op jit(solution)/shard_map/ppermute | solution.py:71
  4.7 1.6 %collective-permute-start.3 = (bf16[1,8,2048]{2,1,0:T(8,128)(2,1)}, bf16[1,8,2048]{2,1,0:T(8,128)(2,1)S(1)}, u32[]{:S(2)}, u32[]{:S(2)}) collective-permute-start(bf16[1,8,2048]{2,1,0:T(8,128)(2,1)} %bitcast.114), channel_id=1, source_target_pairs={{0,4},{1,5},{2,6},{3,7},{4,0},{5,1},{6,2},{7,3},{8,12},{9,13},{10,... | collective-permute-start | bytes 98312 | tf_op jit(solution)/shard_map/ppermute | solution.py:71
  6.3 0.8 %maximum_bitcast_fusion.2 = bf16[1,8,4096]{2,1,0:T(8,128)(2,1)S(1)} fusion(bf16[8,2048]{1,0:T(8,128)(2,1)} %param.11, bf16[8,2048]{1,0:T(8,128)(2,1)} %param.10), kind=kLoop, calls=%fused_computation.74 | loop fusion | flops 131072 | bytes 131072 | tf_op jit(solution)/shard_map/broadcast_in_dim | solution.py:29
  7.1 1.9 %collective-permute-start = (bf16[1,8,4096]{2,1,0:T(8,128)(2,1)S(1)}, bf16[1,8,4096]{2,1,0:T(8,128)(2,1)S(1)}, u32[]{:S(2)}, u32[]{:S(2)}) collective-permute-start(bf16[1,8,4096]{2,1,0:T(8,128)(2,1)S(1)} %maximum_bitcast_fusion.2), channel_id=1, source_target_pairs={{0,8},{1,9},{2,10},{3,11},{4,12},{5,13},{6,14},{7,15},{8,0},{9,1},... | collective-permute-start | bytes 196616 | tf_op jit(solution)/shard_map/ppermute | solution.py:23
  9.0 3.2 %collective-permute-done.2 = bf16[1,8,2048]{2,1,0:T(8,128)(2,1)S(1)} collective-permute-done((bf16[1,8,2048]{2,1,0:T(8,128)(2,1)}, bf16[1,8,2048]{2,1,0:T(8,128)(2,1)S(1)}, u32[]{:S(2)}, u32[]{:S(2)}) %collective-permute-start.2) | collective-permute-done | bytes 32800 | tf_op jit(solution)/shard_map/ppermute | solution.py:71
  12.2 0.8 %select_bitcast_fusion.23 = (bf16[1,1,8,2048]{3,2,1,0:T(8,128)(2,1)S(1)}, bf16[1,1,8,2048]{3,2,1,0:T(8,128)(2,1)S(1)}, bf16[1,1,8,2048]{3,2,1,0:T(8,128)(2,1)S(1)}, bf16[1,1,8,2048]{3,2,1,0:T(8,128)(2,1)S(1)}) fusion(bf16[1,8,2048]{2,1,0:T(8,128)(2,1)S(1)} %collective-permute-done.2, bf16[1,8,2048]{2,1,0:T(8,128)(2,1)S(1)} %collective-permute-done.3, ...), kind=kLoop, calls=%fused_computation.98 | loop fusion | flops 196608 | bytes 262156 | tf_op jit(solution)/shard_map/stack | solution.py:79
  13.0 1.6 %collective-permute-start.5 = (bf16[4,8,2048]{2,1,0:T(8,128)(2,1)S(1)}, bf16[4,8,2048]{2,1,0:T(8,128)(2,1)S(1)}, u32[]{:S(2)}, u32[]{:S(2)}) collective-permute-start(bf16[4,8,2048]{2,1,0:T(8,128)(2,1)S(1)} %maximum_bitcast_fusion.1), channel_id=1, source_target_pairs={{0,2},{1,3},{2,0},{3,1},{4,6},{5,7},{6,4},{7,5},{8,10},{9,11},{10,... | collective-permute-start | bytes 393224 | tf_op jit(solution)/shard_map/ppermute | solution.py:71
  14.6 0.8 %select_bitcast_fusion.19 = (bf16[1,1,8,4096]{3,2,1,0:T(8,128)(2,1)S(1)}, bf16[1,1,8,4096]{3,2,1,0:T(8,128)(2,1)S(1)}) fusion(bf16[1,8,4096]{2,1,0:T(8,128)(2,1)S(1)} %collective-permute-done, pred[]{:T(512)S(6)} %ne.98, bf16[8,2048]{1,0:T(8,128)(2,1)} %param.11, bf16[8,2048]{1,0:T(8,128)(2,1)} %param.10), kind=kLoop, calls=%fused_computation.76 | loop fusion | flops 196608 | bytes 262145 | tf_op jit(solution)/shard_map/stack | solution.py:45
  15.5 0.1 collective-permute-start.1
  15.6 2.5 %collective-permute-done.5 = bf16[4,8,2048]{2,1,0:T(8,128)(2,1)S(1)} collective-permute-done((bf16[4,8,2048]{2,1,0:T(8,128)(2,1)S(1)}, bf16[4,8,2048]{2,1,0:T(8,128)(2,1)S(1)}, u32[]{:S(2)}, u32[]{:S(2)}) %collective-permute-start.5) | collective-permute-done | bytes 131104 | tf_op jit(solution)/shard_map/ppermute | solution.py:71
  18.2 2.3 %collective-permute-done.1 = bf16[2,8,4096]{2,1,0:T(8,128)(2,1)S(1)} collective-permute-done((bf16[2,8,4096]{2,1,0:T(8,128)(2,1)S(1)}, bf16[2,8,4096]{2,1,0:T(8,128)(2,1)S(1)}, u32[]{:S(2)}, u32[]{:S(2)}) %collective-permute-start.1) | collective-permute-done | bytes 131104 | tf_op jit(solution)/shard_map/ppermute | solution.py:23
  20.7 0.8 %copy.20 = bf16[8,2,8,2048]{3,2,1,0:T(8,128)(2,1)} copy(bf16[8,2,8,2048]{3,2,0,1:T(8,128)(2,1)S(1)} %pad_maximum_fusion.1) | data formatting | bytes 1048576 | tf_op jit(solution)/shard_map/stack | solution.py:79
  21.5 0.7 %collective-permute-start.7 = (bf16[4,8,4096]{2,1,0:T(8,128)(2,1)S(1)}, bf16[4,8,4096]{2,1,0:T(8,128)(2,1)S(1)}, u32[]{:S(2)}, u32[]{:S(2)}) collective-permute-start(bf16[4,8,4096]{2,1,0:T(8,128)(2,1)S(1)} %bitcast.101), channel_id=1, source_target_pairs={{0,2},{1,3},{2,0},{3,1},{4,6},{5,7},{6,4},{7,5},{8,10},{9,11},{10,... | collective-permute-start | bytes 786440 | tf_op jit(solution)/shard_map/ppermute | solution.py:23
  22.2 3.3 %shard_map.78 = (f32[128,512]{1,0:T(8,128)}, f32[128,8]{1,0:T(8,128)}, f32[128,8]{1,0:T(8,128)}) custom-call(bf16[128,2048]{1,0:T(8,128)(2,1)} %bitcast.90, bf16[512,2048]{1,0:T(8,128)(2,1)} %key_ref.7, bf16[512,2048]{1,0:T(8,128)(2,1)} %value_ref.7), custom_call_target="tpu_custom_call" | custom-call | flops 268435456 | bytes 1441792 | tf_op jit(solution)/shard_map/pallas_call | solution.py:283
  25.6 3.4 %shard_map.77 = (f32[128,512]{1,0:T(8,128)}, f32[128,8]{1,0:T(8,128)}, f32[128,8]{1,0:T(8,128)}) custom-call(bf16[128,2048]{1,0:T(8,128)(2,1)} %bitcast.91, bf16[512,2048]{1,0:T(8,128)(2,1)} %key_ref.7, bf16[512,2048]{1,0:T(8,128)(2,1)} %value_ref.7), custom_call_target="tpu_custom_call" | custom-call | flops 268435456 | bytes 1441792 | tf_op jit(solution)/shard_map/pallas_call | solution.py:283
  28.9 0.1 collective-permute-done.7
  29.3 3.4 %shard_map.80 = (f32[128,512]{1,0:T(8,128)}, f32[128,8]{1,0:T(8,128)}, f32[128,8]{1,0:T(8,128)}) custom-call(bf16[128,2048]{1,0:T(8,128)(2,1)} %bitcast.92, bf16[512,2048]{1,0:T(8,128)(2,1)} %key_ref.7, bf16[512,2048]{1,0:T(8,128)(2,1)} %value_ref.7), custom_call_target="tpu_custom_call" | custom-call | flops 268435456 | bytes 1441792 | tf_op jit(solution)/shard_map/pallas_call | solution.py:283
  32.7 3.5 %shard_map.79 = (f32[128,512]{1,0:T(8,128)}, f32[128,8]{1,0:T(8,128)}, f32[128,8]{1,0:T(8,128)}) custom-call(bf16[128,2048]{1,0:T(8,128)(2,1)} %bitcast.93, bf16[512,2048]{1,0:T(8,128)(2,1)} %key_ref.7, bf16[512,2048]{1,0:T(8,128)(2,1)} %value_ref.7), custom_call_target="tpu_custom_call" | custom-call | flops 268435456 | bytes 1441792 | tf_op jit(solution)/shard_map/pallas_call | solution.py:283
  36.3 1.2 %concatenate.40 = f32[128,2112]{1,0:T(8,128)S(1)} concatenate(f32[128,512]{1,0:T(8,128)S(1)} %copy-done.1, f32[128,512]{1,0:T(8,128)S(1)} %copy-done, f32[128,512]{1,0:T(8,128)} %get-tuple-element.65, f32[128,512]{1,0:T(8,128)S(1)} %copy-done.2, f32[128,8]{1,0:T(8,128)S(1)} %copy-done.5, f32[128,8]{1,0:T(8,128)S(1)} %copy-done.3, f32[128,8]{1,0:T(8,128)} %get-tuple-element.69, ...), dimensions={1} | concatenate | bytes 2162688 | tf_op jit(solution)/shard_map/concatenate | solution.py:329
  37.6 0.1 fusion.35
  37.8 0.1 pad_maximum_fusion
  37.9 0.1 copy.22
  38.0 0.1 concatenate.41
  38.1 0.6 collective-permute-start.9
  38.7 1.1 %fusion.62 = (bf16[128,2048]{1,0:T(8,128)(2,1)}, bf16[128,2048]{1,0:T(8,128)(2,1)}) fusion(bf16[128,4096]{1,0:T(8,128)(2,1)S(1)} %bitcast.95), kind=kLoop, calls=%fused_computation.162 | loop fusion | bytes 2097152 | tf_op jit(solution)/shard_map/slice | solution.py:328
  39.7 3.5 %shard_map.81.refs_0_ = bf16[512,2048]{1,0:T(8,128)(2,1)} custom-call(bf16[512,2048]{1,0:T(8,128)(2,1)} %query_ref.7, bf16[128,2048]{1,0:T(8,128)(2,1)} %get-tuple-element.99.key_ref, bf16[128,2048]{1,0:T(8,128)(2,1)} %get-tuple-element.98.value_ref), custom_call_target="tpu_custom_call" | custom-call | flops 268435456 | bytes 1310720 | tf_op jit(solution)/shard_map/pallas_call | solution.py:237
  43.4 0.1 concatenate.42
  43.5 0.1 fusion.36
  43.6 0.4 convolution_multiply_fusion.1
  44.0 0.4 fusion
  44.7 0.1 concatenate.44
  44.8 1.6 %collective-permute-start.10 = (bf16[4,8,2208]{2,1,0:T(8,128)(2,1)S(1)}, bf16[4,8,2208]{2,1,0:T(8,128)(2,1)S(1)}, u32[]{:S(2)}, u32[]{:S(2)}) collective-permute-start(bf16[4,8,2208]{2,1,0:T(8,128)(2,1)S(1)} %concatenate.44), channel_id=1, source_target_pairs={{0,2},{1,3},{2,0},{3,1},{4,6},{5,7},{6,4},{7,5},{8,10},{9,11},{10,... | collective-permute-start | bytes 423944 | tf_op jit(solution)/shard_map/ppermute | solution.py:23
  46.4 3.5 %shard_map.82.refs_0_ = bf16[512,2048]{1,0:T(8,128)(2,1)} custom-call(bf16[512,2048]{1,0:T(8,128)(2,1)} %query_ref.7, bf16[128,2048]{1,0:T(8,128)(2,1)} %get-tuple-element.99.key_ref, bf16[128,2048]{1,0:T(8,128)(2,1)} %get-tuple-element.98.value_ref, bf16[512,2048]{1,0:T(8,128)(2,1)} %shard_map.81.refs_0_), custom_call_target="tpu_custom_call", output_to_operand_aliasing={{}: (3, {})} | custom-call | flops 268435456 | bytes 1310720 | tf_op jit(solution)/shard_map/pallas_call | solution.py:237
  49.9 0.7 %collective-permute-done.10 = bf16[4,8,2208]{2,1,0:T(8,128)(2,1)S(1)} collective-permute-done((bf16[4,8,2208]{2,1,0:T(8,128)(2,1)S(1)}, bf16[4,8,2208]{2,1,0:T(8,128)(2,1)S(1)}, u32[]{:S(2)}, u32[]{:S(2)}) %collective-permute-start.10) | collective-permute-done | bytes 141344 | tf_op jit(solution)/shard_map/ppermute | solution.py:23
  50.8 0.1 fusion.41
  50.9 0.3 convolution_multiply_fusion.2
  51.2 0.3 fusion.1
  51.8 0.1 concatenate.47
  51.9 3.5 %shard_map.83.refs_0_ = bf16[512,2048]{1,0:T(8,128)(2,1)} custom-call(bf16[512,2048]{1,0:T(8,128)(2,1)} %query_ref.7, bf16[128,2048]{1,0:T(8,128)(2,1)} %get-tuple-element.99.key_ref, bf16[128,2048]{1,0:T(8,128)(2,1)} %get-tuple-element.98.value_ref, bf16[512,2048]{1,0:T(8,128)(2,1)} %shard_map.82.refs_0_), custom_call_target="tpu_custom_call", output_to_operand_aliasing={{}: (3, {})} | custom-call | flops 268435456 | bytes 1310720 | tf_op jit(solution)/shard_map/pallas_call | solution.py:237
  55.4 0.8 %collective-permute-done.11 = bf16[2,8,2208]{2,1,0:T(8,128)(2,1)S(1)} collective-permute-done((bf16[2,8,2208]{2,1,0:T(8,128)(2,1)S(1)}, bf16[2,8,2208]{2,1,0:T(8,128)(2,1)S(1)}, u32[]{:S(2)}, u32[]{:S(2)}) %collective-permute-start.11) | collective-permute-done | bytes 70688 | tf_op jit(solution)/shard_map/ppermute | solution.py:23
  56.5 0.3 convolution_multiply_fusion.5
  56.7 0.3 fusion.2
  57.2 0.1 concatenate.50
  57.3 1.9 %collective-permute-start.12 = (bf16[1,8,2208]{2,1,0:T(8,128)(2,1)S(1)}, bf16[1,8,2208]{2,1,0:T(8,128)(2,1)S(1)}, u32[]{:S(2)}, u32[]{:S(2)}) collective-permute-start(bf16[1,8,2208]{2,1,0:T(8,128)(2,1)S(1)} %concatenate.50), channel_id=1, source_target_pairs={{0,8},{1,9},{2,10},{3,11},{4,12},{5,13},{6,14},{7,15},{8,0},{9,1},... | collective-permute-start | bytes 105992 | tf_op jit(solution)/shard_map/ppermute | solution.py:23
  59.2 3.5 %shard_map.84 = bf16[512,2048]{1,0:T(8,128)(2,1)} custom-call(bf16[512,2048]{1,0:T(8,128)(2,1)} %query_ref.7, bf16[128,2048]{1,0:T(8,128)(2,1)} %get-tuple-element.99.key_ref, bf16[128,2048]{1,0:T(8,128)(2,1)} %get-tuple-element.98.value_ref, bf16[512,2048]{1,0:T(8,128)(2,1)} %shard_map.83.refs_0_), custom_call_target="tpu_custom_call", output_to_operand_aliasing={{}: (3, {})} | custom-call | flops 268435456 | bytes 1310720 | tf_op jit(solution)/shard_map/pallas_call | solution.py:237
  62.9 0.2 convolution_multiply_fusion.7
  63.1 0.3 fusion.3
  63.4 0.9 %fusion.4 = bf16[8,2048]{1,0:T(8,128)(2,1)} fusion(f32[8,2048]{1,0:T(8,128)S(1)} %fusion.3, s32[2048]{0:T(1024)S(1)} %get-tuple-element.150, s32[2048]{0:T(1024)S(1)} %get-tuple-element.151, pred[2048]{0:T(1024)(128)(4,1)S(1)} %fusion.49, f32[8,2112]{1,0:T(8,128)S(1)} %bitcast.112, f32[8,2112]{1,0:T(8,128)S(1)} %get-tuple-element.128), kind=kOutput, calls=%fused_computation.13 | convolution fusion | flops 6456832 | bytes 133120 | tf_op jit(solution)/shard_map/dot_general | solution.py:16
  (69 shorter events, 2.1 us)
Async XLA Ops:
  0.6 8.4 %collective-permute-start.4 = (bf16[1,8,2048]{2,1,0:T(8,128)(2,1)}, bf16[1,8,2048]{2,1,0:T(8,128)(2,1)S(1)}, u32[]{:S(2)}, u32[]{:S(2)}) collective-permute-start(bf16[1,8,2048]{2,1,0:T(8,128)(2,1)} %bitcast.113), channel_id=1, source_target_pairs={{0,8},{1,9},{2,10},{3,11},{4,12},{5,13},{6,14},{7,15},{8,0},{9,1},... | collective-permute-start | bytes 98312 | tf_op jit(solution)/shard_map/ppermute | solution.py:71
  4.7 4.3 %collective-permute-start.3 = (bf16[1,8,2048]{2,1,0:T(8,128)(2,1)}, bf16[1,8,2048]{2,1,0:T(8,128)(2,1)S(1)}, u32[]{:S(2)}, u32[]{:S(2)}) collective-permute-start(bf16[1,8,2048]{2,1,0:T(8,128)(2,1)} %bitcast.114), channel_id=1, source_target_pairs={{0,4},{1,5},{2,6},{3,7},{4,0},{5,1},{6,2},{7,3},{8,12},{9,13},{10,... | collective-permute-start | bytes 98312 | tf_op jit(solution)/shard_map/ppermute | solution.py:71
  6.3 5.9 %collective-permute-start.2 = (bf16[1,8,2048]{2,1,0:T(8,128)(2,1)}, bf16[1,8,2048]{2,1,0:T(8,128)(2,1)S(1)}, u32[]{:S(2)}, u32[]{:S(2)}) collective-permute-start(bf16[1,8,2048]{2,1,0:T(8,128)(2,1)} %bitcast.115), channel_id=1, source_target_pairs={{0,12},{1,13},{2,14},{3,15},{4,8},{5,9},{6,10},{7,11},{8,4},{9,5},... | collective-permute-start | bytes 98312 | tf_op jit(solution)/shard_map/ppermute | solution.py:71
  7.1 7.5 %collective-permute-start = (bf16[1,8,4096]{2,1,0:T(8,128)(2,1)S(1)}, bf16[1,8,4096]{2,1,0:T(8,128)(2,1)S(1)}, u32[]{:S(2)}, u32[]{:S(2)}) collective-permute-start(bf16[1,8,4096]{2,1,0:T(8,128)(2,1)S(1)} %maximum_bitcast_fusion.2), channel_id=1, source_target_pairs={{0,8},{1,9},{2,10},{3,11},{4,12},{5,13},{6,14},{7,15},{8,0},{9,1},... | collective-permute-start | bytes 196616 | tf_op jit(solution)/shard_map/ppermute | solution.py:23
  13.0 5.0 %collective-permute-start.5 = (bf16[4,8,2048]{2,1,0:T(8,128)(2,1)S(1)}, bf16[4,8,2048]{2,1,0:T(8,128)(2,1)S(1)}, u32[]{:S(2)}, u32[]{:S(2)}) collective-permute-start(bf16[4,8,2048]{2,1,0:T(8,128)(2,1)S(1)} %maximum_bitcast_fusion.1), channel_id=1, source_target_pairs={{0,2},{1,3},{2,0},{3,1},{4,6},{5,7},{6,4},{7,5},{8,10},{9,11},{10,... | collective-permute-start | bytes 393224 | tf_op jit(solution)/shard_map/ppermute | solution.py:71
  15.5 5.0 %collective-permute-start.1 = (bf16[2,8,4096]{2,1,0:T(8,128)(2,1)S(1)}, bf16[2,8,4096]{2,1,0:T(8,128)(2,1)S(1)}, u32[]{:S(2)}, u32[]{:S(2)}) collective-permute-start(bf16[2,8,4096]{2,1,0:T(8,128)(2,1)S(1)} %maximum_bitcast_fusion), channel_id=1, source_target_pairs={{0,4},{1,5},{2,6},{3,7},{4,0},{5,1},{6,2},{7,3},{8,12},{9,13},{10,... | collective-permute-start | bytes 393224 | tf_op jit(solution)/shard_map/ppermute | solution.py:23
  18.1 2.4 %collective-permute-start.6 = (bf16[8,8,2048]{2,1,0:T(8,128)(2,1)S(1)}, bf16[8,8,2048]{2,1,0:T(8,128)(2,1)S(1)}, u32[]{:S(2)}, u32[]{:S(2)}) collective-permute-start(bf16[8,8,2048]{2,1,0:T(8,128)(2,1)S(1)} %bitcast.100), channel_id=1, source_target_pairs={{0,1},{1,0},{2,3},{3,2},{4,5},{5,4},{6,7},{7,6},{8,9},{9,8},{10,11... | collective-permute-start | bytes 786440 | tf_op jit(solution)/shard_map/ppermute | solution.py:71
  21.5 7.5 %collective-permute-start.7 = (bf16[4,8,4096]{2,1,0:T(8,128)(2,1)S(1)}, bf16[4,8,4096]{2,1,0:T(8,128)(2,1)S(1)}, u32[]{:S(2)}, u32[]{:S(2)}) collective-permute-start(bf16[4,8,4096]{2,1,0:T(8,128)(2,1)S(1)} %bitcast.101), channel_id=1, source_target_pairs={{0,2},{1,3},{2,0},{3,1},{4,6},{5,7},{6,4},{7,5},{8,10},{9,11},{10,... | collective-permute-start | bytes 786440 | tf_op jit(solution)/shard_map/ppermute | solution.py:23
  29.2 7.0 %collective-permute-start.8 = (bf16[8,8,4096]{2,1,0:T(8,128)(2,1)S(1)}, bf16[8,8,4096]{2,1,0:T(8,128)(2,1)S(1)}, u32[]{:S(2)}, u32[]{:S(2)}) collective-permute-start(bf16[8,8,4096]{2,1,0:T(8,128)(2,1)S(1)} %bitcast.97), channel_id=1, source_target_pairs={{0,1},{1,0},{2,3},{3,2},{4,5},{5,4},{6,7},{7,6},{8,9},{9,8},{10,11... | collective-permute-start | bytes 1572872 | tf_op jit(solution)/shard_map/ppermute | solution.py:23
  32.7 3.5 %copy-start = (f32[128,512]{1,0:T(8,128)S(1)}, f32[128,512]{1,0:T(8,128)}, u32[]{:S(2)}) copy-start(f32[128,512]{1,0:T(8,128)} %get-tuple-element.55) | copy-start | bytes 786436
  32.7 3.5 %copy-start.1 = (f32[128,512]{1,0:T(8,128)S(1)}, f32[128,512]{1,0:T(8,128)}, u32[]{:S(2)}) copy-start(f32[128,512]{1,0:T(8,128)} %get-tuple-element.54) | copy-start | bytes 786436
  32.7 3.5 %copy-start.2 = (f32[128,512]{1,0:T(8,128)S(1)}, f32[128,512]{1,0:T(8,128)}, u32[]{:S(2)}) copy-start(f32[128,512]{1,0:T(8,128)} %get-tuple-element.66) | copy-start | bytes 786436
  32.7 3.6 %copy-start.3 = (f32[128,8]{1,0:T(8,128)S(1)}, f32[128,8]{1,0:T(8,128)}, u32[]{:S(2)}) copy-start(f32[128,8]{1,0:T(8,128)} %get-tuple-element.68) | copy-start | bytes 12292
  32.7 3.6 %copy-start.4 = (f32[128,8]{1,0:T(8,128)S(1)}, f32[128,8]{1,0:T(8,128)}, u32[]{:S(2)}) copy-start(f32[128,8]{1,0:T(8,128)} %get-tuple-element.72) | copy-start | bytes 12292
  32.7 3.6 %copy-start.5 = (f32[128,8]{1,0:T(8,128)S(1)}, f32[128,8]{1,0:T(8,128)}, u32[]{:S(2)}) copy-start(f32[128,8]{1,0:T(8,128)} %get-tuple-element.67) | copy-start | bytes 12292
  32.7 3.6 %copy-start.6 = (f32[128,8]{1,0:T(8,128)S(1)}, f32[128,8]{1,0:T(8,128)}, u32[]{:S(2)}) copy-start(f32[128,8]{1,0:T(8,128)} %get-tuple-element.71) | copy-start | bytes 12292
  32.7 3.6 %copy-start.7 = (f32[128,8]{1,0:T(8,128)S(1)}, f32[128,8]{1,0:T(8,128)}, u32[]{:S(2)}) copy-start(f32[128,8]{1,0:T(8,128)} %get-tuple-element.70) | copy-start | bytes 12292
  32.7 3.6 %copy-start.8 = (f32[128,8]{1,0:T(8,128)S(1)}, f32[128,8]{1,0:T(8,128)}, u32[]{:S(2)}) copy-start(f32[128,8]{1,0:T(8,128)} %get-tuple-element.74) | copy-start | bytes 12292
  38.1 5.1 %collective-permute-start.9 = (bf16[8,8,2208]{2,1,0:T(8,128)(2,1)S(1)}, bf16[8,8,2208]{2,1,0:T(8,128)(2,1)S(1)}, u32[]{:S(2)}, u32[]{:S(2)}) collective-permute-start(bf16[8,8,2208]{2,1,0:T(8,128)(2,1)S(1)} %concatenate.41), channel_id=1, source_target_pairs={{0,1},{1,0},{2,3},{3,2},{4,5},{5,4},{6,7},{7,6},{8,9},{9,8},{10,11... | collective-permute-start | bytes 847880 | tf_op jit(solution)/shard_map/ppermute | solution.py:23
  44.8 5.8 %collective-permute-start.10 = (bf16[4,8,2208]{2,1,0:T(8,128)(2,1)S(1)}, bf16[4,8,2208]{2,1,0:T(8,128)(2,1)S(1)}, u32[]{:S(2)}, u32[]{:S(2)}) collective-permute-start(bf16[4,8,2208]{2,1,0:T(8,128)(2,1)S(1)} %concatenate.44), channel_id=1, source_target_pairs={{0,2},{1,3},{2,0},{3,1},{4,6},{5,7},{6,4},{7,5},{8,10},{9,11},{10,... | collective-permute-start | bytes 423944 | tf_op jit(solution)/shard_map/ppermute | solution.py:23
  51.9 4.4 %collective-permute-start.11 = (bf16[2,8,2208]{2,1,0:T(8,128)(2,1)S(1)}, bf16[2,8,2208]{2,1,0:T(8,128)(2,1)S(1)}, u32[]{:S(2)}, u32[]{:S(2)}) collective-permute-start(bf16[2,8,2208]{2,1,0:T(8,128)(2,1)S(1)} %concatenate.47), channel_id=1, source_target_pairs={{0,4},{1,5},{2,6},{3,7},{4,0},{5,1},{6,2},{7,3},{8,12},{9,13},{10,... | collective-permute-start | bytes 211976 | tf_op jit(solution)/shard_map/ppermute | solution.py:23
  57.3 5.4 %collective-permute-start.12 = (bf16[1,8,2208]{2,1,0:T(8,128)(2,1)S(1)}, bf16[1,8,2208]{2,1,0:T(8,128)(2,1)S(1)}, u32[]{:S(2)}, u32[]{:S(2)}) collective-permute-start(bf16[1,8,2208]{2,1,0:T(8,128)(2,1)S(1)} %concatenate.50), channel_id=1, source_target_pairs={{0,8},{1,9},{2,10},{3,11},{4,12},{5,13},{6,14},{7,15},{8,0},{9,1},... | collective-permute-start | bytes 105992 | tf_op jit(solution)/shard_map/ppermute | solution.py:23

commit v13 on v12

--- a/solution.py
+++ b/solution.py
@@ -184,7 +184,7 @@
     return summed, tops, counts
 
 
-PER_STEP = 2
+PER_STEP = 4
 
 
 def video_kernel(query_ref, key_ref, value_ref, *refs):

time: 64.8 us -> 65.1 us (level)
  transfers between devices with their start and end apart: 13 -> 13, of which waited for: 6 -> 5; matrix products, arithmetic and copies ran while one was open for 6% -> 6% of each run, Pallas kernels for 43% -> 43%
where the time goes in v13:
time: 65.1 us; the launch traced here: 64.6 us
  Pallas kernels  27.8 us (43%)
  starting transfers between devices  14.2 us (22%)
  waiting for transfers between devices  9.59 us (15%)
  local copies, waits for them, and re-layouts  4.46 us (7%)
  other arithmetic  4.01 us (6%)
  matrix products  3.47 us (5%)
  between operations  1.06 us (2%)
    pallas_call x4, Pallas kernels, video_part(): pl.pallas_call(video_kernel, grid=(pairs // PER_STEP,), in_specs=specs, o...  14 us
    pallas_call x4, Pallas kernels, audio_partial(): pl.pallas_call(audio_kernel, grid=(heads // 2 // PER_STEP,), in_specs=[pl...  13.8 us
    ppermute x5, starting transfers between devices, gather_levels(): pieces[offset] = lax.ppermute(held, 'seq', pairs)  7.34 us
    ppermute x8, starting transfers between devices, exchange(): return lax.ppermute(value, 'seq', pairs)  6.91 us
    ppermute x5, waiting for transfers between devices, gather_levels(): pieces[offset] = lax.ppermute(held, 'seq', pairs)  5.74 us
    ppermute x8, waiting for transfers between devices, exchange(): return lax.ppermute(value, 'seq', pairs)  3.85 us
    dot_general x9, matrix products, spread(): jnp.dot(scales, expand, precision=lax.Precision.HIGHEST, preferred_elemen...  3.47 us
    concatenate x1, local copies, waits for them, and re-layouts, local(): jnp.concatenate([part[0] for part in parts] + [part[1] for part in parts]...  1.41 us
  transfers between devices with their start and end apart: 13, of which 5 were waited for; matrix products, arithmetic and copies ran while one was open for 6% of the time, Pallas kernels for 43%

profile of v13, /device:TPU:0, one launch (start us, length us, event | category | flops | bytes accessed | tf_op | source)
XLA Modules:
  0.0 64.6 jit_solution(13059448387529690253)
XLA Ops:
  0.6 4.1 %collective-permute-start.4 = (bf16[1,8,2048]{2,1,0:T(8,128)(2,1)}, bf16[1,8,2048]{2,1,0:T(8,128)(2,1)S(1)}, u32[]{:S(2)}, u32[]{:S(2)}) collective-permute-start(bf16[1,8,2048]{2,1,0:T(8,128)(2,1)} %bitcast.113), channel_id=1, source_target_pairs={{0,8},{1,9},{2,10},{3,11},{4,12},{5,13},{6,14},{7,15},{8,0},{9,1},... | collective-permute-start | bytes 98312 | tf_op jit(solution)/shard_map/ppermute | solution.py:71
  4.7 1.6 %collective-permute-start.3 = (bf16[1,8,2048]{2,1,0:T(8,128)(2,1)}, bf16[1,8,2048]{2,1,0:T(8,128)(2,1)S(1)}, u32[]{:S(2)}, u32[]{:S(2)}) collective-permute-start(bf16[1,8,2048]{2,1,0:T(8,128)(2,1)} %bitcast.114), channel_id=1, source_target_pairs={{0,4},{1,5},{2,6},{3,7},{4,0},{5,1},{6,2},{7,3},{8,12},{9,13},{10,... | collective-permute-start | bytes 98312 | tf_op jit(solution)/shard_map/ppermute | solution.py:71
  6.3 0.8 %maximum_bitcast_fusion.2 = bf16[1,8,4096]{2,1,0:T(8,128)(2,1)S(1)} fusion(bf16[8,2048]{1,0:T(8,128)(2,1)} %param.11, bf16[8,2048]{1,0:T(8,128)(2,1)} %param.10), kind=kLoop, calls=%fused_computation.74 | loop fusion | flops 131072 | bytes 131072 | tf_op jit(solution)/shard_map/broadcast_in_dim | solution.py:29
  7.1 1.9 %collective-permute-start = (bf16[1,8,4096]{2,1,0:T(8,128)(2,1)S(1)}, bf16[1,8,4096]{2,1,0:T(8,128)(2,1)S(1)}, u32[]{:S(2)}, u32[]{:S(2)}) collective-permute-start(bf16[1,8,4096]{2,1,0:T(8,128)(2,1)S(1)} %maximum_bitcast_fusion.2), channel_id=1, source_target_pairs={{0,8},{1,9},{2,10},{3,11},{4,12},{5,13},{6,14},{7,15},{8,0},{9,1},... | collective-permute-start | bytes 196616 | tf_op jit(solution)/shard_map/ppermute | solution.py:23
  9.0 3.2 %collective-permute-done.2 = bf16[1,8,2048]{2,1,0:T(8,128)(2,1)S(1)} collective-permute-done((bf16[1,8,2048]{2,1,0:T(8,128)(2,1)}, bf16[1,8,2048]{2,1,0:T(8,128)(2,1)S(1)}, u32[]{:S(2)}, u32[]{:S(2)}) %collective-permute-start.2) | collective-permute-done | bytes 32800 | tf_op jit(solution)/shard_map/ppermute | solution.py:71
  12.2 0.8 %select_bitcast_fusion.23 = (bf16[1,1,8,2048]{3,2,1,0:T(8,128)(2,1)S(1)}, bf16[1,1,8,2048]{3,2,1,0:T(8,128)(2,1)S(1)}, bf16[1,1,8,2048]{3,2,1,0:T(8,128)(2,1)S(1)}, bf16[1,1,8,2048]{3,2,1,0:T(8,128)(2,1)S(1)}) fusion(bf16[1,8,2048]{2,1,0:T(8,128)(2,1)S(1)} %collective-permute-done.2, bf16[1,8,2048]{2,1,0:T(8,128)(2,1)S(1)} %collective-permute-done.3, ...), kind=kLoop, calls=%fused_computation.98 | loop fusion | flops 196608 | bytes 262156 | tf_op jit(solution)/shard_map/stack | solution.py:79
  13.0 1.6 %collective-permute-start.5 = (bf16[4,8,2048]{2,1,0:T(8,128)(2,1)S(1)}, bf16[4,8,2048]{2,1,0:T(8,128)(2,1)S(1)}, u32[]{:S(2)}, u32[]{:S(2)}) collective-permute-start(bf16[4,8,2048]{2,1,0:T(8,128)(2,1)S(1)} %maximum_bitcast_fusion.1), channel_id=1, source_target_pairs={{0,2},{1,3},{2,0},{3,1},{4,6},{5,7},{6,4},{7,5},{8,10},{9,11},{10,... | collective-permute-start | bytes 393224 | tf_op jit(solution)/shard_map/ppermute | solution.py:71
  14.6 0.8 %select_bitcast_fusion.19 = (bf16[1,1,8,4096]{3,2,1,0:T(8,128)(2,1)S(1)}, bf16[1,1,8,4096]{3,2,1,0:T(8,128)(2,1)S(1)}) fusion(bf16[1,8,4096]{2,1,0:T(8,128)(2,1)S(1)} %collective-permute-done, pred[]{:T(512)S(6)} %ne.98, bf16[8,2048]{1,0:T(8,128)(2,1)} %param.11, bf16[8,2048]{1,0:T(8,128)(2,1)} %param.10), kind=kLoop, calls=%fused_computation.76 | loop fusion | flops 196608 | bytes 262145 | tf_op jit(solution)/shard_map/stack | solution.py:45
  15.5 0.1 collective-permute-start.1
  15.6 2.5 %collective-permute-done.5 = bf16[4,8,2048]{2,1,0:T(8,128)(2,1)S(1)} collective-permute-done((bf16[4,8,2048]{2,1,0:T(8,128)(2,1)S(1)}, bf16[4,8,2048]{2,1,0:T(8,128)(2,1)S(1)}, u32[]{:S(2)}, u32[]{:S(2)}) %collective-permute-start.5) | collective-permute-done | bytes 131104 | tf_op jit(solution)/shard_map/ppermute | solution.py:71
  18.2 2.3 %collective-permute-done.1 = bf16[2,8,4096]{2,1,0:T(8,128)(2,1)S(1)} collective-permute-done((bf16[2,8,4096]{2,1,0:T(8,128)(2,1)S(1)}, bf16[2,8,4096]{2,1,0:T(8,128)(2,1)S(1)}, u32[]{:S(2)}, u32[]{:S(2)}) %collective-permute-start.1) | collective-permute-done | bytes 131104 | tf_op jit(solution)/shard_map/ppermute | solution.py:23
  20.7 0.8 %copy.20 = bf16[8,2,8,2048]{3,2,1,0:T(8,128)(2,1)} copy(bf16[8,2,8,2048]{3,2,0,1:T(8,128)(2,1)S(1)} %pad_maximum_fusion.1) | data formatting | bytes 1048576 | tf_op jit(solution)/shard_map/stack | solution.py:79
  21.5 0.7 %collective-permute-start.7 = (bf16[4,8,4096]{2,1,0:T(8,128)(2,1)S(1)}, bf16[4,8,4096]{2,1,0:T(8,128)(2,1)S(1)}, u32[]{:S(2)}, u32[]{:S(2)}) collective-permute-start(bf16[4,8,4096]{2,1,0:T(8,128)(2,1)S(1)} %bitcast.101), channel_id=1, source_target_pairs={{0,2},{1,3},{2,0},{3,1},{4,6},{5,7},{6,4},{7,5},{8,10},{9,11},{10,... | collective-permute-start | bytes 786440 | tf_op jit(solution)/shard_map/ppermute | solution.py:23
  22.2 3.4 %shard_map.78 = (f32[128,512]{1,0:T(8,128)}, f32[128,8]{1,0:T(8,128)}, f32[128,8]{1,0:T(8,128)}) custom-call(bf16[128,2048]{1,0:T(8,128)(2,1)} %bitcast.90, bf16[512,2048]{1,0:T(8,128)(2,1)} %key_ref.7, bf16[512,2048]{1,0:T(8,128)(2,1)} %value_ref.7), custom_call_target="tpu_custom_call" | custom-call | flops 268435456 | bytes 1441792 | tf_op jit(solution)/shard_map/pallas_call | solution.py:283
  25.6 3.4 %shard_map.77 = (f32[128,512]{1,0:T(8,128)}, f32[128,8]{1,0:T(8,128)}, f32[128,8]{1,0:T(8,128)}) custom-call(bf16[128,2048]{1,0:T(8,128)(2,1)} %bitcast.91, bf16[512,2048]{1,0:T(8,128)(2,1)} %key_ref.7, bf16[512,2048]{1,0:T(8,128)(2,1)} %value_ref.7), custom_call_target="tpu_custom_call" | custom-call | flops 268435456 | bytes 1441792 | tf_op jit(solution)/shard_map/pallas_call | solution.py:283
  29.3 3.4 %shard_map.80 = (f32[128,512]{1,0:T(8,128)}, f32[128,8]{1,0:T(8,128)}, f32[128,8]{1,0:T(8,128)}) custom-call(bf16[128,2048]{1,0:T(8,128)(2,1)} %bitcast.92, bf16[512,2048]{1,0:T(8,128)(2,1)} %key_ref.7, bf16[512,2048]{1,0:T(8,128)(2,1)} %value_ref.7), custom_call_target="tpu_custom_call" | custom-call | flops 268435456 | bytes 1441792 | tf_op jit(solution)/shard_map/pallas_call | solution.py:283
  32.8 3.5 %shard_map.79 = (f32[128,512]{1,0:T(8,128)}, f32[128,8]{1,0:T(8,128)}, f32[128,8]{1,0:T(8,128)}) custom-call(bf16[128,2048]{1,0:T(8,128)(2,1)} %bitcast.93, bf16[512,2048]{1,0:T(8,128)(2,1)} %key_ref.7, bf16[512,2048]{1,0:T(8,128)(2,1)} %value_ref.7), custom_call_target="tpu_custom_call" | custom-call | flops 268435456 | bytes 1441792 | tf_op jit(solution)/shard_map/pallas_call | solution.py:283
  36.4 1.4 %concatenate.40 = f32[128,2112]{1,0:T(8,128)S(1)} concatenate(f32[128,512]{1,0:T(8,128)S(1)} %copy-done.1, f32[128,512]{1,0:T(8,128)S(1)} %copy-done, f32[128,512]{1,0:T(8,128)} %get-tuple-element.65, f32[128,512]{1,0:T(8,128)S(1)} %copy-done.2, f32[128,8]{1,0:T(8,128)S(1)} %copy-done.5, f32[128,8]{1,0:T(8,128)S(1)} %copy-done.3, f32[128,8]{1,0:T(8,128)} %get-tuple-element.69, ...), dimensions={1} | concatenate | bytes 2162688 | tf_op jit(solution)/shard_map/concatenate | solution.py:329
  37.9 0.1 fusion.35
  38.1 0.1 pad_maximum_fusion
  38.2 0.1 copy.22
  38.3 0.1 concatenate.41
  38.4 0.6 collective-permute-start.9
  39.0 1.1 %fusion.62 = (bf16[128,2048]{1,0:T(8,128)(2,1)}, bf16[128,2048]{1,0:T(8,128)(2,1)}) fusion(bf16[128,4096]{1,0:T(8,128)(2,1)S(1)} %bitcast.95), kind=kLoop, calls=%fused_computation.162 | loop fusion | bytes 2097152 | tf_op jit(solution)/shard_map/slice | solution.py:328
  40.0 3.5 %shard_map.81.refs_0_ = bf16[512,2048]{1,0:T(8,128)(2,1)} custom-call(bf16[512,2048]{1,0:T(8,128)(2,1)} %query_ref.7, bf16[128,2048]{1,0:T(8,128)(2,1)} %get-tuple-element.99.key_ref, bf16[128,2048]{1,0:T(8,128)(2,1)} %get-tuple-element.98.value_ref), custom_call_target="tpu_custom_call" | custom-call | flops 268435456 | bytes 1310720 | tf_op jit(solution)/shard_map/pallas_call | solution.py:237
  43.7 0.1 concatenate.42
  43.8 0.1 fusion.36
  43.9 0.4 convolution_multiply_fusion.1
  44.3 0.4 fusion
  44.8 0.1 concatenate.43
  45.0 0.1 concatenate.44
  45.1 1.6 %collective-permute-start.10 = (bf16[4,8,2208]{2,1,0:T(8,128)(2,1)S(1)}, bf16[4,8,2208]{2,1,0:T(8,128)(2,1)S(1)}, u32[]{:S(2)}, u32[]{:S(2)}) collective-permute-start(bf16[4,8,2208]{2,1,0:T(8,128)(2,1)S(1)} %concatenate.44), channel_id=1, source_target_pairs={{0,2},{1,3},{2,0},{3,1},{4,6},{5,7},{6,4},{7,5},{8,10},{9,11},{10,... | collective-permute-start | bytes 423944 | tf_op jit(solution)/shard_map/ppermute | solution.py:23
  46.6 3.5 %shard_map.82.refs_0_ = bf16[512,2048]{1,0:T(8,128)(2,1)} custom-call(bf16[512,2048]{1,0:T(8,128)(2,1)} %query_ref.7, bf16[128,2048]{1,0:T(8,128)(2,1)} %get-tuple-element.99.key_ref, bf16[128,2048]{1,0:T(8,128)(2,1)} %get-tuple-element.98.value_ref, bf16[512,2048]{1,0:T(8,128)(2,1)} %shard_map.81.refs_0_), custom_call_target="tpu_custom_call", output_to_operand_aliasing={{}: (3, {})} | custom-call | flops 268435456 | bytes 1310720 | tf_op jit(solution)/shard_map/pallas_call | solution.py:237
  50.1 0.8 %collective-permute-done.10 = bf16[4,8,2208]{2,1,0:T(8,128)(2,1)S(1)} collective-permute-done((bf16[4,8,2208]{2,1,0:T(8,128)(2,1)S(1)}, bf16[4,8,2208]{2,1,0:T(8,128)(2,1)S(1)}, u32[]{:S(2)}, u32[]{:S(2)}) %collective-permute-start.10) | collective-permute-done | bytes 141344 | tf_op jit(solution)/shard_map/ppermute | solution.py:23
  51.1 0.1 fusion.41
  51.2 0.3 convolution_multiply_fusion.2
  51.5 0.3 fusion.1
  52.1 0.1 concatenate.47
  52.2 3.5 %shard_map.83.refs_0_ = bf16[512,2048]{1,0:T(8,128)(2,1)} custom-call(bf16[512,2048]{1,0:T(8,128)(2,1)} %query_ref.7, bf16[128,2048]{1,0:T(8,128)(2,1)} %get-tuple-element.99.key_ref, bf16[128,2048]{1,0:T(8,128)(2,1)} %get-tuple-element.98.value_ref, bf16[512,2048]{1,0:T(8,128)(2,1)} %shard_map.82.refs_0_), custom_call_target="tpu_custom_call", output_to_operand_aliasing={{}: (3, {})} | custom-call | flops 268435456 | bytes 1310720 | tf_op jit(solution)/shard_map/pallas_call | solution.py:237
  55.7 0.8 %collective-permute-done.11 = bf16[2,8,2208]{2,1,0:T(8,128)(2,1)S(1)} collective-permute-done((bf16[2,8,2208]{2,1,0:T(8,128)(2,1)S(1)}, bf16[2,8,2208]{2,1,0:T(8,128)(2,1)S(1)}, u32[]{:S(2)}, u32[]{:S(2)}) %collective-permute-start.11) | collective-permute-done | bytes 70688 | tf_op jit(solution)/shard_map/ppermute | solution.py:23
  56.8 0.3 convolution_multiply_fusion.5
  57.0 0.3 fusion.2
  57.5 0.1 concatenate.50
  57.6 2.0 %collective-permute-start.12 = (bf16[1,8,2208]{2,1,0:T(8,128)(2,1)S(1)}, bf16[1,8,2208]{2,1,0:T(8,128)(2,1)S(1)}, u32[]{:S(2)}, u32[]{:S(2)}) collective-permute-start(bf16[1,8,2208]{2,1,0:T(8,128)(2,1)S(1)} %concatenate.50), channel_id=1, source_target_pairs={{0,8},{1,9},{2,10},{3,11},{4,12},{5,13},{6,14},{7,15},{8,0},{9,1},... | collective-permute-start | bytes 105992 | tf_op jit(solution)/shard_map/ppermute | solution.py:23
  59.5 3.5 %shard_map.84 = bf16[512,2048]{1,0:T(8,128)(2,1)} custom-call(bf16[512,2048]{1,0:T(8,128)(2,1)} %query_ref.7, bf16[128,2048]{1,0:T(8,128)(2,1)} %get-tuple-element.99.key_ref, bf16[128,2048]{1,0:T(8,128)(2,1)} %get-tuple-element.98.value_ref, bf16[512,2048]{1,0:T(8,128)(2,1)} %shard_map.83.refs_0_), custom_call_target="tpu_custom_call", output_to_operand_aliasing={{}: (3, {})} | custom-call | flops 268435456 | bytes 1310720 | tf_op jit(solution)/shard_map/pallas_call | solution.py:237
  63.2 0.2 convolution_multiply_fusion.7
  63.5 0.3 fusion.3
  63.7 0.9 %fusion.4 = bf16[8,2048]{1,0:T(8,128)(2,1)} fusion(f32[8,2048]{1,0:T(8,128)S(1)} %fusion.3, s32[2048]{0:T(1024)S(1)} %get-tuple-element.150, s32[2048]{0:T(1024)S(1)} %get-tuple-element.151, pred[2048]{0:T(1024)(128)(4,1)S(1)} %fusion.49, f32[8,2112]{1,0:T(8,128)S(1)} %bitcast.112, f32[8,2112]{1,0:T(8,128)S(1)} %get-tuple-element.128), kind=kOutput, calls=%fused_computation.13 | convolution fusion | flops 6456832 | bytes 133120 | tf_op jit(solution)/shard_map/dot_general | solution.py:16
  (69 shorter events, 2.0 us)
Async XLA Ops:
  0.6 8.4 %collective-permute-start.4 = (bf16[1,8,2048]{2,1,0:T(8,128)(2,1)}, bf16[1,8,2048]{2,1,0:T(8,128)(2,1)S(1)}, u32[]{:S(2)}, u32[]{:S(2)}) collective-permute-start(bf16[1,8,2048]{2,1,0:T(8,128)(2,1)} %bitcast.113), channel_id=1, source_target_pairs={{0,8},{1,9},{2,10},{3,11},{4,12},{5,13},{6,14},{7,15},{8,0},{9,1},... | collective-permute-start | bytes 98312 | tf_op jit(solution)/shard_map/ppermute | solution.py:71
  4.7 4.3 %collective-permute-start.3 = (bf16[1,8,2048]{2,1,0:T(8,128)(2,1)}, bf16[1,8,2048]{2,1,0:T(8,128)(2,1)S(1)}, u32[]{:S(2)}, u32[]{:S(2)}) collective-permute-start(bf16[1,8,2048]{2,1,0:T(8,128)(2,1)} %bitcast.114), channel_id=1, source_target_pairs={{0,4},{1,5},{2,6},{3,7},{4,0},{5,1},{6,2},{7,3},{8,12},{9,13},{10,... | collective-permute-start | bytes 98312 | tf_op jit(solution)/shard_map/ppermute | solution.py:71
  6.3 5.9 %collective-permute-start.2 = (bf16[1,8,2048]{2,1,0:T(8,128)(2,1)}, bf16[1,8,2048]{2,1,0:T(8,128)(2,1)S(1)}, u32[]{:S(2)}, u32[]{:S(2)}) collective-permute-start(bf16[1,8,2048]{2,1,0:T(8,128)(2,1)} %bitcast.115), channel_id=1, source_target_pairs={{0,12},{1,13},{2,14},{3,15},{4,8},{5,9},{6,10},{7,11},{8,4},{9,5},... | collective-permute-start | bytes 98312 | tf_op jit(solution)/shard_map/ppermute | solution.py:71
  7.1 7.5 %collective-permute-start = (bf16[1,8,4096]{2,1,0:T(8,128)(2,1)S(1)}, bf16[1,8,4096]{2,1,0:T(8,128)(2,1)S(1)}, u32[]{:S(2)}, u32[]{:S(2)}) collective-permute-start(bf16[1,8,4096]{2,1,0:T(8,128)(2,1)S(1)} %maximum_bitcast_fusion.2), channel_id=1, source_target_pairs={{0,8},{1,9},{2,10},{3,11},{4,12},{5,13},{6,14},{7,15},{8,0},{9,1},... | collective-permute-start | bytes 196616 | tf_op jit(solution)/shard_map/ppermute | solution.py:23
  13.0 5.0 %collective-permute-start.5 = (bf16[4,8,2048]{2,1,0:T(8,128)(2,1)S(1)}, bf16[4,8,2048]{2,1,0:T(8,128)(2,1)S(1)}, u32[]{:S(2)}, u32[]{:S(2)}) collective-permute-start(bf16[4,8,2048]{2,1,0:T(8,128)(2,1)S(1)} %maximum_bitcast_fusion.1), channel_id=1, source_target_pairs={{0,2},{1,3},{2,0},{3,1},{4,6},{5,7},{6,4},{7,5},{8,10},{9,11},{10,... | collective-permute-start | bytes 393224 | tf_op jit(solution)/shard_map/ppermute | solution.py:71
  15.5 5.0 %collective-permute-start.1 = (bf16[2,8,4096]{2,1,0:T(8,128)(2,1)S(1)}, bf16[2,8,4096]{2,1,0:T(8,128)(2,1)S(1)}, u32[]{:S(2)}, u32[]{:S(2)}) collective-permute-start(bf16[2,8,4096]{2,1,0:T(8,128)(2,1)S(1)} %maximum_bitcast_fusion), channel_id=1, source_target_pairs={{0,4},{1,5},{2,6},{3,7},{4,0},{5,1},{6,2},{7,3},{8,12},{9,13},{10,... | collective-permute-start | bytes 393224 | tf_op jit(solution)/shard_map/ppermute | solution.py:23
  18.1 2.4 %collective-permute-start.6 = (bf16[8,8,2048]{2,1,0:T(8,128)(2,1)S(1)}, bf16[8,8,2048]{2,1,0:T(8,128)(2,1)S(1)}, u32[]{:S(2)}, u32[]{:S(2)}) collective-permute-start(bf16[8,8,2048]{2,1,0:T(8,128)(2,1)S(1)} %bitcast.100), channel_id=1, source_target_pairs={{0,1},{1,0},{2,3},{3,2},{4,5},{5,4},{6,7},{7,6},{8,9},{9,8},{10,11... | collective-permute-start | bytes 786440 | tf_op jit(solution)/shard_map/ppermute | solution.py:71
  21.5 7.5 %collective-permute-start.7 = (bf16[4,8,4096]{2,1,0:T(8,128)(2,1)S(1)}, bf16[4,8,4096]{2,1,0:T(8,128)(2,1)S(1)}, u32[]{:S(2)}, u32[]{:S(2)}) collective-permute-start(bf16[4,8,4096]{2,1,0:T(8,128)(2,1)S(1)} %bitcast.101), channel_id=1, source_target_pairs={{0,2},{1,3},{2,0},{3,1},{4,6},{5,7},{6,4},{7,5},{8,10},{9,11},{10,... | collective-permute-start | bytes 786440 | tf_op jit(solution)/shard_map/ppermute | solution.py:23
  29.2 7.1 %collective-permute-start.8 = (bf16[8,8,4096]{2,1,0:T(8,128)(2,1)S(1)}, bf16[8,8,4096]{2,1,0:T(8,128)(2,1)S(1)}, u32[]{:S(2)}, u32[]{:S(2)}) collective-permute-start(bf16[8,8,4096]{2,1,0:T(8,128)(2,1)S(1)} %bitcast.97), channel_id=1, source_target_pairs={{0,1},{1,0},{2,3},{3,2},{4,5},{5,4},{6,7},{7,6},{8,9},{9,8},{10,11... | collective-permute-start | bytes 1572872 | tf_op jit(solution)/shard_map/ppermute | solution.py:23
  32.7 3.6 %copy-start = (f32[128,512]{1,0:T(8,128)S(1)}, f32[128,512]{1,0:T(8,128)}, u32[]{:S(2)}) copy-start(f32[128,512]{1,0:T(8,128)} %get-tuple-element.55) | copy-start | bytes 786436
  32.7 3.6 %copy-start.1 = (f32[128,512]{1,0:T(8,128)S(1)}, f32[128,512]{1,0:T(8,128)}, u32[]{:S(2)}) copy-start(f32[128,512]{1,0:T(8,128)} %get-tuple-element.54) | copy-start | bytes 786436
  32.8 3.6 %copy-start.2 = (f32[128,512]{1,0:T(8,128)S(1)}, f32[128,512]{1,0:T(8,128)}, u32[]{:S(2)}) copy-start(f32[128,512]{1,0:T(8,128)} %get-tuple-element.66) | copy-start | bytes 786436
  32.8 3.6 %copy-start.3 = (f32[128,8]{1,0:T(8,128)S(1)}, f32[128,8]{1,0:T(8,128)}, u32[]{:S(2)}) copy-start(f32[128,8]{1,0:T(8,128)} %get-tuple-element.68) | copy-start | bytes 12292
  32.8 3.6 %copy-start.4 = (f32[128,8]{1,0:T(8,128)S(1)}, f32[128,8]{1,0:T(8,128)}, u32[]{:S(2)}) copy-start(f32[128,8]{1,0:T(8,128)} %get-tuple-element.72) | copy-start | bytes 12292
  32.8 3.6 %copy-start.5 = (f32[128,8]{1,0:T(8,128)S(1)}, f32[128,8]{1,0:T(8,128)}, u32[]{:S(2)}) copy-start(f32[128,8]{1,0:T(8,128)} %get-tuple-element.67) | copy-start | bytes 12292
  32.8 3.6 %copy-start.6 = (f32[128,8]{1,0:T(8,128)S(1)}, f32[128,8]{1,0:T(8,128)}, u32[]{:S(2)}) copy-start(f32[128,8]{1,0:T(8,128)} %get-tuple-element.71) | copy-start | bytes 12292
  32.8 3.6 %copy-start.7 = (f32[128,8]{1,0:T(8,128)S(1)}, f32[128,8]{1,0:T(8,128)}, u32[]{:S(2)}) copy-start(f32[128,8]{1,0:T(8,128)} %get-tuple-element.70) | copy-start | bytes 12292
  32.8 3.6 %copy-start.8 = (f32[128,8]{1,0:T(8,128)S(1)}, f32[128,8]{1,0:T(8,128)}, u32[]{:S(2)}) copy-start(f32[128,8]{1,0:T(8,128)} %get-tuple-element.74) | copy-start | bytes 12292
  38.4 5.1 %collective-permute-start.9 = (bf16[8,8,2208]{2,1,0:T(8,128)(2,1)S(1)}, bf16[8,8,2208]{2,1,0:T(8,128)(2,1)S(1)}, u32[]{:S(2)}, u32[]{:S(2)}) collective-permute-start(bf16[8,8,2208]{2,1,0:T(8,128)(2,1)S(1)} %concatenate.41), channel_id=1, source_target_pairs={{0,1},{1,0},{2,3},{3,2},{4,5},{5,4},{6,7},{7,6},{8,9},{9,8},{10,11... | collective-permute-start | bytes 847880 | tf_op jit(solution)/shard_map/ppermute | solution.py:23
  45.1 5.8 %collective-permute-start.10 = (bf16[4,8,2208]{2,1,0:T(8,128)(2,1)S(1)}, bf16[4,8,2208]{2,1,0:T(8,128)(2,1)S(1)}, u32[]{:S(2)}, u32[]{:S(2)}) collective-permute-start(bf16[4,8,2208]{2,1,0:T(8,128)(2,1)S(1)} %concatenate.44), channel_id=1, source_target_pairs={{0,2},{1,3},{2,0},{3,1},{4,6},{5,7},{6,4},{7,5},{8,10},{9,11},{10,... | collective-permute-start | bytes 423944 | tf_op jit(solution)/shard_map/ppermute | solution.py:23
  52.1 4.4 %collective-permute-start.11 = (bf16[2,8,2208]{2,1,0:T(8,128)(2,1)S(1)}, bf16[2,8,2208]{2,1,0:T(8,128)(2,1)S(1)}, u32[]{:S(2)}, u32[]{:S(2)}) collective-permute-start(bf16[2,8,2208]{2,1,0:T(8,128)(2,1)S(1)} %concatenate.47), channel_id=1, source_target_pairs={{0,4},{1,5},{2,6},{3,7},{4,0},{5,1},{6,2},{7,3},{8,12},{9,13},{10,... | collective-permute-start | bytes 211976 | tf_op jit(solution)/shard_map/ppermute | solution.py:23
  57.6 5.5 %collective-permute-start.12 = (bf16[1,8,2208]{2,1,0:T(8,128)(2,1)S(1)}, bf16[1,8,2208]{2,1,0:T(8,128)(2,1)S(1)}, u32[]{:S(2)}, u32[]{:S(2)}) collective-permute-start(bf16[1,8,2208]{2,1,0:T(8,128)(2,1)S(1)} %concatenate.50), channel_id=1, source_target_pairs={{0,8},{1,9},{2,10},{3,11},{4,12},{5,13},{6,14},{7,15},{8,0},{9,1},... | collective-permute-start | bytes 105992 | tf_op jit(solution)/shard_map/ppermute | solution.py:23

commit v14 on v12

--- a/solution.py
+++ b/solution.py
@@ -162,11 +162,9 @@
 
 def pair_attention(queries, keys, values):
     key_rows = keys.shape[0]
-    scores = (
-        lax.dot_general(
-            queries, split_pair(keys), (((1,), (1,)), ((), ())), preferred_element_type=jnp.float32
-        )
-        * 0.125
+    scaled = queries * jnp.asarray(0.125, queries.dtype)
+    scores = lax.dot_general(
+        scaled, split_pair(keys), (((1,), (1,)), ((), ())), preferred_element_type=jnp.float32
     )
     weights = []
     tops = []
@@ -192,13 +190,10 @@
     key_rows = key_ref.shape[0]
     for sub in range(PER_STEP):
         lanes = slice(sub * 2 * HEAD_DIM, (sub + 1) * 2 * HEAD_DIM)
-        queries = query_ref[:, lanes]
-        scores = (
-            lax.dot_general(
-                split_pair(key_ref[:, lanes]), queries, (((1,), (1,)), ((), ())),
-                preferred_element_type=jnp.float32,
-            )
-            * 0.125
+        queries = query_ref[:, lanes] * jnp.asarray(0.125, query_ref.dtype)
+        scores = lax.dot_general(
+            split_pair(key_ref[:, lanes]), queries, (((1,), (1,)), ((), ())),
+            preferred_element_type=jnp.float32,
         )
         weights = []
         counts = []
@@ -213,8 +208,8 @@
             (((0,), (0,)), ((), ())), preferred_element_type=jnp.float32,
         )
         lane = lax.broadcasted_iota(jnp.int32, summed.shape, 0)
-        totals = jnp.where(lane < HEAD_DIM, counts[0], counts[1])
-        out_ref[:, lanes] = (summed / totals).T.astype(out_ref.dtype)
+        inverse = jnp.where(lane < HEAD_DIM, 1.0 / counts[0], 1.0 / counts[1])
+        out_ref[:, lanes] = (summed * inverse).T.astype(out_ref.dtype)
 
 
 def video_part(queries, keys, values, earlier, group, groups):

time: 64.8 us -> 64.6 us (level)
  no operation moved by 1% of the time
where the time goes in v14:
time: 64.6 us; the launch traced here: 64.1 us
  Pallas kernels  27.4 us (42%)
  starting transfers between devices  14.1 us (22%)
  waiting for transfers between devices  9.76 us (15%)
  local copies, waits for them, and re-layouts  4.28 us (7%)
  other arithmetic  4.01 us (6%)
  matrix products  3.45 us (5%)
  between operations  1.07 us (2%)
    pallas_call x4, Pallas kernels, video_part(): pl.pallas_call(video_kernel, grid=(pairs // PER_STEP,), in_specs=specs, o...  13.9 us
    pallas_call x4, Pallas kernels, audio_partial(): pl.pallas_call(audio_kernel, grid=(heads // 2 // PER_STEP,), in_specs=[pl...  13.5 us
    ppermute x5, starting transfers between devices, gather_levels(): pieces[offset] = lax.ppermute(held, 'seq', pairs)  7.34 us
    ppermute x8, starting transfers between devices, exchange(): return lax.ppermute(value, 'seq', pairs)  6.79 us
    ppermute x5, waiting for transfers between devices, gather_levels(): pieces[offset] = lax.ppermute(held, 'seq', pairs)  5.74 us
    ppermute x8, waiting for transfers between devices, exchange(): return lax.ppermute(value, 'seq', pairs)  4.02 us
    dot_general x9, matrix products, spread(): jnp.dot(scales, expand, precision=lax.Precision.HIGHEST, preferred_elemen...  3.45 us
  transfers between devices with their start and end apart: 13, of which 6 were waited for; matrix products, arithmetic and copies ran while one was open for 6% of the time, Pallas kernels for 43%

profile of v14, /device:TPU:0, one launch (start us, length us, event | category | flops | bytes accessed | tf_op | source)
XLA Modules:
  0.0 64.1 jit_solution(1980748213855584842)
XLA Ops:
  0.6 4.1 %collective-permute-start.4 = (bf16[1,8,2048]{2,1,0:T(8,128)(2,1)}, bf16[1,8,2048]{2,1,0:T(8,128)(2,1)S(1)}, u32[]{:S(2)}, u32[]{:S(2)}) collective-permute-start(bf16[1,8,2048]{2,1,0:T(8,128)(2,1)} %bitcast.113), channel_id=1, source_target_pairs={{0,8},{1,9},{2,10},{3,11},{4,12},{5,13},{6,14},{7,15},{8,0},{9,1},... | collective-permute-start | bytes 98312 | tf_op jit(solution)/shard_map/ppermute | solution.py:71
  4.7 1.6 %collective-permute-start.3 = (bf16[1,8,2048]{2,1,0:T(8,128)(2,1)}, bf16[1,8,2048]{2,1,0:T(8,128)(2,1)S(1)}, u32[]{:S(2)}, u32[]{:S(2)}) collective-permute-start(bf16[1,8,2048]{2,1,0:T(8,128)(2,1)} %bitcast.114), channel_id=1, source_target_pairs={{0,4},{1,5},{2,6},{3,7},{4,0},{5,1},{6,2},{7,3},{8,12},{9,13},{10,... | collective-permute-start | bytes 98312 | tf_op jit(solution)/shard_map/ppermute | solution.py:71
  6.3 0.8 %maximum_bitcast_fusion.2 = bf16[1,8,4096]{2,1,0:T(8,128)(2,1)S(1)} fusion(bf16[8,2048]{1,0:T(8,128)(2,1)} %param.11, bf16[8,2048]{1,0:T(8,128)(2,1)} %param.10), kind=kLoop, calls=%fused_computation.74 | loop fusion | flops 131072 | bytes 131072 | tf_op jit(solution)/shard_map/broadcast_in_dim | solution.py:29
  7.1 1.9 %collective-permute-start = (bf16[1,8,4096]{2,1,0:T(8,128)(2,1)S(1)}, bf16[1,8,4096]{2,1,0:T(8,128)(2,1)S(1)}, u32[]{:S(2)}, u32[]{:S(2)}) collective-permute-start(bf16[1,8,4096]{2,1,0:T(8,128)(2,1)S(1)} %maximum_bitcast_fusion.2), channel_id=1, source_target_pairs={{0,8},{1,9},{2,10},{3,11},{4,12},{5,13},{6,14},{7,15},{8,0},{9,1},... | collective-permute-start | bytes 196616 | tf_op jit(solution)/shard_map/ppermute | solution.py:23
  9.0 3.2 %collective-permute-done.2 = bf16[1,8,2048]{2,1,0:T(8,128)(2,1)S(1)} collective-permute-done((bf16[1,8,2048]{2,1,0:T(8,128)(2,1)}, bf16[1,8,2048]{2,1,0:T(8,128)(2,1)S(1)}, u32[]{:S(2)}, u32[]{:S(2)}) %collective-permute-start.2) | collective-permute-done | bytes 32800 | tf_op jit(solution)/shard_map/ppermute | solution.py:71
  12.2 0.8 %select_bitcast_fusion.23 = (bf16[1,1,8,2048]{3,2,1,0:T(8,128)(2,1)S(1)}, bf16[1,1,8,2048]{3,2,1,0:T(8,128)(2,1)S(1)}, bf16[1,1,8,2048]{3,2,1,0:T(8,128)(2,1)S(1)}, bf16[1,1,8,2048]{3,2,1,0:T(8,128)(2,1)S(1)}) fusion(bf16[1,8,2048]{2,1,0:T(8,128)(2,1)S(1)} %collective-permute-done.2, bf16[1,8,2048]{2,1,0:T(8,128)(2,1)S(1)} %collective-permute-done.3, ...), kind=kLoop, calls=%fused_computation.98 | loop fusion | flops 196608 | bytes 262156 | tf_op jit(solution)/shard_map/stack | solution.py:79
  13.0 1.6 %collective-permute-start.5 = (bf16[4,8,2048]{2,1,0:T(8,128)(2,1)S(1)}, bf16[4,8,2048]{2,1,0:T(8,128)(2,1)S(1)}, u32[]{:S(2)}, u32[]{:S(2)}) collective-permute-start(bf16[4,8,2048]{2,1,0:T(8,128)(2,1)S(1)} %maximum_bitcast_fusion.1), channel_id=1, source_target_pairs={{0,2},{1,3},{2,0},{3,1},{4,6},{5,7},{6,4},{7,5},{8,10},{9,11},{10,... | collective-permute-start | bytes 393224 | tf_op jit(solution)/shard_map/ppermute | solution.py:71
  14.6 0.8 %select_bitcast_fusion.19 = (bf16[1,1,8,4096]{3,2,1,0:T(8,128)(2,1)S(1)}, bf16[1,1,8,4096]{3,2,1,0:T(8,128)(2,1)S(1)}) fusion(bf16[1,8,4096]{2,1,0:T(8,128)(2,1)S(1)} %collective-permute-done, pred[]{:T(512)S(6)} %ne.98, bf16[8,2048]{1,0:T(8,128)(2,1)} %param.11, bf16[8,2048]{1,0:T(8,128)(2,1)} %param.10), kind=kLoop, calls=%fused_computation.76 | loop fusion | flops 196608 | bytes 262145 | tf_op jit(solution)/shard_map/stack | solution.py:45
  15.5 0.1 collective-permute-start.1
  15.6 2.5 %collective-permute-done.5 = bf16[4,8,2048]{2,1,0:T(8,128)(2,1)S(1)} collective-permute-done((bf16[4,8,2048]{2,1,0:T(8,128)(2,1)S(1)}, bf16[4,8,2048]{2,1,0:T(8,128)(2,1)S(1)}, u32[]{:S(2)}, u32[]{:S(2)}) %collective-permute-start.5) | collective-permute-done | bytes 131104 | tf_op jit(solution)/shard_map/ppermute | solution.py:71
  18.2 2.3 %collective-permute-done.1 = bf16[2,8,4096]{2,1,0:T(8,128)(2,1)S(1)} collective-permute-done((bf16[2,8,4096]{2,1,0:T(8,128)(2,1)S(1)}, bf16[2,8,4096]{2,1,0:T(8,128)(2,1)S(1)}, u32[]{:S(2)}, u32[]{:S(2)}) %collective-permute-start.1) | collective-permute-done | bytes 131104 | tf_op jit(solution)/shard_map/ppermute | solution.py:23
  20.7 0.8 %copy.20 = bf16[8,2,8,2048]{3,2,1,0:T(8,128)(2,1)} copy(bf16[8,2,8,2048]{3,2,0,1:T(8,128)(2,1)S(1)} %pad_maximum_fusion.1) | data formatting | bytes 1048576 | tf_op jit(solution)/shard_map/stack | solution.py:79
  21.5 0.7 %collective-permute-start.7 = (bf16[4,8,4096]{2,1,0:T(8,128)(2,1)S(1)}, bf16[4,8,4096]{2,1,0:T(8,128)(2,1)S(1)}, u32[]{:S(2)}, u32[]{:S(2)}) collective-permute-start(bf16[4,8,4096]{2,1,0:T(8,128)(2,1)S(1)} %bitcast.101), channel_id=1, source_target_pairs={{0,2},{1,3},{2,0},{3,1},{4,6},{5,7},{6,4},{7,5},{8,10},{9,11},{10,... | collective-permute-start | bytes 786440 | tf_op jit(solution)/shard_map/ppermute | solution.py:23
  22.2 3.3 %shard_map.78 = (f32[128,512]{1,0:T(8,128)}, f32[128,8]{1,0:T(8,128)}, f32[128,8]{1,0:T(8,128)}) custom-call(bf16[128,2048]{1,0:T(8,128)(2,1)} %bitcast.90, bf16[512,2048]{1,0:T(8,128)(2,1)} %key_ref.7, bf16[512,2048]{1,0:T(8,128)(2,1)} %value_ref.7), custom_call_target="tpu_custom_call" | custom-call | flops 268435456 | bytes 1441792 | tf_op jit(solution)/shard_map/pallas_call | solution.py:278
  25.6 3.4 %shard_map.77 = (f32[128,512]{1,0:T(8,128)}, f32[128,8]{1,0:T(8,128)}, f32[128,8]{1,0:T(8,128)}) custom-call(bf16[128,2048]{1,0:T(8,128)(2,1)} %bitcast.91, bf16[512,2048]{1,0:T(8,128)(2,1)} %key_ref.7, bf16[512,2048]{1,0:T(8,128)(2,1)} %value_ref.7), custom_call_target="tpu_custom_call" | custom-call | flops 268435456 | bytes 1441792 | tf_op jit(solution)/shard_map/pallas_call | solution.py:278
  28.9 0.1 collective-permute-done.7
  29.3 3.4 %shard_map.80 = (f32[128,512]{1,0:T(8,128)}, f32[128,8]{1,0:T(8,128)}, f32[128,8]{1,0:T(8,128)}) custom-call(bf16[128,2048]{1,0:T(8,128)(2,1)} %bitcast.92, bf16[512,2048]{1,0:T(8,128)(2,1)} %key_ref.7, bf16[512,2048]{1,0:T(8,128)(2,1)} %value_ref.7), custom_call_target="tpu_custom_call" | custom-call | flops 268435456 | bytes 1441792 | tf_op jit(solution)/shard_map/pallas_call | solution.py:278
  32.7 3.5 %shard_map.79 = (f32[128,512]{1,0:T(8,128)}, f32[128,8]{1,0:T(8,128)}, f32[128,8]{1,0:T(8,128)}) custom-call(bf16[128,2048]{1,0:T(8,128)(2,1)} %bitcast.93, bf16[512,2048]{1,0:T(8,128)(2,1)} %key_ref.7, bf16[512,2048]{1,0:T(8,128)(2,1)} %value_ref.7), custom_call_target="tpu_custom_call" | custom-call | flops 268435456 | bytes 1441792 | tf_op jit(solution)/shard_map/pallas_call | solution.py:278
  36.3 1.2 %concatenate.40 = f32[128,2112]{1,0:T(8,128)S(1)} concatenate(f32[128,512]{1,0:T(8,128)S(1)} %copy-done.1, f32[128,512]{1,0:T(8,128)S(1)} %copy-done, f32[128,512]{1,0:T(8,128)} %get-tuple-element.65, f32[128,512]{1,0:T(8,128)S(1)} %copy-done.2, f32[128,8]{1,0:T(8,128)S(1)} %copy-done.5, f32[128,8]{1,0:T(8,128)S(1)} %copy-done.3, f32[128,8]{1,0:T(8,128)} %get-tuple-element.69, ...), dimensions={1} | concatenate | bytes 2162688 | tf_op jit(solution)/shard_map/concatenate | solution.py:324
  37.6 0.1 fusion.35
  37.8 0.1 pad_maximum_fusion
  37.9 0.1 copy.22
  38.0 0.1 concatenate.41
  38.1 0.5 collective-permute-start.9
  38.7 1.1 %fusion.62 = (bf16[128,2048]{1,0:T(8,128)(2,1)}, bf16[128,2048]{1,0:T(8,128)(2,1)}) fusion(bf16[128,4096]{1,0:T(8,128)(2,1)S(1)} %bitcast.95), kind=kLoop, calls=%fused_computation.162 | loop fusion | bytes 2097152 | tf_op jit(solution)/shard_map/slice | solution.py:323
  39.7 3.5 %shard_map.81.refs_0_ = bf16[512,2048]{1,0:T(8,128)(2,1)} custom-call(bf16[512,2048]{1,0:T(8,128)(2,1)} %query_ref.7, bf16[128,2048]{1,0:T(8,128)(2,1)} %get-tuple-element.99.key_ref, bf16[128,2048]{1,0:T(8,128)(2,1)} %get-tuple-element.98.value_ref), custom_call_target="tpu_custom_call" | custom-call | flops 268435456 | bytes 1310720 | tf_op jit(solution)/shard_map/pallas_call | solution.py:232
  43.3 0.1 concatenate.42
  43.4 0.1 fusion.36
  43.5 0.4 convolution_multiply_fusion.1
  44.0 0.4 fusion
  44.6 0.1 concatenate.44
  44.7 1.6 %collective-permute-start.10 = (bf16[4,8,2208]{2,1,0:T(8,128)(2,1)S(1)}, bf16[4,8,2208]{2,1,0:T(8,128)(2,1)S(1)}, u32[]{:S(2)}, u32[]{:S(2)}) collective-permute-start(bf16[4,8,2208]{2,1,0:T(8,128)(2,1)S(1)} %concatenate.44), channel_id=1, source_target_pairs={{0,2},{1,3},{2,0},{3,1},{4,6},{5,7},{6,4},{7,5},{8,10},{9,11},{10,... | collective-permute-start | bytes 423944 | tf_op jit(solution)/shard_map/ppermute | solution.py:23
  46.3 3.5 %shard_map.82.refs_0_ = bf16[512,2048]{1,0:T(8,128)(2,1)} custom-call(bf16[512,2048]{1,0:T(8,128)(2,1)} %query_ref.7, bf16[128,2048]{1,0:T(8,128)(2,1)} %get-tuple-element.99.key_ref, bf16[128,2048]{1,0:T(8,128)(2,1)} %get-tuple-element.98.value_ref, bf16[512,2048]{1,0:T(8,128)(2,1)} %shard_map.81.refs_0_), custom_call_target="tpu_custom_call", output_to_operand_aliasing={{}: (3, {})} | custom-call | flops 268435456 | bytes 1310720 | tf_op jit(solution)/shard_map/pallas_call | solution.py:232
  49.8 0.8 %collective-permute-done.10 = bf16[4,8,2208]{2,1,0:T(8,128)(2,1)S(1)} collective-permute-done((bf16[4,8,2208]{2,1,0:T(8,128)(2,1)S(1)}, bf16[4,8,2208]{2,1,0:T(8,128)(2,1)S(1)}, u32[]{:S(2)}, u32[]{:S(2)}) %collective-permute-start.10) | collective-permute-done | bytes 141344 | tf_op jit(solution)/shard_map/ppermute | solution.py:23
  50.7 0.1 fusion.41
  50.8 0.3 convolution_multiply_fusion.2
  51.2 0.3 fusion.1
  51.7 0.1 concatenate.47
  51.8 3.5 %shard_map.83.refs_0_ = bf16[512,2048]{1,0:T(8,128)(2,1)} custom-call(bf16[512,2048]{1,0:T(8,128)(2,1)} %query_ref.7, bf16[128,2048]{1,0:T(8,128)(2,1)} %get-tuple-element.99.key_ref, bf16[128,2048]{1,0:T(8,128)(2,1)} %get-tuple-element.98.value_ref, bf16[512,2048]{1,0:T(8,128)(2,1)} %shard_map.82.refs_0_), custom_call_target="tpu_custom_call", output_to_operand_aliasing={{}: (3, {})} | custom-call | flops 268435456 | bytes 1310720 | tf_op jit(solution)/shard_map/pallas_call | solution.py:232
  55.3 0.8 %collective-permute-done.11 = bf16[2,8,2208]{2,1,0:T(8,128)(2,1)S(1)} collective-permute-done((bf16[2,8,2208]{2,1,0:T(8,128)(2,1)S(1)}, bf16[2,8,2208]{2,1,0:T(8,128)(2,1)S(1)}, u32[]{:S(2)}, u32[]{:S(2)}) %collective-permute-start.11) | collective-permute-done | bytes 70688 | tf_op jit(solution)/shard_map/ppermute | solution.py:23
  56.4 0.3 convolution_multiply_fusion.5
  56.7 0.3 fusion.2
  57.1 0.1 concatenate.50
  57.2 1.8 %collective-permute-start.12 = (bf16[1,8,2208]{2,1,0:T(8,128)(2,1)S(1)}, bf16[1,8,2208]{2,1,0:T(8,128)(2,1)S(1)}, u32[]{:S(2)}, u32[]{:S(2)}) collective-permute-start(bf16[1,8,2208]{2,1,0:T(8,128)(2,1)S(1)} %concatenate.50), channel_id=1, source_target_pairs={{0,8},{1,9},{2,10},{3,11},{4,12},{5,13},{6,14},{7,15},{8,0},{9,1},... | collective-permute-start | bytes 105992 | tf_op jit(solution)/shard_map/ppermute | solution.py:23
  59.1 3.5 %shard_map.84 = bf16[512,2048]{1,0:T(8,128)(2,1)} custom-call(bf16[512,2048]{1,0:T(8,128)(2,1)} %query_ref.7, bf16[128,2048]{1,0:T(8,128)(2,1)} %get-tuple-element.99.key_ref, bf16[128,2048]{1,0:T(8,128)(2,1)} %get-tuple-element.98.value_ref, bf16[512,2048]{1,0:T(8,128)(2,1)} %shard_map.83.refs_0_), custom_call_target="tpu_custom_call", output_to_operand_aliasing={{}: (3, {})} | custom-call | flops 268435456 | bytes 1310720 | tf_op jit(solution)/shard_map/pallas_call | solution.py:232
  62.7 0.3 convolution_multiply_fusion.7
  63.0 0.3 fusion.3
  63.2 0.9 %fusion.4 = bf16[8,2048]{1,0:T(8,128)(2,1)} fusion(f32[8,2048]{1,0:T(8,128)S(1)} %fusion.3, s32[2048]{0:T(1024)S(1)} %get-tuple-element.150, s32[2048]{0:T(1024)S(1)} %get-tuple-element.151, pred[2048]{0:T(1024)(128)(4,1)S(1)} %fusion.49, f32[8,2112]{1,0:T(8,128)S(1)} %bitcast.112, f32[8,2112]{1,0:T(8,128)S(1)} %get-tuple-element.128), kind=kOutput, calls=%fused_computation.13 | convolution fusion | flops 6456832 | bytes 133120 | tf_op jit(solution)/shard_map/dot_general | solution.py:16
  (69 shorter events, 2.1 us)
Async XLA Ops:
  0.6 8.4 %collective-permute-start.4 = (bf16[1,8,2048]{2,1,0:T(8,128)(2,1)}, bf16[1,8,2048]{2,1,0:T(8,128)(2,1)S(1)}, u32[]{:S(2)}, u32[]{:S(2)}) collective-permute-start(bf16[1,8,2048]{2,1,0:T(8,128)(2,1)} %bitcast.113), channel_id=1, source_target_pairs={{0,8},{1,9},{2,10},{3,11},{4,12},{5,13},{6,14},{7,15},{8,0},{9,1},... | collective-permute-start | bytes 98312 | tf_op jit(solution)/shard_map/ppermute | solution.py:71
  4.7 4.3 %collective-permute-start.3 = (bf16[1,8,2048]{2,1,0:T(8,128)(2,1)}, bf16[1,8,2048]{2,1,0:T(8,128)(2,1)S(1)}, u32[]{:S(2)}, u32[]{:S(2)}) collective-permute-start(bf16[1,8,2048]{2,1,0:T(8,128)(2,1)} %bitcast.114), channel_id=1, source_target_pairs={{0,4},{1,5},{2,6},{3,7},{4,0},{5,1},{6,2},{7,3},{8,12},{9,13},{10,... | collective-permute-start | bytes 98312 | tf_op jit(solution)/shard_map/ppermute | solution.py:71
  6.3 5.9 %collective-permute-start.2 = (bf16[1,8,2048]{2,1,0:T(8,128)(2,1)}, bf16[1,8,2048]{2,1,0:T(8,128)(2,1)S(1)}, u32[]{:S(2)}, u32[]{:S(2)}) collective-permute-start(bf16[1,8,2048]{2,1,0:T(8,128)(2,1)} %bitcast.115), channel_id=1, source_target_pairs={{0,12},{1,13},{2,14},{3,15},{4,8},{5,9},{6,10},{7,11},{8,4},{9,5},... | collective-permute-start | bytes 98312 | tf_op jit(solution)/shard_map/ppermute | solution.py:71
  7.1 7.5 %collective-permute-start = (bf16[1,8,4096]{2,1,0:T(8,128)(2,1)S(1)}, bf16[1,8,4096]{2,1,0:T(8,128)(2,1)S(1)}, u32[]{:S(2)}, u32[]{:S(2)}) collective-permute-start(bf16[1,8,4096]{2,1,0:T(8,128)(2,1)S(1)} %maximum_bitcast_fusion.2), channel_id=1, source_target_pairs={{0,8},{1,9},{2,10},{3,11},{4,12},{5,13},{6,14},{7,15},{8,0},{9,1},... | collective-permute-start | bytes 196616 | tf_op jit(solution)/shard_map/ppermute | solution.py:23
  13.0 5.0 %collective-permute-start.5 = (bf16[4,8,2048]{2,1,0:T(8,128)(2,1)S(1)}, bf16[4,8,2048]{2,1,0:T(8,128)(2,1)S(1)}, u32[]{:S(2)}, u32[]{:S(2)}) collective-permute-start(bf16[4,8,2048]{2,1,0:T(8,128)(2,1)S(1)} %maximum_bitcast_fusion.1), channel_id=1, source_target_pairs={{0,2},{1,3},{2,0},{3,1},{4,6},{5,7},{6,4},{7,5},{8,10},{9,11},{10,... | collective-permute-start | bytes 393224 | tf_op jit(solution)/shard_map/ppermute | solution.py:71
  15.5 5.0 %collective-permute-start.1 = (bf16[2,8,4096]{2,1,0:T(8,128)(2,1)S(1)}, bf16[2,8,4096]{2,1,0:T(8,128)(2,1)S(1)}, u32[]{:S(2)}, u32[]{:S(2)}) collective-permute-start(bf16[2,8,4096]{2,1,0:T(8,128)(2,1)S(1)} %maximum_bitcast_fusion), channel_id=1, source_target_pairs={{0,4},{1,5},{2,6},{3,7},{4,0},{5,1},{6,2},{7,3},{8,12},{9,13},{10,... | collective-permute-start | bytes 393224 | tf_op jit(solution)/shard_map/ppermute | solution.py:23
  18.1 2.4 %collective-permute-start.6 = (bf16[8,8,2048]{2,1,0:T(8,128)(2,1)S(1)}, bf16[8,8,2048]{2,1,0:T(8,128)(2,1)S(1)}, u32[]{:S(2)}, u32[]{:S(2)}) collective-permute-start(bf16[8,8,2048]{2,1,0:T(8,128)(2,1)S(1)} %bitcast.100), channel_id=1, source_target_pairs={{0,1},{1,0},{2,3},{3,2},{4,5},{5,4},{6,7},{7,6},{8,9},{9,8},{10,11... | collective-permute-start | bytes 786440 | tf_op jit(solution)/shard_map/ppermute | solution.py:71
  21.5 7.5 %collective-permute-start.7 = (bf16[4,8,4096]{2,1,0:T(8,128)(2,1)S(1)}, bf16[4,8,4096]{2,1,0:T(8,128)(2,1)S(1)}, u32[]{:S(2)}, u32[]{:S(2)}) collective-permute-start(bf16[4,8,4096]{2,1,0:T(8,128)(2,1)S(1)} %bitcast.101), channel_id=1, source_target_pairs={{0,2},{1,3},{2,0},{3,1},{4,6},{5,7},{6,4},{7,5},{8,10},{9,11},{10,... | collective-permute-start | bytes 786440 | tf_op jit(solution)/shard_map/ppermute | solution.py:23
  29.2 7.0 %collective-permute-start.8 = (bf16[8,8,4096]{2,1,0:T(8,128)(2,1)S(1)}, bf16[8,8,4096]{2,1,0:T(8,128)(2,1)S(1)}, u32[]{:S(2)}, u32[]{:S(2)}) collective-permute-start(bf16[8,8,4096]{2,1,0:T(8,128)(2,1)S(1)} %bitcast.97), channel_id=1, source_target_pairs={{0,1},{1,0},{2,3},{3,2},{4,5},{5,4},{6,7},{7,6},{8,9},{9,8},{10,11... | collective-permute-start | bytes 1572872 | tf_op jit(solution)/shard_map/ppermute | solution.py:23
  32.7 3.5 %copy-start = (f32[128,512]{1,0:T(8,128)S(1)}, f32[128,512]{1,0:T(8,128)}, u32[]{:S(2)}) copy-start(f32[128,512]{1,0:T(8,128)} %get-tuple-element.55) | copy-start | bytes 786436
  32.7 3.5 %copy-start.1 = (f32[128,512]{1,0:T(8,128)S(1)}, f32[128,512]{1,0:T(8,128)}, u32[]{:S(2)}) copy-start(f32[128,512]{1,0:T(8,128)} %get-tuple-element.54) | copy-start | bytes 786436
  32.7 3.5 %copy-start.2 = (f32[128,512]{1,0:T(8,128)S(1)}, f32[128,512]{1,0:T(8,128)}, u32[]{:S(2)}) copy-start(f32[128,512]{1,0:T(8,128)} %get-tuple-element.66) | copy-start | bytes 786436
  32.7 3.5 %copy-start.3 = (f32[128,8]{1,0:T(8,128)S(1)}, f32[128,8]{1,0:T(8,128)}, u32[]{:S(2)}) copy-start(f32[128,8]{1,0:T(8,128)} %get-tuple-element.68) | copy-start | bytes 12292
  32.7 3.5 %copy-start.4 = (f32[128,8]{1,0:T(8,128)S(1)}, f32[128,8]{1,0:T(8,128)}, u32[]{:S(2)}) copy-start(f32[128,8]{1,0:T(8,128)} %get-tuple-element.72) | copy-start | bytes 12292
  32.7 3.5 %copy-start.5 = (f32[128,8]{1,0:T(8,128)S(1)}, f32[128,8]{1,0:T(8,128)}, u32[]{:S(2)}) copy-start(f32[128,8]{1,0:T(8,128)} %get-tuple-element.67) | copy-start | bytes 12292
  32.7 3.5 %copy-start.6 = (f32[128,8]{1,0:T(8,128)S(1)}, f32[128,8]{1,0:T(8,128)}, u32[]{:S(2)}) copy-start(f32[128,8]{1,0:T(8,128)} %get-tuple-element.71) | copy-start | bytes 12292
  32.7 3.5 %copy-start.7 = (f32[128,8]{1,0:T(8,128)S(1)}, f32[128,8]{1,0:T(8,128)}, u32[]{:S(2)}) copy-start(f32[128,8]{1,0:T(8,128)} %get-tuple-element.70) | copy-start | bytes 12292
  32.7 3.5 %copy-start.8 = (f32[128,8]{1,0:T(8,128)S(1)}, f32[128,8]{1,0:T(8,128)}, u32[]{:S(2)}) copy-start(f32[128,8]{1,0:T(8,128)} %get-tuple-element.74) | copy-start | bytes 12292
  38.1 5.1 %collective-permute-start.9 = (bf16[8,8,2208]{2,1,0:T(8,128)(2,1)S(1)}, bf16[8,8,2208]{2,1,0:T(8,128)(2,1)S(1)}, u32[]{:S(2)}, u32[]{:S(2)}) collective-permute-start(bf16[8,8,2208]{2,1,0:T(8,128)(2,1)S(1)} %concatenate.41), channel_id=1, source_target_pairs={{0,1},{1,0},{2,3},{3,2},{4,5},{5,4},{6,7},{7,6},{8,9},{9,8},{10,11... | collective-permute-start | bytes 847880 | tf_op jit(solution)/shard_map/ppermute | solution.py:23
  44.7 5.8 %collective-permute-start.10 = (bf16[4,8,2208]{2,1,0:T(8,128)(2,1)S(1)}, bf16[4,8,2208]{2,1,0:T(8,128)(2,1)S(1)}, u32[]{:S(2)}, u32[]{:S(2)}) collective-permute-start(bf16[4,8,2208]{2,1,0:T(8,128)(2,1)S(1)} %concatenate.44), channel_id=1, source_target_pairs={{0,2},{1,3},{2,0},{3,1},{4,6},{5,7},{6,4},{7,5},{8,10},{9,11},{10,... | collective-permute-start | bytes 423944 | tf_op jit(solution)/shard_map/ppermute | solution.py:23
  51.8 4.4 %collective-permute-start.11 = (bf16[2,8,2208]{2,1,0:T(8,128)(2,1)S(1)}, bf16[2,8,2208]{2,1,0:T(8,128)(2,1)S(1)}, u32[]{:S(2)}, u32[]{:S(2)}) collective-permute-start(bf16[2,8,2208]{2,1,0:T(8,128)(2,1)S(1)} %concatenate.47), channel_id=1, source_target_pairs={{0,4},{1,5},{2,6},{3,7},{4,0},{5,1},{6,2},{7,3},{8,12},{9,13},{10,... | collective-permute-start | bytes 211976 | tf_op jit(solution)/shard_map/ppermute | solution.py:23
  57.2 5.3 %collective-permute-start.12 = (bf16[1,8,2208]{2,1,0:T(8,128)(2,1)S(1)}, bf16[1,8,2208]{2,1,0:T(8,128)(2,1)S(1)}, u32[]{:S(2)}, u32[]{:S(2)}) collective-permute-start(bf16[1,8,2208]{2,1,0:T(8,128)(2,1)S(1)} %concatenate.50), channel_id=1, source_target_pairs={{0,8},{1,9},{2,10},{3,11},{4,12},{5,13},{6,14},{7,15},{8,0},{9,1},... | collective-permute-start | bytes 105992 | tf_op jit(solution)/shard_map/ppermute | solution.py:23

commit v15 on v14

--- a/solution.py
+++ b/solution.py
@@ -122,16 +122,18 @@
 def scatter_rows(state, heads, during=()):
     count = lax.axis_size("seq")
     me = lax.axis_index("seq")
-    rows = state.shape[0] // count
-    held = state.reshape((count, rows, state.shape[1]))
+    pieces = state
+    rows = pieces[0].shape[0] // count
+    columns = sum(piece.shape[1] for piece in pieces)
+    held = [piece.reshape((count, rows, piece.shape[1])) for piece in pieces]
     carried = None
     bit = 1
     step = 0
     while bit < count:
-        pairs = held.reshape((-1, 2, rows, state.shape[1]))
         upper = (me & bit) != 0
-        keep = jnp.where(upper, pairs[:, 1], pairs[:, 0])
-        give = jnp.where(upper, pairs[:, 0], pairs[:, 1])
+        pairs = [piece.reshape((-1, 2, rows, piece.shape[-1])) for piece in held]
+        keep = jnp.concatenate([jnp.where(upper, p[:, 1], p[:, 0]) for p in pairs], axis=-1)
+        give = jnp.concatenate([jnp.where(upper, p[:, 0], p[:, 1]) for p in pairs], axis=-1)
         work = during[step] if step < len(during) else None
         if work is not None:
             give, carried = lax.optimization_barrier((give, carried))
@@ -139,14 +141,16 @@
         if work is not None:
             carried = work(carried)
             arrived, carried = lax.optimization_barrier((arrived, carried))
-        held = merge(
-            keep.reshape((-1, state.shape[1])), arrived.reshape((-1, state.shape[1])), heads
-        ).reshape((-1, rows, state.shape[1]))
+        held = [
+            merge(keep.reshape((-1, columns)), arrived.reshape((-1, columns)), heads).reshape(
+                (-1, rows, columns)
+            )
+        ]
         bit *= 2
         step += 1
     for work in during[step:]:
         carried = work(carried)
-    return held.reshape((rows, state.shape[1])), carried
+    return held[0].reshape((rows, columns)), carried
 
 
 def head_masks(rows):
@@ -321,10 +325,7 @@
     parts = [part for result in results for part in result]
     all_keys = gathered[:, :width]
     all_values = gathered[:, width:]
-    state = jnp.concatenate(
-        [part[0] for part in parts] + [part[1] for part in parts] + [part[2] for part in parts],
-        axis=1,
-    )
+    state = [part[0] for part in parts] + [part[1] for part in parts] + [part[2] for part in parts]
     video_calls = [
         lambda earlier, g=g: video_part(video_q, all_keys, all_values, earlier, g, groups)
         for g in range(groups)

time: 64.6 us -> 65.3 us (1.011)
  other arithmetic: 4.01 us -> 5.09 us
    concatenate x1, local copies, waits for them, and re-layouts: 1.23 us -> 0.13 us  [scatter_rows(): jnp.concatenate([jnp.where(upper, p[:, 0], p[:, 1]) for p in pairs], axis...]
    select_n x4 -> x11, other arithmetic: 0.15 us -> 1.2 us  [the longest x4 1.07 us: scatter_rows(): jnp.where(upper, p[:, 0], p[:, 1])]
  transfers between devices with their start and end apart: 13 -> 13, of which waited for: 6 -> 6; matrix products, arithmetic and copies ran while one was open for 6% -> 6% of each run, Pallas kernels for 43% -> 42%
where the time goes in v15:
time: 65.3 us; the launch traced here: 64.7 us
  Pallas kernels  27.4 us (42%)
  starting transfers between devices  13.7 us (21%)
  waiting for transfers between devices  10.2 us (16%)
  other arithmetic  5.09 us (8%)
  local copies, waits for them, and re-layouts  3.74 us (6%)
  matrix products  3.41 us (5%)
  between operations  1.11 us (2%)
    pallas_call x4, Pallas kernels, video_part(): pl.pallas_call(video_kernel, grid=(pairs // PER_STEP,), in_specs=specs, o...  13.9 us
    pallas_call x4, Pallas kernels, audio_partial(): pl.pallas_call(audio_kernel, grid=(heads // 2 // PER_STEP,), in_specs=[pl...  13.5 us
    ppermute x5, starting transfers between devices, gather_levels(): pieces[offset] = lax.ppermute(held, 'seq', pairs)  7.34 us
    ppermute x8, starting transfers between devices, exchange(): return lax.ppermute(value, 'seq', pairs)  6.39 us
    ppermute x5, waiting for transfers between devices, gather_levels(): pieces[offset] = lax.ppermute(held, 'seq', pairs)  5.74 us
    ppermute x8, waiting for transfers between devices, exchange(): return lax.ppermute(value, 'seq', pairs)  4.49 us
    dot_general x9, matrix products, spread(): jnp.dot(scales, expand, precision=lax.Precision.HIGHEST, preferred_elemen...  3.41 us
  transfers between devices with their start and end apart: 13, of which 6 were waited for; matrix products, arithmetic and copies ran while one was open for 6% of the time, Pallas kernels for 42%

profile of v15, /device:TPU:0, one launch (start us, length us, event | category | flops | bytes accessed | tf_op | source)
XLA Modules:
  0.0 64.7 jit_solution(4672623835305741262)
XLA Ops:
  0.6 4.1 %collective-permute-start.4 = (bf16[1,8,2048]{2,1,0:T(8,128)(2,1)}, bf16[1,8,2048]{2,1,0:T(8,128)(2,1)S(1)}, u32[]{:S(2)}, u32[]{:S(2)}) collective-permute-start(bf16[1,8,2048]{2,1,0:T(8,128)(2,1)} %bitcast.226), channel_id=1, source_target_pairs={{0,8},{1,9},{2,10},{3,11},{4,12},{5,13},{6,14},{7,15},{8,0},{9,1},... | collective-permute-start | bytes 98312 | tf_op jit(solution)/shard_map/ppermute | solution.py:71
  4.7 1.6 %collective-permute-start.3 = (bf16[1,8,2048]{2,1,0:T(8,128)(2,1)}, bf16[1,8,2048]{2,1,0:T(8,128)(2,1)S(1)}, u32[]{:S(2)}, u32[]{:S(2)}) collective-permute-start(bf16[1,8,2048]{2,1,0:T(8,128)(2,1)} %bitcast.227), channel_id=1, source_target_pairs={{0,4},{1,5},{2,6},{3,7},{4,0},{5,1},{6,2},{7,3},{8,12},{9,13},{10,... | collective-permute-start | bytes 98312 | tf_op jit(solution)/shard_map/ppermute | solution.py:71
  6.3 0.8 %maximum_bitcast_fusion.2 = bf16[1,8,4096]{2,1,0:T(8,128)(2,1)S(1)} fusion(bf16[8,2048]{1,0:T(8,128)(2,1)} %param.11, bf16[8,2048]{1,0:T(8,128)(2,1)} %param.10), kind=kLoop, calls=%fused_computation.87 | loop fusion | flops 131072 | bytes 131072 | tf_op jit(solution)/shard_map/broadcast_in_dim | solution.py:29
  7.1 1.9 %collective-permute-start = (bf16[1,8,4096]{2,1,0:T(8,128)(2,1)S(1)}, bf16[1,8,4096]{2,1,0:T(8,128)(2,1)S(1)}, u32[]{:S(2)}, u32[]{:S(2)}) collective-permute-start(bf16[1,8,4096]{2,1,0:T(8,128)(2,1)S(1)} %maximum_bitcast_fusion.2), channel_id=1, source_target_pairs={{0,8},{1,9},{2,10},{3,11},{4,12},{5,13},{6,14},{7,15},{8,0},{9,1},... | collective-permute-start | bytes 196616 | tf_op jit(solution)/shard_map/ppermute | solution.py:23
  9.0 3.2 %collective-permute-done.2 = bf16[1,8,2048]{2,1,0:T(8,128)(2,1)S(1)} collective-permute-done((bf16[1,8,2048]{2,1,0:T(8,128)(2,1)}, bf16[1,8,2048]{2,1,0:T(8,128)(2,1)S(1)}, u32[]{:S(2)}, u32[]{:S(2)}) %collective-permute-start.2) | collective-permute-done | bytes 32800 | tf_op jit(solution)/shard_map/ppermute | solution.py:71
  12.2 0.8 %select_bitcast_fusion.44 = (bf16[1,1,8,2048]{3,2,1,0:T(8,128)(2,1)S(1)}, bf16[1,1,8,2048]{3,2,1,0:T(8,128)(2,1)S(1)}, bf16[1,1,8,2048]{3,2,1,0:T(8,128)(2,1)S(1)}, bf16[1,1,8,2048]{3,2,1,0:T(8,128)(2,1)S(1)}) fusion(bf16[1,8,2048]{2,1,0:T(8,128)(2,1)S(1)} %collective-permute-done.2, bf16[1,8,2048]{2,1,0:T(8,128)(2,1)S(1)} %collective-permute-done.3, ...), kind=kLoop, calls=%fused_computation.128 | loop fusion | flops 196608 | bytes 262156 | tf_op jit(solution)/shard_map/stack | solution.py:79
  13.0 1.6 %collective-permute-start.5 = (bf16[4,8,2048]{2,1,0:T(8,128)(2,1)S(1)}, bf16[4,8,2048]{2,1,0:T(8,128)(2,1)S(1)}, u32[]{:S(2)}, u32[]{:S(2)}) collective-permute-start(bf16[4,8,2048]{2,1,0:T(8,128)(2,1)S(1)} %maximum_bitcast_fusion.1), channel_id=1, source_target_pairs={{0,2},{1,3},{2,0},{3,1},{4,6},{5,7},{6,4},{7,5},{8,10},{9,11},{10,... | collective-permute-start | bytes 393224 | tf_op jit(solution)/shard_map/ppermute | solution.py:71
  14.6 0.8 %select_bitcast_fusion.24 = (bf16[1,1,8,4096]{3,2,1,0:T(8,128)(2,1)S(1)}, bf16[1,1,8,4096]{3,2,1,0:T(8,128)(2,1)S(1)}) fusion(bf16[1,8,4096]{2,1,0:T(8,128)(2,1)S(1)} %collective-permute-done, pred[]{:T(512)S(6)} %ne.98, bf16[8,2048]{1,0:T(8,128)(2,1)} %param.11, bf16[8,2048]{1,0:T(8,128)(2,1)} %param.10), kind=kLoop, calls=%fused_computation.89 | loop fusion | flops 196608 | bytes 262145 | tf_op jit(solution)/shard_map/stack | solution.py:45
  15.5 0.1 collective-permute-start.1
  15.6 2.5 %collective-permute-done.5 = bf16[4,8,2048]{2,1,0:T(8,128)(2,1)S(1)} collective-permute-done((bf16[4,8,2048]{2,1,0:T(8,128)(2,1)S(1)}, bf16[4,8,2048]{2,1,0:T(8,128)(2,1)S(1)}, u32[]{:S(2)}, u32[]{:S(2)}) %collective-permute-start.5) | collective-permute-done | bytes 131104 | tf_op jit(solution)/shard_map/ppermute | solution.py:71
  18.2 2.3 %collective-permute-done.1 = bf16[2,8,4096]{2,1,0:T(8,128)(2,1)S(1)} collective-permute-done((bf16[2,8,4096]{2,1,0:T(8,128)(2,1)S(1)}, bf16[2,8,4096]{2,1,0:T(8,128)(2,1)S(1)}, u32[]{:S(2)}, u32[]{:S(2)}) %collective-permute-start.1) | collective-permute-done | bytes 131104 | tf_op jit(solution)/shard_map/ppermute | solution.py:23
  20.7 0.8 %copy.40 = bf16[8,2,8,2048]{3,2,1,0:T(8,128)(2,1)} copy(bf16[8,2,8,2048]{3,2,0,1:T(8,128)(2,1)S(1)} %pad_maximum_fusion.1) | data formatting | bytes 1048576 | tf_op jit(solution)/shard_map/stack | solution.py:79
  21.5 0.7 %collective-permute-start.7 = (bf16[4,8,4096]{2,1,0:T(8,128)(2,1)S(1)}, bf16[4,8,4096]{2,1,0:T(8,128)(2,1)S(1)}, u32[]{:S(2)}, u32[]{:S(2)}) collective-permute-start(bf16[4,8,4096]{2,1,0:T(8,128)(2,1)S(1)} %bitcast.203), channel_id=1, source_target_pairs={{0,2},{1,3},{2,0},{3,1},{4,6},{5,7},{6,4},{7,5},{8,10},{9,11},{10,... | collective-permute-start | bytes 786440 | tf_op jit(solution)/shard_map/ppermute | solution.py:23
  22.2 3.4 %shard_map.78 = (f32[128,512]{1,0:T(8,128)}, f32[128,8]{1,0:T(8,128)}, f32[128,8]{1,0:T(8,128)}) custom-call(bf16[128,2048]{1,0:T(8,128)(2,1)} %bitcast.191, bf16[512,2048]{1,0:T(8,128)(2,1)} %key_ref.7, bf16[512,2048]{1,0:T(8,128)(2,1)} %value_ref.7), custom_call_target="tpu_custom_call" | custom-call | flops 268435456 | bytes 1441792 | tf_op jit(solution)/shard_map/pallas_call | solution.py:282
  25.6 3.3 %shard_map.77 = (f32[128,512]{1,0:T(8,128)}, f32[128,8]{1,0:T(8,128)}, f32[128,8]{1,0:T(8,128)}) custom-call(bf16[128,2048]{1,0:T(8,128)(2,1)} %bitcast.192, bf16[512,2048]{1,0:T(8,128)(2,1)} %key_ref.7, bf16[512,2048]{1,0:T(8,128)(2,1)} %value_ref.7), custom_call_target="tpu_custom_call" | custom-call | flops 268435456 | bytes 1441792 | tf_op jit(solution)/shard_map/pallas_call | solution.py:282
  28.9 0.1 collective-permute-done.7
  29.3 0.5 copy-done.9
  29.8 3.4 %shard_map.80 = (f32[128,512]{1,0:T(8,128)}, f32[128,8]{1,0:T(8,128)}, f32[128,8]{1,0:T(8,128)}) custom-call(bf16[128,2048]{1,0:T(8,128)(2,1)} %bitcast.193, bf16[512,2048]{1,0:T(8,128)(2,1)} %key_ref.7, bf16[512,2048]{1,0:T(8,128)(2,1)} %value_ref.7), custom_call_target="tpu_custom_call" | custom-call | flops 268435456 | bytes 1441792 | tf_op jit(solution)/shard_map/pallas_call | solution.py:282
  33.2 3.4 %shard_map.79 = (f32[128,512]{1,0:T(8,128)}, f32[128,8]{1,0:T(8,128)}, f32[128,8]{1,0:T(8,128)}) custom-call(bf16[128,2048]{1,0:T(8,128)(2,1)} %bitcast.194, bf16[512,2048]{1,0:T(8,128)(2,1)} %key_ref.7, bf16[512,2048]{1,0:T(8,128)(2,1)} %value_ref.7), custom_call_target="tpu_custom_call" | custom-call | flops 268435456 | bytes 1441792 | tf_op jit(solution)/shard_map/pallas_call | solution.py:282
  36.8 1.0 %select_bitcast_fusion.11 = (f32[8,8,512]{2,1,0:T(8,128)S(1)}, f32[64,512]{1,0:T(8,128)S(1)}, f32[64,512]{1,0:T(8,128)S(1)}, f32[8,8,512]{2,1,0:T(8,128)S(1)}) fusion(f32[8,2,8,512]{3,2,1,0:T(8,128)} %bitcast.212, pred[]{:T(512)S(6)} %ne.101, f32[8,2,8,512]{3,2,1,0:T(8,128)S(1)} %bitcast.211), kind=kLoop, calls=%fused_computation.64 | loop fusion | flops 131072 | bytes 1048577 | tf_op jit(solution)/shard_map/jit(_where)/select_n | solution.py:136
  37.9 0.1 concatenate.53
  38.1 0.1 fusion.36
  38.3 0.1 pad_maximum_fusion
  38.4 0.1 copy.52
  38.5 0.1 concatenate.54
  38.7 1.1 %fusion.63 = (bf16[128,2048]{1,0:T(8,128)(2,1)}, bf16[128,2048]{1,0:T(8,128)(2,1)}) fusion(bf16[128,4096]{1,0:T(8,128)(2,1)S(1)} %bitcast.195), kind=kLoop, calls=%fused_computation.192 | loop fusion | bytes 2097152 | tf_op jit(solution)/shard_map/slice | solution.py:327
  39.7 3.5 %shard_map.81.refs_0_ = bf16[512,2048]{1,0:T(8,128)(2,1)} custom-call(bf16[512,2048]{1,0:T(8,128)(2,1)} %query_ref.7, bf16[128,2048]{1,0:T(8,128)(2,1)} %get-tuple-element.98.key_ref, bf16[128,2048]{1,0:T(8,128)(2,1)} %get-tuple-element.97.value_ref), custom_call_target="tpu_custom_call" | custom-call | flops 268435456 | bytes 1310720 | tf_op jit(solution)/shard_map/pallas_call | solution.py:236
  43.5 0.1 fusion.37
  43.6 0.4 convolution_multiply_fusion.1
  44.0 0.4 fusion
  44.7 0.1 concatenate.58
  44.8 1.5 %collective-permute-start.10 = (bf16[4,8,2208]{2,1,0:T(8,128)(2,1)S(1)}, bf16[4,8,2208]{2,1,0:T(8,128)(2,1)S(1)}, u32[]{:S(2)}, u32[]{:S(2)}) collective-permute-start(bf16[4,8,2208]{2,1,0:T(8,128)(2,1)S(1)} %concatenate.58), channel_id=1, source_target_pairs={{0,2},{1,3},{2,0},{3,1},{4,6},{5,7},{6,4},{7,5},{8,10},{9,11},{10,... | collective-permute-start | bytes 423944 | tf_op jit(solution)/shard_map/ppermute | solution.py:23
  46.3 3.5 %shard_map.82.refs_0_ = bf16[512,2048]{1,0:T(8,128)(2,1)} custom-call(bf16[512,2048]{1,0:T(8,128)(2,1)} %query_ref.7, bf16[128,2048]{1,0:T(8,128)(2,1)} %get-tuple-element.98.key_ref, bf16[128,2048]{1,0:T(8,128)(2,1)} %get-tuple-element.97.value_ref, bf16[512,2048]{1,0:T(8,128)(2,1)} %shard_map.81.refs_0_), custom_call_target="tpu_custom_call", output_to_operand_aliasing={{}: (3, {})} | custom-call | flops 268435456 | bytes 1310720 | tf_op jit(solution)/shard_map/pallas_call | solution.py:236
  49.8 1.3 %collective-permute-done.10 = bf16[4,8,2208]{2,1,0:T(8,128)(2,1)S(1)} collective-permute-done((bf16[4,8,2208]{2,1,0:T(8,128)(2,1)S(1)}, bf16[4,8,2208]{2,1,0:T(8,128)(2,1)S(1)}, u32[]{:S(2)}, u32[]{:S(2)}) %collective-permute-start.10) | collective-permute-done | bytes 141344 | tf_op jit(solution)/shard_map/ppermute | solution.py:23
  51.2 0.1 fusion.42
  51.3 0.3 convolution_multiply_fusion.2
  51.7 0.3 fusion.1
  52.2 0.1 concatenate.61
  52.4 3.5 %shard_map.83.refs_0_ = bf16[512,2048]{1,0:T(8,128)(2,1)} custom-call(bf16[512,2048]{1,0:T(8,128)(2,1)} %query_ref.7, bf16[128,2048]{1,0:T(8,128)(2,1)} %get-tuple-element.98.key_ref, bf16[128,2048]{1,0:T(8,128)(2,1)} %get-tuple-element.97.value_ref, bf16[512,2048]{1,0:T(8,128)(2,1)} %shard_map.82.refs_0_), custom_call_target="tpu_custom_call", output_to_operand_aliasing={{}: (3, {})} | custom-call | flops 268435456 | bytes 1310720 | tf_op jit(solution)/shard_map/pallas_call | solution.py:236
  55.8 0.8 %collective-permute-done.11 = bf16[2,8,2208]{2,1,0:T(8,128)(2,1)S(1)} collective-permute-done((bf16[2,8,2208]{2,1,0:T(8,128)(2,1)S(1)}, bf16[2,8,2208]{2,1,0:T(8,128)(2,1)S(1)}, u32[]{:S(2)}, u32[]{:S(2)}) %collective-permute-start.11) | collective-permute-done | bytes 70688 | tf_op jit(solution)/shard_map/ppermute | solution.py:23
  56.9 0.3 convolution_multiply_fusion.5
  57.2 0.3 fusion.2
  57.6 0.1 concatenate.64
  57.7 2.0 %collective-permute-start.12 = (bf16[1,8,2208]{2,1,0:T(8,128)(2,1)S(1)}, bf16[1,8,2208]{2,1,0:T(8,128)(2,1)S(1)}, u32[]{:S(2)}, u32[]{:S(2)}) collective-permute-start(bf16[1,8,2208]{2,1,0:T(8,128)(2,1)S(1)} %concatenate.64), channel_id=1, source_target_pairs={{0,8},{1,9},{2,10},{3,11},{4,12},{5,13},{6,14},{7,15},{8,0},{9,1},... | collective-permute-start | bytes 105992 | tf_op jit(solution)/shard_map/ppermute | solution.py:23
  59.7 3.5 %shard_map.84 = bf16[512,2048]{1,0:T(8,128)(2,1)} custom-call(bf16[512,2048]{1,0:T(8,128)(2,1)} %query_ref.7, bf16[128,2048]{1,0:T(8,128)(2,1)} %get-tuple-element.98.key_ref, bf16[128,2048]{1,0:T(8,128)(2,1)} %get-tuple-element.97.value_ref, bf16[512,2048]{1,0:T(8,128)(2,1)} %shard_map.83.refs_0_), custom_call_target="tpu_custom_call", output_to_operand_aliasing={{}: (3, {})} | custom-call | flops 268435456 | bytes 1310720 | tf_op jit(solution)/shard_map/pallas_call | solution.py:236
  63.3 0.3 convolution_multiply_fusion.7
  63.6 0.3 fusion.3
  63.9 0.9 %fusion.4 = bf16[8,2048]{1,0:T(8,128)(2,1)} fusion(f32[8,2048]{1,0:T(8,128)S(1)} %fusion.3, s32[2048]{0:T(1024)S(1)} %get-tuple-element.181, s32[2048]{0:T(1024)S(1)} %get-tuple-element.182, pred[2048]{0:T(1024)(128)(4,1)S(1)} %fusion.50, f32[8,2112]{1,0:T(8,128)S(1)} %bitcast.217, f32[8,2112]{1,0:T(8,128)S(1)} %get-tuple-element.133), kind=kOutput, calls=%fused_computation.13 | convolution fusion | flops 6456832 | bytes 133120 | tf_op jit(solution)/shard_map/dot_general | solution.py:16
  (80 shorter events, 2.3 us)
Async XLA Ops:
  0.6 8.4 %collective-permute-start.4 = (bf16[1,8,2048]{2,1,0:T(8,128)(2,1)}, bf16[1,8,2048]{2,1,0:T(8,128)(2,1)S(1)}, u32[]{:S(2)}, u32[]{:S(2)}) collective-permute-start(bf16[1,8,2048]{2,1,0:T(8,128)(2,1)} %bitcast.226), channel_id=1, source_target_pairs={{0,8},{1,9},{2,10},{3,11},{4,12},{5,13},{6,14},{7,15},{8,0},{9,1},... | collective-permute-start | bytes 98312 | tf_op jit(solution)/shard_map/ppermute | solution.py:71
  4.7 4.3 %collective-permute-start.3 = (bf16[1,8,2048]{2,1,0:T(8,128)(2,1)}, bf16[1,8,2048]{2,1,0:T(8,128)(2,1)S(1)}, u32[]{:S(2)}, u32[]{:S(2)}) collective-permute-start(bf16[1,8,2048]{2,1,0:T(8,128)(2,1)} %bitcast.227), channel_id=1, source_target_pairs={{0,4},{1,5},{2,6},{3,7},{4,0},{5,1},{6,2},{7,3},{8,12},{9,13},{10,... | collective-permute-start | bytes 98312 | tf_op jit(solution)/shard_map/ppermute | solution.py:71
  6.3 5.9 %collective-permute-start.2 = (bf16[1,8,2048]{2,1,0:T(8,128)(2,1)}, bf16[1,8,2048]{2,1,0:T(8,128)(2,1)S(1)}, u32[]{:S(2)}, u32[]{:S(2)}) collective-permute-start(bf16[1,8,2048]{2,1,0:T(8,128)(2,1)} %bitcast.228), channel_id=1, source_target_pairs={{0,12},{1,13},{2,14},{3,15},{4,8},{5,9},{6,10},{7,11},{8,4},{9,5},... | collective-permute-start | bytes 98312 | tf_op jit(solution)/shard_map/ppermute | solution.py:71
  7.1 7.5 %collective-permute-start = (bf16[1,8,4096]{2,1,0:T(8,128)(2,1)S(1)}, bf16[1,8,4096]{2,1,0:T(8,128)(2,1)S(1)}, u32[]{:S(2)}, u32[]{:S(2)}) collective-permute-start(bf16[1,8,4096]{2,1,0:T(8,128)(2,1)S(1)} %maximum_bitcast_fusion.2), channel_id=1, source_target_pairs={{0,8},{1,9},{2,10},{3,11},{4,12},{5,13},{6,14},{7,15},{8,0},{9,1},... | collective-permute-start | bytes 196616 | tf_op jit(solution)/shard_map/ppermute | solution.py:23
  13.0 5.0 %collective-permute-start.5 = (bf16[4,8,2048]{2,1,0:T(8,128)(2,1)S(1)}, bf16[4,8,2048]{2,1,0:T(8,128)(2,1)S(1)}, u32[]{:S(2)}, u32[]{:S(2)}) collective-permute-start(bf16[4,8,2048]{2,1,0:T(8,128)(2,1)S(1)} %maximum_bitcast_fusion.1), channel_id=1, source_target_pairs={{0,2},{1,3},{2,0},{3,1},{4,6},{5,7},{6,4},{7,5},{8,10},{9,11},{10,... | collective-permute-start | bytes 393224 | tf_op jit(solution)/shard_map/ppermute | solution.py:71
  15.5 5.0 %collective-permute-start.1 = (bf16[2,8,4096]{2,1,0:T(8,128)(2,1)S(1)}, bf16[2,8,4096]{2,1,0:T(8,128)(2,1)S(1)}, u32[]{:S(2)}, u32[]{:S(2)}) collective-permute-start(bf16[2,8,4096]{2,1,0:T(8,128)(2,1)S(1)} %maximum_bitcast_fusion), channel_id=1, source_target_pairs={{0,4},{1,5},{2,6},{3,7},{4,0},{5,1},{6,2},{7,3},{8,12},{9,13},{10,... | collective-permute-start | bytes 393224 | tf_op jit(solution)/shard_map/ppermute | solution.py:23
  18.1 2.4 %collective-permute-start.6 = (bf16[8,8,2048]{2,1,0:T(8,128)(2,1)S(1)}, bf16[8,8,2048]{2,1,0:T(8,128)(2,1)S(1)}, u32[]{:S(2)}, u32[]{:S(2)}) collective-permute-start(bf16[8,8,2048]{2,1,0:T(8,128)(2,1)S(1)} %bitcast.200), channel_id=1, source_target_pairs={{0,1},{1,0},{2,3},{3,2},{4,5},{5,4},{6,7},{7,6},{8,9},{9,8},{10,11... | collective-permute-start | bytes 786440 | tf_op jit(solution)/shard_map/ppermute | solution.py:71
  21.5 7.5 %collective-permute-start.7 = (bf16[4,8,4096]{2,1,0:T(8,128)(2,1)S(1)}, bf16[4,8,4096]{2,1,0:T(8,128)(2,1)S(1)}, u32[]{:S(2)}, u32[]{:S(2)}) collective-permute-start(bf16[4,8,4096]{2,1,0:T(8,128)(2,1)S(1)} %bitcast.203), channel_id=1, source_target_pairs={{0,2},{1,3},{2,0},{3,1},{4,6},{5,7},{6,4},{7,5},{8,10},{9,11},{10,... | collective-permute-start | bytes 786440 | tf_op jit(solution)/shard_map/ppermute | solution.py:23
  28.9 0.8 %copy-start.9 = (f32[128,8]{1,0:T(8,128)S(1)}, f32[128,8]{1,0:T(8,128)}, u32[]{:S(2)}) copy-start(f32[128,8]{1,0:T(8,128)} %get-tuple-element.68) | copy-start | bytes 12292
  28.9 0.9 %copy-start.10 = (f32[128,8]{1,0:T(8,128)S(1)}, f32[128,8]{1,0:T(8,128)}, u32[]{:S(2)}) copy-start(f32[128,8]{1,0:T(8,128)} %get-tuple-element.67) | copy-start | bytes 12292
  29.2 7.6 %collective-permute-start.8 = (bf16[8,8,4096]{2,1,0:T(8,128)(2,1)S(1)}, bf16[8,8,4096]{2,1,0:T(8,128)(2,1)S(1)}, u32[]{:S(2)}, u32[]{:S(2)}) collective-permute-start(bf16[8,8,4096]{2,1,0:T(8,128)(2,1)S(1)} %bitcast.197), channel_id=1, source_target_pairs={{0,1},{1,0},{2,3},{3,2},{4,5},{5,4},{6,7},{7,6},{8,9},{9,8},{10,11... | collective-permute-start | bytes 1572872 | tf_op jit(solution)/shard_map/ppermute | solution.py:23
  33.2 3.5 %copy-start.3 = (f32[128,8]{1,0:T(8,128)S(1)}, f32[128,8]{1,0:T(8,128)}, u32[]{:S(2)}) copy-start(f32[128,8]{1,0:T(8,128)} %get-tuple-element.72) | copy-start | bytes 12292
  33.2 3.5 %copy-start.4 = (f32[128,8]{1,0:T(8,128)S(1)}, f32[128,8]{1,0:T(8,128)}, u32[]{:S(2)}) copy-start(f32[128,8]{1,0:T(8,128)} %get-tuple-element.71) | copy-start | bytes 12292
  33.2 3.5 %copy-start.1 = (f32[128,512]{1,0:T(8,128)S(1)}, f32[128,512]{1,0:T(8,128)}, u32[]{:S(2)}) copy-start(f32[128,512]{1,0:T(8,128)} %get-tuple-element.54) | copy-start | bytes 786436
  33.2 3.6 %copy-start = (f32[128,512]{1,0:T(8,128)S(1)}, f32[128,512]{1,0:T(8,128)}, u32[]{:S(2)}) copy-start(f32[128,512]{1,0:T(8,128)} %get-tuple-element.66) | copy-start | bytes 786436
  33.2 3.6 %copy-start.2 = (f32[128,512]{1,0:T(8,128)S(1)}, f32[128,512]{1,0:T(8,128)}, u32[]{:S(2)}) copy-start(f32[128,512]{1,0:T(8,128)} %get-tuple-element.55) | copy-start | bytes 786436
  36.7 1.2 %copy-start.7 = (f32[128,8]{1,0:T(8,128)S(1)}, f32[128,8]{1,0:T(8,128)}, u32[]{:S(2)}) copy-start(f32[128,8]{1,0:T(8,128)} %get-tuple-element.70) | copy-start | bytes 12292
  36.7 1.2 %copy-start.8 = (f32[128,8]{1,0:T(8,128)S(1)}, f32[128,8]{1,0:T(8,128)}, u32[]{:S(2)}) copy-start(f32[128,8]{1,0:T(8,128)} %get-tuple-element.69) | copy-start | bytes 12292
  36.7 1.2 %copy-start.5 = (f32[128,8]{1,0:T(8,128)S(1)}, f32[128,8]{1,0:T(8,128)}, u32[]{:S(2)}) copy-start(f32[128,8]{1,0:T(8,128)} %get-tuple-element.74) | copy-start | bytes 12292
  36.7 1.2 %copy-start.6 = (f32[128,8]{1,0:T(8,128)S(1)}, f32[128,8]{1,0:T(8,128)}, u32[]{:S(2)}) copy-start(f32[128,8]{1,0:T(8,128)} %get-tuple-element.73) | copy-start | bytes 12292
  38.6 4.7 %collective-permute-start.9 = (bf16[8,8,2208]{2,1,0:T(8,128)(2,1)S(1)}, bf16[8,8,2208]{2,1,0:T(8,128)(2,1)S(1)}, u32[]{:S(2)}, u32[]{:S(2)}) collective-permute-start(bf16[8,8,2208]{2,1,0:T(8,128)(2,1)S(1)} %concatenate.54), channel_id=1, source_target_pairs={{0,1},{1,0},{2,3},{3,2},{4,5},{5,4},{6,7},{7,6},{8,9},{9,8},{10,11... | collective-permute-start | bytes 847880 | tf_op jit(solution)/shard_map/ppermute | solution.py:23
  44.8 6.3 %collective-permute-start.10 = (bf16[4,8,2208]{2,1,0:T(8,128)(2,1)S(1)}, bf16[4,8,2208]{2,1,0:T(8,128)(2,1)S(1)}, u32[]{:S(2)}, u32[]{:S(2)}) collective-permute-start(bf16[4,8,2208]{2,1,0:T(8,128)(2,1)S(1)} %concatenate.58), channel_id=1, source_target_pairs={{0,2},{1,3},{2,0},{3,1},{4,6},{5,7},{6,4},{7,5},{8,10},{9,11},{10,... | collective-permute-start | bytes 423944 | tf_op jit(solution)/shard_map/ppermute | solution.py:23
  52.3 4.4 %collective-permute-start.11 = (bf16[2,8,2208]{2,1,0:T(8,128)(2,1)S(1)}, bf16[2,8,2208]{2,1,0:T(8,128)(2,1)S(1)}, u32[]{:S(2)}, u32[]{:S(2)}) collective-permute-start(bf16[2,8,2208]{2,1,0:T(8,128)(2,1)S(1)} %concatenate.61), channel_id=1, source_target_pairs={{0,4},{1,5},{2,6},{3,7},{4,0},{5,1},{6,2},{7,3},{8,12},{9,13},{10,... | collective-permute-start | bytes 211976 | tf_op jit(solution)/shard_map/ppermute | solution.py:23
  57.7 5.4 %collective-permute-start.12 = (bf16[1,8,2208]{2,1,0:T(8,128)(2,1)S(1)}, bf16[1,8,2208]{2,1,0:T(8,128)(2,1)S(1)}, u32[]{:S(2)}, u32[]{:S(2)}) collective-permute-start(bf16[1,8,2208]{2,1,0:T(8,128)(2,1)S(1)} %concatenate.64), channel_id=1, source_target_pairs={{0,8},{1,9},{2,10},{3,11},{4,12},{5,13},{6,14},{7,15},{8,0},{9,1},... | collective-permute-start | bytes 105992 | tf_op jit(solution)/shard_map/ppermute | solution.py:23

commit v16 on v12

--- a/solution.py
+++ b/solution.py
@@ -320,10 +320,9 @@
         )
         for gs in ((0, 1), (2, 3))
     ]
-    gathered, results = gather_rows(
-        jnp.concatenate([audio_k, audio_v], axis=1), [None] * (steps - 2) + audio_calls
-    )
-    parts = [part for result in results for part in result]
+    gathered, ignored = gather_rows(jnp.concatenate([audio_k, audio_v], axis=1))
+    ready, gathered = lax.optimization_barrier((all_queries, gathered))
+    parts = [part for call in audio_calls for part in call[0](ready)]
     all_keys = gathered[:, :width]
     all_values = gathered[:, width:]
     state = jnp.concatenate(

time: 64.8 us -> 70.7 us (1.091)
  waiting for transfers between devices: 9.66 us -> 15.6 us
    ppermute x8, waiting for transfers between devices: 3.92 us -> 12.4 us  [exchange(): return lax.ppermute(value, 'seq', pairs)]
    ppermute x5, waiting for transfers between devices: 5.74 us -> 3.17 us  [gather_levels(): pieces[offset] = lax.ppermute(held, 'seq', pairs)]
  transfers between devices with their start and end apart: 13 -> 13, of which waited for: 6 -> 7; matrix products, arithmetic and copies ran while one was open for 6% -> 5% of each run, Pallas kernels for 43% -> 20%
where the time goes in v16:
time: 70.7 us; the launch traced here: 70.2 us
  Pallas kernels  27.7 us (39%)
  waiting for transfers between devices  15.6 us (22%)
  starting transfers between devices  14 us (20%)
  local copies, waits for them, and re-layouts  4.3 us (6%)
  other arithmetic  4.05 us (6%)
  matrix products  3.47 us (5%)
  between operations  1.12 us (2%)
    pallas_call x4, Pallas kernels, video_part(): pl.pallas_call(video_kernel, grid=(pairs // PER_STEP,), in_specs=specs, o...  14.1 us
    pallas_call x4, Pallas kernels, audio_partial(): pl.pallas_call(audio_kernel, grid=(heads // 2 // PER_STEP,), in_specs=[pl...  13.6 us
    ppermute x8, waiting for transfers between devices, exchange(): return lax.ppermute(value, 'seq', pairs)  12.4 us
    ppermute x5, starting transfers between devices, gather_levels(): pieces[offset] = lax.ppermute(held, 'seq', pairs)  7.34 us
    ppermute x8, starting transfers between devices, exchange(): return lax.ppermute(value, 'seq', pairs)  6.67 us
    dot_general x9, matrix products, spread(): jnp.dot(scales, expand, precision=lax.Precision.HIGHEST, preferred_elemen...  3.47 us
    ppermute x5, waiting for transfers between devices, gather_levels(): pieces[offset] = lax.ppermute(held, 'seq', pairs)  3.17 us
  transfers between devices with their start and end apart: 13, of which 7 were waited for; matrix products, arithmetic and copies ran while one was open for 5% of the time, Pallas kernels for 20%

profile of v16, /device:TPU:0, one launch (start us, length us, event | category | flops | bytes accessed | tf_op | source)
XLA Modules:
  0.0 70.2 jit_solution(10684646599230667453)
XLA Ops:
  0.6 4.1 %collective-permute-start.2 = (bf16[1,8,2048]{2,1,0:T(8,128)(2,1)}, bf16[1,8,2048]{2,1,0:T(8,128)(2,1)S(1)}, u32[]{:S(2)}, u32[]{:S(2)}) collective-permute-start(bf16[1,8,2048]{2,1,0:T(8,128)(2,1)} %bitcast.115), channel_id=1, source_target_pairs={{0,8},{1,9},{2,10},{3,11},{4,12},{5,13},{6,14},{7,15},{8,0},{9,1},... | collective-permute-start | bytes 98312 | tf_op jit(solution)/shard_map/ppermute | solution.py:71
  4.7 1.6 %collective-permute-start.1 = (bf16[1,8,2048]{2,1,0:T(8,128)(2,1)}, bf16[1,8,2048]{2,1,0:T(8,128)(2,1)S(1)}, u32[]{:S(2)}, u32[]{:S(2)}) collective-permute-start(bf16[1,8,2048]{2,1,0:T(8,128)(2,1)} %bitcast.116), channel_id=1, source_target_pairs={{0,4},{1,5},{2,6},{3,7},{4,0},{5,1},{6,2},{7,3},{8,12},{9,13},{10,... | collective-permute-start | bytes 98312 | tf_op jit(solution)/shard_map/ppermute | solution.py:71
  6.3 0.8 %maximum_bitcast_fusion.2 = bf16[1,8,4096]{2,1,0:T(8,128)(2,1)S(1)} fusion(bf16[8,2048]{1,0:T(8,128)(2,1)} %param.11, bf16[8,2048]{1,0:T(8,128)(2,1)} %param.10), kind=kLoop, calls=%fused_computation.74 | loop fusion | flops 131072 | bytes 131072 | tf_op jit(solution)/shard_map/broadcast_in_dim | solution.py:29
  7.1 1.9 %collective-permute-start.5 = (bf16[1,8,4096]{2,1,0:T(8,128)(2,1)S(1)}, bf16[1,8,4096]{2,1,0:T(8,128)(2,1)S(1)}, u32[]{:S(2)}, u32[]{:S(2)}) collective-permute-start(bf16[1,8,4096]{2,1,0:T(8,128)(2,1)S(1)} %maximum_bitcast_fusion.2), channel_id=1, source_target_pairs={{0,8},{1,9},{2,10},{3,11},{4,12},{5,13},{6,14},{7,15},{8,0},{9,1},... | collective-permute-start | bytes 196616 | tf_op jit(solution)/shard_map/ppermute | solution.py:23
  9.1 3.2 %collective-permute-done = bf16[1,8,2048]{2,1,0:T(8,128)(2,1)S(1)} collective-permute-done((bf16[1,8,2048]{2,1,0:T(8,128)(2,1)}, bf16[1,8,2048]{2,1,0:T(8,128)(2,1)S(1)}, u32[]{:S(2)}, u32[]{:S(2)}) %collective-permute-start) | collective-permute-done | bytes 32800 | tf_op jit(solution)/shard_map/ppermute | solution.py:71
  12.2 0.8 %select_bitcast_fusion.23 = (bf16[1,1,8,2048]{3,2,1,0:T(8,128)(2,1)S(1)}, bf16[1,1,8,2048]{3,2,1,0:T(8,128)(2,1)S(1)}, bf16[1,1,8,2048]{3,2,1,0:T(8,128)(2,1)S(1)}, bf16[1,1,8,2048]{3,2,1,0:T(8,128)(2,1)S(1)}) fusion(bf16[1,8,2048]{2,1,0:T(8,128)(2,1)S(1)} %collective-permute-done, bf16[1,8,2048]{2,1,0:T(8,128)(2,1)S(1)} %collective-permute-done.1, ...), kind=kLoop, calls=%fused_computation.98 | loop fusion | flops 196608 | bytes 262156 | tf_op jit(solution)/shard_map/stack | solution.py:79
  13.0 0.7 %collective-permute-done.5 = bf16[1,8,4096]{2,1,0:T(8,128)(2,1)S(1)} collective-permute-done((bf16[1,8,4096]{2,1,0:T(8,128)(2,1)S(1)}, bf16[1,8,4096]{2,1,0:T(8,128)(2,1)S(1)}, u32[]{:S(2)}, u32[]{:S(2)}) %collective-permute-start.5) | collective-permute-done | bytes 65568 | tf_op jit(solution)/shard_map/ppermute | solution.py:23
  13.7 0.8 %select_bitcast_fusion.19 = (bf16[1,1,8,4096]{3,2,1,0:T(8,128)(2,1)S(1)}, bf16[1,1,8,4096]{3,2,1,0:T(8,128)(2,1)S(1)}) fusion(bf16[1,8,4096]{2,1,0:T(8,128)(2,1)S(1)} %collective-permute-done.5, pred[]{:T(512)S(6)} %ne.98, bf16[8,2048]{1,0:T(8,128)(2,1)} %param.11, bf16[8,2048]{1,0:T(8,128)(2,1)} %param.10), kind=kLoop, calls=%fused_computation.76 | loop fusion | flops 196608 | bytes 262145 | tf_op jit(solution)/shard_map/stack | solution.py:45
  14.7 1.6 %collective-permute-start.3 = (bf16[4,8,2048]{2,1,0:T(8,128)(2,1)S(1)}, bf16[4,8,2048]{2,1,0:T(8,128)(2,1)S(1)}, u32[]{:S(2)}, u32[]{:S(2)}) collective-permute-start(bf16[4,8,2048]{2,1,0:T(8,128)(2,1)S(1)} %maximum_bitcast_fusion), channel_id=1, source_target_pairs={{0,2},{1,3},{2,0},{3,1},{4,6},{5,7},{6,4},{7,5},{8,10},{9,11},{10,... | collective-permute-start | bytes 393224 | tf_op jit(solution)/shard_map/ppermute | solution.py:71
  16.2 3.4 %collective-permute-done.6 = bf16[2,8,4096]{2,1,0:T(8,128)(2,1)S(1)} collective-permute-done((bf16[2,8,4096]{2,1,0:T(8,128)(2,1)S(1)}, bf16[2,8,4096]{2,1,0:T(8,128)(2,1)S(1)}, u32[]{:S(2)}, u32[]{:S(2)}) %collective-permute-start.6) | collective-permute-done | bytes 131104 | tf_op jit(solution)/shard_map/ppermute | solution.py:23
  19.7 1.5 %collective-permute-start.7 = (bf16[4,8,4096]{2,1,0:T(8,128)(2,1)S(1)}, bf16[4,8,4096]{2,1,0:T(8,128)(2,1)S(1)}, u32[]{:S(2)}, u32[]{:S(2)}) collective-permute-start(bf16[4,8,4096]{2,1,0:T(8,128)(2,1)S(1)} %bitcast.104), channel_id=1, source_target_pairs={{0,2},{1,3},{2,0},{3,1},{4,6},{5,7},{6,4},{7,5},{8,10},{9,11},{10,... | collective-permute-start | bytes 786440 | tf_op jit(solution)/shard_map/ppermute | solution.py:23
  21.4 5.4 %collective-permute-done.7 = bf16[4,8,4096]{2,1,0:T(8,128)(2,1)S(1)} collective-permute-done((bf16[4,8,4096]{2,1,0:T(8,128)(2,1)S(1)}, bf16[4,8,4096]{2,1,0:T(8,128)(2,1)S(1)}, u32[]{:S(2)}, u32[]{:S(2)}) %collective-permute-start.7) | collective-permute-done | bytes 262176 | tf_op jit(solution)/shard_map/ppermute | solution.py:23
  27.1 0.8 %copy.19 = bf16[8,2,8,2048]{3,2,1,0:T(8,128)(2,1)} copy(bf16[8,2,8,2048]{3,2,0,1:T(8,128)(2,1)S(1)} %pad_maximum_fusion.1) | data formatting | bytes 1048576 | tf_op jit(solution)/shard_map/stack | solution.py:79
  28.0 0.9 %collective-permute-done.8 = bf16[8,8,4096]{2,1,0:T(8,128)(2,1)S(1)} collective-permute-done((bf16[8,8,4096]{2,1,0:T(8,128)(2,1)S(1)}, bf16[8,8,4096]{2,1,0:T(8,128)(2,1)S(1)}, u32[]{:S(2)}, u32[]{:S(2)}) %collective-permute-start.8) | collective-permute-done | bytes 524320 | tf_op jit(solution)/shard_map/ppermute | solution.py:23
  28.9 0.1 select_bitcast_fusion.3
  29.0 0.1 pad_maximum_fusion
  29.1 0.1 copy.22
  29.2 3.4 %shard_map.80 = (f32[128,512]{1,0:T(8,128)}, f32[128,8]{1,0:T(8,128)}, f32[128,8]{1,0:T(8,128)}) custom-call(bf16[128,2048]{1,0:T(8,128)(2,1)} %bitcast.94, bf16[512,2048]{1,0:T(8,128)(2,1)} %key_ref.7, bf16[512,2048]{1,0:T(8,128)(2,1)} %value_ref.7), custom_call_target="tpu_custom_call" | custom-call | flops 268435456 | bytes 1441792 | tf_op jit(solution)/shard_map/pallas_call | solution.py:283
  32.6 3.4 %shard_map.79 = (f32[128,512]{1,0:T(8,128)}, f32[128,8]{1,0:T(8,128)}, f32[128,8]{1,0:T(8,128)}) custom-call(bf16[128,2048]{1,0:T(8,128)(2,1)} %bitcast.95, bf16[512,2048]{1,0:T(8,128)(2,1)} %key_ref.7, bf16[512,2048]{1,0:T(8,128)(2,1)} %value_ref.7), custom_call_target="tpu_custom_call" | custom-call | flops 268435456 | bytes 1441792 | tf_op jit(solution)/shard_map/pallas_call | solution.py:283
  36.0 3.4 %shard_map.78 = (f32[128,512]{1,0:T(8,128)}, f32[128,8]{1,0:T(8,128)}, f32[128,8]{1,0:T(8,128)}) custom-call(bf16[128,2048]{1,0:T(8,128)(2,1)} %bitcast.96, bf16[512,2048]{1,0:T(8,128)(2,1)} %key_ref.7, bf16[512,2048]{1,0:T(8,128)(2,1)} %value_ref.7), custom_call_target="tpu_custom_call" | custom-call | flops 268435456 | bytes 1441792 | tf_op jit(solution)/shard_map/pallas_call | solution.py:283
  39.4 3.4 %shard_map.77 = (f32[128,512]{1,0:T(8,128)}, f32[128,8]{1,0:T(8,128)}, f32[128,8]{1,0:T(8,128)}) custom-call(bf16[128,2048]{1,0:T(8,128)(2,1)} %bitcast.97, bf16[512,2048]{1,0:T(8,128)(2,1)} %key_ref.7, bf16[512,2048]{1,0:T(8,128)(2,1)} %value_ref.7), custom_call_target="tpu_custom_call" | custom-call | flops 268435456 | bytes 1441792 | tf_op jit(solution)/shard_map/pallas_call | solution.py:283
  42.9 1.2 %concatenate.40 = f32[128,2112]{1,0:T(8,128)S(1)} concatenate(f32[128,512]{1,0:T(8,128)} %get-tuple-element.31, f32[128,512]{1,0:T(8,128)S(1)} %copy-done.2, f32[128,512]{1,0:T(8,128)S(1)} %copy-done.1, f32[128,512]{1,0:T(8,128)S(1)} %copy-done, f32[128,8]{1,0:T(8,128)} %get-tuple-element.35, f32[128,8]{1,0:T(8,128)S(1)} %copy-done.7, f32[128,8]{1,0:T(8,128)S(1)} %copy-done.5, ...), dimensions={1} | concatenate | bytes 2162688 | tf_op jit(solution)/shard_map/concatenate | solution.py:328
  44.4 0.1 concatenate.41
  44.5 0.2 collective-permute-start.9
  44.7 1.1 %fusion.62 = (bf16[128,2048]{1,0:T(8,128)(2,1)}, bf16[128,2048]{1,0:T(8,128)(2,1)}) fusion(bf16[128,4096]{1,0:T(8,128)(2,1)S(1)} %bitcast.99), kind=kLoop, calls=%fused_computation.162 | loop fusion | bytes 2097152 | tf_op jit(solution)/shard_map/slice | solution.py:327
  45.8 3.5 %shard_map.81.refs_0_ = bf16[512,2048]{1,0:T(8,128)(2,1)} custom-call(bf16[512,2048]{1,0:T(8,128)(2,1)} %query_ref.7, bf16[128,2048]{1,0:T(8,128)(2,1)} %get-tuple-element.67.key_ref, bf16[128,2048]{1,0:T(8,128)(2,1)} %get-tuple-element.66.value_ref), custom_call_target="tpu_custom_call" | custom-call | flops 268435456 | bytes 1310720 | tf_op jit(solution)/shard_map/pallas_call | solution.py:237
  49.5 0.1 fusion.36
  49.6 0.4 convolution_multiply_fusion.1
  50.0 0.4 fusion
  50.7 0.1 concatenate.44
  50.8 0.9 %collective-permute-start.10 = (bf16[4,8,2208]{2,1,0:T(8,128)(2,1)S(1)}, bf16[4,8,2208]{2,1,0:T(8,128)(2,1)S(1)}, u32[]{:S(2)}, u32[]{:S(2)}) collective-permute-start(bf16[4,8,2208]{2,1,0:T(8,128)(2,1)S(1)} %concatenate.44), channel_id=1, source_target_pairs={{0,2},{1,3},{2,0},{3,1},{4,6},{5,7},{6,4},{7,5},{8,10},{9,11},{10,... | collective-permute-start | bytes 423944 | tf_op jit(solution)/shard_map/ppermute | solution.py:23
  51.7 3.5 %shard_map.82.refs_0_ = bf16[512,2048]{1,0:T(8,128)(2,1)} custom-call(bf16[512,2048]{1,0:T(8,128)(2,1)} %query_ref.7, bf16[128,2048]{1,0:T(8,128)(2,1)} %get-tuple-element.67.key_ref, bf16[128,2048]{1,0:T(8,128)(2,1)} %get-tuple-element.66.value_ref, bf16[512,2048]{1,0:T(8,128)(2,1)} %shard_map.81.refs_0_), custom_call_target="tpu_custom_call", output_to_operand_aliasing={{}: (3, {})} | custom-call | flops 268435456 | bytes 1310720 | tf_op jit(solution)/shard_map/pallas_call | solution.py:237
  55.2 1.7 %collective-permute-done.10 = bf16[4,8,2208]{2,1,0:T(8,128)(2,1)S(1)} collective-permute-done((bf16[4,8,2208]{2,1,0:T(8,128)(2,1)S(1)}, bf16[4,8,2208]{2,1,0:T(8,128)(2,1)S(1)}, u32[]{:S(2)}, u32[]{:S(2)}) %collective-permute-start.10) | collective-permute-done | bytes 141344 | tf_op jit(solution)/shard_map/ppermute | solution.py:23
  57.2 0.1 fusion.41
  57.3 0.3 convolution_multiply_fusion.2
  57.6 0.3 fusion.1
  58.1 0.1 concatenate.47
  58.2 0.6 collective-permute-start.11
  58.8 3.5 %shard_map.83.refs_0_ = bf16[512,2048]{1,0:T(8,128)(2,1)} custom-call(bf16[512,2048]{1,0:T(8,128)(2,1)} %query_ref.7, bf16[128,2048]{1,0:T(8,128)(2,1)} %get-tuple-element.67.key_ref, bf16[128,2048]{1,0:T(8,128)(2,1)} %get-tuple-element.66.value_ref, bf16[512,2048]{1,0:T(8,128)(2,1)} %shard_map.82.refs_0_), custom_call_target="tpu_custom_call", output_to_operand_aliasing={{}: (3, {})} | custom-call | flops 268435456 | bytes 1310720 | tf_op jit(solution)/shard_map/pallas_call | solution.py:237
  62.4 0.2 collective-permute-done.11
  62.8 0.3 convolution_multiply_fusion.5
  63.1 0.3 fusion.2
  63.6 0.1 concatenate.50
  63.7 1.4 %collective-permute-start.12 = (bf16[1,8,2208]{2,1,0:T(8,128)(2,1)S(1)}, bf16[1,8,2208]{2,1,0:T(8,128)(2,1)S(1)}, u32[]{:S(2)}, u32[]{:S(2)}) collective-permute-start(bf16[1,8,2208]{2,1,0:T(8,128)(2,1)S(1)} %concatenate.50), channel_id=1, source_target_pairs={{0,8},{1,9},{2,10},{3,11},{4,12},{5,13},{6,14},{7,15},{8,0},{9,1},... | collective-permute-start | bytes 105992 | tf_op jit(solution)/shard_map/ppermute | solution.py:23
  65.1 3.5 %shard_map.84 = bf16[512,2048]{1,0:T(8,128)(2,1)} custom-call(bf16[512,2048]{1,0:T(8,128)(2,1)} %query_ref.7, bf16[128,2048]{1,0:T(8,128)(2,1)} %get-tuple-element.67.key_ref, bf16[128,2048]{1,0:T(8,128)(2,1)} %get-tuple-element.66.value_ref, bf16[512,2048]{1,0:T(8,128)(2,1)} %shard_map.83.refs_0_), custom_call_target="tpu_custom_call", output_to_operand_aliasing={{}: (3, {})} | custom-call | flops 268435456 | bytes 1310720 | tf_op jit(solution)/shard_map/pallas_call | solution.py:237
  68.8 0.3 convolution_multiply_fusion.7
  69.0 0.3 fusion.3
  69.3 0.9 %fusion.4 = bf16[8,2048]{1,0:T(8,128)(2,1)} fusion(f32[8,2048]{1,0:T(8,128)S(1)} %fusion.3, s32[2048]{0:T(1024)S(1)} %get-tuple-element.118, s32[2048]{0:T(1024)S(1)} %get-tuple-element.119, pred[2048]{0:T(1024)(128)(4,1)S(1)} %fusion.49, f32[8,2112]{1,0:T(8,128)S(1)} %bitcast.114, f32[8,2112]{1,0:T(8,128)S(1)} %get-tuple-element.96), kind=kOutput, calls=%fused_computation.13 | convolution fusion | flops 6456832 | bytes 133120 | tf_op jit(solution)/shard_map/dot_general | solution.py:16
  (69 shorter events, 2.2 us)
Async XLA Ops:
  0.6 8.4 %collective-permute-start.2 = (bf16[1,8,2048]{2,1,0:T(8,128)(2,1)}, bf16[1,8,2048]{2,1,0:T(8,128)(2,1)S(1)}, u32[]{:S(2)}, u32[]{:S(2)}) collective-permute-start(bf16[1,8,2048]{2,1,0:T(8,128)(2,1)} %bitcast.115), channel_id=1, source_target_pairs={{0,8},{1,9},{2,10},{3,11},{4,12},{5,13},{6,14},{7,15},{8,0},{9,1},... | collective-permute-start | bytes 98312 | tf_op jit(solution)/shard_map/ppermute | solution.py:71
  4.7 4.3 %collective-permute-start.1 = (bf16[1,8,2048]{2,1,0:T(8,128)(2,1)}, bf16[1,8,2048]{2,1,0:T(8,128)(2,1)S(1)}, u32[]{:S(2)}, u32[]{:S(2)}) collective-permute-start(bf16[1,8,2048]{2,1,0:T(8,128)(2,1)} %bitcast.116), channel_id=1, source_target_pairs={{0,4},{1,5},{2,6},{3,7},{4,0},{5,1},{6,2},{7,3},{8,12},{9,13},{10,... | collective-permute-start | bytes 98312 | tf_op jit(solution)/shard_map/ppermute | solution.py:71
  6.3 5.9 %collective-permute-start = (bf16[1,8,2048]{2,1,0:T(8,128)(2,1)}, bf16[1,8,2048]{2,1,0:T(8,128)(2,1)S(1)}, u32[]{:S(2)}, u32[]{:S(2)}) collective-permute-start(bf16[1,8,2048]{2,1,0:T(8,128)(2,1)} %bitcast.117), channel_id=1, source_target_pairs={{0,12},{1,13},{2,14},{3,15},{4,8},{5,9},{6,10},{7,11},{8,4},{9,5},... | collective-permute-start | bytes 98312 | tf_op jit(solution)/shard_map/ppermute | solution.py:71
  7.1 6.6 %collective-permute-start.5 = (bf16[1,8,4096]{2,1,0:T(8,128)(2,1)S(1)}, bf16[1,8,4096]{2,1,0:T(8,128)(2,1)S(1)}, u32[]{:S(2)}, u32[]{:S(2)}) collective-permute-start(bf16[1,8,4096]{2,1,0:T(8,128)(2,1)S(1)} %maximum_bitcast_fusion.2), channel_id=1, source_target_pairs={{0,8},{1,9},{2,10},{3,11},{4,12},{5,13},{6,14},{7,15},{8,0},{9,1},... | collective-permute-start | bytes 196616 | tf_op jit(solution)/shard_map/ppermute | solution.py:23
  14.5 5.1 %collective-permute-start.6 = (bf16[2,8,4096]{2,1,0:T(8,128)(2,1)S(1)}, bf16[2,8,4096]{2,1,0:T(8,128)(2,1)S(1)}, u32[]{:S(2)}, u32[]{:S(2)}) collective-permute-start(bf16[2,8,4096]{2,1,0:T(8,128)(2,1)S(1)} %maximum_bitcast_fusion.1), channel_id=1, source_target_pairs={{0,4},{1,5},{2,6},{3,7},{4,0},{5,1},{6,2},{7,3},{8,12},{9,13},{10,... | collective-permute-start | bytes 393224 | tf_op jit(solution)/shard_map/ppermute | solution.py:23
  14.7 6.6 %collective-permute-start.3 = (bf16[4,8,2048]{2,1,0:T(8,128)(2,1)S(1)}, bf16[4,8,2048]{2,1,0:T(8,128)(2,1)S(1)}, u32[]{:S(2)}, u32[]{:S(2)}) collective-permute-start(bf16[4,8,2048]{2,1,0:T(8,128)(2,1)S(1)} %maximum_bitcast_fusion), channel_id=1, source_target_pairs={{0,2},{1,3},{2,0},{3,1},{4,6},{5,7},{6,4},{7,5},{8,10},{9,11},{10,... | collective-permute-start | bytes 393224 | tf_op jit(solution)/shard_map/ppermute | solution.py:71
  19.7 7.0 %collective-permute-start.7 = (bf16[4,8,4096]{2,1,0:T(8,128)(2,1)S(1)}, bf16[4,8,4096]{2,1,0:T(8,128)(2,1)S(1)}, u32[]{:S(2)}, u32[]{:S(2)}) collective-permute-start(bf16[4,8,4096]{2,1,0:T(8,128)(2,1)S(1)} %bitcast.104), channel_id=1, source_target_pairs={{0,2},{1,3},{2,0},{3,1},{4,6},{5,7},{6,4},{7,5},{8,10},{9,11},{10,... | collective-permute-start | bytes 786440 | tf_op jit(solution)/shard_map/ppermute | solution.py:23
  21.3 5.7 %collective-permute-start.4 = (bf16[8,8,2048]{2,1,0:T(8,128)(2,1)S(1)}, bf16[8,8,2048]{2,1,0:T(8,128)(2,1)S(1)}, u32[]{:S(2)}, u32[]{:S(2)}) collective-permute-start(bf16[8,8,2048]{2,1,0:T(8,128)(2,1)S(1)} %bitcast.103), channel_id=1, source_target_pairs={{0,1},{1,0},{2,3},{3,2},{4,5},{5,4},{6,7},{7,6},{8,9},{9,8},{10,11... | collective-permute-start | bytes 786440 | tf_op jit(solution)/shard_map/ppermute | solution.py:71
  26.9 2.0 %collective-permute-start.8 = (bf16[8,8,4096]{2,1,0:T(8,128)(2,1)S(1)}, bf16[8,8,4096]{2,1,0:T(8,128)(2,1)S(1)}, u32[]{:S(2)}, u32[]{:S(2)}) collective-permute-start(bf16[8,8,4096]{2,1,0:T(8,128)(2,1)S(1)} %bitcast.101), channel_id=1, source_target_pairs={{0,1},{1,0},{2,3},{3,2},{4,5},{5,4},{6,7},{7,6},{8,9},{9,8},{10,11... | collective-permute-start | bytes 1572872 | tf_op jit(solution)/shard_map/ppermute | solution.py:23
  39.3 3.5 %copy-start = (f32[128,512]{1,0:T(8,128)S(1)}, f32[128,512]{1,0:T(8,128)}, u32[]{:S(2)}) copy-start(f32[128,512]{1,0:T(8,128)} %get-tuple-element.34) | copy-start | bytes 786436
  39.3 3.5 %copy-start.1 = (f32[128,512]{1,0:T(8,128)S(1)}, f32[128,512]{1,0:T(8,128)}, u32[]{:S(2)}) copy-start(f32[128,512]{1,0:T(8,128)} %get-tuple-element.33) | copy-start | bytes 786436
  39.3 3.5 %copy-start.2 = (f32[128,512]{1,0:T(8,128)S(1)}, f32[128,512]{1,0:T(8,128)}, u32[]{:S(2)}) copy-start(f32[128,512]{1,0:T(8,128)} %get-tuple-element.32) | copy-start | bytes 786436
  39.3 3.5 %copy-start.3 = (f32[128,8]{1,0:T(8,128)S(1)}, f32[128,8]{1,0:T(8,128)}, u32[]{:S(2)}) copy-start(f32[128,8]{1,0:T(8,128)} %get-tuple-element.38) | copy-start | bytes 12292
  39.3 3.5 %copy-start.4 = (f32[128,8]{1,0:T(8,128)S(1)}, f32[128,8]{1,0:T(8,128)}, u32[]{:S(2)}) copy-start(f32[128,8]{1,0:T(8,128)} %get-tuple-element.42) | copy-start | bytes 12292
  39.4 3.5 %copy-start.5 = (f32[128,8]{1,0:T(8,128)S(1)}, f32[128,8]{1,0:T(8,128)}, u32[]{:S(2)}) copy-start(f32[128,8]{1,0:T(8,128)} %get-tuple-element.37) | copy-start | bytes 12292
  39.4 3.5 %copy-start.6 = (f32[128,8]{1,0:T(8,128)S(1)}, f32[128,8]{1,0:T(8,128)}, u32[]{:S(2)}) copy-start(f32[128,8]{1,0:T(8,128)} %get-tuple-element.41) | copy-start | bytes 12292
  39.4 3.5 %copy-start.7 = (f32[128,8]{1,0:T(8,128)S(1)}, f32[128,8]{1,0:T(8,128)}, u32[]{:S(2)}) copy-start(f32[128,8]{1,0:T(8,128)} %get-tuple-element.36) | copy-start | bytes 12292
  39.4 3.5 %copy-start.8 = (f32[128,8]{1,0:T(8,128)S(1)}, f32[128,8]{1,0:T(8,128)}, u32[]{:S(2)}) copy-start(f32[128,8]{1,0:T(8,128)} %get-tuple-element.40) | copy-start | bytes 12292
  44.5 4.8 %collective-permute-start.9 = (bf16[8,8,2208]{2,1,0:T(8,128)(2,1)S(1)}, bf16[8,8,2208]{2,1,0:T(8,128)(2,1)S(1)}, u32[]{:S(2)}, u32[]{:S(2)}) collective-permute-start(bf16[8,8,2208]{2,1,0:T(8,128)(2,1)S(1)} %concatenate.41), channel_id=1, source_target_pairs={{0,1},{1,0},{2,3},{3,2},{4,5},{5,4},{6,7},{7,6},{8,9},{9,8},{10,11... | collective-permute-start | bytes 847880 | tf_op jit(solution)/shard_map/ppermute | solution.py:23
  50.8 6.2 %collective-permute-start.10 = (bf16[4,8,2208]{2,1,0:T(8,128)(2,1)S(1)}, bf16[4,8,2208]{2,1,0:T(8,128)(2,1)S(1)}, u32[]{:S(2)}, u32[]{:S(2)}) collective-permute-start(bf16[4,8,2208]{2,1,0:T(8,128)(2,1)S(1)} %concatenate.44), channel_id=1, source_target_pairs={{0,2},{1,3},{2,0},{3,1},{4,6},{5,7},{6,4},{7,5},{8,10},{9,11},{10,... | collective-permute-start | bytes 423944 | tf_op jit(solution)/shard_map/ppermute | solution.py:23
  58.2 4.4 %collective-permute-start.11 = (bf16[2,8,2208]{2,1,0:T(8,128)(2,1)S(1)}, bf16[2,8,2208]{2,1,0:T(8,128)(2,1)S(1)}, u32[]{:S(2)}, u32[]{:S(2)}) collective-permute-start(bf16[2,8,2208]{2,1,0:T(8,128)(2,1)S(1)} %concatenate.47), channel_id=1, source_target_pairs={{0,4},{1,5},{2,6},{3,7},{4,0},{5,1},{6,2},{7,3},{8,12},{9,13},{10,... | collective-permute-start | bytes 211976 | tf_op jit(solution)/shard_map/ppermute | solution.py:23
  63.7 4.9 %collective-permute-start.12 = (bf16[1,8,2208]{2,1,0:T(8,128)(2,1)S(1)}, bf16[1,8,2208]{2,1,0:T(8,128)(2,1)S(1)}, u32[]{:S(2)}, u32[]{:S(2)}) collective-permute-start(bf16[1,8,2208]{2,1,0:T(8,128)(2,1)S(1)} %concatenate.50), channel_id=1, source_target_pairs={{0,8},{1,9},{2,10},{3,11},{4,12},{5,13},{6,14},{7,15},{8,0},{9,1},... | collective-permute-start | bytes 105992 | tf_op jit(solution)/shard_map/ppermute | solution.py:23

commit v17 on v12

--- a/solution.py
+++ b/solution.py
@@ -46,38 +46,6 @@
         bit //= 2
         step += 1
     return held.reshape((count * block.shape[0],) + block.shape[1:]), results
-
-
-def gather_levels(block):
-    count = lax.axis_size("seq")
-    me = lax.axis_index("seq")
-    held = block[None]
-    levels = []
-    bit = count // 2
-    if bit >= 2:
-        levels.append((bit, bit // 2))
-        bit //= 4
-    while bit >= 1:
-        levels.append((bit,))
-        bit //= 2
-    for level in levels:
-        mask = sum(level)
-        offsets = [0]
-        for b in level:
-            offsets = offsets + [o + b for o in offsets]
-        pieces = {0: held}
-        for offset in offsets[1:]:
-            pairs = [(source, source ^ offset) for source in range(count)]
-            pieces[offset] = lax.ppermute(held, "seq", pairs)
-        mine = me & mask
-        ordered = []
-        for target in sorted(offsets):
-            choice = pieces[0]
-            for offset in offsets[1:]:
-                choice = jnp.where((mine ^ offset) == target, pieces[offset], choice)
-            ordered.append(choice)
-        held = jnp.stack(ordered, axis=1).reshape((-1,) + block.shape)
-    return held.reshape((count * block.shape[0],) + block.shape[1:])
 
 
 def merge(first, second, heads):
@@ -312,7 +280,7 @@
     heads = width // HEAD_DIM
     groups = 4
     steps = (lax.axis_size("seq") - 1).bit_length()
-    all_queries = gather_levels(audio_q)
+    all_queries, ignored = gather_rows(audio_q)
     audio_calls = [
         (
             lambda q, gs=gs: tuple(audio_partial(q, video_k, video_v, g, groups) for g in gs),

time: 64.8 us -> 67.5 us (1.042)
  starting transfers between devices: 14.2 us -> 18.4 us
  waiting for transfers between devices: 9.66 us -> 8.2 us
    ppermute x8 -> x12, starting transfers between devices: 6.84 us -> 18.4 us  [exchange(): return lax.ppermute(value, 'seq', pairs)]
    ppermute x5 -> x0, starting transfers between devices: 7.34 us -> none  [gather_levels(): pieces[offset] = lax.ppermute(held, 'seq', pairs)]
    ppermute x5 -> x0, waiting for transfers between devices: 5.74 us -> none  [gather_levels(): pieces[offset] = lax.ppermute(held, 'seq', pairs)]
    ppermute x8 -> x12, waiting for transfers between devices: 3.92 us -> 8.2 us  [exchange(): return lax.ppermute(value, 'seq', pairs)]
    another operation x7 -> x14, other arithmetic: 1.11 us -> 2.07 us  [gather_rows(): held = jnp.stack([low, high], axis=1).reshape((-1,) + block.shape)]
    another operation x5 -> x0, other arithmetic: 0.95 us -> none  [gather_levels(): held = jnp.stack(ordered, axis=1).reshape((-1,) + block.shape)]
    another operation x2 -> x4, local copies, waits for them, and re-layouts: 0.13 us -> 0.97 us  [gather_rows(): held = jnp.stack([low, high], axis=1).reshape((-1,) + block.shape)]
    another operation x1 -> x0, local copies, waits for them, and re-layouts: 0.83 us -> none  [gather_levels(): held = jnp.stack(ordered, axis=1).reshape((-1,) + block.shape)]
  transfers between devices with their start and end apart: 13 -> 12, of which waited for: 6 -> 7; matrix products, arithmetic and copies ran while one was open for 6% -> 5% of each run, Pallas kernels for 43% -> 41%
where the time goes in v17:
time: 67.5 us; the launch traced here: 67 us
  Pallas kernels  27.6 us (41%)
  starting transfers between devices  18.4 us (27%)
  waiting for transfers between devices  8.2 us (12%)
  local copies, waits for them, and re-layouts  4.3 us (6%)
  other arithmetic  4 us (6%)
  matrix products  3.45 us (5%)
  between operations  1.07 us (2%)
    ppermute x12, starting transfers between devices, exchange(): return lax.ppermute(value, 'seq', pairs)  18.4 us
    pallas_call x4, Pallas kernels, video_part(): pl.pallas_call(video_kernel, grid=(pairs // PER_STEP,), in_specs=specs, o...  14.1 us
    pallas_call x4, Pallas kernels, audio_partial(): pl.pallas_call(audio_kernel, grid=(heads // 2 // PER_STEP,), in_specs=[pl...  13.5 us
    ppermute x12, waiting for transfers between devices, exchange(): return lax.ppermute(value, 'seq', pairs)  8.2 us
    dot_general x9, matrix products, spread(): jnp.dot(scales, expand, precision=lax.Precision.HIGHEST, preferred_elemen...  3.45 us
    another operation x14, other arithmetic, gather_rows(): held = jnp.stack([low, high], axis=1).reshape((-1,) + block.shape)  2.07 us
  transfers between devices with their start and end apart: 12, of which 7 were waited for; matrix products, arithmetic and copies ran while one was open for 5% of the time, Pallas kernels for 41%

profile of v17, /device:TPU:0, one launch (start us, length us, event | category | flops | bytes accessed | tf_op | source)
XLA Modules:
  0.0 67.0 jit_solution(16119018502764961296)
XLA Ops:
  0.6 4.1 %collective-permute-start.2 = (bf16[1,8,2048]{2,1,0:T(8,128)(2,1)}, bf16[1,8,2048]{2,1,0:T(8,128)(2,1)S(1)}, u32[]{:S(2)}, u32[]{:S(2)}) collective-permute-start(bf16[1,8,2048]{2,1,0:T(8,128)(2,1)} %bitcast.115), channel_id=1, source_target_pairs={{0,8},{1,9},{2,10},{3,11},{4,12},{5,13},{6,14},{7,15},{8,0},{9,1},... | collective-permute-start | bytes 98312 | tf_op jit(solution)/shard_map/ppermute | solution.py:23
  4.7 0.8 %maximum_bitcast_fusion.1 = bf16[1,8,4096]{2,1,0:T(8,128)(2,1)S(1)} fusion(bf16[8,2048]{1,0:T(8,128)(2,1)} %param.11, bf16[8,2048]{1,0:T(8,128)(2,1)} %param.10), kind=kLoop, calls=%fused_computation.74 | loop fusion | flops 131072 | bytes 131072 | tf_op jit(solution)/shard_map/broadcast_in_dim | solution.py:29
  5.5 1.7 %collective-permute-done.2 = bf16[1,8,2048]{2,1,0:T(8,128)(2,1)S(1)} collective-permute-done((bf16[1,8,2048]{2,1,0:T(8,128)(2,1)}, bf16[1,8,2048]{2,1,0:T(8,128)(2,1)S(1)}, u32[]{:S(2)}, u32[]{:S(2)}) %collective-permute-start.2) | collective-permute-done | bytes 32800 | tf_op jit(solution)/shard_map/ppermute | solution.py:23
  7.2 0.8 %select_bitcast_fusion.23 = (bf16[1,1,8,2048]{3,2,1,0:T(8,128)(2,1)S(1)}, bf16[1,1,8,2048]{3,2,1,0:T(8,128)(2,1)S(1)}) fusion(bf16[1,8,2048]{2,1,0:T(8,128)(2,1)S(1)} %collective-permute-done.2, pred[]{:T(512)S(6)} %ne.102, bf16[8,2048]{1,0:T(8,128)(2,1)} %param.9), kind=kLoop, calls=%fused_computation.99 | loop fusion | flops 32768 | bytes 131073 | tf_op jit(solution)/shard_map/stack | solution.py:45
  8.0 2.2 %collective-permute-start.3 = (bf16[2,8,2048]{2,1,0:T(8,128)(2,1)S(1)}, bf16[2,8,2048]{2,1,0:T(8,128)(2,1)S(1)}, u32[]{:S(2)}, u32[]{:S(2)}) collective-permute-start(bf16[2,8,2048]{2,1,0:T(8,128)(2,1)S(1)} %maximum_bitcast_fusion.2), channel_id=1, source_target_pairs={{0,4},{1,5},{2,6},{3,7},{4,0},{5,1},{6,2},{7,3},{8,12},{9,13},{10,... | collective-permute-start | bytes 196616 | tf_op jit(solution)/shard_map/ppermute | solution.py:23
  10.2 0.8 %collective-permute-done = bf16[1,8,4096]{2,1,0:T(8,128)(2,1)S(1)} collective-permute-done((bf16[1,8,4096]{2,1,0:T(8,128)(2,1)S(1)}, bf16[1,8,4096]{2,1,0:T(8,128)(2,1)S(1)}, u32[]{:S(2)}, u32[]{:S(2)}) %collective-permute-start) | collective-permute-done | bytes 65568 | tf_op jit(solution)/shard_map/ppermute | solution.py:23
  11.0 0.8 %select_bitcast_fusion.21 = (bf16[1,1,8,4096]{3,2,1,0:T(8,128)(2,1)S(1)}, bf16[1,1,8,4096]{3,2,1,0:T(8,128)(2,1)S(1)}) fusion(bf16[1,8,4096]{2,1,0:T(8,128)(2,1)S(1)} %collective-permute-done, pred[]{:T(512)S(6)} %ne.102, bf16[8,2048]{1,0:T(8,128)(2,1)} %param.11, bf16[8,2048]{1,0:T(8,128)(2,1)} %param.10), kind=kLoop, calls=%fused_computation.79 | loop fusion | flops 196608 | bytes 262145 | tf_op jit(solution)/shard_map/stack | solution.py:45
  11.8 1.3 %collective-permute-start.1 = (bf16[2,8,4096]{2,1,0:T(8,128)(2,1)S(1)}, bf16[2,8,4096]{2,1,0:T(8,128)(2,1)S(1)}, u32[]{:S(2)}, u32[]{:S(2)}) collective-permute-start(bf16[2,8,4096]{2,1,0:T(8,128)(2,1)S(1)} %maximum_bitcast_fusion), channel_id=1, source_target_pairs={{0,4},{1,5},{2,6},{3,7},{4,0},{5,1},{6,2},{7,3},{8,12},{9,13},{10,... | collective-permute-start | bytes 393224 | tf_op jit(solution)/shard_map/ppermute | solution.py:23
  13.2 1.6 %collective-permute-start.4 = (bf16[4,8,2048]{2,1,0:T(8,128)(2,1)S(1)}, bf16[4,8,2048]{2,1,0:T(8,128)(2,1)S(1)}, u32[]{:S(2)}, u32[]{:S(2)}) collective-permute-start(bf16[4,8,2048]{2,1,0:T(8,128)(2,1)S(1)} %bitcast.107), channel_id=1, source_target_pairs={{0,2},{1,3},{2,0},{3,1},{4,6},{5,7},{6,4},{7,5},{8,10},{9,11},{10,... | collective-permute-start | bytes 393224 | tf_op jit(solution)/shard_map/ppermute | solution.py:23
  14.8 2.1 %collective-permute-done.1 = bf16[2,8,4096]{2,1,0:T(8,128)(2,1)S(1)} collective-permute-done((bf16[2,8,4096]{2,1,0:T(8,128)(2,1)S(1)}, bf16[2,8,4096]{2,1,0:T(8,128)(2,1)S(1)}, u32[]{:S(2)}, u32[]{:S(2)}) %collective-permute-start.1) | collective-permute-done | bytes 131104 | tf_op jit(solution)/shard_map/ppermute | solution.py:23
  16.9 1.4 %collective-permute-done.4 = bf16[4,8,2048]{2,1,0:T(8,128)(2,1)S(1)} collective-permute-done((bf16[4,8,2048]{2,1,0:T(8,128)(2,1)S(1)}, bf16[4,8,2048]{2,1,0:T(8,128)(2,1)S(1)}, u32[]{:S(2)}, u32[]{:S(2)}) %collective-permute-start.4) | collective-permute-done | bytes 131104 | tf_op jit(solution)/shard_map/ppermute | solution.py:23
  18.4 1.5 %collective-permute-done.5 = bf16[8,8,2048]{2,1,0:T(8,128)(2,1)S(1)} collective-permute-done((bf16[8,8,2048]{2,1,0:T(8,128)(2,1)S(1)}, bf16[8,8,2048]{2,1,0:T(8,128)(2,1)S(1)}, u32[]{:S(2)}, u32[]{:S(2)}) %collective-permute-start.5) | collective-permute-done | bytes 262176 | tf_op jit(solution)/shard_map/ppermute | solution.py:23
  20.0 0.8 %copy.22 = bf16[8,2,8,2048]{3,2,1,0:T(8,128)(2,1)} copy(bf16[8,2,8,2048]{3,2,0,1:T(8,128)(2,1)S(1)} %pad_maximum_fusion.1) | data formatting | bytes 1048576 | tf_op jit(solution)/shard_map/stack | solution.py:45
  20.9 1.5 %collective-permute-start.6 = (bf16[4,8,4096]{2,1,0:T(8,128)(2,1)S(1)}, bf16[4,8,4096]{2,1,0:T(8,128)(2,1)S(1)}, u32[]{:S(2)}, u32[]{:S(2)}) collective-permute-start(bf16[4,8,4096]{2,1,0:T(8,128)(2,1)S(1)} %bitcast.101), channel_id=1, source_target_pairs={{0,2},{1,3},{2,0},{3,1},{4,6},{5,7},{6,4},{7,5},{8,10},{9,11},{10,... | collective-permute-start | bytes 786440 | tf_op jit(solution)/shard_map/ppermute | solution.py:23
  22.4 3.3 %shard_map.78 = (f32[128,512]{1,0:T(8,128)}, f32[128,8]{1,0:T(8,128)}, f32[128,8]{1,0:T(8,128)}) custom-call(bf16[128,2048]{1,0:T(8,128)(2,1)} %bitcast.91, bf16[512,2048]{1,0:T(8,128)(2,1)} %key_ref.7, bf16[512,2048]{1,0:T(8,128)(2,1)} %value_ref.7), custom_call_target="tpu_custom_call" | custom-call | flops 268435456 | bytes 1441792 | tf_op jit(solution)/shard_map/pallas_call | solution.py:251
  25.7 3.4 %shard_map.77 = (f32[128,512]{1,0:T(8,128)}, f32[128,8]{1,0:T(8,128)}, f32[128,8]{1,0:T(8,128)}) custom-call(bf16[128,2048]{1,0:T(8,128)(2,1)} %bitcast.92, bf16[512,2048]{1,0:T(8,128)(2,1)} %key_ref.7, bf16[512,2048]{1,0:T(8,128)(2,1)} %value_ref.7), custom_call_target="tpu_custom_call" | custom-call | flops 268435456 | bytes 1441792 | tf_op jit(solution)/shard_map/pallas_call | solution.py:251
  29.1 0.1 collective-permute-done.6
  29.5 3.4 %shard_map.80 = (f32[128,512]{1,0:T(8,128)}, f32[128,8]{1,0:T(8,128)}, f32[128,8]{1,0:T(8,128)}) custom-call(bf16[128,2048]{1,0:T(8,128)(2,1)} %bitcast.93, bf16[512,2048]{1,0:T(8,128)(2,1)} %key_ref.7, bf16[512,2048]{1,0:T(8,128)(2,1)} %value_ref.7), custom_call_target="tpu_custom_call" | custom-call | flops 268435456 | bytes 1441792 | tf_op jit(solution)/shard_map/pallas_call | solution.py:251
  32.9 3.5 %shard_map.79 = (f32[128,512]{1,0:T(8,128)}, f32[128,8]{1,0:T(8,128)}, f32[128,8]{1,0:T(8,128)}) custom-call(bf16[128,2048]{1,0:T(8,128)(2,1)} %bitcast.94, bf16[512,2048]{1,0:T(8,128)(2,1)} %key_ref.7, bf16[512,2048]{1,0:T(8,128)(2,1)} %value_ref.7), custom_call_target="tpu_custom_call" | custom-call | flops 268435456 | bytes 1441792 | tf_op jit(solution)/shard_map/pallas_call | solution.py:251
  36.4 1.2 %concatenate.40 = f32[128,2112]{1,0:T(8,128)S(1)} concatenate(f32[128,512]{1,0:T(8,128)S(1)} %copy-done.1, f32[128,512]{1,0:T(8,128)S(1)} %copy-done, f32[128,512]{1,0:T(8,128)} %get-tuple-element.65, f32[128,512]{1,0:T(8,128)S(1)} %copy-done.2, f32[128,8]{1,0:T(8,128)S(1)} %copy-done.5, f32[128,8]{1,0:T(8,128)S(1)} %copy-done.3, f32[128,8]{1,0:T(8,128)} %get-tuple-element.69, ...), dimensions={1} | concatenate | bytes 2162688 | tf_op jit(solution)/shard_map/concatenate | solution.py:297
  37.8 0.1 fusion.35
  38.0 0.1 pad_maximum_fusion
  38.1 0.1 copy.24
  38.2 0.1 concatenate.41
  38.3 0.6 collective-permute-start.8
  38.8 1.1 %fusion.62 = (bf16[128,2048]{1,0:T(8,128)(2,1)}, bf16[128,2048]{1,0:T(8,128)(2,1)}) fusion(bf16[128,4096]{1,0:T(8,128)(2,1)S(1)} %bitcast.96), kind=kLoop, calls=%fused_computation.163 | loop fusion | bytes 2097152 | tf_op jit(solution)/shard_map/slice | solution.py:296
  39.9 3.5 %shard_map.81.refs_0_ = bf16[512,2048]{1,0:T(8,128)(2,1)} custom-call(bf16[512,2048]{1,0:T(8,128)(2,1)} %query_ref.7, bf16[128,2048]{1,0:T(8,128)(2,1)} %get-tuple-element.99.key_ref, bf16[128,2048]{1,0:T(8,128)(2,1)} %get-tuple-element.98.value_ref), custom_call_target="tpu_custom_call" | custom-call | flops 268435456 | bytes 1310720 | tf_op jit(solution)/shard_map/pallas_call | solution.py:205
  43.6 0.1 fusion.36
  43.8 0.4 convolution_multiply_fusion.1
  44.2 0.4 fusion
  44.9 0.1 concatenate.44
  45.0 1.6 %collective-permute-start.9 = (bf16[4,8,2208]{2,1,0:T(8,128)(2,1)S(1)}, bf16[4,8,2208]{2,1,0:T(8,128)(2,1)S(1)}, u32[]{:S(2)}, u32[]{:S(2)}) collective-permute-start(bf16[4,8,2208]{2,1,0:T(8,128)(2,1)S(1)} %concatenate.44), channel_id=1, source_target_pairs={{0,2},{1,3},{2,0},{3,1},{4,6},{5,7},{6,4},{7,5},{8,10},{9,11},{10,... | collective-permute-start | bytes 423944 | tf_op jit(solution)/shard_map/ppermute | solution.py:23
  46.5 3.5 %shard_map.82.refs_0_ = bf16[512,2048]{1,0:T(8,128)(2,1)} custom-call(bf16[512,2048]{1,0:T(8,128)(2,1)} %query_ref.7, bf16[128,2048]{1,0:T(8,128)(2,1)} %get-tuple-element.99.key_ref, bf16[128,2048]{1,0:T(8,128)(2,1)} %get-tuple-element.98.value_ref, bf16[512,2048]{1,0:T(8,128)(2,1)} %shard_map.81.refs_0_), custom_call_target="tpu_custom_call", output_to_operand_aliasing={{}: (3, {})} | custom-call | flops 268435456 | bytes 1310720 | tf_op jit(solution)/shard_map/pallas_call | solution.py:205
  50.1 0.7 %collective-permute-done.9 = bf16[4,8,2208]{2,1,0:T(8,128)(2,1)S(1)} collective-permute-done((bf16[4,8,2208]{2,1,0:T(8,128)(2,1)S(1)}, bf16[4,8,2208]{2,1,0:T(8,128)(2,1)S(1)}, u32[]{:S(2)}, u32[]{:S(2)}) %collective-permute-start.9) | collective-permute-done | bytes 141344 | tf_op jit(solution)/shard_map/ppermute | solution.py:23
  51.0 0.1 fusion.41
  51.1 0.3 convolution_multiply_fusion.2
  51.4 0.3 fusion.1
  51.9 0.1 concatenate.47
  52.0 1.7 %collective-permute-start.10 = (bf16[2,8,2208]{2,1,0:T(8,128)(2,1)S(1)}, bf16[2,8,2208]{2,1,0:T(8,128)(2,1)S(1)}, u32[]{:S(2)}, u32[]{:S(2)}) collective-permute-start(bf16[2,8,2208]{2,1,0:T(8,128)(2,1)S(1)} %concatenate.47), channel_id=1, source_target_pairs={{0,4},{1,5},{2,6},{3,7},{4,0},{5,1},{6,2},{7,3},{8,12},{9,13},{10,... | collective-permute-start | bytes 211976 | tf_op jit(solution)/shard_map/ppermute | solution.py:23
  53.7 3.5 %shard_map.83.refs_0_ = bf16[512,2048]{1,0:T(8,128)(2,1)} custom-call(bf16[512,2048]{1,0:T(8,128)(2,1)} %query_ref.7, bf16[128,2048]{1,0:T(8,128)(2,1)} %get-tuple-element.99.key_ref, bf16[128,2048]{1,0:T(8,128)(2,1)} %get-tuple-element.98.value_ref, bf16[512,2048]{1,0:T(8,128)(2,1)} %shard_map.82.refs_0_), custom_call_target="tpu_custom_call", output_to_operand_aliasing={{}: (3, {})} | custom-call | flops 268435456 | bytes 1310720 | tf_op jit(solution)/shard_map/pallas_call | solution.py:205
  57.5 0.3 convolution_multiply_fusion.5
  57.8 0.3 fusion.2
  58.2 0.1 concatenate.50
  58.3 3.6 %collective-permute-start.11 = (bf16[1,8,2208]{2,1,0:T(8,128)(2,1)S(1)}, bf16[1,8,2208]{2,1,0:T(8,128)(2,1)S(1)}, u32[]{:S(2)}, u32[]{:S(2)}) collective-permute-start(bf16[1,8,2208]{2,1,0:T(8,128)(2,1)S(1)} %concatenate.50), channel_id=1, source_target_pairs={{0,8},{1,9},{2,10},{3,11},{4,12},{5,13},{6,14},{7,15},{8,0},{9,1},... | collective-permute-start | bytes 105992 | tf_op jit(solution)/shard_map/ppermute | solution.py:23
  61.9 3.5 %shard_map.84 = bf16[512,2048]{1,0:T(8,128)(2,1)} custom-call(bf16[512,2048]{1,0:T(8,128)(2,1)} %query_ref.7, bf16[128,2048]{1,0:T(8,128)(2,1)} %get-tuple-element.99.key_ref, bf16[128,2048]{1,0:T(8,128)(2,1)} %get-tuple-element.98.value_ref, bf16[512,2048]{1,0:T(8,128)(2,1)} %shard_map.83.refs_0_), custom_call_target="tpu_custom_call", output_to_operand_aliasing={{}: (3, {})} | custom-call | flops 268435456 | bytes 1310720 | tf_op jit(solution)/shard_map/pallas_call | solution.py:205
  65.6 0.2 convolution_multiply_fusion.7
  65.9 0.3 fusion.3
  66.2 0.9 %fusion.4 = bf16[8,2048]{1,0:T(8,128)(2,1)} fusion(f32[8,2048]{1,0:T(8,128)S(1)} %fusion.3, s32[2048]{0:T(1024)S(1)} %get-tuple-element.150, s32[2048]{0:T(1024)S(1)} %get-tuple-element.151, pred[2048]{0:T(1024)(128)(4,1)S(1)} %fusion.49, f32[8,2112]{1,0:T(8,128)S(1)} %bitcast.114, f32[8,2112]{1,0:T(8,128)S(1)} %get-tuple-element.128), kind=kOutput, calls=%fused_computation.13 | convolution fusion | flops 6456832 | bytes 133120 | tf_op jit(solution)/shard_map/dot_general | solution.py:16
  (70 shorter events, 2.2 us)
Async XLA Ops:
  0.6 6.6 %collective-permute-start.2 = (bf16[1,8,2048]{2,1,0:T(8,128)(2,1)}, bf16[1,8,2048]{2,1,0:T(8,128)(2,1)S(1)}, u32[]{:S(2)}, u32[]{:S(2)}) collective-permute-start(bf16[1,8,2048]{2,1,0:T(8,128)(2,1)} %bitcast.115), channel_id=1, source_target_pairs={{0,8},{1,9},{2,10},{3,11},{4,12},{5,13},{6,14},{7,15},{8,0},{9,1},... | collective-permute-start | bytes 98312 | tf_op jit(solution)/shard_map/ppermute | solution.py:23
  5.5 5.5 %collective-permute-start = (bf16[1,8,4096]{2,1,0:T(8,128)(2,1)S(1)}, bf16[1,8,4096]{2,1,0:T(8,128)(2,1)S(1)}, u32[]{:S(2)}, u32[]{:S(2)}) collective-permute-start(bf16[1,8,4096]{2,1,0:T(8,128)(2,1)S(1)} %maximum_bitcast_fusion.1), channel_id=1, source_target_pairs={{0,8},{1,9},{2,10},{3,11},{4,12},{5,13},{6,14},{7,15},{8,0},{9,1},... | collective-permute-start | bytes 196616 | tf_op jit(solution)/shard_map/ppermute | solution.py:23
  8.0 5.2 %collective-permute-start.3 = (bf16[2,8,2048]{2,1,0:T(8,128)(2,1)S(1)}, bf16[2,8,2048]{2,1,0:T(8,128)(2,1)S(1)}, u32[]{:S(2)}, u32[]{:S(2)}) collective-permute-start(bf16[2,8,2048]{2,1,0:T(8,128)(2,1)S(1)} %maximum_bitcast_fusion.2), channel_id=1, source_target_pairs={{0,4},{1,5},{2,6},{3,7},{4,0},{5,1},{6,2},{7,3},{8,12},{9,13},{10,... | collective-permute-start | bytes 196616 | tf_op jit(solution)/shard_map/ppermute | solution.py:23
  11.8 5.0 %collective-permute-start.1 = (bf16[2,8,4096]{2,1,0:T(8,128)(2,1)S(1)}, bf16[2,8,4096]{2,1,0:T(8,128)(2,1)S(1)}, u32[]{:S(2)}, u32[]{:S(2)}) collective-permute-start(bf16[2,8,4096]{2,1,0:T(8,128)(2,1)S(1)} %maximum_bitcast_fusion), channel_id=1, source_target_pairs={{0,4},{1,5},{2,6},{3,7},{4,0},{5,1},{6,2},{7,3},{8,12},{9,13},{10,... | collective-permute-start | bytes 393224 | tf_op jit(solution)/shard_map/ppermute | solution.py:23
  13.2 5.0 %collective-permute-start.4 = (bf16[4,8,2048]{2,1,0:T(8,128)(2,1)S(1)}, bf16[4,8,2048]{2,1,0:T(8,128)(2,1)S(1)}, u32[]{:S(2)}, u32[]{:S(2)}) collective-permute-start(bf16[4,8,2048]{2,1,0:T(8,128)(2,1)S(1)} %bitcast.107), channel_id=1, source_target_pairs={{0,2},{1,3},{2,0},{3,1},{4,6},{5,7},{6,4},{7,5},{8,10},{9,11},{10,... | collective-permute-start | bytes 393224 | tf_op jit(solution)/shard_map/ppermute | solution.py:23
  18.3 1.6 %collective-permute-start.5 = (bf16[8,8,2048]{2,1,0:T(8,128)(2,1)S(1)}, bf16[8,8,2048]{2,1,0:T(8,128)(2,1)S(1)}, u32[]{:S(2)}, u32[]{:S(2)}) collective-permute-start(bf16[8,8,2048]{2,1,0:T(8,128)(2,1)S(1)} %bitcast.103), channel_id=1, source_target_pairs={{0,1},{1,0},{2,3},{3,2},{4,5},{5,4},{6,7},{7,6},{8,9},{9,8},{10,11... | collective-permute-start | bytes 786440 | tf_op jit(solution)/shard_map/ppermute | solution.py:23
  20.9 8.3 %collective-permute-start.6 = (bf16[4,8,4096]{2,1,0:T(8,128)(2,1)S(1)}, bf16[4,8,4096]{2,1,0:T(8,128)(2,1)S(1)}, u32[]{:S(2)}, u32[]{:S(2)}) collective-permute-start(bf16[4,8,4096]{2,1,0:T(8,128)(2,1)S(1)} %bitcast.101), channel_id=1, source_target_pairs={{0,2},{1,3},{2,0},{3,1},{4,6},{5,7},{6,4},{7,5},{8,10},{9,11},{10,... | collective-permute-start | bytes 786440 | tf_op jit(solution)/shard_map/ppermute | solution.py:23
  29.4 7.0 %collective-permute-start.7 = (bf16[8,8,4096]{2,1,0:T(8,128)(2,1)S(1)}, bf16[8,8,4096]{2,1,0:T(8,128)(2,1)S(1)}, u32[]{:S(2)}, u32[]{:S(2)}) collective-permute-start(bf16[8,8,4096]{2,1,0:T(8,128)(2,1)S(1)} %bitcast.98), channel_id=1, source_target_pairs={{0,1},{1,0},{2,3},{3,2},{4,5},{5,4},{6,7},{7,6},{8,9},{9,8},{10,11... | collective-permute-start | bytes 1572872 | tf_op jit(solution)/shard_map/ppermute | solution.py:23
  32.8 3.5 %copy-start = (f32[128,512]{1,0:T(8,128)S(1)}, f32[128,512]{1,0:T(8,128)}, u32[]{:S(2)}) copy-start(f32[128,512]{1,0:T(8,128)} %get-tuple-element.55) | copy-start | bytes 786436
  32.8 3.5 %copy-start.1 = (f32[128,512]{1,0:T(8,128)S(1)}, f32[128,512]{1,0:T(8,128)}, u32[]{:S(2)}) copy-start(f32[128,512]{1,0:T(8,128)} %get-tuple-element.54) | copy-start | bytes 786436
  32.8 3.5 %copy-start.2 = (f32[128,512]{1,0:T(8,128)S(1)}, f32[128,512]{1,0:T(8,128)}, u32[]{:S(2)}) copy-start(f32[128,512]{1,0:T(8,128)} %get-tuple-element.66) | copy-start | bytes 786436
  32.8 3.5 %copy-start.3 = (f32[128,8]{1,0:T(8,128)S(1)}, f32[128,8]{1,0:T(8,128)}, u32[]{:S(2)}) copy-start(f32[128,8]{1,0:T(8,128)} %get-tuple-element.68) | copy-start | bytes 12292
  32.9 3.5 %copy-start.4 = (f32[128,8]{1,0:T(8,128)S(1)}, f32[128,8]{1,0:T(8,128)}, u32[]{:S(2)}) copy-start(f32[128,8]{1,0:T(8,128)} %get-tuple-element.72) | copy-start | bytes 12292
  32.9 3.5 %copy-start.5 = (f32[128,8]{1,0:T(8,128)S(1)}, f32[128,8]{1,0:T(8,128)}, u32[]{:S(2)}) copy-start(f32[128,8]{1,0:T(8,128)} %get-tuple-element.67) | copy-start | bytes 12292
  32.9 3.5 %copy-start.6 = (f32[128,8]{1,0:T(8,128)S(1)}, f32[128,8]{1,0:T(8,128)}, u32[]{:S(2)}) copy-start(f32[128,8]{1,0:T(8,128)} %get-tuple-element.71) | copy-start | bytes 12292
  32.9 3.5 %copy-start.7 = (f32[128,8]{1,0:T(8,128)S(1)}, f32[128,8]{1,0:T(8,128)}, u32[]{:S(2)}) copy-start(f32[128,8]{1,0:T(8,128)} %get-tuple-element.70) | copy-start | bytes 12292
  32.9 3.5 %copy-start.8 = (f32[128,8]{1,0:T(8,128)S(1)}, f32[128,8]{1,0:T(8,128)}, u32[]{:S(2)}) copy-start(f32[128,8]{1,0:T(8,128)} %get-tuple-element.74) | copy-start | bytes 12292
  38.3 5.1 %collective-permute-start.8 = (bf16[8,8,2208]{2,1,0:T(8,128)(2,1)S(1)}, bf16[8,8,2208]{2,1,0:T(8,128)(2,1)S(1)}, u32[]{:S(2)}, u32[]{:S(2)}) collective-permute-start(bf16[8,8,2208]{2,1,0:T(8,128)(2,1)S(1)} %concatenate.41), channel_id=1, source_target_pairs={{0,1},{1,0},{2,3},{3,2},{4,5},{5,4},{6,7},{7,6},{8,9},{9,8},{10,11... | collective-permute-start | bytes 847880 | tf_op jit(solution)/shard_map/ppermute | solution.py:23
  45.0 5.8 %collective-permute-start.9 = (bf16[4,8,2208]{2,1,0:T(8,128)(2,1)S(1)}, bf16[4,8,2208]{2,1,0:T(8,128)(2,1)S(1)}, u32[]{:S(2)}, u32[]{:S(2)}) collective-permute-start(bf16[4,8,2208]{2,1,0:T(8,128)(2,1)S(1)} %concatenate.44), channel_id=1, source_target_pairs={{0,2},{1,3},{2,0},{3,1},{4,6},{5,7},{6,4},{7,5},{8,10},{9,11},{10,... | collective-permute-start | bytes 423944 | tf_op jit(solution)/shard_map/ppermute | solution.py:23
  52.0 5.2 %collective-permute-start.10 = (bf16[2,8,2208]{2,1,0:T(8,128)(2,1)S(1)}, bf16[2,8,2208]{2,1,0:T(8,128)(2,1)S(1)}, u32[]{:S(2)}, u32[]{:S(2)}) collective-permute-start(bf16[2,8,2208]{2,1,0:T(8,128)(2,1)S(1)} %concatenate.47), channel_id=1, source_target_pairs={{0,4},{1,5},{2,6},{3,7},{4,0},{5,1},{6,2},{7,3},{8,12},{9,13},{10,... | collective-permute-start | bytes 211976 | tf_op jit(solution)/shard_map/ppermute | solution.py:23
  58.3 7.1 %collective-permute-start.11 = (bf16[1,8,2208]{2,1,0:T(8,128)(2,1)S(1)}, bf16[1,8,2208]{2,1,0:T(8,128)(2,1)S(1)}, u32[]{:S(2)}, u32[]{:S(2)}) collective-permute-start(bf16[1,8,2208]{2,1,0:T(8,128)(2,1)S(1)} %concatenate.50), channel_id=1, source_target_pairs={{0,8},{1,9},{2,10},{3,11},{4,12},{5,13},{6,14},{7,15},{8,0},{9,1},... | collective-permute-start | bytes 105992 | tf_op jit(solution)/shard_map/ppermute | solution.py:23

commit v18 on v12

--- a/solution.py
+++ b/solution.py
@@ -315,10 +315,10 @@
     all_queries = gather_levels(audio_q)
     audio_calls = [
         (
-            lambda q, gs=gs: tuple(audio_partial(q, video_k, video_v, g, groups) for g in gs),
+            lambda q, g=g: (audio_partial(q, video_k, video_v, g, 2),),
             all_queries,
         )
-        for gs in ((0, 1), (2, 3))
+        for g in range(2)
     ]
     gathered, results = gather_rows(
         jnp.concatenate([audio_k, audio_v], axis=1), [None] * (steps - 2) + audio_calls

time: 64.8 us -> 62.7 us (0.968)
  Pallas kernels: 27.6 us -> 24.8 us
  waiting for transfers between devices: 9.66 us -> 11.9 us
  starting transfers between devices: 14.2 us -> 12.8 us
    pallas_call x4 -> x2, Pallas kernels: 13.5 us -> 10.7 us  [audio_partial(): pl.pallas_call(audio_kernel, grid=(heads // 2 // PER_STEP,), in_specs=[pl...]
    ppermute x8, waiting for transfers between devices: 3.92 us -> 6.14 us  [exchange(): return lax.ppermute(value, 'seq', pairs)]
    ppermute x8, starting transfers between devices: 6.84 us -> 5.44 us  [exchange(): return lax.ppermute(value, 'seq', pairs)]
  transfers between devices with their start and end apart: 13 -> 13, of which waited for: 6 -> 7; matrix products, arithmetic and copies ran while one was open for 6% -> 6% of each run, Pallas kernels for 43% -> 40%
where the time goes in v18:
time: 62.7 us; the launch traced here: 62.2 us
  Pallas kernels  24.8 us (40%)
  starting transfers between devices  12.8 us (20%)
  waiting for transfers between devices  11.9 us (19%)
  local copies, waits for them, and re-layouts  4.24 us (7%)
  other arithmetic  4.01 us (6%)
  matrix products  3.45 us (6%)
  between operations  1 us (2%)
    pallas_call x4, Pallas kernels, video_part(): pl.pallas_call(video_kernel, grid=(pairs // PER_STEP,), in_specs=specs, o...  14.1 us
    pallas_call x2, Pallas kernels, audio_partial(): pl.pallas_call(audio_kernel, grid=(heads // 2 // PER_STEP,), in_specs=[pl...  10.7 us
    ppermute x5, starting transfers between devices, gather_levels(): pieces[offset] = lax.ppermute(held, 'seq', pairs)  7.34 us
    ppermute x8, waiting for transfers between devices, exchange(): return lax.ppermute(value, 'seq', pairs)  6.14 us
    ppermute x5, waiting for transfers between devices, gather_levels(): pieces[offset] = lax.ppermute(held, 'seq', pairs)  5.74 us
    ppermute x8, starting transfers between devices, exchange(): return lax.ppermute(value, 'seq', pairs)  5.44 us
    dot_general x9, matrix products, spread(): jnp.dot(scales, expand, precision=lax.Precision.HIGHEST, preferred_elemen...  3.45 us
  transfers between devices with their start and end apart: 13, of which 7 were waited for; matrix products, arithmetic and copies ran while one was open for 6% of the time, Pallas kernels for 40%

profile of v18, /device:TPU:0, one launch (start us, length us, event | category | flops | bytes accessed | tf_op | source)
XLA Modules:
  0.0 62.2 jit_solution(3804772197401561615)
XLA Ops:
  0.6 4.1 %collective-permute-start.4 = (bf16[1,8,2048]{2,1,0:T(8,128)(2,1)}, bf16[1,8,2048]{2,1,0:T(8,128)(2,1)S(1)}, u32[]{:S(2)}, u32[]{:S(2)}) collective-permute-start(bf16[1,8,2048]{2,1,0:T(8,128)(2,1)} %bitcast.111), channel_id=1, source_target_pairs={{0,8},{1,9},{2,10},{3,11},{4,12},{5,13},{6,14},{7,15},{8,0},{9,1},... | collective-permute-start | bytes 98312 | tf_op jit(solution)/shard_map/ppermute | solution.py:71
  4.7 1.6 %collective-permute-start.3 = (bf16[1,8,2048]{2,1,0:T(8,128)(2,1)}, bf16[1,8,2048]{2,1,0:T(8,128)(2,1)S(1)}, u32[]{:S(2)}, u32[]{:S(2)}) collective-permute-start(bf16[1,8,2048]{2,1,0:T(8,128)(2,1)} %bitcast.112), channel_id=1, source_target_pairs={{0,4},{1,5},{2,6},{3,7},{4,0},{5,1},{6,2},{7,3},{8,12},{9,13},{10,... | collective-permute-start | bytes 98312 | tf_op jit(solution)/shard_map/ppermute | solution.py:71
  6.3 0.8 %maximum_bitcast_fusion.2 = bf16[1,8,4096]{2,1,0:T(8,128)(2,1)S(1)} fusion(bf16[8,2048]{1,0:T(8,128)(2,1)} %param.11, bf16[8,2048]{1,0:T(8,128)(2,1)} %param.10), kind=kLoop, calls=%fused_computation.74 | loop fusion | flops 131072 | bytes 131072 | tf_op jit(solution)/shard_map/broadcast_in_dim | solution.py:29
  7.1 1.9 %collective-permute-start = (bf16[1,8,4096]{2,1,0:T(8,128)(2,1)S(1)}, bf16[1,8,4096]{2,1,0:T(8,128)(2,1)S(1)}, u32[]{:S(2)}, u32[]{:S(2)}) collective-permute-start(bf16[1,8,4096]{2,1,0:T(8,128)(2,1)S(1)} %maximum_bitcast_fusion.2), channel_id=1, source_target_pairs={{0,8},{1,9},{2,10},{3,11},{4,12},{5,13},{6,14},{7,15},{8,0},{9,1},... | collective-permute-start | bytes 196616 | tf_op jit(solution)/shard_map/ppermute | solution.py:23
  9.0 3.2 %collective-permute-done.2 = bf16[1,8,2048]{2,1,0:T(8,128)(2,1)S(1)} collective-permute-done((bf16[1,8,2048]{2,1,0:T(8,128)(2,1)}, bf16[1,8,2048]{2,1,0:T(8,128)(2,1)S(1)}, u32[]{:S(2)}, u32[]{:S(2)}) %collective-permute-start.2) | collective-permute-done | bytes 32800 | tf_op jit(solution)/shard_map/ppermute | solution.py:71
  12.2 0.8 %select_bitcast_fusion.23 = (bf16[1,1,8,2048]{3,2,1,0:T(8,128)(2,1)S(1)}, bf16[1,1,8,2048]{3,2,1,0:T(8,128)(2,1)S(1)}, bf16[1,1,8,2048]{3,2,1,0:T(8,128)(2,1)S(1)}, bf16[1,1,8,2048]{3,2,1,0:T(8,128)(2,1)S(1)}) fusion(bf16[1,8,2048]{2,1,0:T(8,128)(2,1)S(1)} %collective-permute-done.2, bf16[1,8,2048]{2,1,0:T(8,128)(2,1)S(1)} %collective-permute-done.3, ...), kind=kLoop, calls=%fused_computation.98 | loop fusion | flops 196608 | bytes 262156 | tf_op jit(solution)/shard_map/stack | solution.py:79
  13.0 1.6 %collective-permute-start.5 = (bf16[4,8,2048]{2,1,0:T(8,128)(2,1)S(1)}, bf16[4,8,2048]{2,1,0:T(8,128)(2,1)S(1)}, u32[]{:S(2)}, u32[]{:S(2)}) collective-permute-start(bf16[4,8,2048]{2,1,0:T(8,128)(2,1)S(1)} %maximum_bitcast_fusion.1), channel_id=1, source_target_pairs={{0,2},{1,3},{2,0},{3,1},{4,6},{5,7},{6,4},{7,5},{8,10},{9,11},{10,... | collective-permute-start | bytes 393224 | tf_op jit(solution)/shard_map/ppermute | solution.py:71
  14.6 0.8 %select_bitcast_fusion.19 = (bf16[1,1,8,4096]{3,2,1,0:T(8,128)(2,1)S(1)}, bf16[1,1,8,4096]{3,2,1,0:T(8,128)(2,1)S(1)}) fusion(bf16[1,8,4096]{2,1,0:T(8,128)(2,1)S(1)} %collective-permute-done, pred[]{:T(512)S(6)} %ne.98, bf16[8,2048]{1,0:T(8,128)(2,1)} %param.11, bf16[8,2048]{1,0:T(8,128)(2,1)} %param.10), kind=kLoop, calls=%fused_computation.76 | loop fusion | flops 196608 | bytes 262145 | tf_op jit(solution)/shard_map/stack | solution.py:45
  15.5 0.1 collective-permute-start.1
  15.6 2.5 %collective-permute-done.5 = bf16[4,8,2048]{2,1,0:T(8,128)(2,1)S(1)} collective-permute-done((bf16[4,8,2048]{2,1,0:T(8,128)(2,1)S(1)}, bf16[4,8,2048]{2,1,0:T(8,128)(2,1)S(1)}, u32[]{:S(2)}, u32[]{:S(2)}) %collective-permute-start.5) | collective-permute-done | bytes 131104 | tf_op jit(solution)/shard_map/ppermute | solution.py:71
  18.2 2.3 %collective-permute-done.1 = bf16[2,8,4096]{2,1,0:T(8,128)(2,1)S(1)} collective-permute-done((bf16[2,8,4096]{2,1,0:T(8,128)(2,1)S(1)}, bf16[2,8,4096]{2,1,0:T(8,128)(2,1)S(1)}, u32[]{:S(2)}, u32[]{:S(2)}) %collective-permute-start.1) | collective-permute-done | bytes 131104 | tf_op jit(solution)/shard_map/ppermute | solution.py:23
  20.7 0.8 %copy.20 = bf16[8,2,8,2048]{3,2,1,0:T(8,128)(2,1)} copy(bf16[8,2,8,2048]{3,2,0,1:T(8,128)(2,1)S(1)} %pad_maximum_fusion.1) | data formatting | bytes 1048576 | tf_op jit(solution)/shard_map/stack | solution.py:79
  21.5 0.7 %collective-permute-start.7 = (bf16[4,8,4096]{2,1,0:T(8,128)(2,1)S(1)}, bf16[4,8,4096]{2,1,0:T(8,128)(2,1)S(1)}, u32[]{:S(2)}, u32[]{:S(2)}) collective-permute-start(bf16[4,8,4096]{2,1,0:T(8,128)(2,1)S(1)} %bitcast.99), channel_id=1, source_target_pairs={{0,2},{1,3},{2,0},{3,1},{4,6},{5,7},{6,4},{7,5},{8,10},{9,11},{10,... | collective-permute-start | bytes 786440 | tf_op jit(solution)/shard_map/ppermute | solution.py:23
  22.2 5.3 %shard_map.77 = (f32[128,1024]{1,0:T(8,128)}, f32[128,16]{1,0:T(8,128)}, f32[128,16]{1,0:T(8,128)}) custom-call(bf16[128,2048]{1,0:T(8,128)(2,1)} %bitcast.90, bf16[512,2048]{1,0:T(8,128)(2,1)} %key_ref.3, bf16[512,2048]{1,0:T(8,128)(2,1)} %value_ref.3), custom_call_target="tpu_custom_call" | custom-call | flops 536870912 | bytes 2883584 | tf_op jit(solution)/shard_map/pallas_call | solution.py:283
  27.5 1.5 %collective-permute-done.7 = bf16[4,8,4096]{2,1,0:T(8,128)(2,1)S(1)} collective-permute-done((bf16[4,8,4096]{2,1,0:T(8,128)(2,1)S(1)}, bf16[4,8,4096]{2,1,0:T(8,128)(2,1)S(1)}, u32[]{:S(2)}, u32[]{:S(2)}) %collective-permute-start.7) | collective-permute-done | bytes 262176 | tf_op jit(solution)/shard_map/ppermute | solution.py:23
  29.3 5.4 %shard_map.78 = (f32[128,1024]{1,0:T(8,128)}, f32[128,16]{1,0:T(8,128)}, f32[128,16]{1,0:T(8,128)}) custom-call(bf16[128,2048]{1,0:T(8,128)(2,1)} %bitcast.91, bf16[512,2048]{1,0:T(8,128)(2,1)} %key_ref.3, bf16[512,2048]{1,0:T(8,128)(2,1)} %value_ref.3), custom_call_target="tpu_custom_call" | custom-call | flops 536870912 | bytes 2883584 | tf_op jit(solution)/shard_map/pallas_call | solution.py:283
  34.8 1.2 %concatenate.40 = f32[128,2112]{1,0:T(8,128)S(1)} concatenate(f32[128,1024]{1,0:T(8,128)S(1)} %copy-done, f32[128,1024]{1,0:T(8,128)} %get-tuple-element.46, f32[128,16]{1,0:T(8,128)S(1)} %copy-done.1, f32[128,16]{1,0:T(8,128)} %get-tuple-element.48, f32[128,16]{1,0:T(8,128)S(1)} %copy-done.2, f32[128,16]{1,0:T(8,128)} %get-tuple-element.50), dimensions={1} | concatenate | bytes 2162688 | tf_op jit(solution)/shard_map/concatenate | solution.py:329
  36.1 0.1 fusion.35
  36.3 0.1 pad_maximum_fusion
  36.4 0.1 copy.22
  36.5 0.1 concatenate.41
  36.6 0.5 collective-permute-start.9
  37.1 1.1 %fusion.62 = (bf16[128,2048]{1,0:T(8,128)(2,1)}, bf16[128,2048]{1,0:T(8,128)(2,1)}) fusion(bf16[128,4096]{1,0:T(8,128)(2,1)S(1)} %bitcast.93), kind=kLoop, calls=%fused_computation.162 | loop fusion | bytes 2097152 | tf_op jit(solution)/shard_map/slice | solution.py:328
  38.2 3.5 %shard_map.79.refs_0_ = bf16[512,2048]{1,0:T(8,128)(2,1)} custom-call(bf16[512,2048]{1,0:T(8,128)(2,1)} %query_ref.7, bf16[128,2048]{1,0:T(8,128)(2,1)} %get-tuple-element.75.key_ref, bf16[128,2048]{1,0:T(8,128)(2,1)} %get-tuple-element.74.value_ref), custom_call_target="tpu_custom_call" | custom-call | flops 268435456 | bytes 1310720 | tf_op jit(solution)/shard_map/pallas_call | solution.py:237
  41.9 0.1 concatenate.42
  41.9 0.1 fusion.36
  42.0 0.4 convolution_multiply_fusion.1
  42.5 0.4 fusion
  42.9 0.1 concatenate.43
  43.2 0.1 concatenate.44
  43.3 1.6 %collective-permute-start.10 = (bf16[4,8,2208]{2,1,0:T(8,128)(2,1)S(1)}, bf16[4,8,2208]{2,1,0:T(8,128)(2,1)S(1)}, u32[]{:S(2)}, u32[]{:S(2)}) collective-permute-start(bf16[4,8,2208]{2,1,0:T(8,128)(2,1)S(1)} %concatenate.44), channel_id=1, source_target_pairs={{0,2},{1,3},{2,0},{3,1},{4,6},{5,7},{6,4},{7,5},{8,10},{9,11},{10,... | collective-permute-start | bytes 423944 | tf_op jit(solution)/shard_map/ppermute | solution.py:23
  44.8 3.5 %shard_map.80.refs_0_ = bf16[512,2048]{1,0:T(8,128)(2,1)} custom-call(bf16[512,2048]{1,0:T(8,128)(2,1)} %query_ref.7, bf16[128,2048]{1,0:T(8,128)(2,1)} %get-tuple-element.75.key_ref, bf16[128,2048]{1,0:T(8,128)(2,1)} %get-tuple-element.74.value_ref, bf16[512,2048]{1,0:T(8,128)(2,1)} %shard_map.79.refs_0_), custom_call_target="tpu_custom_call", output_to_operand_aliasing={{}: (3, {})} | custom-call | flops 268435456 | bytes 1310720 | tf_op jit(solution)/shard_map/pallas_call | solution.py:237
  48.4 0.7 %collective-permute-done.10 = bf16[4,8,2208]{2,1,0:T(8,128)(2,1)S(1)} collective-permute-done((bf16[4,8,2208]{2,1,0:T(8,128)(2,1)S(1)}, bf16[4,8,2208]{2,1,0:T(8,128)(2,1)S(1)}, u32[]{:S(2)}, u32[]{:S(2)}) %collective-permute-start.10) | collective-permute-done | bytes 141344 | tf_op jit(solution)/shard_map/ppermute | solution.py:23
  49.3 0.1 fusion.41
  49.4 0.3 convolution_multiply_fusion.2
  49.7 0.3 fusion.1
  50.2 0.1 concatenate.47
  50.4 3.5 %shard_map.81.refs_0_ = bf16[512,2048]{1,0:T(8,128)(2,1)} custom-call(bf16[512,2048]{1,0:T(8,128)(2,1)} %query_ref.7, bf16[128,2048]{1,0:T(8,128)(2,1)} %get-tuple-element.75.key_ref, bf16[128,2048]{1,0:T(8,128)(2,1)} %get-tuple-element.74.value_ref, bf16[512,2048]{1,0:T(8,128)(2,1)} %shard_map.80.refs_0_), custom_call_target="tpu_custom_call", output_to_operand_aliasing={{}: (3, {})} | custom-call | flops 268435456 | bytes 1310720 | tf_op jit(solution)/shard_map/pallas_call | solution.py:237
  53.9 0.8 %collective-permute-done.11 = bf16[2,8,2208]{2,1,0:T(8,128)(2,1)S(1)} collective-permute-done((bf16[2,8,2208]{2,1,0:T(8,128)(2,1)S(1)}, bf16[2,8,2208]{2,1,0:T(8,128)(2,1)S(1)}, u32[]{:S(2)}, u32[]{:S(2)}) %collective-permute-start.11) | collective-permute-done | bytes 70688 | tf_op jit(solution)/shard_map/ppermute | solution.py:23
  54.9 0.3 convolution_multiply_fusion.5
  55.2 0.3 fusion.2
  55.7 0.1 concatenate.50
  55.7 0.5 collective-permute-start.12
  56.2 3.5 %shard_map.82 = bf16[512,2048]{1,0:T(8,128)(2,1)} custom-call(bf16[512,2048]{1,0:T(8,128)(2,1)} %query_ref.7, bf16[128,2048]{1,0:T(8,128)(2,1)} %get-tuple-element.75.key_ref, bf16[128,2048]{1,0:T(8,128)(2,1)} %get-tuple-element.74.value_ref, bf16[512,2048]{1,0:T(8,128)(2,1)} %shard_map.81.refs_0_), custom_call_target="tpu_custom_call", output_to_operand_aliasing={{}: (3, {})} | custom-call | flops 268435456 | bytes 1310720 | tf_op jit(solution)/shard_map/pallas_call | solution.py:237
  59.8 0.8 %collective-permute-done.12 = bf16[1,8,2208]{2,1,0:T(8,128)(2,1)S(1)} collective-permute-done((bf16[1,8,2208]{2,1,0:T(8,128)(2,1)S(1)}, bf16[1,8,2208]{2,1,0:T(8,128)(2,1)S(1)}, u32[]{:S(2)}, u32[]{:S(2)}) %collective-permute-start.12) | collective-permute-done | bytes 35360 | tf_op jit(solution)/shard_map/ppermute | solution.py:23
  60.8 0.2 convolution_multiply_fusion.7
  61.0 0.3 fusion.3
  61.3 0.9 %fusion.4 = bf16[8,2048]{1,0:T(8,128)(2,1)} fusion(f32[8,2048]{1,0:T(8,128)S(1)} %fusion.3, s32[2048]{0:T(1024)S(1)} %get-tuple-element.126, s32[2048]{0:T(1024)S(1)} %get-tuple-element.127, pred[2048]{0:T(1024)(128)(4,1)S(1)} %fusion.49, f32[8,2112]{1,0:T(8,128)S(1)} %bitcast.110, f32[8,2112]{1,0:T(8,128)S(1)} %get-tuple-element.104), kind=kOutput, calls=%fused_computation.13 | convolution fusion | flops 6456832 | bytes 133120 | tf_op jit(solution)/shard_map/dot_general | solution.py:16
  (55 shorter events, 2.0 us)
Async XLA Ops:
  0.6 8.4 %collective-permute-start.4 = (bf16[1,8,2048]{2,1,0:T(8,128)(2,1)}, bf16[1,8,2048]{2,1,0:T(8,128)(2,1)S(1)}, u32[]{:S(2)}, u32[]{:S(2)}) collective-permute-start(bf16[1,8,2048]{2,1,0:T(8,128)(2,1)} %bitcast.111), channel_id=1, source_target_pairs={{0,8},{1,9},{2,10},{3,11},{4,12},{5,13},{6,14},{7,15},{8,0},{9,1},... | collective-permute-start | bytes 98312 | tf_op jit(solution)/shard_map/ppermute | solution.py:71
  4.7 4.3 %collective-permute-start.3 = (bf16[1,8,2048]{2,1,0:T(8,128)(2,1)}, bf16[1,8,2048]{2,1,0:T(8,128)(2,1)S(1)}, u32[]{:S(2)}, u32[]{:S(2)}) collective-permute-start(bf16[1,8,2048]{2,1,0:T(8,128)(2,1)} %bitcast.112), channel_id=1, source_target_pairs={{0,4},{1,5},{2,6},{3,7},{4,0},{5,1},{6,2},{7,3},{8,12},{9,13},{10,... | collective-permute-start | bytes 98312 | tf_op jit(solution)/shard_map/ppermute | solution.py:71
  6.3 5.9 %collective-permute-start.2 = (bf16[1,8,2048]{2,1,0:T(8,128)(2,1)}, bf16[1,8,2048]{2,1,0:T(8,128)(2,1)S(1)}, u32[]{:S(2)}, u32[]{:S(2)}) collective-permute-start(bf16[1,8,2048]{2,1,0:T(8,128)(2,1)} %bitcast.113), channel_id=1, source_target_pairs={{0,12},{1,13},{2,14},{3,15},{4,8},{5,9},{6,10},{7,11},{8,4},{9,5},... | collective-permute-start | bytes 98312 | tf_op jit(solution)/shard_map/ppermute | solution.py:71
  7.1 7.5 %collective-permute-start = (bf16[1,8,4096]{2,1,0:T(8,128)(2,1)S(1)}, bf16[1,8,4096]{2,1,0:T(8,128)(2,1)S(1)}, u32[]{:S(2)}, u32[]{:S(2)}) collective-permute-start(bf16[1,8,4096]{2,1,0:T(8,128)(2,1)S(1)} %maximum_bitcast_fusion.2), channel_id=1, source_target_pairs={{0,8},{1,9},{2,10},{3,11},{4,12},{5,13},{6,14},{7,15},{8,0},{9,1},... | collective-permute-start | bytes 196616 | tf_op jit(solution)/shard_map/ppermute | solution.py:23
  13.0 5.0 %collective-permute-start.5 = (bf16[4,8,2048]{2,1,0:T(8,128)(2,1)S(1)}, bf16[4,8,2048]{2,1,0:T(8,128)(2,1)S(1)}, u32[]{:S(2)}, u32[]{:S(2)}) collective-permute-start(bf16[4,8,2048]{2,1,0:T(8,128)(2,1)S(1)} %maximum_bitcast_fusion.1), channel_id=1, source_target_pairs={{0,2},{1,3},{2,0},{3,1},{4,6},{5,7},{6,4},{7,5},{8,10},{9,11},{10,... | collective-permute-start | bytes 393224 | tf_op jit(solution)/shard_map/ppermute | solution.py:71
  15.5 5.0 %collective-permute-start.1 = (bf16[2,8,4096]{2,1,0:T(8,128)(2,1)S(1)}, bf16[2,8,4096]{2,1,0:T(8,128)(2,1)S(1)}, u32[]{:S(2)}, u32[]{:S(2)}) collective-permute-start(bf16[2,8,4096]{2,1,0:T(8,128)(2,1)S(1)} %maximum_bitcast_fusion), channel_id=1, source_target_pairs={{0,4},{1,5},{2,6},{3,7},{4,0},{5,1},{6,2},{7,3},{8,12},{9,13},{10,... | collective-permute-start | bytes 393224 | tf_op jit(solution)/shard_map/ppermute | solution.py:23
  18.1 2.4 %collective-permute-start.6 = (bf16[8,8,2048]{2,1,0:T(8,128)(2,1)S(1)}, bf16[8,8,2048]{2,1,0:T(8,128)(2,1)S(1)}, u32[]{:S(2)}, u32[]{:S(2)}) collective-permute-start(bf16[8,8,2048]{2,1,0:T(8,128)(2,1)S(1)} %bitcast.98), channel_id=1, source_target_pairs={{0,1},{1,0},{2,3},{3,2},{4,5},{5,4},{6,7},{7,6},{8,9},{9,8},{10,11... | collective-permute-start | bytes 786440 | tf_op jit(solution)/shard_map/ppermute | solution.py:71
  21.5 7.5 %collective-permute-start.7 = (bf16[4,8,4096]{2,1,0:T(8,128)(2,1)S(1)}, bf16[4,8,4096]{2,1,0:T(8,128)(2,1)S(1)}, u32[]{:S(2)}, u32[]{:S(2)}) collective-permute-start(bf16[4,8,4096]{2,1,0:T(8,128)(2,1)S(1)} %bitcast.99), channel_id=1, source_target_pairs={{0,2},{1,3},{2,0},{3,1},{4,6},{5,7},{6,4},{7,5},{8,10},{9,11},{10,... | collective-permute-start | bytes 786440 | tf_op jit(solution)/shard_map/ppermute | solution.py:23
  29.2 5.5 %collective-permute-start.8 = (bf16[8,8,4096]{2,1,0:T(8,128)(2,1)S(1)}, bf16[8,8,4096]{2,1,0:T(8,128)(2,1)S(1)}, u32[]{:S(2)}, u32[]{:S(2)}) collective-permute-start(bf16[8,8,4096]{2,1,0:T(8,128)(2,1)S(1)} %bitcast.95), channel_id=1, source_target_pairs={{0,1},{1,0},{2,3},{3,2},{4,5},{5,4},{6,7},{7,6},{8,9},{9,8},{10,11... | collective-permute-start | bytes 1572872 | tf_op jit(solution)/shard_map/ppermute | solution.py:23
  29.3 5.4 %copy-start = (f32[128,1024]{1,0:T(8,128)S(1)}, f32[128,1024]{1,0:T(8,128)}, u32[]{:S(2)}) copy-start(f32[128,1024]{1,0:T(8,128)} %get-tuple-element.39) | copy-start | bytes 1572868
  29.3 5.4 %copy-start.1 = (f32[128,16]{1,0:T(8,128)S(1)}, f32[128,16]{1,0:T(8,128)}, u32[]{:S(2)}) copy-start(f32[128,16]{1,0:T(8,128)} %get-tuple-element.47) | copy-start | bytes 24580
  29.3 5.4 %copy-start.2 = (f32[128,16]{1,0:T(8,128)S(1)}, f32[128,16]{1,0:T(8,128)}, u32[]{:S(2)}) copy-start(f32[128,16]{1,0:T(8,128)} %get-tuple-element.49) | copy-start | bytes 24580
  36.6 5.1 %collective-permute-start.9 = (bf16[8,8,2208]{2,1,0:T(8,128)(2,1)S(1)}, bf16[8,8,2208]{2,1,0:T(8,128)(2,1)S(1)}, u32[]{:S(2)}, u32[]{:S(2)}) collective-permute-start(bf16[8,8,2208]{2,1,0:T(8,128)(2,1)S(1)} %concatenate.41), channel_id=1, source_target_pairs={{0,1},{1,0},{2,3},{3,2},{4,5},{5,4},{6,7},{7,6},{8,9},{9,8},{10,11... | collective-permute-start | bytes 847880 | tf_op jit(solution)/shard_map/ppermute | solution.py:23
  43.3 5.8 %collective-permute-start.10 = (bf16[4,8,2208]{2,1,0:T(8,128)(2,1)S(1)}, bf16[4,8,2208]{2,1,0:T(8,128)(2,1)S(1)}, u32[]{:S(2)}, u32[]{:S(2)}) collective-permute-start(bf16[4,8,2208]{2,1,0:T(8,128)(2,1)S(1)} %concatenate.44), channel_id=1, source_target_pairs={{0,2},{1,3},{2,0},{3,1},{4,6},{5,7},{6,4},{7,5},{8,10},{9,11},{10,... | collective-permute-start | bytes 423944 | tf_op jit(solution)/shard_map/ppermute | solution.py:23
  50.3 4.4 %collective-permute-start.11 = (bf16[2,8,2208]{2,1,0:T(8,128)(2,1)S(1)}, bf16[2,8,2208]{2,1,0:T(8,128)(2,1)S(1)}, u32[]{:S(2)}, u32[]{:S(2)}) collective-permute-start(bf16[2,8,2208]{2,1,0:T(8,128)(2,1)S(1)} %concatenate.47), channel_id=1, source_target_pairs={{0,4},{1,5},{2,6},{3,7},{4,0},{5,1},{6,2},{7,3},{8,12},{9,13},{10,... | collective-permute-start | bytes 211976 | tf_op jit(solution)/shard_map/ppermute | solution.py:23
  55.7 4.9 %collective-permute-start.12 = (bf16[1,8,2208]{2,1,0:T(8,128)(2,1)S(1)}, bf16[1,8,2208]{2,1,0:T(8,128)(2,1)S(1)}, u32[]{:S(2)}, u32[]{:S(2)}) collective-permute-start(bf16[1,8,2208]{2,1,0:T(8,128)(2,1)S(1)} %concatenate.50), channel_id=1, source_target_pairs={{0,8},{1,9},{2,10},{3,11},{4,12},{5,13},{6,14},{7,15},{8,0},{9,1},... | collective-permute-start | bytes 105992 | tf_op jit(solution)/shard_map/ppermute | solution.py:23

commit v19 on v18

--- a/solution.py
+++ b/solution.py
@@ -249,6 +249,9 @@
     )(*operands)
 
 
+AUDIO_STEP = 4
+
+
 def audio_kernel(query_ref, key_ref, value_ref, sum_ref, total_ref, top_ref):
     step = pl.program_id(0)
 
@@ -260,13 +263,13 @@
     column = lax.broadcasted_iota(jnp.int32, total_ref.shape, 1)
     totals_now = total_ref[...]
     tops_now = top_ref[...]
-    for sub in range(PER_STEP):
+    for sub in range(AUDIO_STEP):
         lanes = slice(sub * 2 * HEAD_DIM, (sub + 1) * 2 * HEAD_DIM)
         summed, tops, counts = pair_attention(
             query_ref[:, lanes], key_ref[:, lanes], value_ref[:, lanes]
         )
         for half in range(2):
-            here = column == 2 * (step * PER_STEP + sub) + half
+            here = column == 2 * (step * AUDIO_STEP + sub) + half
             totals_now = jnp.where(here, counts[half], totals_now)
             tops_now = jnp.where(here, tops[half], tops_now)
         sum_ref[:, lanes] = summed
@@ -277,12 +280,12 @@
 def audio_partial(queries, keys, values, group, groups):
     rows, width = queries.shape
     heads = width // HEAD_DIM // groups
-    first_pair = group * heads // 2 // PER_STEP
-    lanes = 2 * HEAD_DIM * PER_STEP
+    first_pair = group * heads // 2 // AUDIO_STEP
+    lanes = 2 * HEAD_DIM * AUDIO_STEP
     key_rows = keys.shape[0]
     return pl.pallas_call(
         audio_kernel,
-        grid=(heads // 2 // PER_STEP,),
+        grid=(heads // 2 // AUDIO_STEP,),
         in_specs=[
             pl.BlockSpec((rows, lanes), lambda p: (0, p + first_pair)),
             pl.BlockSpec((key_rows, lanes), lambda p: (0, p + first_pair)),

time: 62.7 us -> 62.2 us (level)
  Pallas kernels: 24.8 us -> 23.9 us
    pallas_call x2, Pallas kernels: 10.7 us -> 9.81 us  [audio_partial(): pl.pallas_call(audio_kernel, grid=(heads // 2 // AUDIO_STEP,), in_specs=[...]
  transfers between devices with their start and end apart: 13 -> 13, of which waited for: 7 -> 7; matrix products, arithmetic and copies ran while one was open for 6% -> 6% of each run, Pallas kernels for 40% -> 39%
where the time goes in v19:
time: 62.2 us; the launch traced here: 61.7 us
  Pallas kernels  23.9 us (38%)
  starting transfers between devices  12.7 us (20%)
  waiting for transfers between devices  12.4 us (20%)
  local copies, waits for them, and re-layouts  4.24 us (7%)
  other arithmetic  4.01 us (6%)
  matrix products  3.45 us (6%)
  between operations  1 us (2%)
    pallas_call x4, Pallas kernels, video_part(): pl.pallas_call(video_kernel, grid=(pairs // PER_STEP,), in_specs=specs, o...  14.1 us
    pallas_call x2, Pallas kernels, audio_partial(): pl.pallas_call(audio_kernel, grid=(heads // 2 // AUDIO_STEP,), in_specs=[...  9.81 us
    ppermute x5, starting transfers between devices, gather_levels(): pieces[offset] = lax.ppermute(held, 'seq', pairs)  7.34 us
    ppermute x8, waiting for transfers between devices, exchange(): return lax.ppermute(value, 'seq', pairs)  6.69 us
    ppermute x5, waiting for transfers between devices, gather_levels(): pieces[offset] = lax.ppermute(held, 'seq', pairs)  5.74 us
    ppermute x8, starting transfers between devices, exchange(): return lax.ppermute(value, 'seq', pairs)  5.32 us
    dot_general x9, matrix products, spread(): jnp.dot(scales, expand, precision=lax.Precision.HIGHEST, preferred_elemen...  3.45 us
  transfers between devices with their start and end apart: 13, of which 7 were waited for; matrix products, arithmetic and copies ran while one was open for 6% of the time, Pallas kernels for 39%

profile of v19, /device:TPU:0, one launch (start us, length us, event | category | flops | bytes accessed | tf_op | source)
XLA Modules:
  0.0 61.7 jit_solution(4500748245930166442)
XLA Ops:
  0.6 4.1 %collective-permute-start.4 = (bf16[1,8,2048]{2,1,0:T(8,128)(2,1)}, bf16[1,8,2048]{2,1,0:T(8,128)(2,1)S(1)}, u32[]{:S(2)}, u32[]{:S(2)}) collective-permute-start(bf16[1,8,2048]{2,1,0:T(8,128)(2,1)} %bitcast.111), channel_id=1, source_target_pairs={{0,8},{1,9},{2,10},{3,11},{4,12},{5,13},{6,14},{7,15},{8,0},{9,1},... | collective-permute-start | bytes 98312 | tf_op jit(solution)/shard_map/ppermute | solution.py:71
  4.7 1.6 %collective-permute-start.3 = (bf16[1,8,2048]{2,1,0:T(8,128)(2,1)}, bf16[1,8,2048]{2,1,0:T(8,128)(2,1)S(1)}, u32[]{:S(2)}, u32[]{:S(2)}) collective-permute-start(bf16[1,8,2048]{2,1,0:T(8,128)(2,1)} %bitcast.112), channel_id=1, source_target_pairs={{0,4},{1,5},{2,6},{3,7},{4,0},{5,1},{6,2},{7,3},{8,12},{9,13},{10,... | collective-permute-start | bytes 98312 | tf_op jit(solution)/shard_map/ppermute | solution.py:71
  6.3 0.8 %maximum_bitcast_fusion.2 = bf16[1,8,4096]{2,1,0:T(8,128)(2,1)S(1)} fusion(bf16[8,2048]{1,0:T(8,128)(2,1)} %param.11, bf16[8,2048]{1,0:T(8,128)(2,1)} %param.10), kind=kLoop, calls=%fused_computation.74 | loop fusion | flops 131072 | bytes 131072 | tf_op jit(solution)/shard_map/broadcast_in_dim | solution.py:29
  7.1 1.9 %collective-permute-start = (bf16[1,8,4096]{2,1,0:T(8,128)(2,1)S(1)}, bf16[1,8,4096]{2,1,0:T(8,128)(2,1)S(1)}, u32[]{:S(2)}, u32[]{:S(2)}) collective-permute-start(bf16[1,8,4096]{2,1,0:T(8,128)(2,1)S(1)} %maximum_bitcast_fusion.2), channel_id=1, source_target_pairs={{0,8},{1,9},{2,10},{3,11},{4,12},{5,13},{6,14},{7,15},{8,0},{9,1},... | collective-permute-start | bytes 196616 | tf_op jit(solution)/shard_map/ppermute | solution.py:23
  9.0 3.2 %collective-permute-done.2 = bf16[1,8,2048]{2,1,0:T(8,128)(2,1)S(1)} collective-permute-done((bf16[1,8,2048]{2,1,0:T(8,128)(2,1)}, bf16[1,8,2048]{2,1,0:T(8,128)(2,1)S(1)}, u32[]{:S(2)}, u32[]{:S(2)}) %collective-permute-start.2) | collective-permute-done | bytes 32800 | tf_op jit(solution)/shard_map/ppermute | solution.py:71
  12.2 0.8 %select_bitcast_fusion.23 = (bf16[1,1,8,2048]{3,2,1,0:T(8,128)(2,1)S(1)}, bf16[1,1,8,2048]{3,2,1,0:T(8,128)(2,1)S(1)}, bf16[1,1,8,2048]{3,2,1,0:T(8,128)(2,1)S(1)}, bf16[1,1,8,2048]{3,2,1,0:T(8,128)(2,1)S(1)}) fusion(bf16[1,8,2048]{2,1,0:T(8,128)(2,1)S(1)} %collective-permute-done.2, bf16[1,8,2048]{2,1,0:T(8,128)(2,1)S(1)} %collective-permute-done.3, ...), kind=kLoop, calls=%fused_computation.98 | loop fusion | flops 196608 | bytes 262156 | tf_op jit(solution)/shard_map/stack | solution.py:79
  13.0 1.6 %collective-permute-start.5 = (bf16[4,8,2048]{2,1,0:T(8,128)(2,1)S(1)}, bf16[4,8,2048]{2,1,0:T(8,128)(2,1)S(1)}, u32[]{:S(2)}, u32[]{:S(2)}) collective-permute-start(bf16[4,8,2048]{2,1,0:T(8,128)(2,1)S(1)} %maximum_bitcast_fusion.1), channel_id=1, source_target_pairs={{0,2},{1,3},{2,0},{3,1},{4,6},{5,7},{6,4},{7,5},{8,10},{9,11},{10,... | collective-permute-start | bytes 393224 | tf_op jit(solution)/shard_map/ppermute | solution.py:71
  14.6 0.8 %select_bitcast_fusion.19 = (bf16[1,1,8,4096]{3,2,1,0:T(8,128)(2,1)S(1)}, bf16[1,1,8,4096]{3,2,1,0:T(8,128)(2,1)S(1)}) fusion(bf16[1,8,4096]{2,1,0:T(8,128)(2,1)S(1)} %collective-permute-done, pred[]{:T(512)S(6)} %ne.98, bf16[8,2048]{1,0:T(8,128)(2,1)} %param.11, bf16[8,2048]{1,0:T(8,128)(2,1)} %param.10), kind=kLoop, calls=%fused_computation.76 | loop fusion | flops 196608 | bytes 262145 | tf_op jit(solution)/shard_map/stack | solution.py:45
  15.5 0.1 collective-permute-start.1
  15.6 2.5 %collective-permute-done.5 = bf16[4,8,2048]{2,1,0:T(8,128)(2,1)S(1)} collective-permute-done((bf16[4,8,2048]{2,1,0:T(8,128)(2,1)S(1)}, bf16[4,8,2048]{2,1,0:T(8,128)(2,1)S(1)}, u32[]{:S(2)}, u32[]{:S(2)}) %collective-permute-start.5) | collective-permute-done | bytes 131104 | tf_op jit(solution)/shard_map/ppermute | solution.py:71
  18.2 2.3 %collective-permute-done.1 = bf16[2,8,4096]{2,1,0:T(8,128)(2,1)S(1)} collective-permute-done((bf16[2,8,4096]{2,1,0:T(8,128)(2,1)S(1)}, bf16[2,8,4096]{2,1,0:T(8,128)(2,1)S(1)}, u32[]{:S(2)}, u32[]{:S(2)}) %collective-permute-start.1) | collective-permute-done | bytes 131104 | tf_op jit(solution)/shard_map/ppermute | solution.py:23
  20.7 0.8 %copy.20 = bf16[8,2,8,2048]{3,2,1,0:T(8,128)(2,1)} copy(bf16[8,2,8,2048]{3,2,0,1:T(8,128)(2,1)S(1)} %pad_maximum_fusion.1) | data formatting | bytes 1048576 | tf_op jit(solution)/shard_map/stack | solution.py:79
  21.5 0.7 %collective-permute-start.7 = (bf16[4,8,4096]{2,1,0:T(8,128)(2,1)S(1)}, bf16[4,8,4096]{2,1,0:T(8,128)(2,1)S(1)}, u32[]{:S(2)}, u32[]{:S(2)}) collective-permute-start(bf16[4,8,4096]{2,1,0:T(8,128)(2,1)S(1)} %bitcast.99), channel_id=1, source_target_pairs={{0,2},{1,3},{2,0},{3,1},{4,6},{5,7},{6,4},{7,5},{8,10},{9,11},{10,... | collective-permute-start | bytes 786440 | tf_op jit(solution)/shard_map/ppermute | solution.py:23
  22.2 4.9 %shard_map.77 = (f32[128,1024]{1,0:T(8,128)}, f32[128,16]{1,0:T(8,128)}, f32[128,16]{1,0:T(8,128)}) custom-call(bf16[128,2048]{1,0:T(8,128)(2,1)} %bitcast.90, bf16[512,2048]{1,0:T(8,128)(2,1)} %key_ref.3, bf16[512,2048]{1,0:T(8,128)(2,1)} %value_ref.3), custom_call_target="tpu_custom_call" | custom-call | flops 536870912 | bytes 2883584 | tf_op jit(solution)/shard_map/pallas_call | solution.py:286
  27.1 1.9 %collective-permute-done.7 = bf16[4,8,4096]{2,1,0:T(8,128)(2,1)S(1)} collective-permute-done((bf16[4,8,4096]{2,1,0:T(8,128)(2,1)S(1)}, bf16[4,8,4096]{2,1,0:T(8,128)(2,1)S(1)}, u32[]{:S(2)}, u32[]{:S(2)}) %collective-permute-start.7) | collective-permute-done | bytes 262176 | tf_op jit(solution)/shard_map/ppermute | solution.py:23
  29.3 4.9 %shard_map.78 = (f32[128,1024]{1,0:T(8,128)}, f32[128,16]{1,0:T(8,128)}, f32[128,16]{1,0:T(8,128)}) custom-call(bf16[128,2048]{1,0:T(8,128)(2,1)} %bitcast.91, bf16[512,2048]{1,0:T(8,128)(2,1)} %key_ref.3, bf16[512,2048]{1,0:T(8,128)(2,1)} %value_ref.3), custom_call_target="tpu_custom_call" | custom-call | flops 536870912 | bytes 2883584 | tf_op jit(solution)/shard_map/pallas_call | solution.py:286
  34.3 1.2 %concatenate.40 = f32[128,2112]{1,0:T(8,128)S(1)} concatenate(f32[128,1024]{1,0:T(8,128)S(1)} %copy-done, f32[128,1024]{1,0:T(8,128)} %get-tuple-element.46, f32[128,16]{1,0:T(8,128)S(1)} %copy-done.1, f32[128,16]{1,0:T(8,128)} %get-tuple-element.48, f32[128,16]{1,0:T(8,128)S(1)} %copy-done.2, f32[128,16]{1,0:T(8,128)} %get-tuple-element.50), dimensions={1} | concatenate | bytes 2162688 | tf_op jit(solution)/shard_map/concatenate | solution.py:332
  35.6 0.1 fusion.35
  35.8 0.1 pad_maximum_fusion
  35.9 0.1 copy.22
  36.0 0.1 concatenate.41
  36.1 0.6 collective-permute-start.9
  36.7 1.1 %fusion.62 = (bf16[128,2048]{1,0:T(8,128)(2,1)}, bf16[128,2048]{1,0:T(8,128)(2,1)}) fusion(bf16[128,4096]{1,0:T(8,128)(2,1)S(1)} %bitcast.93), kind=kLoop, calls=%fused_computation.162 | loop fusion | bytes 2097152 | tf_op jit(solution)/shard_map/slice | solution.py:331
  37.7 3.5 %shard_map.79.refs_0_ = bf16[512,2048]{1,0:T(8,128)(2,1)} custom-call(bf16[512,2048]{1,0:T(8,128)(2,1)} %query_ref.7, bf16[128,2048]{1,0:T(8,128)(2,1)} %get-tuple-element.75.key_ref, bf16[128,2048]{1,0:T(8,128)(2,1)} %get-tuple-element.74.value_ref), custom_call_target="tpu_custom_call" | custom-call | flops 268435456 | bytes 1310720 | tf_op jit(solution)/shard_map/pallas_call | solution.py:237
  41.4 0.1 concatenate.42
  41.5 0.1 fusion.36
  41.6 0.4 convolution_multiply_fusion.1
  42.0 0.4 fusion
  42.5 0.1 concatenate.43
  42.7 0.1 concatenate.44
  42.8 1.6 %collective-permute-start.10 = (bf16[4,8,2208]{2,1,0:T(8,128)(2,1)S(1)}, bf16[4,8,2208]{2,1,0:T(8,128)(2,1)S(1)}, u32[]{:S(2)}, u32[]{:S(2)}) collective-permute-start(bf16[4,8,2208]{2,1,0:T(8,128)(2,1)S(1)} %concatenate.44), channel_id=1, source_target_pairs={{0,2},{1,3},{2,0},{3,1},{4,6},{5,7},{6,4},{7,5},{8,10},{9,11},{10,... | collective-permute-start | bytes 423944 | tf_op jit(solution)/shard_map/ppermute | solution.py:23
  44.4 3.5 %shard_map.80.refs_0_ = bf16[512,2048]{1,0:T(8,128)(2,1)} custom-call(bf16[512,2048]{1,0:T(8,128)(2,1)} %query_ref.7, bf16[128,2048]{1,0:T(8,128)(2,1)} %get-tuple-element.75.key_ref, bf16[128,2048]{1,0:T(8,128)(2,1)} %get-tuple-element.74.value_ref, bf16[512,2048]{1,0:T(8,128)(2,1)} %shard_map.79.refs_0_), custom_call_target="tpu_custom_call", output_to_operand_aliasing={{}: (3, {})} | custom-call | flops 268435456 | bytes 1310720 | tf_op jit(solution)/shard_map/pallas_call | solution.py:237
  47.9 0.7 %collective-permute-done.10 = bf16[4,8,2208]{2,1,0:T(8,128)(2,1)S(1)} collective-permute-done((bf16[4,8,2208]{2,1,0:T(8,128)(2,1)S(1)}, bf16[4,8,2208]{2,1,0:T(8,128)(2,1)S(1)}, u32[]{:S(2)}, u32[]{:S(2)}) %collective-permute-start.10) | collective-permute-done | bytes 141344 | tf_op jit(solution)/shard_map/ppermute | solution.py:23
  48.8 0.1 fusion.41
  48.9 0.3 convolution_multiply_fusion.2
  49.2 0.3 fusion.1
  49.8 0.1 concatenate.47
  49.9 3.5 %shard_map.81.refs_0_ = bf16[512,2048]{1,0:T(8,128)(2,1)} custom-call(bf16[512,2048]{1,0:T(8,128)(2,1)} %query_ref.7, bf16[128,2048]{1,0:T(8,128)(2,1)} %get-tuple-element.75.key_ref, bf16[128,2048]{1,0:T(8,128)(2,1)} %get-tuple-element.74.value_ref, bf16[512,2048]{1,0:T(8,128)(2,1)} %shard_map.80.refs_0_), custom_call_target="tpu_custom_call", output_to_operand_aliasing={{}: (3, {})} | custom-call | flops 268435456 | bytes 1310720 | tf_op jit(solution)/shard_map/pallas_call | solution.py:237
  53.4 0.8 %collective-permute-done.11 = bf16[2,8,2208]{2,1,0:T(8,128)(2,1)S(1)} collective-permute-done((bf16[2,8,2208]{2,1,0:T(8,128)(2,1)S(1)}, bf16[2,8,2208]{2,1,0:T(8,128)(2,1)S(1)}, u32[]{:S(2)}, u32[]{:S(2)}) %collective-permute-start.11) | collective-permute-done | bytes 70688 | tf_op jit(solution)/shard_map/ppermute | solution.py:23
  54.5 0.3 convolution_multiply_fusion.5
  54.7 0.3 fusion.2
  55.2 0.1 concatenate.50
  55.3 0.4 collective-permute-start.12
  55.6 3.5 %shard_map.82 = bf16[512,2048]{1,0:T(8,128)(2,1)} custom-call(bf16[512,2048]{1,0:T(8,128)(2,1)} %query_ref.7, bf16[128,2048]{1,0:T(8,128)(2,1)} %get-tuple-element.75.key_ref, bf16[128,2048]{1,0:T(8,128)(2,1)} %get-tuple-element.74.value_ref, bf16[512,2048]{1,0:T(8,128)(2,1)} %shard_map.81.refs_0_), custom_call_target="tpu_custom_call", output_to_operand_aliasing={{}: (3, {})} | custom-call | flops 268435456 | bytes 1310720 | tf_op jit(solution)/shard_map/pallas_call | solution.py:237
  59.2 1.0 %collective-permute-done.12 = bf16[1,8,2208]{2,1,0:T(8,128)(2,1)S(1)} collective-permute-done((bf16[1,8,2208]{2,1,0:T(8,128)(2,1)S(1)}, bf16[1,8,2208]{2,1,0:T(8,128)(2,1)S(1)}, u32[]{:S(2)}, u32[]{:S(2)}) %collective-permute-start.12) | collective-permute-done | bytes 35360 | tf_op jit(solution)/shard_map/ppermute | solution.py:23
  60.3 0.2 convolution_multiply_fusion.7
  60.6 0.3 fusion.3
  60.8 0.9 %fusion.4 = bf16[8,2048]{1,0:T(8,128)(2,1)} fusion(f32[8,2048]{1,0:T(8,128)S(1)} %fusion.3, s32[2048]{0:T(1024)S(1)} %get-tuple-element.126, s32[2048]{0:T(1024)S(1)} %get-tuple-element.127, pred[2048]{0:T(1024)(128)(4,1)S(1)} %fusion.49, f32[8,2112]{1,0:T(8,128)S(1)} %bitcast.110, f32[8,2112]{1,0:T(8,128)S(1)} %get-tuple-element.104), kind=kOutput, calls=%fused_computation.13 | convolution fusion | flops 6456832 | bytes 133120 | tf_op jit(solution)/shard_map/dot_general | solution.py:16
  (55 shorter events, 2.0 us)
Async XLA Ops:
  0.6 8.4 %collective-permute-start.4 = (bf16[1,8,2048]{2,1,0:T(8,128)(2,1)}, bf16[1,8,2048]{2,1,0:T(8,128)(2,1)S(1)}, u32[]{:S(2)}, u32[]{:S(2)}) collective-permute-start(bf16[1,8,2048]{2,1,0:T(8,128)(2,1)} %bitcast.111), channel_id=1, source_target_pairs={{0,8},{1,9},{2,10},{3,11},{4,12},{5,13},{6,14},{7,15},{8,0},{9,1},... | collective-permute-start | bytes 98312 | tf_op jit(solution)/shard_map/ppermute | solution.py:71
  4.7 4.3 %collective-permute-start.3 = (bf16[1,8,2048]{2,1,0:T(8,128)(2,1)}, bf16[1,8,2048]{2,1,0:T(8,128)(2,1)S(1)}, u32[]{:S(2)}, u32[]{:S(2)}) collective-permute-start(bf16[1,8,2048]{2,1,0:T(8,128)(2,1)} %bitcast.112), channel_id=1, source_target_pairs={{0,4},{1,5},{2,6},{3,7},{4,0},{5,1},{6,2},{7,3},{8,12},{9,13},{10,... | collective-permute-start | bytes 98312 | tf_op jit(solution)/shard_map/ppermute | solution.py:71
  6.3 5.9 %collective-permute-start.2 = (bf16[1,8,2048]{2,1,0:T(8,128)(2,1)}, bf16[1,8,2048]{2,1,0:T(8,128)(2,1)S(1)}, u32[]{:S(2)}, u32[]{:S(2)}) collective-permute-start(bf16[1,8,2048]{2,1,0:T(8,128)(2,1)} %bitcast.113), channel_id=1, source_target_pairs={{0,12},{1,13},{2,14},{3,15},{4,8},{5,9},{6,10},{7,11},{8,4},{9,5},... | collective-permute-start | bytes 98312 | tf_op jit(solution)/shard_map/ppermute | solution.py:71
  7.1 7.5 %collective-permute-start = (bf16[1,8,4096]{2,1,0:T(8,128)(2,1)S(1)}, bf16[1,8,4096]{2,1,0:T(8,128)(2,1)S(1)}, u32[]{:S(2)}, u32[]{:S(2)}) collective-permute-start(bf16[1,8,4096]{2,1,0:T(8,128)(2,1)S(1)} %maximum_bitcast_fusion.2), channel_id=1, source_target_pairs={{0,8},{1,9},{2,10},{3,11},{4,12},{5,13},{6,14},{7,15},{8,0},{9,1},... | collective-permute-start | bytes 196616 | tf_op jit(solution)/shard_map/ppermute | solution.py:23
  13.0 5.0 %collective-permute-start.5 = (bf16[4,8,2048]{2,1,0:T(8,128)(2,1)S(1)}, bf16[4,8,2048]{2,1,0:T(8,128)(2,1)S(1)}, u32[]{:S(2)}, u32[]{:S(2)}) collective-permute-start(bf16[4,8,2048]{2,1,0:T(8,128)(2,1)S(1)} %maximum_bitcast_fusion.1), channel_id=1, source_target_pairs={{0,2},{1,3},{2,0},{3,1},{4,6},{5,7},{6,4},{7,5},{8,10},{9,11},{10,... | collective-permute-start | bytes 393224 | tf_op jit(solution)/shard_map/ppermute | solution.py:71
  15.5 5.0 %collective-permute-start.1 = (bf16[2,8,4096]{2,1,0:T(8,128)(2,1)S(1)}, bf16[2,8,4096]{2,1,0:T(8,128)(2,1)S(1)}, u32[]{:S(2)}, u32[]{:S(2)}) collective-permute-start(bf16[2,8,4096]{2,1,0:T(8,128)(2,1)S(1)} %maximum_bitcast_fusion), channel_id=1, source_target_pairs={{0,4},{1,5},{2,6},{3,7},{4,0},{5,1},{6,2},{7,3},{8,12},{9,13},{10,... | collective-permute-start | bytes 393224 | tf_op jit(solution)/shard_map/ppermute | solution.py:23
  18.1 2.4 %collective-permute-start.6 = (bf16[8,8,2048]{2,1,0:T(8,128)(2,1)S(1)}, bf16[8,8,2048]{2,1,0:T(8,128)(2,1)S(1)}, u32[]{:S(2)}, u32[]{:S(2)}) collective-permute-start(bf16[8,8,2048]{2,1,0:T(8,128)(2,1)S(1)} %bitcast.98), channel_id=1, source_target_pairs={{0,1},{1,0},{2,3},{3,2},{4,5},{5,4},{6,7},{7,6},{8,9},{9,8},{10,11... | collective-permute-start | bytes 786440 | tf_op jit(solution)/shard_map/ppermute | solution.py:71
  21.5 7.5 %collective-permute-start.7 = (bf16[4,8,4096]{2,1,0:T(8,128)(2,1)S(1)}, bf16[4,8,4096]{2,1,0:T(8,128)(2,1)S(1)}, u32[]{:S(2)}, u32[]{:S(2)}) collective-permute-start(bf16[4,8,4096]{2,1,0:T(8,128)(2,1)S(1)} %bitcast.99), channel_id=1, source_target_pairs={{0,2},{1,3},{2,0},{3,1},{4,6},{5,7},{6,4},{7,5},{8,10},{9,11},{10,... | collective-permute-start | bytes 786440 | tf_op jit(solution)/shard_map/ppermute | solution.py:23
  29.2 5.1 %collective-permute-start.8 = (bf16[8,8,4096]{2,1,0:T(8,128)(2,1)S(1)}, bf16[8,8,4096]{2,1,0:T(8,128)(2,1)S(1)}, u32[]{:S(2)}, u32[]{:S(2)}) collective-permute-start(bf16[8,8,4096]{2,1,0:T(8,128)(2,1)S(1)} %bitcast.95), channel_id=1, source_target_pairs={{0,1},{1,0},{2,3},{3,2},{4,5},{5,4},{6,7},{7,6},{8,9},{9,8},{10,11... | collective-permute-start | bytes 1572872 | tf_op jit(solution)/shard_map/ppermute | solution.py:23
  29.3 5.0 %copy-start = (f32[128,1024]{1,0:T(8,128)S(1)}, f32[128,1024]{1,0:T(8,128)}, u32[]{:S(2)}) copy-start(f32[128,1024]{1,0:T(8,128)} %get-tuple-element.39) | copy-start | bytes 1572868
  29.3 5.0 %copy-start.1 = (f32[128,16]{1,0:T(8,128)S(1)}, f32[128,16]{1,0:T(8,128)}, u32[]{:S(2)}) copy-start(f32[128,16]{1,0:T(8,128)} %get-tuple-element.47) | copy-start | bytes 24580
  29.3 5.0 %copy-start.2 = (f32[128,16]{1,0:T(8,128)S(1)}, f32[128,16]{1,0:T(8,128)}, u32[]{:S(2)}) copy-start(f32[128,16]{1,0:T(8,128)} %get-tuple-element.49) | copy-start | bytes 24580
  36.1 5.1 %collective-permute-start.9 = (bf16[8,8,2208]{2,1,0:T(8,128)(2,1)S(1)}, bf16[8,8,2208]{2,1,0:T(8,128)(2,1)S(1)}, u32[]{:S(2)}, u32[]{:S(2)}) collective-permute-start(bf16[8,8,2208]{2,1,0:T(8,128)(2,1)S(1)} %concatenate.41), channel_id=1, source_target_pairs={{0,1},{1,0},{2,3},{3,2},{4,5},{5,4},{6,7},{7,6},{8,9},{9,8},{10,11... | collective-permute-start | bytes 847880 | tf_op jit(solution)/shard_map/ppermute | solution.py:23
  42.8 5.8 %collective-permute-start.10 = (bf16[4,8,2208]{2,1,0:T(8,128)(2,1)S(1)}, bf16[4,8,2208]{2,1,0:T(8,128)(2,1)S(1)}, u32[]{:S(2)}, u32[]{:S(2)}) collective-permute-start(bf16[4,8,2208]{2,1,0:T(8,128)(2,1)S(1)} %concatenate.44), channel_id=1, source_target_pairs={{0,2},{1,3},{2,0},{3,1},{4,6},{5,7},{6,4},{7,5},{8,10},{9,11},{10,... | collective-permute-start | bytes 423944 | tf_op jit(solution)/shard_map/ppermute | solution.py:23
  49.8 4.4 %collective-permute-start.11 = (bf16[2,8,2208]{2,1,0:T(8,128)(2,1)S(1)}, bf16[2,8,2208]{2,1,0:T(8,128)(2,1)S(1)}, u32[]{:S(2)}, u32[]{:S(2)}) collective-permute-start(bf16[2,8,2208]{2,1,0:T(8,128)(2,1)S(1)} %concatenate.47), channel_id=1, source_target_pairs={{0,4},{1,5},{2,6},{3,7},{4,0},{5,1},{6,2},{7,3},{8,12},{9,13},{10,... | collective-permute-start | bytes 211976 | tf_op jit(solution)/shard_map/ppermute | solution.py:23
  55.3 4.9 %collective-permute-start.12 = (bf16[1,8,2208]{2,1,0:T(8,128)(2,1)S(1)}, bf16[1,8,2208]{2,1,0:T(8,128)(2,1)S(1)}, u32[]{:S(2)}, u32[]{:S(2)}) collective-permute-start(bf16[1,8,2208]{2,1,0:T(8,128)(2,1)S(1)} %concatenate.50), channel_id=1, source_target_pairs={{0,8},{1,9},{2,10},{3,11},{4,12},{5,13},{6,14},{7,15},{8,0},{9,1},... | collective-permute-start | bytes 105992 | tf_op jit(solution)/shard_map/ppermute | solution.py:23

commit v20 on v19

--- a/solution.py
+++ b/solution.py
@@ -318,13 +318,13 @@
     all_queries = gather_levels(audio_q)
     audio_calls = [
         (
-            lambda q, g=g: (audio_partial(q, video_k, video_v, g, 2),),
+            lambda q: (audio_partial(q, video_k, video_v, 0, 1),),
             all_queries,
         )
-        for g in range(2)
+        for ignored in range(1)
     ]
     gathered, results = gather_rows(
-        jnp.concatenate([audio_k, audio_v], axis=1), [None] * (steps - 2) + audio_calls
+        jnp.concatenate([audio_k, audio_v], axis=1), [None] * (steps - 2) + audio_calls + [None]
     )
     parts = [part for result in results for part in result]
     all_keys = gathered[:, :width]

time: 62.2 us -> 60.6 us (0.974)
  Pallas kernels: 23.9 us -> 21.9 us
  starting transfers between devices: 12.7 us -> 14.1 us
  waiting for transfers between devices: 12.4 us -> 11.4 us
    pallas_call x2 -> x1, Pallas kernels: 9.81 us -> 7.75 us  [audio_partial(): pl.pallas_call(audio_kernel, grid=(heads // 2 // AUDIO_STEP,), in_specs=[...]
    ppermute x8, starting transfers between devices: 5.32 us -> 6.78 us  [exchange(): return lax.ppermute(value, 'seq', pairs)]
    ppermute x8, waiting for transfers between devices: 6.69 us -> 5.63 us  [exchange(): return lax.ppermute(value, 'seq', pairs)]
  transfers between devices with their start and end apart: 13 -> 13, of which waited for: 7 -> 7; matrix products, arithmetic and copies ran while one was open for 6% -> 5% of each run, Pallas kernels for 39% -> 31%
where the time goes in v20:
time: 60.6 us; the launch traced here: 60.1 us
  Pallas kernels  21.9 us (36%)
  starting transfers between devices  14.1 us (23%)
  waiting for transfers between devices  11.4 us (19%)
  local copies, waits for them, and re-layouts  4.34 us (7%)
  other arithmetic  4.03 us (7%)
  matrix products  3.47 us (6%)
  between operations  0.93 us (2%)
    pallas_call x4, Pallas kernels, video_part(): pl.pallas_call(video_kernel, grid=(pairs // PER_STEP,), in_specs=specs, o...  14.1 us
    pallas_call x1, Pallas kernels, audio_partial(): pl.pallas_call(audio_kernel, grid=(heads // 2 // AUDIO_STEP,), in_specs=[...  7.75 us
    ppermute x5, starting transfers between devices, gather_levels(): pieces[offset] = lax.ppermute(held, 'seq', pairs)  7.34 us
    ppermute x8, starting transfers between devices, exchange(): return lax.ppermute(value, 'seq', pairs)  6.78 us
    ppermute x5, waiting for transfers between devices, gather_levels(): pieces[offset] = lax.ppermute(held, 'seq', pairs)  5.74 us
    ppermute x8, waiting for transfers between devices, exchange(): return lax.ppermute(value, 'seq', pairs)  5.63 us
    dot_general x9, matrix products, spread(): jnp.dot(scales, expand, precision=lax.Precision.HIGHEST, preferred_elemen...  3.47 us
    concatenate x1, local copies, waits for them, and re-layouts, local(): jnp.concatenate([part[0] for part in parts] + [part[1] for part in parts]...  1.34 us
  transfers between devices with their start and end apart: 13, of which 7 were waited for; matrix products, arithmetic and copies ran while one was open for 5% of the time, Pallas kernels for 31%

profile of v20, /device:TPU:0, one launch (start us, length us, event | category | flops | bytes accessed | tf_op | source)
XLA Modules:
  0.0 60.1 jit_solution(1721928849101855467)
XLA Ops:
  0.6 4.1 %collective-permute-start.4 = (bf16[1,8,2048]{2,1,0:T(8,128)(2,1)}, bf16[1,8,2048]{2,1,0:T(8,128)(2,1)S(1)}, u32[]{:S(2)}, u32[]{:S(2)}) collective-permute-start(bf16[1,8,2048]{2,1,0:T(8,128)(2,1)} %bitcast.111), channel_id=1, source_target_pairs={{0,8},{1,9},{2,10},{3,11},{4,12},{5,13},{6,14},{7,15},{8,0},{9,1},... | collective-permute-start | bytes 98312 | tf_op jit(solution)/shard_map/ppermute | solution.py:71
  4.7 1.6 %collective-permute-start.3 = (bf16[1,8,2048]{2,1,0:T(8,128)(2,1)}, bf16[1,8,2048]{2,1,0:T(8,128)(2,1)S(1)}, u32[]{:S(2)}, u32[]{:S(2)}) collective-permute-start(bf16[1,8,2048]{2,1,0:T(8,128)(2,1)} %bitcast.112), channel_id=1, source_target_pairs={{0,4},{1,5},{2,6},{3,7},{4,0},{5,1},{6,2},{7,3},{8,12},{9,13},{10,... | collective-permute-start | bytes 98312 | tf_op jit(solution)/shard_map/ppermute | solution.py:71
  6.3 0.8 %maximum_bitcast_fusion.2 = bf16[1,8,4096]{2,1,0:T(8,128)(2,1)S(1)} fusion(bf16[8,2048]{1,0:T(8,128)(2,1)} %param.11, bf16[8,2048]{1,0:T(8,128)(2,1)} %param.10), kind=kLoop, calls=%fused_computation.74 | loop fusion | flops 131072 | bytes 131072 | tf_op jit(solution)/shard_map/broadcast_in_dim | solution.py:29
  7.1 1.9 %collective-permute-start = (bf16[1,8,4096]{2,1,0:T(8,128)(2,1)S(1)}, bf16[1,8,4096]{2,1,0:T(8,128)(2,1)S(1)}, u32[]{:S(2)}, u32[]{:S(2)}) collective-permute-start(bf16[1,8,4096]{2,1,0:T(8,128)(2,1)S(1)} %maximum_bitcast_fusion.2), channel_id=1, source_target_pairs={{0,8},{1,9},{2,10},{3,11},{4,12},{5,13},{6,14},{7,15},{8,0},{9,1},... | collective-permute-start | bytes 196616 | tf_op jit(solution)/shard_map/ppermute | solution.py:23
  9.0 3.2 %collective-permute-done.2 = bf16[1,8,2048]{2,1,0:T(8,128)(2,1)S(1)} collective-permute-done((bf16[1,8,2048]{2,1,0:T(8,128)(2,1)}, bf16[1,8,2048]{2,1,0:T(8,128)(2,1)S(1)}, u32[]{:S(2)}, u32[]{:S(2)}) %collective-permute-start.2) | collective-permute-done | bytes 32800 | tf_op jit(solution)/shard_map/ppermute | solution.py:71
  12.2 0.8 %select_bitcast_fusion.23 = (bf16[1,1,8,2048]{3,2,1,0:T(8,128)(2,1)S(1)}, bf16[1,1,8,2048]{3,2,1,0:T(8,128)(2,1)S(1)}, bf16[1,1,8,2048]{3,2,1,0:T(8,128)(2,1)S(1)}, bf16[1,1,8,2048]{3,2,1,0:T(8,128)(2,1)S(1)}) fusion(bf16[1,8,2048]{2,1,0:T(8,128)(2,1)S(1)} %collective-permute-done.2, bf16[1,8,2048]{2,1,0:T(8,128)(2,1)S(1)} %collective-permute-done.3, ...), kind=kLoop, calls=%fused_computation.98 | loop fusion | flops 196608 | bytes 262156 | tf_op jit(solution)/shard_map/stack | solution.py:79
  13.0 1.6 %collective-permute-start.5 = (bf16[4,8,2048]{2,1,0:T(8,128)(2,1)S(1)}, bf16[4,8,2048]{2,1,0:T(8,128)(2,1)S(1)}, u32[]{:S(2)}, u32[]{:S(2)}) collective-permute-start(bf16[4,8,2048]{2,1,0:T(8,128)(2,1)S(1)} %maximum_bitcast_fusion.1), channel_id=1, source_target_pairs={{0,2},{1,3},{2,0},{3,1},{4,6},{5,7},{6,4},{7,5},{8,10},{9,11},{10,... | collective-permute-start | bytes 393224 | tf_op jit(solution)/shard_map/ppermute | solution.py:71
  14.6 0.8 %select_bitcast_fusion.19 = (bf16[1,1,8,4096]{3,2,1,0:T(8,128)(2,1)S(1)}, bf16[1,1,8,4096]{3,2,1,0:T(8,128)(2,1)S(1)}) fusion(bf16[1,8,4096]{2,1,0:T(8,128)(2,1)S(1)} %collective-permute-done, pred[]{:T(512)S(6)} %ne.98, bf16[8,2048]{1,0:T(8,128)(2,1)} %param.11, bf16[8,2048]{1,0:T(8,128)(2,1)} %param.10), kind=kLoop, calls=%fused_computation.76 | loop fusion | flops 196608 | bytes 262145 | tf_op jit(solution)/shard_map/stack | solution.py:45
  15.5 0.1 collective-permute-start.1
  15.6 2.5 %collective-permute-done.5 = bf16[4,8,2048]{2,1,0:T(8,128)(2,1)S(1)} collective-permute-done((bf16[4,8,2048]{2,1,0:T(8,128)(2,1)S(1)}, bf16[4,8,2048]{2,1,0:T(8,128)(2,1)S(1)}, u32[]{:S(2)}, u32[]{:S(2)}) %collective-permute-start.5) | collective-permute-done | bytes 131104 | tf_op jit(solution)/shard_map/ppermute | solution.py:71
  18.2 2.3 %collective-permute-done.1 = bf16[2,8,4096]{2,1,0:T(8,128)(2,1)S(1)} collective-permute-done((bf16[2,8,4096]{2,1,0:T(8,128)(2,1)S(1)}, bf16[2,8,4096]{2,1,0:T(8,128)(2,1)S(1)}, u32[]{:S(2)}, u32[]{:S(2)}) %collective-permute-start.1) | collective-permute-done | bytes 131104 | tf_op jit(solution)/shard_map/ppermute | solution.py:23
  20.7 0.8 %copy.20 = bf16[8,2,8,2048]{3,2,1,0:T(8,128)(2,1)} copy(bf16[8,2,8,2048]{3,2,0,1:T(8,128)(2,1)S(1)} %pad_maximum_fusion.1) | data formatting | bytes 1048576 | tf_op jit(solution)/shard_map/stack | solution.py:79
  21.5 0.7 %collective-permute-start.7 = (bf16[4,8,4096]{2,1,0:T(8,128)(2,1)S(1)}, bf16[4,8,4096]{2,1,0:T(8,128)(2,1)S(1)}, u32[]{:S(2)}, u32[]{:S(2)}) collective-permute-start(bf16[4,8,4096]{2,1,0:T(8,128)(2,1)S(1)} %bitcast.99), channel_id=1, source_target_pairs={{0,2},{1,3},{2,0},{3,1},{4,6},{5,7},{6,4},{7,5},{8,10},{9,11},{10,... | collective-permute-start | bytes 786440 | tf_op jit(solution)/shard_map/ppermute | solution.py:23
  22.2 7.8 %shard_map.77 = (f32[128,2048]{1,0:T(8,128)}, f32[128,32]{1,0:T(8,128)}, f32[128,32]{1,0:T(8,128)}) custom-call(bf16[128,2048]{1,0:T(8,128)(2,1)} %bitcast.96, bf16[512,2048]{1,0:T(8,128)(2,1)} %key_ref.1, bf16[512,2048]{1,0:T(8,128)(2,1)} %value_ref.1), custom_call_target="tpu_custom_call" | custom-call | flops 1073741824 | bytes 5767168 | tf_op jit(solution)/shard_map/pallas_call | solution.py:286
  30.0 1.3 %concatenate.40 = f32[128,2112]{1,0:T(8,128)S(1)} concatenate(f32[128,2048]{1,0:T(8,128)} %get-tuple-element.30, f32[128,32]{1,0:T(8,128)} %get-tuple-element.31, f32[128,32]{1,0:T(8,128)} %get-tuple-element.32), dimensions={1} | concatenate | bytes 2162688 | tf_op jit(solution)/shard_map/concatenate | solution.py:332
  31.4 0.1 fusion.35
  31.5 0.1 concatenate.41
  31.9 0.6 collective-permute-start.9
  32.4 0.9 %collective-permute-done.8 = bf16[8,8,2208]{2,1,0:T(8,128)(2,1)S(1)} collective-permute-done((bf16[8,8,2208]{2,1,0:T(8,128)(2,1)S(1)}, bf16[8,8,2208]{2,1,0:T(8,128)(2,1)S(1)}, u32[]{:S(2)}, u32[]{:S(2)}) %collective-permute-start.8) | collective-permute-done | bytes 282656 | tf_op jit(solution)/shard_map/ppermute | solution.py:23
  33.4 0.1 concatenate.42
  33.5 0.5 collective-permute-done.9
  34.0 0.1 select_bitcast_fusion.3
  34.1 0.1 pad_maximum_fusion
  34.3 0.1 copy.22
  34.4 1.0 %fusion.62 = (bf16[128,2048]{1,0:T(8,128)(2,1)}, bf16[128,2048]{1,0:T(8,128)(2,1)}) fusion(bf16[128,4096]{1,0:T(8,128)(2,1)S(1)} %bitcast.93), kind=kLoop, calls=%fused_computation.162 | loop fusion | bytes 2097152 | tf_op jit(solution)/shard_map/slice | solution.py:331
  35.4 3.5 %shard_map.78.refs_0_ = bf16[512,2048]{1,0:T(8,128)(2,1)} custom-call(bf16[512,2048]{1,0:T(8,128)(2,1)} %query_ref.7, bf16[128,2048]{1,0:T(8,128)(2,1)} %get-tuple-element.57.key_ref, bf16[128,2048]{1,0:T(8,128)(2,1)} %get-tuple-element.56.value_ref), custom_call_target="tpu_custom_call" | custom-call | flops 268435456 | bytes 1310720 | tf_op jit(solution)/shard_map/pallas_call | solution.py:237
  38.9 0.1 fusion.36
  39.0 0.4 convolution_multiply_fusion.1
  39.5 0.4 fusion
  39.9 0.1 concatenate.43
  40.1 0.1 concatenate.44
  40.2 1.4 %collective-permute-start.10 = (bf16[4,8,2208]{2,1,0:T(8,128)(2,1)S(1)}, bf16[4,8,2208]{2,1,0:T(8,128)(2,1)S(1)}, u32[]{:S(2)}, u32[]{:S(2)}) collective-permute-start(bf16[4,8,2208]{2,1,0:T(8,128)(2,1)S(1)} %concatenate.44), channel_id=1, source_target_pairs={{0,2},{1,3},{2,0},{3,1},{4,6},{5,7},{6,4},{7,5},{8,10},{9,11},{10,... | collective-permute-start | bytes 423944 | tf_op jit(solution)/shard_map/ppermute | solution.py:23
  41.6 3.5 %shard_map.79.refs_0_ = bf16[512,2048]{1,0:T(8,128)(2,1)} custom-call(bf16[512,2048]{1,0:T(8,128)(2,1)} %query_ref.7, bf16[128,2048]{1,0:T(8,128)(2,1)} %get-tuple-element.57.key_ref, bf16[128,2048]{1,0:T(8,128)(2,1)} %get-tuple-element.56.value_ref, bf16[512,2048]{1,0:T(8,128)(2,1)} %shard_map.78.refs_0_), custom_call_target="tpu_custom_call", output_to_operand_aliasing={{}: (3, {})} | custom-call | flops 268435456 | bytes 1310720 | tf_op jit(solution)/shard_map/pallas_call | solution.py:237
  45.1 1.2 %collective-permute-done.10 = bf16[4,8,2208]{2,1,0:T(8,128)(2,1)S(1)} collective-permute-done((bf16[4,8,2208]{2,1,0:T(8,128)(2,1)S(1)}, bf16[4,8,2208]{2,1,0:T(8,128)(2,1)S(1)}, u32[]{:S(2)}, u32[]{:S(2)}) %collective-permute-start.10) | collective-permute-done | bytes 141344 | tf_op jit(solution)/shard_map/ppermute | solution.py:23
  46.5 0.1 fusion.41
  46.6 0.3 convolution_multiply_fusion.2
  46.9 0.3 fusion.1
  47.5 0.1 concatenate.47
  47.6 3.5 %shard_map.80.refs_0_ = bf16[512,2048]{1,0:T(8,128)(2,1)} custom-call(bf16[512,2048]{1,0:T(8,128)(2,1)} %query_ref.7, bf16[128,2048]{1,0:T(8,128)(2,1)} %get-tuple-element.57.key_ref, bf16[128,2048]{1,0:T(8,128)(2,1)} %get-tuple-element.56.value_ref, bf16[512,2048]{1,0:T(8,128)(2,1)} %shard_map.79.refs_0_), custom_call_target="tpu_custom_call", output_to_operand_aliasing={{}: (3, {})} | custom-call | flops 268435456 | bytes 1310720 | tf_op jit(solution)/shard_map/pallas_call | solution.py:237
  51.2 0.8 %collective-permute-done.11 = bf16[2,8,2208]{2,1,0:T(8,128)(2,1)S(1)} collective-permute-done((bf16[2,8,2208]{2,1,0:T(8,128)(2,1)S(1)}, bf16[2,8,2208]{2,1,0:T(8,128)(2,1)S(1)}, u32[]{:S(2)}, u32[]{:S(2)}) %collective-permute-start.11) | collective-permute-done | bytes 70688 | tf_op jit(solution)/shard_map/ppermute | solution.py:23
  52.2 0.3 convolution_multiply_fusion.5
  52.5 0.3 fusion.2
  52.9 0.1 concatenate.50
  53.0 2.0 %collective-permute-start.12 = (bf16[1,8,2208]{2,1,0:T(8,128)(2,1)S(1)}, bf16[1,8,2208]{2,1,0:T(8,128)(2,1)S(1)}, u32[]{:S(2)}, u32[]{:S(2)}) collective-permute-start(bf16[1,8,2208]{2,1,0:T(8,128)(2,1)S(1)} %concatenate.50), channel_id=1, source_target_pairs={{0,8},{1,9},{2,10},{3,11},{4,12},{5,13},{6,14},{7,15},{8,0},{9,1},... | collective-permute-start | bytes 105992 | tf_op jit(solution)/shard_map/ppermute | solution.py:23
  55.0 3.5 %shard_map.81 = bf16[512,2048]{1,0:T(8,128)(2,1)} custom-call(bf16[512,2048]{1,0:T(8,128)(2,1)} %query_ref.7, bf16[128,2048]{1,0:T(8,128)(2,1)} %get-tuple-element.57.key_ref, bf16[128,2048]{1,0:T(8,128)(2,1)} %get-tuple-element.56.value_ref, bf16[512,2048]{1,0:T(8,128)(2,1)} %shard_map.80.refs_0_), custom_call_target="tpu_custom_call", output_to_operand_aliasing={{}: (3, {})} | custom-call | flops 268435456 | bytes 1310720 | tf_op jit(solution)/shard_map/pallas_call | solution.py:237
  58.7 0.2 convolution_multiply_fusion.7
  59.0 0.3 fusion.3
  59.2 0.9 %fusion.4 = bf16[8,2048]{1,0:T(8,128)(2,1)} fusion(f32[8,2048]{1,0:T(8,128)S(1)} %fusion.3, s32[2048]{0:T(1024)S(1)} %get-tuple-element.108, s32[2048]{0:T(1024)S(1)} %get-tuple-element.109, pred[2048]{0:T(1024)(128)(4,1)S(1)} %fusion.49, f32[8,2112]{1,0:T(8,128)S(1)} %bitcast.110, f32[8,2112]{1,0:T(8,128)S(1)} %get-tuple-element.86), kind=kOutput, calls=%fused_computation.13 | convolution fusion | flops 6456832 | bytes 133120 | tf_op jit(solution)/shard_map/dot_general | solution.py:16
  (48 shorter events, 1.9 us)
Async XLA Ops:
  0.6 8.4 %collective-permute-start.4 = (bf16[1,8,2048]{2,1,0:T(8,128)(2,1)}, bf16[1,8,2048]{2,1,0:T(8,128)(2,1)S(1)}, u32[]{:S(2)}, u32[]{:S(2)}) collective-permute-start(bf16[1,8,2048]{2,1,0:T(8,128)(2,1)} %bitcast.111), channel_id=1, source_target_pairs={{0,8},{1,9},{2,10},{3,11},{4,12},{5,13},{6,14},{7,15},{8,0},{9,1},... | collective-permute-start | bytes 98312 | tf_op jit(solution)/shard_map/ppermute | solution.py:71
  4.7 4.3 %collective-permute-start.3 = (bf16[1,8,2048]{2,1,0:T(8,128)(2,1)}, bf16[1,8,2048]{2,1,0:T(8,128)(2,1)S(1)}, u32[]{:S(2)}, u32[]{:S(2)}) collective-permute-start(bf16[1,8,2048]{2,1,0:T(8,128)(2,1)} %bitcast.112), channel_id=1, source_target_pairs={{0,4},{1,5},{2,6},{3,7},{4,0},{5,1},{6,2},{7,3},{8,12},{9,13},{10,... | collective-permute-start | bytes 98312 | tf_op jit(solution)/shard_map/ppermute | solution.py:71
  6.3 5.9 %collective-permute-start.2 = (bf16[1,8,2048]{2,1,0:T(8,128)(2,1)}, bf16[1,8,2048]{2,1,0:T(8,128)(2,1)S(1)}, u32[]{:S(2)}, u32[]{:S(2)}) collective-permute-start(bf16[1,8,2048]{2,1,0:T(8,128)(2,1)} %bitcast.113), channel_id=1, source_target_pairs={{0,12},{1,13},{2,14},{3,15},{4,8},{5,9},{6,10},{7,11},{8,4},{9,5},... | collective-permute-start | bytes 98312 | tf_op jit(solution)/shard_map/ppermute | solution.py:71
  7.1 7.5 %collective-permute-start = (bf16[1,8,4096]{2,1,0:T(8,128)(2,1)S(1)}, bf16[1,8,4096]{2,1,0:T(8,128)(2,1)S(1)}, u32[]{:S(2)}, u32[]{:S(2)}) collective-permute-start(bf16[1,8,4096]{2,1,0:T(8,128)(2,1)S(1)} %maximum_bitcast_fusion.2), channel_id=1, source_target_pairs={{0,8},{1,9},{2,10},{3,11},{4,12},{5,13},{6,14},{7,15},{8,0},{9,1},... | collective-permute-start | bytes 196616 | tf_op jit(solution)/shard_map/ppermute | solution.py:23
  13.0 5.0 %collective-permute-start.5 = (bf16[4,8,2048]{2,1,0:T(8,128)(2,1)S(1)}, bf16[4,8,2048]{2,1,0:T(8,128)(2,1)S(1)}, u32[]{:S(2)}, u32[]{:S(2)}) collective-permute-start(bf16[4,8,2048]{2,1,0:T(8,128)(2,1)S(1)} %maximum_bitcast_fusion.1), channel_id=1, source_target_pairs={{0,2},{1,3},{2,0},{3,1},{4,6},{5,7},{6,4},{7,5},{8,10},{9,11},{10,... | collective-permute-start | bytes 393224 | tf_op jit(solution)/shard_map/ppermute | solution.py:71
  15.5 5.0 %collective-permute-start.1 = (bf16[2,8,4096]{2,1,0:T(8,128)(2,1)S(1)}, bf16[2,8,4096]{2,1,0:T(8,128)(2,1)S(1)}, u32[]{:S(2)}, u32[]{:S(2)}) collective-permute-start(bf16[2,8,4096]{2,1,0:T(8,128)(2,1)S(1)} %maximum_bitcast_fusion), channel_id=1, source_target_pairs={{0,4},{1,5},{2,6},{3,7},{4,0},{5,1},{6,2},{7,3},{8,12},{9,13},{10,... | collective-permute-start | bytes 393224 | tf_op jit(solution)/shard_map/ppermute | solution.py:23
  18.1 2.4 %collective-permute-start.6 = (bf16[8,8,2048]{2,1,0:T(8,128)(2,1)S(1)}, bf16[8,8,2048]{2,1,0:T(8,128)(2,1)S(1)}, u32[]{:S(2)}, u32[]{:S(2)}) collective-permute-start(bf16[8,8,2048]{2,1,0:T(8,128)(2,1)S(1)} %bitcast.98), channel_id=1, source_target_pairs={{0,1},{1,0},{2,3},{3,2},{4,5},{5,4},{6,7},{7,6},{8,9},{9,8},{10,11... | collective-permute-start | bytes 786440 | tf_op jit(solution)/shard_map/ppermute | solution.py:71
  21.5 8.5 %collective-permute-start.7 = (bf16[4,8,4096]{2,1,0:T(8,128)(2,1)S(1)}, bf16[4,8,4096]{2,1,0:T(8,128)(2,1)S(1)}, u32[]{:S(2)}, u32[]{:S(2)}) collective-permute-start(bf16[4,8,4096]{2,1,0:T(8,128)(2,1)S(1)} %bitcast.99), channel_id=1, source_target_pairs={{0,2},{1,3},{2,0},{3,1},{4,6},{5,7},{6,4},{7,5},{8,10},{9,11},{10,... | collective-permute-start | bytes 786440 | tf_op jit(solution)/shard_map/ppermute | solution.py:23
  31.6 1.6 %collective-permute-start.8 = (bf16[8,8,2208]{2,1,0:T(8,128)(2,1)S(1)}, bf16[8,8,2208]{2,1,0:T(8,128)(2,1)S(1)}, u32[]{:S(2)}, u32[]{:S(2)}) collective-permute-start(bf16[8,8,2208]{2,1,0:T(8,128)(2,1)S(1)} %concatenate.41), channel_id=1, source_target_pairs={{0,1},{1,0},{2,3},{3,2},{4,5},{5,4},{6,7},{7,6},{8,9},{9,8},{10,11... | collective-permute-start | bytes 847880 | tf_op jit(solution)/shard_map/ppermute | solution.py:23
  31.9 2.2 %collective-permute-start.9 = (bf16[8,8,4096]{2,1,0:T(8,128)(2,1)S(1)}, bf16[8,8,4096]{2,1,0:T(8,128)(2,1)S(1)}, u32[]{:S(2)}, u32[]{:S(2)}) collective-permute-start(bf16[8,8,4096]{2,1,0:T(8,128)(2,1)S(1)} %bitcast.95), channel_id=1, source_target_pairs={{0,1},{1,0},{2,3},{3,2},{4,5},{5,4},{6,7},{7,6},{8,9},{9,8},{10,11... | collective-permute-start | bytes 1572872 | tf_op jit(solution)/shard_map/ppermute | solution.py:23
  40.2 6.1 %collective-permute-start.10 = (bf16[4,8,2208]{2,1,0:T(8,128)(2,1)S(1)}, bf16[4,8,2208]{2,1,0:T(8,128)(2,1)S(1)}, u32[]{:S(2)}, u32[]{:S(2)}) collective-permute-start(bf16[4,8,2208]{2,1,0:T(8,128)(2,1)S(1)} %concatenate.44), channel_id=1, source_target_pairs={{0,2},{1,3},{2,0},{3,1},{4,6},{5,7},{6,4},{7,5},{8,10},{9,11},{10,... | collective-permute-start | bytes 423944 | tf_op jit(solution)/shard_map/ppermute | solution.py:23
  47.6 4.4 %collective-permute-start.11 = (bf16[2,8,2208]{2,1,0:T(8,128)(2,1)S(1)}, bf16[2,8,2208]{2,1,0:T(8,128)(2,1)S(1)}, u32[]{:S(2)}, u32[]{:S(2)}) collective-permute-start(bf16[2,8,2208]{2,1,0:T(8,128)(2,1)S(1)} %concatenate.47), channel_id=1, source_target_pairs={{0,4},{1,5},{2,6},{3,7},{4,0},{5,1},{6,2},{7,3},{8,12},{9,13},{10,... | collective-permute-start | bytes 211976 | tf_op jit(solution)/shard_map/ppermute | solution.py:23
  53.0 5.5 %collective-permute-start.12 = (bf16[1,8,2208]{2,1,0:T(8,128)(2,1)S(1)}, bf16[1,8,2208]{2,1,0:T(8,128)(2,1)S(1)}, u32[]{:S(2)}, u32[]{:S(2)}) collective-permute-start(bf16[1,8,2208]{2,1,0:T(8,128)(2,1)S(1)} %concatenate.50), channel_id=1, source_target_pairs={{0,8},{1,9},{2,10},{3,11},{4,12},{5,13},{6,14},{7,15},{8,0},{9,1},... | collective-permute-start | bytes 105992 | tf_op jit(solution)/shard_map/ppermute | solution.py:23

commit v21 on v20

--- a/solution.py
+++ b/solution.py
@@ -334,9 +334,10 @@
         axis=1,
     )
     video_calls = [
-        lambda earlier, g=g: video_part(video_q, all_keys, all_values, earlier, g, groups)
-        for g in range(groups)
+        lambda earlier, g=g: video_part(video_q, all_keys, all_values, earlier, g, 2)
+        for g in range(2)
     ]
+    video_calls = [None] * (steps - 3) + [video_calls[0], None, video_calls[1]]
     mine, video_out = scatter_rows(state, heads, video_calls)
     audio_out = (mine[:, :width] / spread(mine[:, width : width + heads])).astype(jnp.bfloat16)
     return video_out, audio_out

time: 60.6 us -> 62.8 us (1.036)
  waiting for transfers between devices: 11.4 us -> 18.2 us
  Pallas kernels: 21.9 us -> 18.8 us
  starting transfers between devices: 14.1 us -> 12.5 us
    ppermute x8, waiting for transfers between devices: 5.63 us -> 12.5 us  [exchange(): return lax.ppermute(value, 'seq', pairs)]
    pallas_call x4 -> x2, Pallas kernels: 14.1 us -> 11.1 us  [video_part(): pl.pallas_call(video_kernel, grid=(pairs // PER_STEP,), in_specs=specs, o...]
    ppermute x8, starting transfers between devices: 6.78 us -> 5.14 us  [exchange(): return lax.ppermute(value, 'seq', pairs)]
  transfers between devices with their start and end apart: 13 -> 13, of which waited for: 7 -> 6; matrix products, arithmetic and copies ran while one was open for 5% -> 5% of each run, Pallas kernels for 31% -> 21%
where the time goes in v21:
time: 62.8 us; the launch traced here: 62.3 us
  Pallas kernels  18.8 us (30%)
  waiting for transfers between devices  18.2 us (29%)
  starting transfers between devices  12.5 us (20%)
  local copies, waits for them, and re-layouts  4.34 us (7%)
  other arithmetic  4.03 us (6%)
  matrix products  3.48 us (6%)
  between operations  0.94 us (1%)
    ppermute x8, waiting for transfers between devices, exchange(): return lax.ppermute(value, 'seq', pairs)  12.5 us
    pallas_call x2, Pallas kernels, video_part(): pl.pallas_call(video_kernel, grid=(pairs // PER_STEP,), in_specs=specs, o...  11.1 us
    pallas_call x1, Pallas kernels, audio_partial(): pl.pallas_call(audio_kernel, grid=(heads // 2 // AUDIO_STEP,), in_specs=[...  7.75 us
    ppermute x5, starting transfers between devices, gather_levels(): pieces[offset] = lax.ppermute(held, 'seq', pairs)  7.34 us
    ppermute x5, waiting for transfers between devices, gather_levels(): pieces[offset] = lax.ppermute(held, 'seq', pairs)  5.74 us
    ppermute x8, starting transfers between devices, exchange(): return lax.ppermute(value, 'seq', pairs)  5.14 us
    dot_general x9, matrix products, spread(): jnp.dot(scales, expand, precision=lax.Precision.HIGHEST, preferred_elemen...  3.48 us
    concatenate x1, local copies, waits for them, and re-layouts, local(): jnp.concatenate([part[0] for part in parts] + [part[1] for part in parts]...  1.34 us
  transfers between devices with their start and end apart: 13, of which 6 were waited for; matrix products, arithmetic and copies ran while one was open for 5% of the time, Pallas kernels for 21%

profile of v21, /device:TPU:0, one launch (start us, length us, event | category | flops | bytes accessed | tf_op | source)
XLA Modules:
  0.0 62.3 jit_solution(13765892399690499283)
XLA Ops:
  0.6 4.1 %collective-permute-start.4 = (bf16[1,8,2048]{2,1,0:T(8,128)(2,1)}, bf16[1,8,2048]{2,1,0:T(8,128)(2,1)S(1)}, u32[]{:S(2)}, u32[]{:S(2)}) collective-permute-start(bf16[1,8,2048]{2,1,0:T(8,128)(2,1)} %bitcast.113), channel_id=1, source_target_pairs={{0,8},{1,9},{2,10},{3,11},{4,12},{5,13},{6,14},{7,15},{8,0},{9,1},... | collective-permute-start | bytes 98312 | tf_op jit(solution)/shard_map/ppermute | solution.py:71
  4.7 1.6 %collective-permute-start.3 = (bf16[1,8,2048]{2,1,0:T(8,128)(2,1)}, bf16[1,8,2048]{2,1,0:T(8,128)(2,1)S(1)}, u32[]{:S(2)}, u32[]{:S(2)}) collective-permute-start(bf16[1,8,2048]{2,1,0:T(8,128)(2,1)} %bitcast.114), channel_id=1, source_target_pairs={{0,4},{1,5},{2,6},{3,7},{4,0},{5,1},{6,2},{7,3},{8,12},{9,13},{10,... | collective-permute-start | bytes 98312 | tf_op jit(solution)/shard_map/ppermute | solution.py:71
  6.3 0.8 %maximum_bitcast_fusion.2 = bf16[1,8,4096]{2,1,0:T(8,128)(2,1)S(1)} fusion(bf16[8,2048]{1,0:T(8,128)(2,1)} %param.11, bf16[8,2048]{1,0:T(8,128)(2,1)} %param.10), kind=kLoop, calls=%fused_computation.76 | loop fusion | flops 131072 | bytes 131072 | tf_op jit(solution)/shard_map/broadcast_in_dim | solution.py:29
  7.1 1.9 %collective-permute-start = (bf16[1,8,4096]{2,1,0:T(8,128)(2,1)S(1)}, bf16[1,8,4096]{2,1,0:T(8,128)(2,1)S(1)}, u32[]{:S(2)}, u32[]{:S(2)}) collective-permute-start(bf16[1,8,4096]{2,1,0:T(8,128)(2,1)S(1)} %maximum_bitcast_fusion.2), channel_id=1, source_target_pairs={{0,8},{1,9},{2,10},{3,11},{4,12},{5,13},{6,14},{7,15},{8,0},{9,1},... | collective-permute-start | bytes 196616 | tf_op jit(solution)/shard_map/ppermute | solution.py:23
  9.0 3.2 %collective-permute-done.2 = bf16[1,8,2048]{2,1,0:T(8,128)(2,1)S(1)} collective-permute-done((bf16[1,8,2048]{2,1,0:T(8,128)(2,1)}, bf16[1,8,2048]{2,1,0:T(8,128)(2,1)S(1)}, u32[]{:S(2)}, u32[]{:S(2)}) %collective-permute-start.2) | collective-permute-done | bytes 32800 | tf_op jit(solution)/shard_map/ppermute | solution.py:71
  12.2 0.8 %select_bitcast_fusion.23 = (bf16[1,1,8,2048]{3,2,1,0:T(8,128)(2,1)S(1)}, bf16[1,1,8,2048]{3,2,1,0:T(8,128)(2,1)S(1)}, bf16[1,1,8,2048]{3,2,1,0:T(8,128)(2,1)S(1)}, bf16[1,1,8,2048]{3,2,1,0:T(8,128)(2,1)S(1)}) fusion(bf16[1,8,2048]{2,1,0:T(8,128)(2,1)S(1)} %collective-permute-done.2, bf16[1,8,2048]{2,1,0:T(8,128)(2,1)S(1)} %collective-permute-done.3, ...), kind=kLoop, calls=%fused_computation.100 | loop fusion | flops 196608 | bytes 262156 | tf_op jit(solution)/shard_map/stack | solution.py:79
  13.0 1.6 %collective-permute-start.5 = (bf16[4,8,2048]{2,1,0:T(8,128)(2,1)S(1)}, bf16[4,8,2048]{2,1,0:T(8,128)(2,1)S(1)}, u32[]{:S(2)}, u32[]{:S(2)}) collective-permute-start(bf16[4,8,2048]{2,1,0:T(8,128)(2,1)S(1)} %maximum_bitcast_fusion.1), channel_id=1, source_target_pairs={{0,2},{1,3},{2,0},{3,1},{4,6},{5,7},{6,4},{7,5},{8,10},{9,11},{10,... | collective-permute-start | bytes 393224 | tf_op jit(solution)/shard_map/ppermute | solution.py:71
  14.6 0.8 %select_bitcast_fusion.19 = (bf16[1,1,8,4096]{3,2,1,0:T(8,128)(2,1)S(1)}, bf16[1,1,8,4096]{3,2,1,0:T(8,128)(2,1)S(1)}) fusion(bf16[1,8,4096]{2,1,0:T(8,128)(2,1)S(1)} %collective-permute-done, pred[]{:T(512)S(6)} %ne.98, bf16[8,2048]{1,0:T(8,128)(2,1)} %param.11, bf16[8,2048]{1,0:T(8,128)(2,1)} %param.10), kind=kLoop, calls=%fused_computation.78 | loop fusion | flops 196608 | bytes 262145 | tf_op jit(solution)/shard_map/stack | solution.py:45
  15.5 0.1 collective-permute-start.1
  15.6 2.5 %collective-permute-done.5 = bf16[4,8,2048]{2,1,0:T(8,128)(2,1)S(1)} collective-permute-done((bf16[4,8,2048]{2,1,0:T(8,128)(2,1)S(1)}, bf16[4,8,2048]{2,1,0:T(8,128)(2,1)S(1)}, u32[]{:S(2)}, u32[]{:S(2)}) %collective-permute-start.5) | collective-permute-done | bytes 131104 | tf_op jit(solution)/shard_map/ppermute | solution.py:71
  18.2 2.3 %collective-permute-done.1 = bf16[2,8,4096]{2,1,0:T(8,128)(2,1)S(1)} collective-permute-done((bf16[2,8,4096]{2,1,0:T(8,128)(2,1)S(1)}, bf16[2,8,4096]{2,1,0:T(8,128)(2,1)S(1)}, u32[]{:S(2)}, u32[]{:S(2)}) %collective-permute-start.1) | collective-permute-done | bytes 131104 | tf_op jit(solution)/shard_map/ppermute | solution.py:23
  20.7 0.8 %copy.18 = bf16[8,2,8,2048]{3,2,1,0:T(8,128)(2,1)} copy(bf16[8,2,8,2048]{3,2,0,1:T(8,128)(2,1)S(1)} %pad_maximum_fusion.1) | data formatting | bytes 1048576 | tf_op jit(solution)/shard_map/stack | solution.py:79
  21.5 0.7 %collective-permute-start.7 = (bf16[4,8,4096]{2,1,0:T(8,128)(2,1)S(1)}, bf16[4,8,4096]{2,1,0:T(8,128)(2,1)S(1)}, u32[]{:S(2)}, u32[]{:S(2)}) collective-permute-start(bf16[4,8,4096]{2,1,0:T(8,128)(2,1)S(1)} %bitcast.102), channel_id=1, source_target_pairs={{0,2},{1,3},{2,0},{3,1},{4,6},{5,7},{6,4},{7,5},{8,10},{9,11},{10,... | collective-permute-start | bytes 786440 | tf_op jit(solution)/shard_map/ppermute | solution.py:23
  22.2 7.8 %shard_map.77 = (f32[128,2048]{1,0:T(8,128)}, f32[128,32]{1,0:T(8,128)}, f32[128,32]{1,0:T(8,128)}) custom-call(bf16[128,2048]{1,0:T(8,128)(2,1)} %bitcast.99, bf16[512,2048]{1,0:T(8,128)(2,1)} %key_ref.1, bf16[512,2048]{1,0:T(8,128)(2,1)} %value_ref.1), custom_call_target="tpu_custom_call" | custom-call | flops 1073741824 | bytes 5767168 | tf_op jit(solution)/shard_map/pallas_call | solution.py:286
  30.0 1.3 %concatenate.40 = f32[128,2112]{1,0:T(8,128)S(1)} concatenate(f32[128,2048]{1,0:T(8,128)} %get-tuple-element.22, f32[128,32]{1,0:T(8,128)} %get-tuple-element.23, f32[128,32]{1,0:T(8,128)} %get-tuple-element.24), dimensions={1} | concatenate | bytes 2162688 | tf_op jit(solution)/shard_map/concatenate | solution.py:332
  31.4 0.1 fusion.37
  31.5 0.1 concatenate.41
  31.8 1.5 %collective-permute-done.8 = bf16[8,8,2208]{2,1,0:T(8,128)(2,1)S(1)} collective-permute-done((bf16[8,8,2208]{2,1,0:T(8,128)(2,1)S(1)}, bf16[8,8,2208]{2,1,0:T(8,128)(2,1)S(1)}, u32[]{:S(2)}, u32[]{:S(2)}) %collective-permute-start.8) | collective-permute-done | bytes 282656 | tf_op jit(solution)/shard_map/ppermute | solution.py:23
  33.4 0.1 concatenate.42
  33.5 0.1 fusion.38
  33.6 0.4 fusion.6
  34.0 0.5 fusion
  34.5 0.1 concatenate.43
  34.7 0.1 fusion.42
  34.8 0.1 concatenate.44
  34.9 1.4 %collective-permute-start.9 = (bf16[4,8,2208]{2,1,0:T(8,128)(2,1)S(1)}, bf16[4,8,2208]{2,1,0:T(8,128)(2,1)S(1)}, u32[]{:S(2)}, u32[]{:S(2)}) collective-permute-start(bf16[4,8,2208]{2,1,0:T(8,128)(2,1)S(1)} %concatenate.44), channel_id=1, source_target_pairs={{0,2},{1,3},{2,0},{3,1},{4,6},{5,7},{6,4},{7,5},{8,10},{9,11},{10,... | collective-permute-start | bytes 423944 | tf_op jit(solution)/shard_map/ppermute | solution.py:23
  36.4 4.4 %collective-permute-done.9 = bf16[4,8,2208]{2,1,0:T(8,128)(2,1)S(1)} collective-permute-done((bf16[4,8,2208]{2,1,0:T(8,128)(2,1)S(1)}, bf16[4,8,2208]{2,1,0:T(8,128)(2,1)S(1)}, u32[]{:S(2)}, u32[]{:S(2)}) %collective-permute-start.9) | collective-permute-done | bytes 141344 | tf_op jit(solution)/shard_map/ppermute | solution.py:23
  41.0 0.1 select_bitcast_fusion.3
  41.1 0.1 pad_maximum_fusion
  41.2 0.1 copy.20
  41.3 1.0 %fusion.64 = (bf16[128,2048]{1,0:T(8,128)(2,1)}, bf16[128,2048]{1,0:T(8,128)(2,1)}) fusion(bf16[128,4096]{1,0:T(8,128)(2,1)S(1)} %bitcast.93), kind=kLoop, calls=%fused_computation.164 | loop fusion | bytes 2097152 | tf_op jit(solution)/shard_map/slice | solution.py:331
  42.3 5.5 %shard_map.78.refs_0_ = bf16[512,2048]{1,0:T(8,128)(2,1)} custom-call(bf16[512,2048]{1,0:T(8,128)(2,1)} %query_ref.3, bf16[128,2048]{1,0:T(8,128)(2,1)} %get-tuple-element.41.key_ref, bf16[128,2048]{1,0:T(8,128)(2,1)} %get-tuple-element.40.value_ref), custom_call_target="tpu_custom_call" | custom-call | flops 536870912 | bytes 2621440 | tf_op jit(solution)/shard_map/pallas_call | solution.py:237
  47.9 0.1 fusion.43
  48.0 0.3 convolution_multiply_fusion.1
  48.3 0.3 fusion.1
  48.7 0.1 fusion.47
  48.8 0.1 concatenate.47
  49.0 4.3 %collective-permute-done.11 = bf16[2,8,2208]{2,1,0:T(8,128)(2,1)S(1)} collective-permute-done((bf16[2,8,2208]{2,1,0:T(8,128)(2,1)S(1)}, bf16[2,8,2208]{2,1,0:T(8,128)(2,1)S(1)}, u32[]{:S(2)}, u32[]{:S(2)}) %collective-permute-start.11) | collective-permute-done | bytes 70688 | tf_op jit(solution)/shard_map/ppermute | solution.py:23
  53.4 0.1 fusion.50
  53.5 0.3 fusion.5
  53.8 0.3 fusion.2
  54.3 0.1 concatenate.50
  54.3 0.8 %collective-permute-start.12 = (bf16[1,8,2208]{2,1,0:T(8,128)(2,1)S(1)}, bf16[1,8,2208]{2,1,0:T(8,128)(2,1)S(1)}, u32[]{:S(2)}, u32[]{:S(2)}) collective-permute-start(bf16[1,8,2208]{2,1,0:T(8,128)(2,1)S(1)} %concatenate.50), channel_id=1, source_target_pairs={{0,8},{1,9},{2,10},{3,11},{4,12},{5,13},{6,14},{7,15},{8,0},{9,1},... | collective-permute-start | bytes 105992 | tf_op jit(solution)/shard_map/ppermute | solution.py:23
  55.2 5.6 %shard_map.79 = bf16[512,2048]{1,0:T(8,128)(2,1)} custom-call(bf16[512,2048]{1,0:T(8,128)(2,1)} %query_ref.3, bf16[128,2048]{1,0:T(8,128)(2,1)} %get-tuple-element.41.key_ref, bf16[128,2048]{1,0:T(8,128)(2,1)} %get-tuple-element.40.value_ref, bf16[512,2048]{1,0:T(8,128)(2,1)} %shard_map.78.refs_0_), custom_call_target="tpu_custom_call", output_to_operand_aliasing={{}: (3, {})} | custom-call | flops 536870912 | bytes 2621440 | tf_op jit(solution)/shard_map/pallas_call | solution.py:237
  60.8 0.1 concatenate.51
  60.9 0.2 convolution_multiply_fusion.5
  61.2 0.3 fusion.3
  61.4 0.9 %fusion.4 = bf16[8,2048]{1,0:T(8,128)(2,1)} fusion(f32[8,2048]{1,0:T(8,128)S(1)} %fusion.3, s32[2048]{0:T(1024)S(1)} %get-tuple-element.92, s32[2048]{0:T(1024)S(1)} %get-tuple-element.93, pred[2048]{0:T(1024)(128)(4,1)S(1)} %fusion.51, f32[8,2112]{1,0:T(8,128)S(1)} %bitcast.112, f32[8,2112]{1,0:T(8,128)S(1)} %get-tuple-element.70), kind=kOutput, calls=%fused_computation.11 | convolution fusion | flops 6456832 | bytes 133120 | tf_op jit(solution)/shard_map/dot_general | solution.py:16
  (46 shorter events, 1.7 us)
Async XLA Ops:
  0.6 8.4 %collective-permute-start.4 = (bf16[1,8,2048]{2,1,0:T(8,128)(2,1)}, bf16[1,8,2048]{2,1,0:T(8,128)(2,1)S(1)}, u32[]{:S(2)}, u32[]{:S(2)}) collective-permute-start(bf16[1,8,2048]{2,1,0:T(8,128)(2,1)} %bitcast.113), channel_id=1, source_target_pairs={{0,8},{1,9},{2,10},{3,11},{4,12},{5,13},{6,14},{7,15},{8,0},{9,1},... | collective-permute-start | bytes 98312 | tf_op jit(solution)/shard_map/ppermute | solution.py:71
  4.7 4.3 %collective-permute-start.3 = (bf16[1,8,2048]{2,1,0:T(8,128)(2,1)}, bf16[1,8,2048]{2,1,0:T(8,128)(2,1)S(1)}, u32[]{:S(2)}, u32[]{:S(2)}) collective-permute-start(bf16[1,8,2048]{2,1,0:T(8,128)(2,1)} %bitcast.114), channel_id=1, source_target_pairs={{0,4},{1,5},{2,6},{3,7},{4,0},{5,1},{6,2},{7,3},{8,12},{9,13},{10,... | collective-permute-start | bytes 98312 | tf_op jit(solution)/shard_map/ppermute | solution.py:71
  6.3 5.9 %collective-permute-start.2 = (bf16[1,8,2048]{2,1,0:T(8,128)(2,1)}, bf16[1,8,2048]{2,1,0:T(8,128)(2,1)S(1)}, u32[]{:S(2)}, u32[]{:S(2)}) collective-permute-start(bf16[1,8,2048]{2,1,0:T(8,128)(2,1)} %bitcast.115), channel_id=1, source_target_pairs={{0,12},{1,13},{2,14},{3,15},{4,8},{5,9},{6,10},{7,11},{8,4},{9,5},... | collective-permute-start | bytes 98312 | tf_op jit(solution)/shard_map/ppermute | solution.py:71
  7.1 7.5 %collective-permute-start = (bf16[1,8,4096]{2,1,0:T(8,128)(2,1)S(1)}, bf16[1,8,4096]{2,1,0:T(8,128)(2,1)S(1)}, u32[]{:S(2)}, u32[]{:S(2)}) collective-permute-start(bf16[1,8,4096]{2,1,0:T(8,128)(2,1)S(1)} %maximum_bitcast_fusion.2), channel_id=1, source_target_pairs={{0,8},{1,9},{2,10},{3,11},{4,12},{5,13},{6,14},{7,15},{8,0},{9,1},... | collective-permute-start | bytes 196616 | tf_op jit(solution)/shard_map/ppermute | solution.py:23
  13.0 5.0 %collective-permute-start.5 = (bf16[4,8,2048]{2,1,0:T(8,128)(2,1)S(1)}, bf16[4,8,2048]{2,1,0:T(8,128)(2,1)S(1)}, u32[]{:S(2)}, u32[]{:S(2)}) collective-permute-start(bf16[4,8,2048]{2,1,0:T(8,128)(2,1)S(1)} %maximum_bitcast_fusion.1), channel_id=1, source_target_pairs={{0,2},{1,3},{2,0},{3,1},{4,6},{5,7},{6,4},{7,5},{8,10},{9,11},{10,... | collective-permute-start | bytes 393224 | tf_op jit(solution)/shard_map/ppermute | solution.py:71
  15.5 5.0 %collective-permute-start.1 = (bf16[2,8,4096]{2,1,0:T(8,128)(2,1)S(1)}, bf16[2,8,4096]{2,1,0:T(8,128)(2,1)S(1)}, u32[]{:S(2)}, u32[]{:S(2)}) collective-permute-start(bf16[2,8,4096]{2,1,0:T(8,128)(2,1)S(1)} %maximum_bitcast_fusion), channel_id=1, source_target_pairs={{0,4},{1,5},{2,6},{3,7},{4,0},{5,1},{6,2},{7,3},{8,12},{9,13},{10,... | collective-permute-start | bytes 393224 | tf_op jit(solution)/shard_map/ppermute | solution.py:23
  18.1 2.4 %collective-permute-start.6 = (bf16[8,8,2048]{2,1,0:T(8,128)(2,1)S(1)}, bf16[8,8,2048]{2,1,0:T(8,128)(2,1)S(1)}, u32[]{:S(2)}, u32[]{:S(2)}) collective-permute-start(bf16[8,8,2048]{2,1,0:T(8,128)(2,1)S(1)} %bitcast.101), channel_id=1, source_target_pairs={{0,1},{1,0},{2,3},{3,2},{4,5},{5,4},{6,7},{7,6},{8,9},{9,8},{10,11... | collective-permute-start | bytes 786440 | tf_op jit(solution)/shard_map/ppermute | solution.py:71
  21.5 8.5 %collective-permute-start.7 = (bf16[4,8,4096]{2,1,0:T(8,128)(2,1)S(1)}, bf16[4,8,4096]{2,1,0:T(8,128)(2,1)S(1)}, u32[]{:S(2)}, u32[]{:S(2)}) collective-permute-start(bf16[4,8,4096]{2,1,0:T(8,128)(2,1)S(1)} %bitcast.102), channel_id=1, source_target_pairs={{0,2},{1,3},{2,0},{3,1},{4,6},{5,7},{6,4},{7,5},{8,10},{9,11},{10,... | collective-permute-start | bytes 786440 | tf_op jit(solution)/shard_map/ppermute | solution.py:23
  31.6 1.6 %collective-permute-start.8 = (bf16[8,8,2208]{2,1,0:T(8,128)(2,1)S(1)}, bf16[8,8,2208]{2,1,0:T(8,128)(2,1)S(1)}, u32[]{:S(2)}, u32[]{:S(2)}) collective-permute-start(bf16[8,8,2208]{2,1,0:T(8,128)(2,1)S(1)} %concatenate.41), channel_id=1, source_target_pairs={{0,1},{1,0},{2,3},{3,2},{4,5},{5,4},{6,7},{7,6},{8,9},{9,8},{10,11... | collective-permute-start | bytes 847880 | tf_op jit(solution)/shard_map/ppermute | solution.py:23
  34.9 5.9 %collective-permute-start.9 = (bf16[4,8,2208]{2,1,0:T(8,128)(2,1)S(1)}, bf16[4,8,2208]{2,1,0:T(8,128)(2,1)S(1)}, u32[]{:S(2)}, u32[]{:S(2)}) collective-permute-start(bf16[4,8,2208]{2,1,0:T(8,128)(2,1)S(1)} %concatenate.44), channel_id=1, source_target_pairs={{0,2},{1,3},{2,0},{3,1},{4,6},{5,7},{6,4},{7,5},{8,10},{9,11},{10,... | collective-permute-start | bytes 423944 | tf_op jit(solution)/shard_map/ppermute | solution.py:23
  36.3 4.6 %collective-permute-start.10 = (bf16[8,8,4096]{2,1,0:T(8,128)(2,1)S(1)}, bf16[8,8,4096]{2,1,0:T(8,128)(2,1)S(1)}, u32[]{:S(2)}, u32[]{:S(2)}) collective-permute-start(bf16[8,8,4096]{2,1,0:T(8,128)(2,1)S(1)} %bitcast.98), channel_id=1, source_target_pairs={{0,1},{1,0},{2,3},{3,2},{4,5},{5,4},{6,7},{7,6},{8,9},{9,8},{10,11... | collective-permute-start | bytes 1572872 | tf_op jit(solution)/shard_map/ppermute | solution.py:23
  48.9 4.4 %collective-permute-start.11 = (bf16[2,8,2208]{2,1,0:T(8,128)(2,1)S(1)}, bf16[2,8,2208]{2,1,0:T(8,128)(2,1)S(1)}, u32[]{:S(2)}, u32[]{:S(2)}) collective-permute-start(bf16[2,8,2208]{2,1,0:T(8,128)(2,1)S(1)} %concatenate.47), channel_id=1, source_target_pairs={{0,4},{1,5},{2,6},{3,7},{4,0},{5,1},{6,2},{7,3},{8,12},{9,13},{10,... | collective-permute-start | bytes 211976 | tf_op jit(solution)/shard_map/ppermute | solution.py:23
  54.3 6.4 %collective-permute-start.12 = (bf16[1,8,2208]{2,1,0:T(8,128)(2,1)S(1)}, bf16[1,8,2208]{2,1,0:T(8,128)(2,1)S(1)}, u32[]{:S(2)}, u32[]{:S(2)}) collective-permute-start(bf16[1,8,2208]{2,1,0:T(8,128)(2,1)S(1)} %concatenate.50), channel_id=1, source_target_pairs={{0,8},{1,9},{2,10},{3,11},{4,12},{5,13},{6,14},{7,15},{8,0},{9,1},... | collective-permute-start | bytes 105992 | tf_op jit(solution)/shard_map/ppermute | solution.py:23

commit v22 on v20

--- a/solution.py
+++ b/solution.py
@@ -249,7 +249,7 @@
     )(*operands)
 
 
-AUDIO_STEP = 4
+AUDIO_STEP = 8
 
 
 def audio_kernel(query_ref, key_ref, value_ref, sum_ref, total_ref, top_ref):

time: 60.6 us -> 60.8 us (level)
  no operation moved by 1% of the time
where the time goes in v22:
time: 60.8 us; the launch traced here: 60.3 us
  Pallas kernels  22.1 us (36%)
  starting transfers between devices  14.1 us (23%)
  waiting for transfers between devices  11.4 us (19%)
  local copies, waits for them, and re-layouts  4.34 us (7%)
  other arithmetic  4.03 us (7%)
  matrix products  3.46 us (6%)
  between operations  0.93 us (2%)
    pallas_call x4, Pallas kernels, video_part(): pl.pallas_call(video_kernel, grid=(pairs // PER_STEP,), in_specs=specs, o...  14.1 us
    pallas_call x1, Pallas kernels, audio_partial(): pl.pallas_call(audio_kernel, grid=(heads // 2 // AUDIO_STEP,), in_specs=[...  7.99 us
    ppermute x5, starting transfers between devices, gather_levels(): pieces[offset] = lax.ppermute(held, 'seq', pairs)  7.34 us
    ppermute x8, starting transfers between devices, exchange(): return lax.ppermute(value, 'seq', pairs)  6.77 us
    ppermute x5, waiting for transfers between devices, gather_levels(): pieces[offset] = lax.ppermute(held, 'seq', pairs)  5.74 us
    ppermute x8, waiting for transfers between devices, exchange(): return lax.ppermute(value, 'seq', pairs)  5.65 us
    dot_general x9, matrix products, spread(): jnp.dot(scales, expand, precision=lax.Precision.HIGHEST, preferred_elemen...  3.46 us
    concatenate x1, local copies, waits for them, and re-layouts, local(): jnp.concatenate([part[0] for part in parts] + [part[1] for part in parts]...  1.34 us
  transfers between devices with their start and end apart: 13, of which 7 were waited for; matrix products, arithmetic and copies ran while one was open for 5% of the time, Pallas kernels for 31%

profile of v22, /device:TPU:0, one launch (start us, length us, event | category | flops | bytes accessed | tf_op | source)
XLA Modules:
  0.0 60.3 jit_solution(3357272966825889842)
XLA Ops:
  0.6 4.1 %collective-permute-start.4 = (bf16[1,8,2048]{2,1,0:T(8,128)(2,1)}, bf16[1,8,2048]{2,1,0:T(8,128)(2,1)S(1)}, u32[]{:S(2)}, u32[]{:S(2)}) collective-permute-start(bf16[1,8,2048]{2,1,0:T(8,128)(2,1)} %bitcast.111), channel_id=1, source_target_pairs={{0,8},{1,9},{2,10},{3,11},{4,12},{5,13},{6,14},{7,15},{8,0},{9,1},... | collective-permute-start | bytes 98312 | tf_op jit(solution)/shard_map/ppermute | solution.py:71
  4.7 1.6 %collective-permute-start.3 = (bf16[1,8,2048]{2,1,0:T(8,128)(2,1)}, bf16[1,8,2048]{2,1,0:T(8,128)(2,1)S(1)}, u32[]{:S(2)}, u32[]{:S(2)}) collective-permute-start(bf16[1,8,2048]{2,1,0:T(8,128)(2,1)} %bitcast.112), channel_id=1, source_target_pairs={{0,4},{1,5},{2,6},{3,7},{4,0},{5,1},{6,2},{7,3},{8,12},{9,13},{10,... | collective-permute-start | bytes 98312 | tf_op jit(solution)/shard_map/ppermute | solution.py:71
  6.3 0.8 %maximum_bitcast_fusion.2 = bf16[1,8,4096]{2,1,0:T(8,128)(2,1)S(1)} fusion(bf16[8,2048]{1,0:T(8,128)(2,1)} %param.11, bf16[8,2048]{1,0:T(8,128)(2,1)} %param.10), kind=kLoop, calls=%fused_computation.74 | loop fusion | flops 131072 | bytes 131072 | tf_op jit(solution)/shard_map/broadcast_in_dim | solution.py:29
  7.1 1.9 %collective-permute-start = (bf16[1,8,4096]{2,1,0:T(8,128)(2,1)S(1)}, bf16[1,8,4096]{2,1,0:T(8,128)(2,1)S(1)}, u32[]{:S(2)}, u32[]{:S(2)}) collective-permute-start(bf16[1,8,4096]{2,1,0:T(8,128)(2,1)S(1)} %maximum_bitcast_fusion.2), channel_id=1, source_target_pairs={{0,8},{1,9},{2,10},{3,11},{4,12},{5,13},{6,14},{7,15},{8,0},{9,1},... | collective-permute-start | bytes 196616 | tf_op jit(solution)/shard_map/ppermute | solution.py:23
  9.0 3.2 %collective-permute-done.2 = bf16[1,8,2048]{2,1,0:T(8,128)(2,1)S(1)} collective-permute-done((bf16[1,8,2048]{2,1,0:T(8,128)(2,1)}, bf16[1,8,2048]{2,1,0:T(8,128)(2,1)S(1)}, u32[]{:S(2)}, u32[]{:S(2)}) %collective-permute-start.2) | collective-permute-done | bytes 32800 | tf_op jit(solution)/shard_map/ppermute | solution.py:71
  12.2 0.8 %select_bitcast_fusion.23 = (bf16[1,1,8,2048]{3,2,1,0:T(8,128)(2,1)S(1)}, bf16[1,1,8,2048]{3,2,1,0:T(8,128)(2,1)S(1)}, bf16[1,1,8,2048]{3,2,1,0:T(8,128)(2,1)S(1)}, bf16[1,1,8,2048]{3,2,1,0:T(8,128)(2,1)S(1)}) fusion(bf16[1,8,2048]{2,1,0:T(8,128)(2,1)S(1)} %collective-permute-done.2, bf16[1,8,2048]{2,1,0:T(8,128)(2,1)S(1)} %collective-permute-done.3, ...), kind=kLoop, calls=%fused_computation.98 | loop fusion | flops 196608 | bytes 262156 | tf_op jit(solution)/shard_map/stack | solution.py:79
  13.0 1.6 %collective-permute-start.5 = (bf16[4,8,2048]{2,1,0:T(8,128)(2,1)S(1)}, bf16[4,8,2048]{2,1,0:T(8,128)(2,1)S(1)}, u32[]{:S(2)}, u32[]{:S(2)}) collective-permute-start(bf16[4,8,2048]{2,1,0:T(8,128)(2,1)S(1)} %maximum_bitcast_fusion.1), channel_id=1, source_target_pairs={{0,2},{1,3},{2,0},{3,1},{4,6},{5,7},{6,4},{7,5},{8,10},{9,11},{10,... | collective-permute-start | bytes 393224 | tf_op jit(solution)/shard_map/ppermute | solution.py:71
  14.6 0.8 %select_bitcast_fusion.19 = (bf16[1,1,8,4096]{3,2,1,0:T(8,128)(2,1)S(1)}, bf16[1,1,8,4096]{3,2,1,0:T(8,128)(2,1)S(1)}) fusion(bf16[1,8,4096]{2,1,0:T(8,128)(2,1)S(1)} %collective-permute-done, pred[]{:T(512)S(6)} %ne.98, bf16[8,2048]{1,0:T(8,128)(2,1)} %param.11, bf16[8,2048]{1,0:T(8,128)(2,1)} %param.10), kind=kLoop, calls=%fused_computation.76 | loop fusion | flops 196608 | bytes 262145 | tf_op jit(solution)/shard_map/stack | solution.py:45
  15.5 0.1 collective-permute-start.1
  15.6 2.5 %collective-permute-done.5 = bf16[4,8,2048]{2,1,0:T(8,128)(2,1)S(1)} collective-permute-done((bf16[4,8,2048]{2,1,0:T(8,128)(2,1)S(1)}, bf16[4,8,2048]{2,1,0:T(8,128)(2,1)S(1)}, u32[]{:S(2)}, u32[]{:S(2)}) %collective-permute-start.5) | collective-permute-done | bytes 131104 | tf_op jit(solution)/shard_map/ppermute | solution.py:71
  18.2 2.3 %collective-permute-done.1 = bf16[2,8,4096]{2,1,0:T(8,128)(2,1)S(1)} collective-permute-done((bf16[2,8,4096]{2,1,0:T(8,128)(2,1)S(1)}, bf16[2,8,4096]{2,1,0:T(8,128)(2,1)S(1)}, u32[]{:S(2)}, u32[]{:S(2)}) %collective-permute-start.1) | collective-permute-done | bytes 131104 | tf_op jit(solution)/shard_map/ppermute | solution.py:23
  20.7 0.8 %copy.20 = bf16[8,2,8,2048]{3,2,1,0:T(8,128)(2,1)} copy(bf16[8,2,8,2048]{3,2,0,1:T(8,128)(2,1)S(1)} %pad_maximum_fusion.1) | data formatting | bytes 1048576 | tf_op jit(solution)/shard_map/stack | solution.py:79
  21.5 0.7 %collective-permute-start.7 = (bf16[4,8,4096]{2,1,0:T(8,128)(2,1)S(1)}, bf16[4,8,4096]{2,1,0:T(8,128)(2,1)S(1)}, u32[]{:S(2)}, u32[]{:S(2)}) collective-permute-start(bf16[4,8,4096]{2,1,0:T(8,128)(2,1)S(1)} %bitcast.99), channel_id=1, source_target_pairs={{0,2},{1,3},{2,0},{3,1},{4,6},{5,7},{6,4},{7,5},{8,10},{9,11},{10,... | collective-permute-start | bytes 786440 | tf_op jit(solution)/shard_map/ppermute | solution.py:23
  22.2 8.0 %shard_map.77 = (f32[128,2048]{1,0:T(8,128)}, f32[128,32]{1,0:T(8,128)}, f32[128,32]{1,0:T(8,128)}) custom-call(bf16[128,2048]{1,0:T(8,128)(2,1)} %bitcast.96, bf16[512,2048]{1,0:T(8,128)(2,1)} %key_ref.1, bf16[512,2048]{1,0:T(8,128)(2,1)} %value_ref.1), custom_call_target="tpu_custom_call" | custom-call | flops 1073741824 | bytes 5767168 | tf_op jit(solution)/shard_map/pallas_call | solution.py:286
  30.2 1.3 %concatenate.40 = f32[128,2112]{1,0:T(8,128)S(1)} concatenate(f32[128,2048]{1,0:T(8,128)} %get-tuple-element.30, f32[128,32]{1,0:T(8,128)} %get-tuple-element.31, f32[128,32]{1,0:T(8,128)} %get-tuple-element.32), dimensions={1} | concatenate | bytes 2162688 | tf_op jit(solution)/shard_map/concatenate | solution.py:332
  31.6 0.1 fusion.35
  31.8 0.1 concatenate.41
  32.1 0.6 collective-permute-start.9
  32.7 0.9 %collective-permute-done.8 = bf16[8,8,2208]{2,1,0:T(8,128)(2,1)S(1)} collective-permute-done((bf16[8,8,2208]{2,1,0:T(8,128)(2,1)S(1)}, bf16[8,8,2208]{2,1,0:T(8,128)(2,1)S(1)}, u32[]{:S(2)}, u32[]{:S(2)}) %collective-permute-start.8) | collective-permute-done | bytes 282656 | tf_op jit(solution)/shard_map/ppermute | solution.py:23
  33.7 0.1 concatenate.42
  33.7 0.5 collective-permute-done.9
  34.3 0.1 select_bitcast_fusion.3
  34.4 0.1 pad_maximum_fusion
  34.5 0.1 copy.22
  34.6 1.0 %fusion.62 = (bf16[128,2048]{1,0:T(8,128)(2,1)}, bf16[128,2048]{1,0:T(8,128)(2,1)}) fusion(bf16[128,4096]{1,0:T(8,128)(2,1)S(1)} %bitcast.93), kind=kLoop, calls=%fused_computation.162 | loop fusion | bytes 2097152 | tf_op jit(solution)/shard_map/slice | solution.py:331
  35.6 3.5 %shard_map.78.refs_0_ = bf16[512,2048]{1,0:T(8,128)(2,1)} custom-call(bf16[512,2048]{1,0:T(8,128)(2,1)} %query_ref.7, bf16[128,2048]{1,0:T(8,128)(2,1)} %get-tuple-element.57.key_ref, bf16[128,2048]{1,0:T(8,128)(2,1)} %get-tuple-element.56.value_ref), custom_call_target="tpu_custom_call" | custom-call | flops 268435456 | bytes 1310720 | tf_op jit(solution)/shard_map/pallas_call | solution.py:237
  39.2 0.1 fusion.36
  39.3 0.4 convolution_multiply_fusion.1
  39.7 0.4 fusion
  40.2 0.1 concatenate.43
  40.4 0.1 concatenate.44
  40.5 1.4 %collective-permute-start.10 = (bf16[4,8,2208]{2,1,0:T(8,128)(2,1)S(1)}, bf16[4,8,2208]{2,1,0:T(8,128)(2,1)S(1)}, u32[]{:S(2)}, u32[]{:S(2)}) collective-permute-start(bf16[4,8,2208]{2,1,0:T(8,128)(2,1)S(1)} %concatenate.44), channel_id=1, source_target_pairs={{0,2},{1,3},{2,0},{3,1},{4,6},{5,7},{6,4},{7,5},{8,10},{9,11},{10,... | collective-permute-start | bytes 423944 | tf_op jit(solution)/shard_map/ppermute | solution.py:23
  41.8 3.5 %shard_map.79.refs_0_ = bf16[512,2048]{1,0:T(8,128)(2,1)} custom-call(bf16[512,2048]{1,0:T(8,128)(2,1)} %query_ref.7, bf16[128,2048]{1,0:T(8,128)(2,1)} %get-tuple-element.57.key_ref, bf16[128,2048]{1,0:T(8,128)(2,1)} %get-tuple-element.56.value_ref, bf16[512,2048]{1,0:T(8,128)(2,1)} %shard_map.78.refs_0_), custom_call_target="tpu_custom_call", output_to_operand_aliasing={{}: (3, {})} | custom-call | flops 268435456 | bytes 1310720 | tf_op jit(solution)/shard_map/pallas_call | solution.py:237
  45.4 1.2 %collective-permute-done.10 = bf16[4,8,2208]{2,1,0:T(8,128)(2,1)S(1)} collective-permute-done((bf16[4,8,2208]{2,1,0:T(8,128)(2,1)S(1)}, bf16[4,8,2208]{2,1,0:T(8,128)(2,1)S(1)}, u32[]{:S(2)}, u32[]{:S(2)}) %collective-permute-start.10) | collective-permute-done | bytes 141344 | tf_op jit(solution)/shard_map/ppermute | solution.py:23
  46.7 0.1 fusion.41
  46.8 0.3 convolution_multiply_fusion.2
  47.2 0.3 fusion.1
  47.7 0.1 concatenate.47
  47.9 3.5 %shard_map.80.refs_0_ = bf16[512,2048]{1,0:T(8,128)(2,1)} custom-call(bf16[512,2048]{1,0:T(8,128)(2,1)} %query_ref.7, bf16[128,2048]{1,0:T(8,128)(2,1)} %get-tuple-element.57.key_ref, bf16[128,2048]{1,0:T(8,128)(2,1)} %get-tuple-element.56.value_ref, bf16[512,2048]{1,0:T(8,128)(2,1)} %shard_map.79.refs_0_), custom_call_target="tpu_custom_call", output_to_operand_aliasing={{}: (3, {})} | custom-call | flops 268435456 | bytes 1310720 | tf_op jit(solution)/shard_map/pallas_call | solution.py:237
  51.4 0.8 %collective-permute-done.11 = bf16[2,8,2208]{2,1,0:T(8,128)(2,1)S(1)} collective-permute-done((bf16[2,8,2208]{2,1,0:T(8,128)(2,1)S(1)}, bf16[2,8,2208]{2,1,0:T(8,128)(2,1)S(1)}, u32[]{:S(2)}, u32[]{:S(2)}) %collective-permute-start.11) | collective-permute-done | bytes 70688 | tf_op jit(solution)/shard_map/ppermute | solution.py:23
  52.4 0.3 convolution_multiply_fusion.5
  52.7 0.3 fusion.2
  53.2 0.1 concatenate.50
  53.2 2.0 %collective-permute-start.12 = (bf16[1,8,2208]{2,1,0:T(8,128)(2,1)S(1)}, bf16[1,8,2208]{2,1,0:T(8,128)(2,1)S(1)}, u32[]{:S(2)}, u32[]{:S(2)}) collective-permute-start(bf16[1,8,2208]{2,1,0:T(8,128)(2,1)S(1)} %concatenate.50), channel_id=1, source_target_pairs={{0,8},{1,9},{2,10},{3,11},{4,12},{5,13},{6,14},{7,15},{8,0},{9,1},... | collective-permute-start | bytes 105992 | tf_op jit(solution)/shard_map/ppermute | solution.py:23
  55.3 3.5 %shard_map.81 = bf16[512,2048]{1,0:T(8,128)(2,1)} custom-call(bf16[512,2048]{1,0:T(8,128)(2,1)} %query_ref.7, bf16[128,2048]{1,0:T(8,128)(2,1)} %get-tuple-element.57.key_ref, bf16[128,2048]{1,0:T(8,128)(2,1)} %get-tuple-element.56.value_ref, bf16[512,2048]{1,0:T(8,128)(2,1)} %shard_map.80.refs_0_), custom_call_target="tpu_custom_call", output_to_operand_aliasing={{}: (3, {})} | custom-call | flops 268435456 | bytes 1310720 | tf_op jit(solution)/shard_map/pallas_call | solution.py:237
  58.9 0.2 convolution_multiply_fusion.7
  59.2 0.3 fusion.3
  59.5 0.9 %fusion.4 = bf16[8,2048]{1,0:T(8,128)(2,1)} fusion(f32[8,2048]{1,0:T(8,128)S(1)} %fusion.3, s32[2048]{0:T(1024)S(1)} %get-tuple-element.108, s32[2048]{0:T(1024)S(1)} %get-tuple-element.109, pred[2048]{0:T(1024)(128)(4,1)S(1)} %fusion.49, f32[8,2112]{1,0:T(8,128)S(1)} %bitcast.110, f32[8,2112]{1,0:T(8,128)S(1)} %get-tuple-element.86), kind=kOutput, calls=%fused_computation.13 | convolution fusion | flops 6456832 | bytes 133120 | tf_op jit(solution)/shard_map/dot_general | solution.py:16
  (48 shorter events, 1.9 us)
Async XLA Ops:
  0.6 8.4 %collective-permute-start.4 = (bf16[1,8,2048]{2,1,0:T(8,128)(2,1)}, bf16[1,8,2048]{2,1,0:T(8,128)(2,1)S(1)}, u32[]{:S(2)}, u32[]{:S(2)}) collective-permute-start(bf16[1,8,2048]{2,1,0:T(8,128)(2,1)} %bitcast.111), channel_id=1, source_target_pairs={{0,8},{1,9},{2,10},{3,11},{4,12},{5,13},{6,14},{7,15},{8,0},{9,1},... | collective-permute-start | bytes 98312 | tf_op jit(solution)/shard_map/ppermute | solution.py:71
  4.7 4.3 %collective-permute-start.3 = (bf16[1,8,2048]{2,1,0:T(8,128)(2,1)}, bf16[1,8,2048]{2,1,0:T(8,128)(2,1)S(1)}, u32[]{:S(2)}, u32[]{:S(2)}) collective-permute-start(bf16[1,8,2048]{2,1,0:T(8,128)(2,1)} %bitcast.112), channel_id=1, source_target_pairs={{0,4},{1,5},{2,6},{3,7},{4,0},{5,1},{6,2},{7,3},{8,12},{9,13},{10,... | collective-permute-start | bytes 98312 | tf_op jit(solution)/shard_map/ppermute | solution.py:71
  6.3 5.9 %collective-permute-start.2 = (bf16[1,8,2048]{2,1,0:T(8,128)(2,1)}, bf16[1,8,2048]{2,1,0:T(8,128)(2,1)S(1)}, u32[]{:S(2)}, u32[]{:S(2)}) collective-permute-start(bf16[1,8,2048]{2,1,0:T(8,128)(2,1)} %bitcast.113), channel_id=1, source_target_pairs={{0,12},{1,13},{2,14},{3,15},{4,8},{5,9},{6,10},{7,11},{8,4},{9,5},... | collective-permute-start | bytes 98312 | tf_op jit(solution)/shard_map/ppermute | solution.py:71
  7.1 7.5 %collective-permute-start = (bf16[1,8,4096]{2,1,0:T(8,128)(2,1)S(1)}, bf16[1,8,4096]{2,1,0:T(8,128)(2,1)S(1)}, u32[]{:S(2)}, u32[]{:S(2)}) collective-permute-start(bf16[1,8,4096]{2,1,0:T(8,128)(2,1)S(1)} %maximum_bitcast_fusion.2), channel_id=1, source_target_pairs={{0,8},{1,9},{2,10},{3,11},{4,12},{5,13},{6,14},{7,15},{8,0},{9,1},... | collective-permute-start | bytes 196616 | tf_op jit(solution)/shard_map/ppermute | solution.py:23
  13.0 5.0 %collective-permute-start.5 = (bf16[4,8,2048]{2,1,0:T(8,128)(2,1)S(1)}, bf16[4,8,2048]{2,1,0:T(8,128)(2,1)S(1)}, u32[]{:S(2)}, u32[]{:S(2)}) collective-permute-start(bf16[4,8,2048]{2,1,0:T(8,128)(2,1)S(1)} %maximum_bitcast_fusion.1), channel_id=1, source_target_pairs={{0,2},{1,3},{2,0},{3,1},{4,6},{5,7},{6,4},{7,5},{8,10},{9,11},{10,... | collective-permute-start | bytes 393224 | tf_op jit(solution)/shard_map/ppermute | solution.py:71
  15.5 5.0 %collective-permute-start.1 = (bf16[2,8,4096]{2,1,0:T(8,128)(2,1)S(1)}, bf16[2,8,4096]{2,1,0:T(8,128)(2,1)S(1)}, u32[]{:S(2)}, u32[]{:S(2)}) collective-permute-start(bf16[2,8,4096]{2,1,0:T(8,128)(2,1)S(1)} %maximum_bitcast_fusion), channel_id=1, source_target_pairs={{0,4},{1,5},{2,6},{3,7},{4,0},{5,1},{6,2},{7,3},{8,12},{9,13},{10,... | collective-permute-start | bytes 393224 | tf_op jit(solution)/shard_map/ppermute | solution.py:23
  18.1 2.4 %collective-permute-start.6 = (bf16[8,8,2048]{2,1,0:T(8,128)(2,1)S(1)}, bf16[8,8,2048]{2,1,0:T(8,128)(2,1)S(1)}, u32[]{:S(2)}, u32[]{:S(2)}) collective-permute-start(bf16[8,8,2048]{2,1,0:T(8,128)(2,1)S(1)} %bitcast.98), channel_id=1, source_target_pairs={{0,1},{1,0},{2,3},{3,2},{4,5},{5,4},{6,7},{7,6},{8,9},{9,8},{10,11... | collective-permute-start | bytes 786440 | tf_op jit(solution)/shard_map/ppermute | solution.py:71
  21.5 8.7 %collective-permute-start.7 = (bf16[4,8,4096]{2,1,0:T(8,128)(2,1)S(1)}, bf16[4,8,4096]{2,1,0:T(8,128)(2,1)S(1)}, u32[]{:S(2)}, u32[]{:S(2)}) collective-permute-start(bf16[4,8,4096]{2,1,0:T(8,128)(2,1)S(1)} %bitcast.99), channel_id=1, source_target_pairs={{0,2},{1,3},{2,0},{3,1},{4,6},{5,7},{6,4},{7,5},{8,10},{9,11},{10,... | collective-permute-start | bytes 786440 | tf_op jit(solution)/shard_map/ppermute | solution.py:23
  31.9 1.6 %collective-permute-start.8 = (bf16[8,8,2208]{2,1,0:T(8,128)(2,1)S(1)}, bf16[8,8,2208]{2,1,0:T(8,128)(2,1)S(1)}, u32[]{:S(2)}, u32[]{:S(2)}) collective-permute-start(bf16[8,8,2208]{2,1,0:T(8,128)(2,1)S(1)} %concatenate.41), channel_id=1, source_target_pairs={{0,1},{1,0},{2,3},{3,2},{4,5},{5,4},{6,7},{7,6},{8,9},{9,8},{10,11... | collective-permute-start | bytes 847880 | tf_op jit(solution)/shard_map/ppermute | solution.py:23
  32.1 2.2 %collective-permute-start.9 = (bf16[8,8,4096]{2,1,0:T(8,128)(2,1)S(1)}, bf16[8,8,4096]{2,1,0:T(8,128)(2,1)S(1)}, u32[]{:S(2)}, u32[]{:S(2)}) collective-permute-start(bf16[8,8,4096]{2,1,0:T(8,128)(2,1)S(1)} %bitcast.95), channel_id=1, source_target_pairs={{0,1},{1,0},{2,3},{3,2},{4,5},{5,4},{6,7},{7,6},{8,9},{9,8},{10,11... | collective-permute-start | bytes 1572872 | tf_op jit(solution)/shard_map/ppermute | solution.py:23
  40.5 6.1 %collective-permute-start.10 = (bf16[4,8,2208]{2,1,0:T(8,128)(2,1)S(1)}, bf16[4,8,2208]{2,1,0:T(8,128)(2,1)S(1)}, u32[]{:S(2)}, u32[]{:S(2)}) collective-permute-start(bf16[4,8,2208]{2,1,0:T(8,128)(2,1)S(1)} %concatenate.44), channel_id=1, source_target_pairs={{0,2},{1,3},{2,0},{3,1},{4,6},{5,7},{6,4},{7,5},{8,10},{9,11},{10,... | collective-permute-start | bytes 423944 | tf_op jit(solution)/shard_map/ppermute | solution.py:23
  47.8 4.4 %collective-permute-start.11 = (bf16[2,8,2208]{2,1,0:T(8,128)(2,1)S(1)}, bf16[2,8,2208]{2,1,0:T(8,128)(2,1)S(1)}, u32[]{:S(2)}, u32[]{:S(2)}) collective-permute-start(bf16[2,8,2208]{2,1,0:T(8,128)(2,1)S(1)} %concatenate.47), channel_id=1, source_target_pairs={{0,4},{1,5},{2,6},{3,7},{4,0},{5,1},{6,2},{7,3},{8,12},{9,13},{10,... | collective-permute-start | bytes 211976 | tf_op jit(solution)/shard_map/ppermute | solution.py:23
  53.2 5.5 %collective-permute-start.12 = (bf16[1,8,2208]{2,1,0:T(8,128)(2,1)S(1)}, bf16[1,8,2208]{2,1,0:T(8,128)(2,1)S(1)}, u32[]{:S(2)}, u32[]{:S(2)}) collective-permute-start(bf16[1,8,2208]{2,1,0:T(8,128)(2,1)S(1)} %concatenate.50), channel_id=1, source_target_pairs={{0,8},{1,9},{2,10},{3,11},{4,12},{5,13},{6,14},{7,15},{8,0},{9,1},... | collective-permute-start | bytes 105992 | tf_op jit(solution)/shard_map/ppermute | solution.py:23
